TPU v7x, 32 devices: a whole 2x2x4 slice. The times are simulated.
32 devices in a mesh: tm: 2 (over x), prow: 4 (over z), pcol: 4 (over y, core).
Axes of the slice: x: 2, y: 2, z: 4, core: 2. Of those that a mesh axis runs over, the one named last changes fastest.
Arguments:
- signal: bfloat16 [2048, 15360], P(('prow', 'pcol'), 'tm'), may hold values from -8 to 8
- offsets: int32 [4], replicated, may hold values from 0 to 511, as said below
- pair_list: int32 [4, 4, 4, 2], P('prow', 'pcol'), may hold values from 0 to 3, as said below
Outputs:
- correlations: bfloat16 [4, 4, 4, 128, 128, 256], P('prow', 'pcol', None, 'tm')
Inputs may be any that keep to these rules, and one draw needn't show every extreme that they name: `offsets`: some window has the largest offset. `pair_list`: entry (a, b) of cell (r, c) pairs row block r n + a with column block b n + c, n the number of devices of pcol, and the row block's number is never above the column block's; pairs may repeat.
All inputs are finite; a program needn't handle non-finite values.
Results may differ from a plain program's by a relative error of at most 0.0058.
Values may be sent and summed in bfloat16 or wider, within the bound.
No kernel may reach another device: no remote copies, remote signals or barrier semaphores. Data moves between devices by JAX's collectives and lax.ppermute only.
A program may use at most 128 MiB of HBM per device.

v0:
```python
import math

import jax
import jax.numpy as jnp
from jax import lax
from jax.sharding import PartitionSpec as P

WIN = 7680
NF = 384
K0 = 32
LAGS = 256
SPAN = 4
NP = 4
STEP = 3840
HALO = 4352


two_pi = 2.0 * math.pi


def from_behind(value, axis, steps):
    count = lax.axis_size(axis)
    initial, last = (max(0, -steps), min(count, count - steps))
    return lax.ppermute(value, axis, [(source, source + steps) for source in range(initial, last)])


def forward_table():
    sample_idx = jnp.arange(WIN, dtype=jnp.int32)
    freq_bins = K0 + jnp.arange(NF, dtype=jnp.int32)
    wrapped = sample_idx[:, None] * freq_bins[None, :] % WIN
    phase_angle = wrapped.astype(jnp.float32) * (two_pi / WIN)
    taper_curve = 0.5 - 0.5 * jnp.cos(sample_idx.astype(jnp.float32) * (two_pi / WIN))
    cosine = taper_curve[:, None] * jnp.cos(phase_angle)
    sine = -taper_curve[:, None] * jnp.sin(phase_angle)
    return jnp.concatenate([cosine, sine], axis=1).astype(jnp.bfloat16)


def lag_table(count):
    freq_bins = K0 + jnp.arange(NF, dtype=jnp.int32)
    shifted = (jnp.arange(LAGS, dtype=jnp.int32) - LAGS // 2) % WIN
    wrapped = freq_bins[:, None] * shifted[None, :] % WIN
    phase_angle = wrapped.astype(jnp.float32) * (two_pi / WIN)
    factor = 1.0 / math.sqrt(NF * count)
    return jnp.concatenate(
        [jnp.cos(phase_angle) * factor, -jnp.sin(phase_angle) * factor], axis=0
    ).astype(jnp.bfloat16)


def whiten(spectra):
    real_part = spectra[..., :NF]
    imag_part = spectra[..., NF:]
    power_sum = real_part * real_part + imag_part * imag_part
    freq_bins = jnp.arange(NF, dtype=jnp.int32)
    band_matrix = (jnp.abs(freq_bins[:, None] - freq_bins[None, :]) <= SPAN).astype(jnp.float32)
    smooth = jnp.einsum(
        "...f,fg->...g", power_sum, band_matrix, precision=lax.Precision.HIGHEST
    ) / (2 * SPAN + 1)
    water_level = jnp.mean(power_sum, axis=-1, keepdims=True)
    weight = lax.rsqrt(smooth + 0.5 * water_level + 1e-06)
    return (spectra * jnp.concatenate([weight, weight], axis=-1)).astype(jnp.bfloat16)


def cross_pair(row_block, col_block, lags):
    row_real = row_block[..., :NF]
    row_imag = row_block[..., NF:]
    col_both = jnp.concatenate([col_block[..., :NF], col_block[..., NF:]], axis=0)
    row_first = jnp.concatenate([row_real, row_imag], axis=0)
    row_second = jnp.concatenate([row_imag, -row_real], axis=0)
    real_sum = jnp.einsum("wif,wjf->ijf", row_first, col_both, preferred_element_type=jnp.float32)
    imag_sum = jnp.einsum("wif,wjf->ijf", row_second, col_both, preferred_element_type=jnp.float32)
    cross = jnp.concatenate([real_sum, imag_sum], axis=-1).astype(jnp.bfloat16)
    flat = cross.reshape(-1, 2 * NF)
    result = jnp.dot(flat, lags, preferred_element_type=jnp.float32).astype(jnp.bfloat16)
    return result.reshape(row_block.shape[1], col_block.shape[1], LAGS)


def on_device(signal, offsets, pair_list):
    channels_here = signal.shape[0]
    samples_here = signal.shape[1]
    w_dev = samples_here // STEP
    n_tm = lax.axis_size("tm")
    tm_index = lax.axis_index("tm")
    dft_table = forward_table()
    head_samples = signal[:, :HALO]
    next_head = from_behind(head_samples, "tm", -1)
    extended = jnp.concatenate([signal, next_head], axis=1)

    def one_window(window):
        first_sample = window * STEP + offsets[tm_index * w_dev + window]
        segment = lax.dynamic_slice_in_dim(extended, first_sample, WIN, 1)
        return jnp.dot(segment, dft_table, preferred_element_type=jnp.float32)

    spectra = lax.map(one_window, jnp.arange(w_dev, dtype=jnp.int32))
    whitened = whiten(spectra)
    own_piece = whitened[None]
    row_gathered = lax.all_gather(own_piece, ("tm", "pcol"), axis=0, tiled=True)
    col_gathered = lax.all_gather(own_piece, ("tm", "prow"), axis=0, tiled=True)
    row_gathered = row_gathered.reshape(n_tm, -1, w_dev, channels_here, 2 * NF)
    col_gathered = col_gathered.reshape(n_tm, -1, w_dev, channels_here, 2 * NF)
    pick_dim = 1
    lags = lag_table(n_tm * w_dev)
    local_pairs = pair_list[0, 0]
    half_rows = channels_here // n_tm
    first_row = tm_index * half_rows

    def one_pair(pair_index):
        row_pick = local_pairs[pair_index, 0]
        col_pick = local_pairs[pair_index, 1]
        row_whole = lax.dynamic_index_in_dim(row_gathered, row_pick, pick_dim, keepdims=False)
        col_whole = lax.dynamic_index_in_dim(col_gathered, col_pick, pick_dim, keepdims=False)
        row_whole = row_whole.reshape(n_tm * w_dev, channels_here, 2 * NF)
        col_whole = col_whole.reshape(n_tm * w_dev, channels_here, 2 * NF)
        row_block = lax.dynamic_slice_in_dim(row_whole, first_row, half_rows, 1)
        return cross_pair(row_block, col_whole, lags)

    result = lax.map(one_pair, jnp.arange(NP, dtype=jnp.int32))
    return result.reshape(1, 1, NP, half_rows, channels_here, LAGS)


def solution(mesh):
    placed = (P(("prow", "pcol"), "tm"), P(), P("prow", "pcol", None, None))
    return jax.shard_map(
        on_device,
        mesh=mesh,
        in_specs=placed,
        out_specs=P("prow", "pcol", None, "tm", None, None),
        check_vma=False,
    )
```

profile of v0, /device:TPU:0, one launch (start us, length us, event | category | flops | bytes accessed | tf_op | source)
XLA Modules:
  0.0 409.2 jit_solution(12209533261240623052)
XLA Ops:
  6.5 1.3 slice.29
  7.9 1.3 collective-permute-start
  9.3 52.4 %multiply_convert_fusion.1 = (bf16[7680,384]{1,0:T(8,128)(2,1)S(1)}, bf16[7680,384]{1,0:T(8,128)(2,1)S(1)}) fusion(s32[384]{0:T(512)S(1)} %iota_add_fusion, f32[7680]{0:T(1024)S(1)} %get-tuple-element.245, f32[7680]{0:T(1024)S(1)} %get-tuple-element.246), kind=kLoop, calls=%fused_computation.36 | loop fusion | flops 38338560 | bytes 11859456 | tf_op jit(solution)/shard_map/convert.8
  61.8 5.0 %pad_maximum_fusion.3 = bf16[7680,768]{1,0:T(8,128)(2,1)} fusion(bf16[7680,384]{1,0:T(8,128)(2,1)S(1)} %get-tuple-element.244, bf16[7680,384]{1,0:T(8,128)(2,1)S(1)} %get-tuple-element.243), kind=kLoop, calls=%fused_computation.34 | loop fusion | flops 23592960 | bytes 23592960 | tf_op jit(solution)/shard_map/concatenate | solution.py:35
  66.7 1.4 pad_maximum_fusion.4
  68.2 19.9 %while.24 = (s32[]{:T(128)}, f32[2,128,768]{2,1,0:T(8,128)}, s32[2]{0:T(128)S(1)}, s32[]{:T(128)}, s32[4]{0:T(128)S(1)}, /*index=5*/bf16[128,12032]{1,0:T(8,128)...) while((s32[]{:T(128)}, f32[2,128,768]{2,1,0:T(8,128)}, ...), condition=%wide.region_1.2_spmd, body=%wide.region_0.1_spmd.sunk | while | flops 1509949440 | bytes 14156537 | solution.py:93
  71.2 7.0 %fusion.61 = f32[2,128,768]{2,1,0:T(8,128)} fusion(f32[2,128,768]{2,1,0:T(8,128)} %get-tuple-element.370, s32[]{:T(128)} %get-tuple-element.369, bf16[7680,768]{1,0:T(8,128)(2,1)} %get-tuple-element.387, bf16[128,12032]{1,0:T(8,128)(2,1)S(1)} %get-tuple-element.386, s32[]{:T(128)S(6)} %select_n.90), kind=kOutput, calls=%fused_computation.3.clone.1 | convolution fusion | flops 1509949440 | bytes 14156292 | tf_op jit(solution)/shard_map/while/body/eval_jaxpr/dot_general | solution.py:91
  81.2 6.9 %fusion.61 = f32[2,128,768]{2,1,0:T(8,128)} fusion(f32[2,128,768]{2,1,0:T(8,128)} %get-tuple-element.370, s32[]{:T(128)} %get-tuple-element.369, bf16[7680,768]{1,0:T(8,128)(2,1)} %get-tuple-element.387, bf16[128,12032]{1,0:T(8,128)(2,1)S(1)} %get-tuple-element.386, s32[]{:T(128)S(6)} %select_n.90), kind=kOutput, calls=%fused_computation.3.clone.1 | convolution fusion | flops 1509949440 | bytes 14156292 | tf_op jit(solution)/shard_map/while/body/eval_jaxpr/dot_general | solution.py:91
  88.2 1.2 fusion.42
  89.4 1.7 fusion.32
  91.1 2.0 fusion.33
  93.2 0.7 all-gather.7.cloned.1.call-update
  93.9 2.0 multiply_convert_fusion.3
  95.9 62.2 %all-gather.5.cloned.1.call-done = bf16[16,128,768]{2,1,0:T(8,128)(2,1)} async-done(((bf16[2,128,768]{2,1,0:T(8,128)(2,1)}), bf16[16,128,768]{2,1,0:T(8,128)(2,1)}) %all-gather.5.cloned.1.call-update) | async-done | bytes 3145744 | tf_op jit(solution)/shard_map/all_gather | solution.py:97
  158.1 32.8 %all-gather.7.cloned.1.call-done = bf16[16,128,768]{2,1,0:T(8,128)(2,1)} async-done(((bf16[2,128,768]{2,1,0:T(8,128)(2,1)}), bf16[16,128,768]{2,1,0:T(8,128)(2,1)}) %all-gather.7.cloned.1.call-update) | async-done | bytes 3145744 | tf_op jit(solution)/shard_map/all_gather | solution.py:96
  190.9 211.1 %while.25 = (s32[]{:T(128)}, bf16[4,64,128,256]{3,2,1,0:T(8,128)(2,1)}, s32[4]{0:T(128)S(1)}, s32[4,2]{0,1:T(2,128)S(1)}, bf16[2,4,2,128,768]{4,3,2,1,0:T(8,128)...) while((s32[]{:T(128)}, ...), condition=%wide.region_4.5_spmd, body=%wide.region_3.4_spmd.sunk | while | flops 3360456704 | bytes 74515224 | solution.py:116
  214.5 0.6 constant_dynamic-slice_fusion.9
  218.8 1.5 constant_dynamic-slice_fusion.10
  222.4 2.2 convolution_convert_fusion.5
  224.5 12.5 %copy.23 = bf16[48,8,64,128]{3,1,2,0:T(8,128)(2,1)S(1)} copy(bf16[48,8,64,128]{3,2,1,0:T(8,128)(2,1)S(1)} %bitcast.66) | data formatting | bytes 12582912 | tf_op jit(solution)/shard_map/while
  237.0 2.2 convolution_convert_fusion.4
  239.2 12.5 %copy.22 = bf16[48,8,64,128]{3,1,2,0:T(8,128)(2,1)S(1)} copy(bf16[48,8,64,128]{3,2,1,0:T(8,128)(2,1)S(1)} %bitcast.65) | data formatting | bytes 12582912 | tf_op jit(solution)/shard_map/while
  251.6 5.6 %fusion.68 = bf16[8192,256]{1,0:T(8,128)(2,1)S(1)} fusion(bf16[768,256]{1,0:T(8,128)(2,1)S(1)} %get-tuple-element.424, bf16[8192,384]{0,1:T(8,128)(2,1)S(1)} %bitcast.68, bf16[8192,384]{0,1:T(8,128)(2,1)S(1)} %bitcast.67), kind=kOutput, calls=%fused_computation.9.clone.1 | convolution fusion | flops 3248488448 | bytes 17170432 | tf_op jit(solution)/shard_map/while/body/eval_jaxpr/dot_general | solution.py:73
  257.2 2.3 constant_dynamic-update-slice_fusion.2
  262.0 0.6 constant_dynamic-slice_fusion.9
  266.3 1.5 constant_dynamic-slice_fusion.10
  269.8 2.2 convolution_convert_fusion.5
  272.0 12.5 %copy.23 = bf16[48,8,64,128]{3,1,2,0:T(8,128)(2,1)S(1)} copy(bf16[48,8,64,128]{3,2,1,0:T(8,128)(2,1)S(1)} %bitcast.66) | data formatting | bytes 12582912 | tf_op jit(solution)/shard_map/while
  284.5 2.2 convolution_convert_fusion.4
  286.6 12.5 %copy.22 = bf16[48,8,64,128]{3,1,2,0:T(8,128)(2,1)S(1)} copy(bf16[48,8,64,128]{3,2,1,0:T(8,128)(2,1)S(1)} %bitcast.65) | data formatting | bytes 12582912 | tf_op jit(solution)/shard_map/while
  299.1 5.6 %fusion.68 = bf16[8192,256]{1,0:T(8,128)(2,1)S(1)} fusion(bf16[768,256]{1,0:T(8,128)(2,1)S(1)} %get-tuple-element.424, bf16[8192,384]{0,1:T(8,128)(2,1)S(1)} %bitcast.68, bf16[8192,384]{0,1:T(8,128)(2,1)S(1)} %bitcast.67), kind=kOutput, calls=%fused_computation.9.clone.1 | convolution fusion | flops 3248488448 | bytes 17170432 | tf_op jit(solution)/shard_map/while/body/eval_jaxpr/dot_general | solution.py:73
  304.7 2.3 constant_dynamic-update-slice_fusion.2
  309.5 0.6 constant_dynamic-slice_fusion.9
  313.7 1.5 constant_dynamic-slice_fusion.10
  317.3 2.2 convolution_convert_fusion.5
  319.5 12.5 %copy.23 = bf16[48,8,64,128]{3,1,2,0:T(8,128)(2,1)S(1)} copy(bf16[48,8,64,128]{3,2,1,0:T(8,128)(2,1)S(1)} %bitcast.66) | data formatting | bytes 12582912 | tf_op jit(solution)/shard_map/while
  332.0 2.2 convolution_convert_fusion.4
  334.1 12.5 %copy.22 = bf16[48,8,64,128]{3,1,2,0:T(8,128)(2,1)S(1)} copy(bf16[48,8,64,128]{3,2,1,0:T(8,128)(2,1)S(1)} %bitcast.65) | data formatting | bytes 12582912 | tf_op jit(solution)/shard_map/while
  346.6 5.6 %fusion.68 = bf16[8192,256]{1,0:T(8,128)(2,1)S(1)} fusion(bf16[768,256]{1,0:T(8,128)(2,1)S(1)} %get-tuple-element.424, bf16[8192,384]{0,1:T(8,128)(2,1)S(1)} %bitcast.68, bf16[8192,384]{0,1:T(8,128)(2,1)S(1)} %bitcast.67), kind=kOutput, calls=%fused_computation.9.clone.1 | convolution fusion | flops 3248488448 | bytes 17170432 | tf_op jit(solution)/shard_map/while/body/eval_jaxpr/dot_general | solution.py:73
  352.2 2.3 constant_dynamic-update-slice_fusion.2
  357.0 0.6 constant_dynamic-slice_fusion.9
  361.2 1.5 constant_dynamic-slice_fusion.10
  364.8 2.2 convolution_convert_fusion.5
  367.0 12.5 %copy.23 = bf16[48,8,64,128]{3,1,2,0:T(8,128)(2,1)S(1)} copy(bf16[48,8,64,128]{3,2,1,0:T(8,128)(2,1)S(1)} %bitcast.66) | data formatting | bytes 12582912 | tf_op jit(solution)/shard_map/while
  379.5 2.2 convolution_convert_fusion.4
  381.6 12.5 %copy.22 = bf16[48,8,64,128]{3,1,2,0:T(8,128)(2,1)S(1)} copy(bf16[48,8,64,128]{3,2,1,0:T(8,128)(2,1)S(1)} %bitcast.65) | data formatting | bytes 12582912 | tf_op jit(solution)/shard_map/while
  394.1 5.6 %fusion.68 = bf16[8192,256]{1,0:T(8,128)(2,1)S(1)} fusion(bf16[768,256]{1,0:T(8,128)(2,1)S(1)} %get-tuple-element.424, bf16[8192,384]{0,1:T(8,128)(2,1)S(1)} %bitcast.68, bf16[8192,384]{0,1:T(8,128)(2,1)S(1)} %bitcast.67), kind=kOutput, calls=%fused_computation.9.clone.1 | convolution fusion | flops 3248488448 | bytes 17170432 | tf_op jit(solution)/shard_map/while/body/eval_jaxpr/dot_general | solution.py:73
  399.7 2.3 constant_dynamic-update-slice_fusion.2
  (43 shorter events, 13.4 us)
Async XLA Ops:
  6.5 151.6 %all-gather.5.cloned.1.call-start = ((), (), s32[]{:S(2)}) async-start(), calls=%async_computation | async-start | bytes 3538944 | tf_op jit(solution)/shard_map/all_gather | solution.py:97
  7.9 58.9 %collective-permute-start = (bf16[128,4352]{1,0:T(8,128)(2,1)S(1)}, bf16[128,4352]{1,0:T(8,128)(2,1)}, u32[]{:S(2)}, u32[]{:S(2)}) collective-permute-start(bf16[128,4352]{1,0:T(8,128)(2,1)S(1)} %slice.29), channel_id=1, source_target_pairs={{16,0},{17,1},{18,2},{19,3},{20,4},{21,5},{22,6},{23,7},{24,8},{25... | collective-permute-start | bytes 3342344 | tf_op jit(solution)/shard_map/ppermute | solution.py:24
  61.8 5.0 %copy-start = (bf16[128,7680]{1,0:T(8,128)(2,1)S(1)}, bf16[128,7680]{1,0:T(8,128)(2,1)}, u32[]{:S(2)}) copy-start(bf16[128,7680]{1,0:T(8,128)(2,1)} %param.7) | copy-start | bytes 5898244
  61.8 6.4 %copy-start.2 = (s32[4]{0:T(128)S(1)}, s32[4]{0:T(128)}, u32[]{:S(2)}) copy-start(s32[4]{0:T(128)} %param.8) | copy-start | bytes 52
  68.2 122.7 %copy-start.1 = (s32[1,1,4,2]{2,3,1,0:T(2,128)S(1)}, s32[1,1,4,2]{2,3,1,0:T(2,128)}, u32[]{:S(2)}) copy-start(s32[1,1,4,2]{2,3,1,0:T(2,128)} %param.9) | copy-start | bytes 100
  93.1 97.8 %all-gather.7.cloned.1.call-start = ((), (), s32[]{:S(2)}) async-start(), calls=%async_computation.1 | async-start | bytes 3538944 | tf_op jit(solution)/shard_map/all_gather | solution.py:96
Sparse Core Ops, SparseCore 0:
  93.2 64.8 all-gather.4
  160.0 30.8 all-gather.6
where the time goes:
time: 415 us; the launch traced here: 409 us
  local copies, waits for them, and re-layouts  130 us (31%)
  waiting for transfers between devices  95.7 us (23%)
  other arithmetic  66.6 us (16%)
  matrix products  55.2 us (13%)
  loops' own time  46.9 us (11%)
  between operations  13.9 us (3%)
    while x8, local copies, waits for them, and re-layouts  99.7 us
    all_gather x1, waiting for transfers between devices, on_device(): col_gathered = lax.all_gather(own_piece, ('tm', 'prow'), axis=0, tiled=True)  62.2 us
    another operation x2, other arithmetic  54.4 us
    another operation x1, loops' own time, on_device(): result = lax.map(one_pair, jnp.arange(NP, dtype=jnp.int32))  43.2 us
    all_gather x1, waiting for transfers between devices, on_device(): row_gathered = lax.all_gather(own_piece, ('tm', 'pcol'), axis=0, tiled=True)  32.8 us
    dot_general x4, matrix products, cross_pair(): jnp.dot(flat, lags, preferred_element_type=jnp.float32).astype(jnp.bfloat16)  22.3 us
    dot_general x2, matrix products, one_window(): return jnp.dot(segment, dft_table, preferred_element_type=jnp.float32)  13.9 us
    dynamic_update_slice x4, local copies, waits for them, and re-layouts, on_device(): result = lax.map(one_pair, jnp.arange(NP, dtype=jnp.int32))  9.16 us
  transfers between devices with their start and end apart: 3, of which 2 were waited for; matrix products, arithmetic and copies ran while one was open for 15% of the time, Pallas kernels for 0%

commit v1 on v0

--- a/solution.py
+++ b/solution.py
@@ -25,13 +25,22 @@
 
 
 def forward_table():
+    coarse = 128
+    n_coarse = WIN // coarse
+    freq_bins = K0 + jnp.arange(NF, dtype=jnp.int32)
+    scale = two_pi / WIN
+    high_idx = (jnp.arange(n_coarse, dtype=jnp.int32) * coarse)[:, None] * freq_bins[None, :] % WIN
+    low_idx = jnp.arange(coarse, dtype=jnp.int32)[:, None] * freq_bins[None, :] % WIN
+    high_angle = high_idx.astype(jnp.float32) * scale
+    low_angle = low_idx.astype(jnp.float32) * scale
+    high_cos, high_sin = jnp.cos(high_angle)[:, None, :], jnp.sin(high_angle)[:, None, :]
+    low_cos, low_sin = jnp.cos(low_angle)[None], jnp.sin(low_angle)[None]
+    cos_full = (high_cos * low_cos - high_sin * low_sin).reshape(WIN, NF)
+    sin_full = (high_sin * low_cos + high_cos * low_sin).reshape(WIN, NF)
     sample_idx = jnp.arange(WIN, dtype=jnp.int32)
-    freq_bins = K0 + jnp.arange(NF, dtype=jnp.int32)
-    wrapped = sample_idx[:, None] * freq_bins[None, :] % WIN
-    phase_angle = wrapped.astype(jnp.float32) * (two_pi / WIN)
     taper_curve = 0.5 - 0.5 * jnp.cos(sample_idx.astype(jnp.float32) * (two_pi / WIN))
-    cosine = taper_curve[:, None] * jnp.cos(phase_angle)
-    sine = -taper_curve[:, None] * jnp.sin(phase_angle)
+    cosine = taper_curve[:, None] * cos_full
+    sine = -taper_curve[:, None] * sin_full
     return jnp.concatenate([cosine, sine], axis=1).astype(jnp.bfloat16)
 
 
@@ -61,13 +70,12 @@
 
 
 def cross_pair(row_block, col_block, lags):
-    row_real = row_block[..., :NF]
-    row_imag = row_block[..., NF:]
-    col_both = jnp.concatenate([col_block[..., :NF], col_block[..., NF:]], axis=0)
-    row_first = jnp.concatenate([row_real, row_imag], axis=0)
-    row_second = jnp.concatenate([row_imag, -row_real], axis=0)
-    real_sum = jnp.einsum("wif,wjf->ijf", row_first, col_both, preferred_element_type=jnp.float32)
-    imag_sum = jnp.einsum("wif,wjf->ijf", row_second, col_both, preferred_element_type=jnp.float32)
+    row_real = row_block[..., :NF].astype(jnp.float32)[:, :, None, :]
+    row_imag = row_block[..., NF:].astype(jnp.float32)[:, :, None, :]
+    col_real = col_block[..., :NF].astype(jnp.float32)[:, None, :, :]
+    col_imag = col_block[..., NF:].astype(jnp.float32)[:, None, :, :]
+    real_sum = jnp.sum(row_real * col_real + row_imag * col_imag, axis=0)
+    imag_sum = jnp.sum(row_imag * col_real - row_real * col_imag, axis=0)
     cross = jnp.concatenate([real_sum, imag_sum], axis=-1).astype(jnp.bfloat16)
     flat = cross.reshape(-1, 2 * NF)
     result = jnp.dot(flat, lags, preferred_element_type=jnp.float32).astype(jnp.bfloat16)

time: 415 us -> 347 us (0.84)
  the two profiles are of different devices: /device:TPU:0 before, /device:TPU:14 now
where the time goes in v1:
time: 347 us; the launch traced here: 344 us
  other arithmetic  151 us (44%)
  waiting for transfers between devices  92.4 us (27%)
  matrix products  31.3 us (9%)
  loops' own time  27 us (8%)
  local copies, waits for them, and re-layouts  24.2 us (7%)
  between operations  13.5 us (4%)
  starting transfers between devices  3.71 us (1%)
    reduce_sum x4, other arithmetic, cross_pair(): real_sum = jnp.sum(row_real * col_real + row_imag * col_imag, axis=0)  116 us
    all_gather x1, waiting for transfers between devices, on_device(): col_gathered = lax.all_gather(own_piece, ('tm', 'prow'), axis=0, tiled=True)  62.2 us
    all_gather x1, waiting for transfers between devices, on_device(): row_gathered = lax.all_gather(own_piece, ('tm', 'pcol'), axis=0, tiled=True)  29.7 us
    another operation x1, loops' own time, on_device(): result = lax.map(one_pair, jnp.arange(NP, dtype=jnp.int32))  23.5 us
    dot_general x4, matrix products, cross_pair(): jnp.dot(flat, lags, preferred_element_type=jnp.float32).astype(jnp.bfloat16)  15.7 us
    dot_general x2, matrix products, one_window(): return jnp.dot(segment, dft_table, preferred_element_type=jnp.float32)  13.9 us
    sub x1, other arithmetic, forward_table(): cos_full = (high_cos * low_cos - high_sin * low_sin).reshape(WIN, NF)  11.8 us
    another operation x2, other arithmetic  11.3 us
  transfers between devices with their start and end apart: 3, of which 2 were waited for; matrix products, arithmetic and copies ran while one was open for 9% of the time, Pallas kernels for 0%

profile of v1, /device:TPU:14, one launch (start us, length us, event | category | flops | bytes accessed | tf_op | source)
XLA Modules:
  0.0 343.6 jit_solution(10284323201007066720)
XLA Ops:
  6.5 1.3 slice.29
  7.9 3.5 %collective-permute-start = (bf16[128,4352]{1,0:T(8,128)(2,1)S(1)}, bf16[128,4352]{1,0:T(8,128)(2,1)}, u32[]{:S(2)}, u32[]{:S(2)}) collective-permute-start(bf16[128,4352]{1,0:T(8,128)(2,1)S(1)} %slice.29), channel_id=1, source_target_pairs={{16,0},{17,1},{18,2},{19,3},{20,4},{21,5},{22,6},{23,7},{24,8},{25... | collective-permute-start | bytes 3342344 | tf_op jit(solution)/shard_map/ppermute | solution.py:24
  11.6 0.8 fusion.36
  12.4 0.5 fusion.43
  12.9 11.8 %multiply_subtract_fusion = (f32[60,128,384]{2,1,0:T(8,128)}, f32[60,128,384]{2,1,0:T(8,128)}) fusion(f32[128,384]{1,0:T(8,128)S(1)} %get-tuple-element.241, f32[60,384]{1,0:T(8,128)S(1)} %get-tuple-element.239, f32[128,384]{1,0:T(8,128)S(1)} %get-tuple-element.240, f32[60,384]{1,0:T(8,128)S(1)} %get-tuple-element.238), kind=kLoop, calls=%fused_computation.28 | loop fusion | flops 17694720 | bytes 24170496 | tf_op jit(solution)/shard_map/sub | solution.py:38
  24.8 9.4 %fusion.17 = (bf16[7680,384]{1,0:T(8,128)(2,1)S(1)}, bf16[7680,384]{1,0:T(8,128)(2,1)S(1)}) fusion(f32[60,128,384]{2,1,0:T(8,128)} %get-tuple-element.235, f32[7680]{0:T(1024)S(1)} %fusion.46, f32[60,128,384]{2,1,0:T(8,128)} %get-tuple-element.234, f32[7680]{0:T(1024)S(1)} %multiply_subtract_fusion.1), kind=kLoop, calls=%fused_computation.24 | loop fusion | flops 11796480 | bytes 35450880 | tf_op jit(solution)/shard_map/convert.7
  34.2 5.0 %pad_maximum_fusion = bf16[7680,768]{1,0:T(8,128)(2,1)} fusion(bf16[7680,384]{1,0:T(8,128)(2,1)S(1)} %get-tuple-element.242, bf16[7680,384]{1,0:T(8,128)(2,1)S(1)} %get-tuple-element.243), kind=kLoop, calls=%fused_computation.22 | loop fusion | flops 23592960 | bytes 23592960 | tf_op jit(solution)/shard_map/concatenate | solution.py:44
  39.1 1.4 pad_maximum_fusion.1
  40.6 19.9 %while.24 = (s32[]{:T(128)}, f32[2,128,768]{2,1,0:T(8,128)}, s32[2]{0:T(128)S(1)}, s32[]{:T(128)}, s32[4]{0:T(128)S(1)}, /*index=5*/bf16[128,12032]{1,0:T(8,128)...) while((s32[]{:T(128)}, f32[2,128,768]{2,1,0:T(8,128)}, ...), condition=%wide.region_1.2_spmd, body=%wide.region_0.1_spmd.sunk | while | flops 1509949440 | bytes 14156537 | solution.py:101
  40.6 0.6 dynamic_slice.65
  41.8 0.6 dynamic_slice.66
  43.6 7.0 %fusion.58 = f32[2,128,768]{2,1,0:T(8,128)} fusion(f32[2,128,768]{2,1,0:T(8,128)} %get-tuple-element.369, s32[]{:T(128)} %get-tuple-element.368, bf16[7680,768]{1,0:T(8,128)(2,1)} %get-tuple-element.386, bf16[128,12032]{1,0:T(8,128)(2,1)S(1)} %get-tuple-element.385, s32[]{:T(128)S(6)} %select_n.122), kind=kOutput, calls=%fused_computation.3.clone.1 | convolution fusion | flops 1509949440 | bytes 14156292 | tf_op jit(solution)/shard_map/while/body/eval_jaxpr/dot_general | solution.py:99
  50.6 0.6 dynamic_slice.65
  51.7 0.6 dynamic_slice.66
  53.5 6.9 %fusion.58 = f32[2,128,768]{2,1,0:T(8,128)} fusion(f32[2,128,768]{2,1,0:T(8,128)} %get-tuple-element.369, s32[]{:T(128)} %get-tuple-element.368, bf16[7680,768]{1,0:T(8,128)(2,1)} %get-tuple-element.386, bf16[128,12032]{1,0:T(8,128)(2,1)S(1)} %get-tuple-element.385, s32[]{:T(128)S(6)} %select_n.122), kind=kOutput, calls=%fused_computation.3.clone.1 | convolution fusion | flops 1509949440 | bytes 14156292 | tf_op jit(solution)/shard_map/while/body/eval_jaxpr/dot_general | solution.py:99
  60.5 1.2 fusion.45
  61.7 1.7 fusion.21
  63.4 2.0 fusion.22
  65.4 0.2 all-gather.7.cloned.1.call-start
  65.6 0.5 all-gather.7.cloned.1.call-update
  66.2 2.0 multiply_convert_fusion.1
  68.2 29.7 %all-gather.5.cloned.1.call-done = bf16[16,128,768]{2,1,0:T(8,128)(2,1)} async-done(((bf16[2,128,768]{2,1,0:T(8,128)(2,1)}), bf16[16,128,768]{2,1,0:T(8,128)(2,1)}) %all-gather.5.cloned.1.call-update) | async-done | bytes 3145744 | tf_op jit(solution)/shard_map/all_gather | solution.py:104
  97.9 62.2 %all-gather.7.cloned.1.call-done = bf16[16,128,768]{2,1,0:T(8,128)(2,1)} async-done(((bf16[2,128,768]{2,1,0:T(8,128)(2,1)}), bf16[16,128,768]{2,1,0:T(8,128)(2,1)}) %all-gather.7.cloned.1.call-update) | async-done | bytes 3145744 | tf_op jit(solution)/shard_map/all_gather | solution.py:105
  160.1 176.7 %while.25 = (s32[]{:T(128)}, bf16[4,64,128,256]{3,2,1,0:T(8,128)(2,1)}, s32[4]{0:T(128)S(1)}, s32[4,2]{0,1:T(2,128)S(1)}, bf16[2,4,2,128,768]{4,3,2,1,0:T(8,128)...) while((s32[]{:T(128)}, ...), condition=%wide.region_6.7_spmd, body=%wide.region_3.6_spmd.sunk | while | flops 3343450112 | bytes 47186712 | solution.py:124
  160.1 0.7 dynamic_slice.69
  162.8 0.7 constant_dynamic-slice_fusion.6
  167.2 1.5 constant_dynamic-slice_fusion.7
  168.9 29.1 %add_reduce_fusion.2 = (bf16[64,128,384]{2,1,0:T(8,128)(2,1)S(1)}, bf16[64,128,384]{2,1,0:T(8,128)(2,1)S(1)}) fusion(f32[4,128,384]{2,1,0:T(8,128)S(1)} %get-tuple-element.349, f32[4,64,384]{2,1,0:T(8,128)S(1)} %get-tuple-element.351, f32[4,128,384]{2,1,0:T(8,128)S(1)} %get-tuple-element.352, f32[4,64,384]{2,1,0:T(8,128)S(1)} %get-tuple-element.353), kind=kLoop, calls=%fused_computation.6.clone.1 | loop fusion | flops 94371840 | bytes 14942208 | tf_op jit(solution)/shard_map/while/body/eval_jaxpr/reduce_sum | solution.py:77
  198.0 3.9 %fusion.61 = bf16[8192,256]{1,0:T(8,128)(2,1)S(1)} fusion(bf16[768,256]{1,0:T(8,128)(2,1)S(1)} %get-tuple-element.423, bf16[8192,384]{1,0:T(8,128)(2,1)S(1)} %bitcast.62, bf16[8192,384]{1,0:T(8,128)(2,1)S(1)} %bitcast.61), kind=kOutput, calls=%fused_computation.11.clone.1 | convolution fusion | flops 3248488448 | bytes 17170432 | tf_op jit(solution)/shard_map/while/body/eval_jaxpr/dot_general | solution.py:81
  202.0 2.3 constant_dynamic-update-slice_fusion.2
  204.3 0.7 dynamic_slice.69
  207.0 0.7 constant_dynamic-slice_fusion.6
  211.4 1.5 constant_dynamic-slice_fusion.7
  213.1 29.1 %add_reduce_fusion.2 = (bf16[64,128,384]{2,1,0:T(8,128)(2,1)S(1)}, bf16[64,128,384]{2,1,0:T(8,128)(2,1)S(1)}) fusion(f32[4,128,384]{2,1,0:T(8,128)S(1)} %get-tuple-element.349, f32[4,64,384]{2,1,0:T(8,128)S(1)} %get-tuple-element.351, f32[4,128,384]{2,1,0:T(8,128)S(1)} %get-tuple-element.352, f32[4,64,384]{2,1,0:T(8,128)S(1)} %get-tuple-element.353), kind=kLoop, calls=%fused_computation.6.clone.1 | loop fusion | flops 94371840 | bytes 14942208 | tf_op jit(solution)/shard_map/while/body/eval_jaxpr/reduce_sum | solution.py:77
  242.2 3.9 %fusion.61 = bf16[8192,256]{1,0:T(8,128)(2,1)S(1)} fusion(bf16[768,256]{1,0:T(8,128)(2,1)S(1)} %get-tuple-element.423, bf16[8192,384]{1,0:T(8,128)(2,1)S(1)} %bitcast.62, bf16[8192,384]{1,0:T(8,128)(2,1)S(1)} %bitcast.61), kind=kOutput, calls=%fused_computation.11.clone.1 | convolution fusion | flops 3248488448 | bytes 17170432 | tf_op jit(solution)/shard_map/while/body/eval_jaxpr/dot_general | solution.py:81
  246.1 2.3 constant_dynamic-update-slice_fusion.2
  248.4 0.7 dynamic_slice.69
  251.2 0.7 constant_dynamic-slice_fusion.6
  255.6 1.5 constant_dynamic-slice_fusion.7
  257.3 29.1 %add_reduce_fusion.2 = (bf16[64,128,384]{2,1,0:T(8,128)(2,1)S(1)}, bf16[64,128,384]{2,1,0:T(8,128)(2,1)S(1)}) fusion(f32[4,128,384]{2,1,0:T(8,128)S(1)} %get-tuple-element.349, f32[4,64,384]{2,1,0:T(8,128)S(1)} %get-tuple-element.351, f32[4,128,384]{2,1,0:T(8,128)S(1)} %get-tuple-element.352, f32[4,64,384]{2,1,0:T(8,128)S(1)} %get-tuple-element.353), kind=kLoop, calls=%fused_computation.6.clone.1 | loop fusion | flops 94371840 | bytes 14942208 | tf_op jit(solution)/shard_map/while/body/eval_jaxpr/reduce_sum | solution.py:77
  286.4 3.9 %fusion.61 = bf16[8192,256]{1,0:T(8,128)(2,1)S(1)} fusion(bf16[768,256]{1,0:T(8,128)(2,1)S(1)} %get-tuple-element.423, bf16[8192,384]{1,0:T(8,128)(2,1)S(1)} %bitcast.62, bf16[8192,384]{1,0:T(8,128)(2,1)S(1)} %bitcast.61), kind=kOutput, calls=%fused_computation.11.clone.1 | convolution fusion | flops 3248488448 | bytes 17170432 | tf_op jit(solution)/shard_map/while/body/eval_jaxpr/dot_general | solution.py:81
  290.3 2.3 constant_dynamic-update-slice_fusion.2
  292.6 0.7 dynamic_slice.69
  295.3 0.7 constant_dynamic-slice_fusion.6
  299.8 1.5 constant_dynamic-slice_fusion.7
  301.4 29.1 %add_reduce_fusion.2 = (bf16[64,128,384]{2,1,0:T(8,128)(2,1)S(1)}, bf16[64,128,384]{2,1,0:T(8,128)(2,1)S(1)}) fusion(f32[4,128,384]{2,1,0:T(8,128)S(1)} %get-tuple-element.349, f32[4,64,384]{2,1,0:T(8,128)S(1)} %get-tuple-element.351, f32[4,128,384]{2,1,0:T(8,128)S(1)} %get-tuple-element.352, f32[4,64,384]{2,1,0:T(8,128)S(1)} %get-tuple-element.353), kind=kLoop, calls=%fused_computation.6.clone.1 | loop fusion | flops 94371840 | bytes 14942208 | tf_op jit(solution)/shard_map/while/body/eval_jaxpr/reduce_sum | solution.py:77
  330.5 3.9 %fusion.61 = bf16[8192,256]{1,0:T(8,128)(2,1)S(1)} fusion(bf16[768,256]{1,0:T(8,128)(2,1)S(1)} %get-tuple-element.423, bf16[8192,384]{1,0:T(8,128)(2,1)S(1)} %bitcast.62, bf16[8192,384]{1,0:T(8,128)(2,1)S(1)} %bitcast.61), kind=kOutput, calls=%fused_computation.11.clone.1 | convolution fusion | flops 3248488448 | bytes 17170432 | tf_op jit(solution)/shard_map/while/body/eval_jaxpr/dot_general | solution.py:81
  334.5 2.3 constant_dynamic-update-slice_fusion.2
  (28 shorter events, 1.1 us)
Async XLA Ops:
  6.5 91.4 %all-gather.5.cloned.1.call-start = ((), (), s32[]{:S(2)}) async-start(), calls=%async_computation | async-start | bytes 3538944 | tf_op jit(solution)/shard_map/all_gather | solution.py:104
  7.9 31.3 %collective-permute-start = (bf16[128,4352]{1,0:T(8,128)(2,1)S(1)}, bf16[128,4352]{1,0:T(8,128)(2,1)}, u32[]{:S(2)}, u32[]{:S(2)}) collective-permute-start(bf16[128,4352]{1,0:T(8,128)(2,1)S(1)} %slice.29), channel_id=1, source_target_pairs={{16,0},{17,1},{18,2},{19,3},{20,4},{21,5},{22,6},{23,7},{24,8},{25... | collective-permute-start | bytes 3342344 | tf_op jit(solution)/shard_map/ppermute | solution.py:24
  34.1 5.0 %copy-start = (bf16[128,7680]{1,0:T(8,128)(2,1)S(1)}, bf16[128,7680]{1,0:T(8,128)(2,1)}, u32[]{:S(2)}) copy-start(bf16[128,7680]{1,0:T(8,128)(2,1)} %param.7) | copy-start | bytes 5898244
  34.2 6.4 %copy-start.2 = (s32[4]{0:T(128)S(1)}, s32[4]{0:T(128)}, u32[]{:S(2)}) copy-start(s32[4]{0:T(128)} %param.8) | copy-start | bytes 52
  40.6 119.5 %copy-start.1 = (s32[1,1,4,2]{2,3,1,0:T(2,128)S(1)}, s32[1,1,4,2]{2,3,1,0:T(2,128)}, u32[]{:S(2)}) copy-start(s32[1,1,4,2]{2,3,1,0:T(2,128)} %param.9) | copy-start | bytes 100
  65.4 94.7 %all-gather.7.cloned.1.call-start = ((), (), s32[]{:S(2)}) async-start(), calls=%async_computation.1 | async-start | bytes 3538944 | tf_op jit(solution)/shard_map/all_gather | solution.py:105
Sparse Core Ops, SparseCore 0:
  65.5 32.3 all-gather.4
  100.0 60.0 all-gather.6

commit v2 on v1

--- a/solution.py
+++ b/solution.py
@@ -4,6 +4,8 @@
 import jax.numpy as jnp
 from jax import lax
 from jax.sharding import PartitionSpec as P
+from jax.experimental import pallas as pl
+from jax.experimental.pallas import tpu as pltpu
 
 WIN = 7680
 NF = 384
@@ -69,17 +71,67 @@
     return (spectra * jnp.concatenate([weight, weight], axis=-1)).astype(jnp.bfloat16)
 
 
-def cross_pair(row_block, col_block, lags):
-    row_real = row_block[..., :NF].astype(jnp.float32)[:, :, None, :]
-    row_imag = row_block[..., NF:].astype(jnp.float32)[:, :, None, :]
-    col_real = col_block[..., :NF].astype(jnp.float32)[:, None, :, :]
-    col_imag = col_block[..., NF:].astype(jnp.float32)[:, None, :, :]
-    real_sum = jnp.sum(row_real * col_real + row_imag * col_imag, axis=0)
-    imag_sum = jnp.sum(row_imag * col_real - row_real * col_imag, axis=0)
-    cross = jnp.concatenate([real_sum, imag_sum], axis=-1).astype(jnp.bfloat16)
-    flat = cross.reshape(-1, 2 * NF)
-    result = jnp.dot(flat, lags, preferred_element_type=jnp.float32).astype(jnp.bfloat16)
-    return result.reshape(row_block.shape[1], col_block.shape[1], LAGS)
+ROW_TILE = 8
+J_CHUNK = 64
+F_CHUNK = 128
+
+
+def pair_kernel(pairs_ref, row_ref, col_ref, lags_ref, out_ref, cross_ref):
+    windows = row_ref.shape[1]
+    cols = col_ref.shape[2]
+
+    for i in range(row_ref.shape[2]):
+        for jc in range(cols // J_CHUNK):
+            js = pl.ds(jc * J_CHUNK, J_CHUNK)
+            for fc in range(NF // F_CHUNK):
+                fr = pl.ds(fc * F_CHUNK, F_CHUNK)
+                fi = pl.ds(NF + fc * F_CHUNK, F_CHUNK)
+                acc_re = jnp.zeros((J_CHUNK, F_CHUNK), jnp.float32)
+                acc_im = jnp.zeros((J_CHUNK, F_CHUNK), jnp.float32)
+                for w in range(windows):
+                    xr = row_ref[0, w, i : i + 1, fr]
+                    xi = row_ref[0, w, i : i + 1, fi]
+                    yr = col_ref[0, w, js, fr]
+                    yi = col_ref[0, w, js, fi]
+                    acc_re = acc_re + xr * yr + xi * yi
+                    acc_im = acc_im + xi * yr - xr * yi
+                rows = pl.ds(i * cols + jc * J_CHUNK, J_CHUNK)
+                cross_ref[rows, fr] = acc_re.astype(jnp.bfloat16)
+                cross_ref[rows, fi] = acc_im.astype(jnp.bfloat16)
+    result = jnp.dot(cross_ref[...], lags_ref[...], preferred_element_type=jnp.float32)
+    out_ref[0] = result.reshape(out_ref.shape[1:]).astype(out_ref.dtype)
+
+
+def all_pairs(pairs, row_all, col_all, lags):
+    n_pairs = pairs.shape[0]
+    windows, rows, cols = row_all.shape[1], row_all.shape[2], col_all.shape[2]
+    tiles = rows // ROW_TILE
+    grid_spec = pltpu.PrefetchScalarGridSpec(
+        num_scalar_prefetch=1,
+        grid=(n_pairs, tiles),
+        in_specs=[
+            pl.BlockSpec((1, windows, ROW_TILE, 2 * NF), lambda p, t, pr: (pr[p, 0], 0, t, 0)),
+            pl.BlockSpec((1, windows, cols, 2 * NF), lambda p, t, pr: (pr[p, 1], 0, 0, 0)),
+            pl.BlockSpec((2 * NF, LAGS), lambda p, t, pr: (0, 0)),
+        ],
+        out_specs=pl.BlockSpec((1, ROW_TILE, cols, LAGS), lambda p, t, pr: (p, t, 0, 0)),
+        scratch_shapes=[pltpu.VMEM((ROW_TILE * cols, 2 * NF), jnp.bfloat16)],
+    )
+    flops = n_pairs * rows * cols * (2 * NF * windows * 4 + 2 * 2 * NF * LAGS)
+    return pl.pallas_call(
+        pair_kernel,
+        grid_spec=grid_spec,
+        out_shape=jax.ShapeDtypeStruct((n_pairs, rows, cols, LAGS), jnp.bfloat16),
+        compiler_params=pltpu.CompilerParams(
+            dimension_semantics=("arbitrary", "arbitrary"),
+            vmem_limit_bytes=48 * 1024 * 1024,
+        ),
+        cost_estimate=pl.CostEstimate(
+            flops=flops,
+            transcendentals=0,
+            bytes_accessed=n_pairs * (rows + cols) * windows * 2 * NF * 4 + n_pairs * rows * cols * LAGS * 2,
+        ),
+    )(pairs, row_all, col_all, lags)
 
 
 def on_device(signal, offsets, pair_list):
@@ -105,23 +157,18 @@
     col_gathered = lax.all_gather(own_piece, ("tm", "prow"), axis=0, tiled=True)
     row_gathered = row_gathered.reshape(n_tm, -1, w_dev, channels_here, 2 * NF)
     col_gathered = col_gathered.reshape(n_tm, -1, w_dev, channels_here, 2 * NF)
-    pick_dim = 1
     lags = lag_table(n_tm * w_dev)
+    n_pcol = row_gathered.shape[1]
+    n_prow = col_gathered.shape[1]
+    half_rows = channels_here // n_tm
+    row_part = lax.dynamic_slice_in_dim(row_gathered, tm_index * half_rows, half_rows, 3)
+    row_all = jnp.transpose(row_part, (1, 0, 2, 3, 4)).reshape(n_pcol, n_tm * w_dev, half_rows, 2 * NF)
+    col_all = jnp.transpose(col_gathered, (1, 0, 2, 3, 4)).reshape(n_prow, n_tm * w_dev, channels_here, 2 * NF)
     local_pairs = pair_list[0, 0]
-    half_rows = channels_here // n_tm
-    first_row = tm_index * half_rows
-
-    def one_pair(pair_index):
-        row_pick = local_pairs[pair_index, 0]
-        col_pick = local_pairs[pair_index, 1]
-        row_whole = lax.dynamic_index_in_dim(row_gathered, row_pick, pick_dim, keepdims=False)
-        col_whole = lax.dynamic_index_in_dim(col_gathered, col_pick, pick_dim, keepdims=False)
-        row_whole = row_whole.reshape(n_tm * w_dev, channels_here, 2 * NF)
-        col_whole = col_whole.reshape(n_tm * w_dev, channels_here, 2 * NF)
-        row_block = lax.dynamic_slice_in_dim(row_whole, first_row, half_rows, 1)
-        return cross_pair(row_block, col_whole, lags)
-
-    result = lax.map(one_pair, jnp.arange(NP, dtype=jnp.int32))
+    pairs = jnp.stack(
+        [jnp.clip(local_pairs[:, 0], 0, n_pcol - 1), jnp.clip(local_pairs[:, 1], 0, n_prow - 1)], axis=1
+    ).astype(jnp.int32)
+    result = all_pairs(pairs, row_all.astype(jnp.float32), col_all.astype(jnp.float32), lags)
     return result.reshape(1, 1, NP, half_rows, channels_here, LAGS)
 
 

time: 347 us -> 244 us (0.70)
  other arithmetic: 151 us -> 36.2 us
  Pallas kernels: 0 us -> 73.4 us
  loops' own time: 27 us -> 3.81 us
  matrix products: 31.3 us -> 15.6 us
  local copies, waits for them, and re-layouts: 24.2 us -> 9.26 us
  waiting for transfers between devices: 92.4 us -> 85.4 us
    reduce_sum x4 -> x0, other arithmetic: 116 us -> none  [cross_pair(): real_sum = jnp.sum(row_real * col_real + row_imag * col_imag, axis=0)]
    pallas_call x0 -> x1, Pallas kernels: none -> 73.4 us  [all_pairs(): pl.pallas_call(pair_kernel, grid_spec=grid_spec, out_shape=jax.ShapeDtype...]
    another operation x1 -> x0, loops' own time: 23.5 us -> none  [on_device(): result = lax.map(one_pair, jnp.arange(NP, dtype=jnp.int32))]
    dot_general x4 -> x0, matrix products: 15.7 us -> none  [cross_pair(): jnp.dot(flat, lags, preferred_element_type=jnp.float32).astype(jnp.bfloat16)]
    dynamic_slice x12 -> x0, local copies, waits for them, and re-layouts: 11.2 us -> none  [the longest x4 5.93 us: one_pair(): lax.dynamic_index_in_dim(col_gathered, col_pick, pick_dim, keepdims=False)]
    dynamic_update_slice x4 -> x0, local copies, waits for them, and re-layouts: 9.16 us -> none  [on_device(): result = lax.map(one_pair, jnp.arange(NP, dtype=jnp.int32))]
    convert_element_type x0 -> x1, local copies, waits for them, and re-layouts: none -> 5.22 us  [on_device(): col_all.astype(jnp.float32)]
    all_gather x1, waiting for transfers between devices: 62.2 us -> 57.3 us  [on_device(): col_gathered = lax.all_gather(own_piece, ('tm', 'prow'), axis=0, tiled=True)]
  transfers between devices with their start and end apart: 3 -> 3, of which waited for: 2 -> 2; matrix products, arithmetic and copies ran while one was open for 9% -> 15% of each run, Pallas kernels for 0% -> 0%
where the time goes in v2:
time: 244 us; the launch traced here: 241 us
  waiting for transfers between devices  85.4 us (35%)
  Pallas kernels  73.4 us (30%)
  other arithmetic  36.2 us (15%)
  matrix products  15.6 us (6%)
  between operations  13.5 us (6%)
  local copies, waits for them, and re-layouts  9.26 us (4%)
  loops' own time  3.81 us (2%)
  starting transfers between devices  3.71 us (2%)
    pallas_call x1, Pallas kernels, all_pairs(): pl.pallas_call(pair_kernel, grid_spec=grid_spec, out_shape=jax.ShapeDtype...  73.4 us
    all_gather x1, waiting for transfers between devices, on_device(): col_gathered = lax.all_gather(own_piece, ('tm', 'prow'), axis=0, tiled=True)  57.3 us
    all_gather x1, waiting for transfers between devices, on_device(): row_gathered = lax.all_gather(own_piece, ('tm', 'pcol'), axis=0, tiled=True)  27.5 us
    dot_general x2, matrix products, one_window(): return jnp.dot(segment, dft_table, preferred_element_type=jnp.float32)  14 us
    sub x1, other arithmetic, forward_table(): cos_full = (high_cos * low_cos - high_sin * low_sin).reshape(WIN, NF)  11.8 us
    another operation x2, other arithmetic  11.3 us
    convert_element_type x1, local copies, waits for them, and re-layouts, on_device(): col_all.astype(jnp.float32)  5.22 us
    concatenate x1, other arithmetic, forward_table(): return jnp.concatenate([cosine, sine], axis=1).astype(jnp.bfloat16)  4.95 us
  transfers between devices with their start and end apart: 3, of which 2 were waited for; matrix products, arithmetic and copies ran while one was open for 15% of the time, Pallas kernels for 0%

profile of v2, /device:TPU:14, one launch (start us, length us, event | category | flops | bytes accessed | tf_op | source)
XLA Modules:
  0.0 240.9 jit_solution(3896095627136617295)
XLA Ops:
  6.5 0.0 all-gather.7.cloned.1.call-start
  6.5 1.3 slice.17
  7.9 3.5 %collective-permute-start = (bf16[128,4352]{1,0:T(8,128)(2,1)S(1)}, bf16[128,4352]{1,0:T(8,128)(2,1)}, u32[]{:S(2)}, u32[]{:S(2)}) collective-permute-start(bf16[128,4352]{1,0:T(8,128)(2,1)S(1)} %slice.17), channel_id=1, source_target_pairs={{16,0},{17,1},{18,2},{19,3},{20,4},{21,5},{22,6},{23,7},{24,8},{25... | collective-permute-start | bytes 3342344 | tf_op jit(solution)/shard_map/ppermute | solution.py:26
  11.3 0.1 fusion.38
  11.5 0.1 multiply_subtract_fusion.1
  11.6 0.8 fusion.28
  12.4 0.5 fusion.35
  12.9 11.8 %multiply_subtract_fusion = (f32[60,128,384]{2,1,0:T(8,128)}, f32[60,128,384]{2,1,0:T(8,128)}) fusion(f32[128,384]{1,0:T(8,128)S(1)} %get-tuple-element.110, f32[60,384]{1,0:T(8,128)S(1)} %get-tuple-element.108, f32[128,384]{1,0:T(8,128)S(1)} %get-tuple-element.109, f32[60,384]{1,0:T(8,128)S(1)} %get-tuple-element.107), kind=kLoop, calls=%fused_computation.11 | loop fusion | flops 17694720 | bytes 24170496 | tf_op jit(solution)/shard_map/sub | solution.py:40
  24.8 9.4 %fusion.9 = (bf16[7680,384]{1,0:T(8,128)(2,1)S(1)}, bf16[7680,384]{1,0:T(8,128)(2,1)S(1)}) fusion(f32[60,128,384]{2,1,0:T(8,128)} %get-tuple-element.104, f32[7680]{0:T(1024)S(1)} %fusion.38, f32[60,128,384]{2,1,0:T(8,128)} %get-tuple-element.103, f32[7680]{0:T(1024)S(1)} %multiply_subtract_fusion.1), kind=kLoop, calls=%fused_computation.7 | loop fusion | flops 11796480 | bytes 35450880 | tf_op jit(solution)/shard_map/convert.8
  34.1 0.0 copy-start
  34.2 5.0 %pad_maximum_fusion = bf16[7680,768]{1,0:T(8,128)(2,1)} fusion(bf16[7680,384]{1,0:T(8,128)(2,1)S(1)} %get-tuple-element.115, bf16[7680,384]{1,0:T(8,128)(2,1)S(1)} %get-tuple-element.116), kind=kLoop, calls=%fused_computation.5 | loop fusion | flops 23592960 | bytes 23592960 | tf_op jit(solution)/shard_map/concatenate | solution.py:46
  39.1 0.0 copy-start.2
  39.1 0.0 collective-permute-done
  39.1 0.0 copy-done
  39.1 1.5 pad_maximum_fusion.1
  40.6 0.0 copy-done.2
  40.6 0.0 copy-start.1
  40.6 20.3 %while.12 = (s32[]{:T(128)}, f32[2,128,768]{2,1,0:T(8,128)}, s32[2]{0:T(128)S(1)}, s32[]{:T(128)}, s32[4]{0:T(128)S(1)}, /*index=5*/bf16[128,12032]{1,0:T(8,128)...) while((s32[]{:T(128)}, f32[2,128,768]{2,1,0:T(8,128)}, ...), condition=%wide.region_1.2_spmd, body=%wide.region_0.1_spmd.sunk | while | flops 1509949440 | bytes 14156537 | solution.py:153
  40.6 0.6 dynamic_slice.32
  41.9 0.6 dynamic_slice.33
  43.8 7.0 %fusion.47 = f32[2,128,768]{2,1,0:T(8,128)} fusion(f32[2,128,768]{2,1,0:T(8,128)} %get-tuple-element.173, s32[]{:T(128)} %get-tuple-element.172, bf16[7680,768]{1,0:T(8,128)(2,1)} %get-tuple-element.190, bf16[128,12032]{1,0:T(8,128)(2,1)S(1)} %get-tuple-element.189, s32[]{:T(128)S(6)} %select_n.100), kind=kOutput, calls=%fused_computation.3.clone.1 | convolution fusion | flops 1509949440 | bytes 14156292 | tf_op jit(solution)/shard_map/while/body/eval_jaxpr/dot_general | solution.py:151
  50.8 0.6 dynamic_slice.32
  52.0 0.6 dynamic_slice.33
  53.9 7.0 %fusion.47 = f32[2,128,768]{2,1,0:T(8,128)} fusion(f32[2,128,768]{2,1,0:T(8,128)} %get-tuple-element.173, s32[]{:T(128)} %get-tuple-element.172, bf16[7680,768]{1,0:T(8,128)(2,1)} %get-tuple-element.190, bf16[128,12032]{1,0:T(8,128)(2,1)S(1)} %get-tuple-element.189, s32[]{:T(128)S(6)} %select_n.100), kind=kOutput, calls=%fused_computation.3.clone.1 | convolution fusion | flops 1509949440 | bytes 14156292 | tf_op jit(solution)/shard_map/while/body/eval_jaxpr/dot_general | solution.py:151
  60.9 1.2 fusion.37
  62.1 1.7 fusion.13
  63.8 2.0 fusion.14
  65.8 0.0 all-gather.7.cloned.1.call-update
  65.8 0.2 all-gather.5.cloned.1.call-start
  66.0 0.5 all-gather.5.cloned.1.call-update
  66.6 0.0 copy-done.1
  66.6 0.1 copy.12
  66.7 0.1 copy.13
  66.8 0.1 pad_add_fusion.pairs_ref
  66.9 1.9 multiply_convert_fusion.1
  68.8 57.3 %all-gather.7.cloned.1.call-done = bf16[16,128,768]{2,1,0:T(8,128)(2,1)} async-done(((bf16[2,128,768]{2,1,0:T(8,128)(2,1)}), bf16[16,128,768]{2,1,0:T(8,128)(2,1)}) %all-gather.7.cloned.1.call-update) | async-done | bytes 3145744 | tf_op jit(solution)/shard_map/all_gather | solution.py:157
  126.2 5.2 %copy.11 = f32[2,4,2,128,768]{4,3,2,0,1:T(8,128)} copy(bf16[2,4,2,128,768]{4,3,2,1,0:T(8,128)(2,1)} %bitcast.39) | data formatting | bytes 9437184 | tf_op jit(solution)/shard_map/convert_element_type | solution.py:171
  131.4 27.5 %all-gather.5.cloned.1.call-done = bf16[16,128,768]{2,1,0:T(8,128)(2,1)} async-done(((bf16[2,128,768]{2,1,0:T(8,128)(2,1)}), bf16[16,128,768]{2,1,0:T(8,128)(2,1)}) %all-gather.5.cloned.1.call-update) | async-done | bytes 3145744 | tf_op jit(solution)/shard_map/all_gather | solution.py:156
  158.9 1.7 copy_convert_fusion
  160.7 73.4 %shard_map.37 = bf16[4,64,128,256]{3,2,1,0:T(8,128)(2,1)} custom-call(s32[4,2]{1,0:T(4,128)S(1)} %pad_add_fusion.pairs_ref, f32[4,4,64,768]{3,2,1,0:T(8,128)S(1)} %bitcast.37, f32[4,4,128,768]{3,2,1,0:T(8,128)} %bitcast.38, bf16[768,256]{1,0:T(8,128)(2,1)S(1)} %pad_maximum_fusion.2.lags_ref), custom_call_target="tpu_custom_call" | custom-call | flops 13287555072 | bytes 26214400 | tf_op jit(solution)/shard_map/pallas_call | solution.py:121
  (9 shorter events, 0.1 us)
Async XLA Ops:
  6.5 119.6 %all-gather.7.cloned.1.call-start = ((), (), s32[]{:S(2)}) async-start(), calls=%async_computation.1 | async-start | bytes 3538944 | tf_op jit(solution)/shard_map/all_gather | solution.py:157
  7.9 31.3 %collective-permute-start = (bf16[128,4352]{1,0:T(8,128)(2,1)S(1)}, bf16[128,4352]{1,0:T(8,128)(2,1)}, u32[]{:S(2)}, u32[]{:S(2)}) collective-permute-start(bf16[128,4352]{1,0:T(8,128)(2,1)S(1)} %slice.17), channel_id=1, source_target_pairs={{16,0},{17,1},{18,2},{19,3},{20,4},{21,5},{22,6},{23,7},{24,8},{25... | collective-permute-start | bytes 3342344 | tf_op jit(solution)/shard_map/ppermute | solution.py:26
  34.1 5.0 %copy-start = (bf16[128,7680]{1,0:T(8,128)(2,1)S(1)}, bf16[128,7680]{1,0:T(8,128)(2,1)}, u32[]{:S(2)}) copy-start(bf16[128,7680]{1,0:T(8,128)(2,1)} %param.5) | copy-start | bytes 5898244
  39.1 1.5 copy-start.2
  40.6 26.0 %copy-start.1 = (s32[1,1,4,2]{2,3,1,0:T(2,128)S(1)}, s32[1,1,4,2]{2,3,1,0:T(2,128)}, u32[]{:S(2)}) copy-start(s32[1,1,4,2]{2,3,1,0:T(2,128)} %param.7) | copy-start | bytes 100
  65.8 93.1 %all-gather.5.cloned.1.call-start = ((), (), s32[]{:S(2)}) async-start(), calls=%async_computation | async-start | bytes 3538944 | tf_op jit(solution)/shard_map/all_gather | solution.py:156
Sparse Core Ops, SparseCore 0:
  65.9 60.2 all-gather.6
  128.1 30.8 all-gather.4

commit v3 on v2

--- a/solution.py
+++ b/solution.py
@@ -1,3 +1,4 @@
+import itertools
 import math
 
 import jax
@@ -35,8 +36,11 @@
     low_idx = jnp.arange(coarse, dtype=jnp.int32)[:, None] * freq_bins[None, :] % WIN
     high_angle = high_idx.astype(jnp.float32) * scale
     low_angle = low_idx.astype(jnp.float32) * scale
-    high_cos, high_sin = jnp.cos(high_angle)[:, None, :], jnp.sin(high_angle)[:, None, :]
-    low_cos, low_sin = jnp.cos(low_angle)[None], jnp.sin(low_angle)[None]
+    high_cos, high_sin, low_cos, low_sin = lax.optimization_barrier(
+        (jnp.cos(high_angle), jnp.sin(high_angle), jnp.cos(low_angle), jnp.sin(low_angle))
+    )
+    high_cos, high_sin = high_cos[:, None, :], high_sin[:, None, :]
+    low_cos, low_sin = low_cos[None], low_sin[None]
     cos_full = (high_cos * low_cos - high_sin * low_sin).reshape(WIN, NF)
     sin_full = (high_sin * low_cos + high_cos * low_sin).reshape(WIN, NF)
     sample_idx = jnp.arange(WIN, dtype=jnp.int32)
@@ -134,40 +138,87 @@
     )(pairs, row_all, col_all, lags)
 
 
+def exchange(value, axes, sizes, moves):
+    pairs = []
+    for source in itertools.product(*[range(s) for s in sizes]):
+        target = moves(source)
+        if target is None:
+            continue
+        pairs.append((linear(source, sizes), linear(target, sizes)))
+    if not pairs:
+        return None
+    return lax.ppermute(value, axes, pairs)
+
+
+def linear(coord, sizes):
+    index = 0
+    for c, s in zip(coord, sizes):
+        index = index * s + c
+    return index
+
+
 def on_device(signal, offsets, pair_list):
     channels_here = signal.shape[0]
     samples_here = signal.shape[1]
     w_dev = samples_here // STEP
     n_tm = lax.axis_size("tm")
+    n_prow = lax.axis_size("prow")
+    n_pcol = lax.axis_size("pcol")
     tm_index = lax.axis_index("tm")
+    prow_index = lax.axis_index("prow")
+    pcol_index = lax.axis_index("pcol")
     dft_table = forward_table()
     head_samples = signal[:, :HALO]
     next_head = from_behind(head_samples, "tm", -1)
     extended = jnp.concatenate([signal, next_head], axis=1)
 
-    def one_window(window):
-        first_sample = window * STEP + offsets[tm_index * w_dev + window]
-        segment = lax.dynamic_slice_in_dim(extended, first_sample, WIN, 1)
-        return jnp.dot(segment, dft_table, preferred_element_type=jnp.float32)
-
-    spectra = lax.map(one_window, jnp.arange(w_dev, dtype=jnp.int32))
+    segments = [
+        lax.dynamic_slice_in_dim(extended, window * STEP + offsets[tm_index * w_dev + window], WIN, 1)
+        for window in range(w_dev)
+    ]
+    stacked = jnp.concatenate(segments, axis=0)
+    spectra = jnp.dot(stacked, dft_table, preferred_element_type=jnp.float32)
+    spectra = spectra.reshape(w_dev, channels_here, 2 * NF)
     whitened = whiten(spectra)
-    own_piece = whitened[None]
-    row_gathered = lax.all_gather(own_piece, ("tm", "pcol"), axis=0, tiled=True)
-    col_gathered = lax.all_gather(own_piece, ("tm", "prow"), axis=0, tiled=True)
-    row_gathered = row_gathered.reshape(n_tm, -1, w_dev, channels_here, 2 * NF)
-    col_gathered = col_gathered.reshape(n_tm, -1, w_dev, channels_here, 2 * NF)
+    half_rows = channels_here // n_tm
+
+    row_slots = []
+    for d in range(n_pcol):
+        per_tm = []
+        for e in range(n_tm):
+            half = (tm_index - e + n_tm) % n_tm
+            payload = lax.dynamic_slice_in_dim(whitened, half * half_rows, half_rows, 1)
+            if d == 0 and e == 0:
+                per_tm.append(payload)
+                continue
+            moved = exchange(
+                payload, ("tm", "pcol"), (n_tm, n_pcol),
+                lambda s, d=d, e=e: ((s[0] - e) % n_tm, (s[1] - d) % n_pcol),
+            )
+            per_tm.append(moved)
+        row_slots.append(jnp.concatenate(per_tm, axis=0))
+    row_all = jnp.stack(row_slots, axis=0)
+
+    col_slots = []
+    for d in range(n_prow):
+        per_tm = []
+        for e in range(n_tm):
+            if d == 0 and e == 0:
+                per_tm.append(whitened)
+                continue
+            moved = exchange(
+                whitened, ("tm", "prow"), (n_tm, n_prow),
+                lambda s, d=d, e=e: ((s[0] - e) % n_tm, s[1] - d) if s[1] - d >= 0 else None,
+            )
+            per_tm.append(moved)
+        col_slots.append(jnp.concatenate(per_tm, axis=0))
+    col_all = jnp.stack(col_slots, axis=0)
+
     lags = lag_table(n_tm * w_dev)
-    n_pcol = row_gathered.shape[1]
-    n_prow = col_gathered.shape[1]
-    half_rows = channels_here // n_tm
-    row_part = lax.dynamic_slice_in_dim(row_gathered, tm_index * half_rows, half_rows, 3)
-    row_all = jnp.transpose(row_part, (1, 0, 2, 3, 4)).reshape(n_pcol, n_tm * w_dev, half_rows, 2 * NF)
-    col_all = jnp.transpose(col_gathered, (1, 0, 2, 3, 4)).reshape(n_prow, n_tm * w_dev, channels_here, 2 * NF)
     local_pairs = pair_list[0, 0]
-    pairs = jnp.stack(
-        [jnp.clip(local_pairs[:, 0], 0, n_pcol - 1), jnp.clip(local_pairs[:, 1], 0, n_prow - 1)], axis=1
-    ).astype(jnp.int32)
+    row_slot = (local_pairs[:, 0] - pcol_index + n_pcol) % n_pcol
+    col_slot = jnp.clip(local_pairs[:, 1] - prow_index, 0, n_prow - 1)
+    pairs = jnp.stack([row_slot, col_slot], axis=1).astype(jnp.int32)
     result = all_pairs(pairs, row_all.astype(jnp.float32), col_all.astype(jnp.float32), lags)
     return result.reshape(1, 1, NP, half_rows, channels_here, LAGS)
 

time: 244 us -> 206 us (0.84)
  waiting for transfers between devices: 85.4 us -> 54.4 us
  starting transfers between devices: 3.71 us -> 31.5 us
  matrix products: 15.6 us -> 5.39 us
  between operations: 13.5 us -> 3.55 us
  other arithmetic: 36.2 us -> 28.8 us
  loops' own time: 3.81 us -> 0 us
  local copies, waits for them, and re-layouts: 9.26 us -> 6.61 us
    all_gather x2 -> x0, waiting for transfers between devices: 84.9 us -> none  [the longest x1 57.3 us: on_device(): col_gathered = lax.all_gather(own_piece, ('tm', 'prow'), axis=0, tiled=True)]
    ppermute x0 -> x14, waiting for transfers between devices: none -> 54.4 us  [exchange(): return lax.ppermute(value, axes, pairs)]
    ppermute x0 -> x14, starting transfers between devices: none -> 29 us  [exchange(): return lax.ppermute(value, axes, pairs)]
    dot_general x2 -> x1, matrix products: 14 us -> 4.82 us  [on_device(): spectra = jnp.dot(stacked, dft_table, preferred_element_type=jnp.float32)]
    concatenate x2 -> x0, other arithmetic: 6.4 us -> none  [the longest x1 4.95 us: forward_table(): return jnp.concatenate([cosine, sine], axis=1).astype(jnp.bfloat16)]
    convert_element_type x1 -> x0, local copies, waits for them, and re-layouts: 5.22 us -> none  [on_device(): col_all.astype(jnp.float32)]
    another operation x1 -> x0, loops' own time: 3.81 us -> none  [on_device(): spectra = lax.map(one_window, jnp.arange(w_dev, dtype=jnp.int32))]
    convert_element_type x0 -> x1, other arithmetic: none -> 2.88 us  [on_device(): col_all.astype(jnp.float32)]
  transfers between devices with their start and end apart: 3 -> 15, of which waited for: 2 -> 7; matrix products, arithmetic and copies ran while one was open for 15% -> 14% of each run, Pallas kernels for 0% -> 0%
where the time goes in v3:
time: 206 us; the launch traced here: 203 us
  Pallas kernels  73.2 us (36%)
  waiting for transfers between devices  54.4 us (26%)
  starting transfers between devices  31.5 us (15%)
  other arithmetic  28.8 us (14%)
  local copies, waits for them, and re-layouts  6.61 us (3%)
  matrix products  5.39 us (3%)
  between operations  3.55 us (2%)
    pallas_call x1, Pallas kernels, all_pairs(): pl.pallas_call(pair_kernel, grid_spec=grid_spec, out_shape=jax.ShapeDtype...  73.2 us
    ppermute x14, waiting for transfers between devices, exchange(): return lax.ppermute(value, axes, pairs)  54.4 us
    ppermute x14, starting transfers between devices, exchange(): return lax.ppermute(value, axes, pairs)  29 us
    sub x1, other arithmetic, forward_table(): cos_full = (high_cos * low_cos - high_sin * low_sin).reshape(WIN, NF)  11.8 us
    another operation x2, other arithmetic  11.4 us
    dot_general x1, matrix products, on_device(): spectra = jnp.dot(stacked, dft_table, preferred_element_type=jnp.float32)  4.82 us
  transfers between devices with their start and end apart: 15, of which 7 were waited for; matrix products, arithmetic and copies ran while one was open for 14% of the time, Pallas kernels for 0%

profile of v3, /device:TPU:14, one launch (start us, length us, event | category | flops | bytes accessed | tf_op | source)
XLA Modules:
  0.0 203.4 jit_solution(8897542299705861110)
XLA Ops:
  0.0 1.3 slice.17
  1.3 2.5 %collective-permute-start = (bf16[128,4352]{1,0:T(8,128)(2,1)S(1)}, bf16[128,4352]{1,0:T(8,128)(2,1)S(1)}, u32[]{:S(2)}, u32[]{:S(2)}) collective-permute-start(bf16[128,4352]{1,0:T(8,128)(2,1)S(1)} %slice.17), channel_id=1, source_target_pairs={{16,0},{17,1},{18,2},{19,3},{20,4},{21,5},{22,6},{23,7},{24,8},{25... | collective-permute-start | bytes 3342344 | tf_op jit(solution)/shard_map/ppermute | solution.py:27
  3.9 0.1 fusion.38
  4.0 0.1 multiply_subtract_fusion.1
  4.2 0.8 fusion.42
  4.9 0.1 copy.6
  5.0 0.1 copy.7
  5.1 0.8 fusion.26
  5.9 0.5 fusion.33
  6.4 1.4 fusion.43
  10.4 2.0 multiply_convert_fusion.1
  13.0 11.8 %multiply_subtract_fusion = (f32[60,128,384]{2,1,0:T(8,128)}, f32[60,128,384]{2,1,0:T(8,128)}) fusion(f32[128,384]{1,0:T(8,128)S(1)} %get-tuple-element.12, f32[60,384]{1,0:T(8,128)S(1)} %get-tuple-element.11, f32[128,384]{1,0:T(8,128)S(1)} %get-tuple-element.10, f32[60,384]{1,0:T(8,128)S(1)} %get-tuple-element.9), kind=kLoop, calls=%fused_computation.9 | loop fusion | flops 17694720 | bytes 24170496 | tf_op jit(solution)/shard_map/sub | solution.py:44
  24.8 9.5 %fusion.4 = (bf16[7680,384]{1,0:T(8,128)(2,1)S(1)}, bf16[7680,384]{1,0:T(8,128)(2,1)S(1)}) fusion(f32[60,128,384]{2,1,0:T(8,128)} %get-tuple-element.16, f32[7680]{0:T(1024)S(1)} %fusion.38, f32[60,128,384]{2,1,0:T(8,128)} %get-tuple-element.15, f32[7680]{0:T(1024)S(1)} %multiply_subtract_fusion.1), kind=kLoop, calls=%fused_computation.5 | loop fusion | flops 11796480 | bytes 35450880 | tf_op jit(solution)/shard_map/convert.3
  34.3 0.1 constant_dynamic-update-slice_fusion.1
  34.5 0.1 constant_dynamic-update-slice_fusion
  34.6 2.7 %constant_dynamic-slice_fusion.3 = (bf16[128,7680]{1,0:T(8,128)(2,1)S(1)}, bf16[128,7680]{1,0:T(8,128)(2,1)}) fusion(bf16[128,12032]{1,0:T(8,128)(2,1)S(1)} %constant_dynamic-update-slice_fusion, s32[]{:T(128)S(6)} %select_n.92, s32[]{:T(128)S(6)} %select_n.94), kind=kLoop, calls=%fused_computation.79 | loop fusion | bytes 7864328 | tf_op jit(solution)/shard_map/dynamic_slice | solution.py:176
  37.3 4.8 %fusion = f32[256,768]{1,0:T(8,128)S(1)} fusion(bf16[7680,384]{1,0:T(8,128)(2,1)S(1)} %get-tuple-element.31, bf16[7680,384]{1,0:T(8,128)(2,1)S(1)} %get-tuple-element.32, bf16[128,7680]{1,0:T(8,128)(2,1)} %get-tuple-element.14, bf16[128,7680]{1,0:T(8,128)(2,1)S(1)} %get-tuple-element.13), kind=kOutput, calls=%fused_computation | convolution fusion | flops 3051356160 | bytes 16515072 | tf_op jit(solution)/shard_map/dot_general | solution.py:180
  42.1 0.1 fusion.36
  42.3 0.6 fusion.11
  42.8 0.1 fusion.12
  43.0 0.1 collective-permute-start.1
  43.1 0.9 collective-permute-start.7
  44.0 1.2 collective-permute-start.6
  45.2 0.1 pad_add_fusion.pairs_ref
  45.3 1.0 collective-permute-start.5
  46.3 0.6 collective-permute-start.4
  46.8 4.0 %collective-permute-done.1 = bf16[2,64,768]{2,1,0:T(8,128)(2,1)S(1)} collective-permute-done((bf16[2,64,768]{2,1,0:T(8,128)(2,1)S(1)}, bf16[2,64,768]{2,1,0:T(8,128)(2,1)S(1)}, u32[]{:S(2)}, u32[]{:S(2)}) %collective-permute-start.1) | collective-permute-done | bytes 196640 | tf_op jit(solution)/shard_map/ppermute | solution.py:150
  50.9 1.7 collective-permute-done.7
  52.5 2.7 %collective-permute-start.2 = (bf16[2,64,768]{2,1,0:T(8,128)(2,1)S(1)}, bf16[2,64,768]{2,1,0:T(8,128)(2,1)S(1)}, u32[]{:S(2)}, u32[]{:S(2)}) collective-permute-start(bf16[2,64,768]{2,1,0:T(8,128)(2,1)S(1)} %get-tuple-element.17), channel_id=1, source_target_pairs={{0,3},{1,0},{2,1},{3,2},{16,19},{17,16},{18,17},{19,18},{4,7},{5,4... | collective-permute-start | bytes 589832 | tf_op jit(solution)/shard_map/ppermute | solution.py:150
  55.2 0.7 collective-permute-start.14
  56.0 3.2 %collective-permute-done.5 = bf16[2,64,768]{2,1,0:T(8,128)(2,1)S(1)} collective-permute-done((bf16[2,64,768]{2,1,0:T(8,128)(2,1)S(1)}, bf16[2,64,768]{2,1,0:T(8,128)(2,1)S(1)}, u32[]{:S(2)}, u32[]{:S(2)}) %collective-permute-start.5) | collective-permute-done | bytes 196640 | tf_op jit(solution)/shard_map/ppermute | solution.py:150
  59.2 0.7 collective-permute-start.13
  59.9 3.0 %collective-permute-start.8 = (bf16[2,128,768]{2,1,0:T(8,128)(2,1)S(1)}, bf16[2,128,768]{2,1,0:T(8,128)(2,1)S(1)}, u32[]{:S(2)}, u32[]{:S(2)}) collective-permute-start(bf16[2,128,768]{2,1,0:T(8,128)(2,1)S(1)} %fusion.12), channel_id=1, source_target_pairs={{0,16},{4,20},{8,24},{12,28},{16,0},{20,4},{24,8},{28,12},{1,17},{... | collective-permute-start | bytes 1179656 | tf_op jit(solution)/shard_map/ppermute | solution.py:150
  63.0 1.3 collective-permute-start.12
  64.3 1.3 collective-permute-start.11
  65.6 0.3 maximum_convert_fusion.1.row_ref
  65.9 7.5 %collective-permute-start.10 = (bf16[2,128,768]{2,1,0:T(8,128)(2,1)S(1)}, bf16[2,128,768]{2,1,0:T(8,128)(2,1)S(1)}, u32[]{:S(2)}, u32[]{:S(2)}) collective-permute-start(bf16[2,128,768]{2,1,0:T(8,128)(2,1)S(1)} %fusion.12), channel_id=1, source_target_pairs={{4,16},{8,20},{12,24},{20,0},{24,4},{28,8},{5,17},{9,21},{13,25},{... | collective-permute-start | bytes 1179656 | tf_op jit(solution)/shard_map/ppermute | solution.py:150
  73.5 8.1 %collective-permute-start.9 = (bf16[2,128,768]{2,1,0:T(8,128)(2,1)S(1)}, bf16[2,128,768]{2,1,0:T(8,128)(2,1)S(1)}, u32[]{:S(2)}, u32[]{:S(2)}) collective-permute-start(bf16[2,128,768]{2,1,0:T(8,128)(2,1)S(1)} %fusion.12), channel_id=1, source_target_pairs={{4,0},{8,4},{12,8},{20,16},{24,20},{28,24},{5,1},{9,5},{13,9},{21,... | collective-permute-start | bytes 1179656 | tf_op jit(solution)/shard_map/ppermute | solution.py:150
  81.6 0.1 maximum_bitcast_fusion
  81.6 0.1 maximum_bitcast_fusion.3
  81.7 4.9 %collective-permute-done.12 = bf16[2,128,768]{2,1,0:T(8,128)(2,1)S(1)} collective-permute-done((bf16[2,128,768]{2,1,0:T(8,128)(2,1)S(1)}, bf16[2,128,768]{2,1,0:T(8,128)(2,1)S(1)}, u32[]{:S(2)}, u32[]{:S(2)}) %collective-permute-start.12) | collective-permute-done | bytes 393248 | tf_op jit(solution)/shard_map/ppermute | solution.py:150
  86.6 7.9 %collective-permute-done.11 = bf16[2,128,768]{2,1,0:T(8,128)(2,1)S(1)} collective-permute-done((bf16[2,128,768]{2,1,0:T(8,128)(2,1)S(1)}, bf16[2,128,768]{2,1,0:T(8,128)(2,1)S(1)}, u32[]{:S(2)}, u32[]{:S(2)}) %collective-permute-start.11) | collective-permute-done | bytes 393248 | tf_op jit(solution)/shard_map/ppermute | solution.py:150
  94.5 0.1 maximum_bitcast_fusion.2
  94.6 25.8 %collective-permute-done.10 = bf16[2,128,768]{2,1,0:T(8,128)(2,1)S(1)} collective-permute-done((bf16[2,128,768]{2,1,0:T(8,128)(2,1)S(1)}, bf16[2,128,768]{2,1,0:T(8,128)(2,1)S(1)}, u32[]{:S(2)}, u32[]{:S(2)}) %collective-permute-start.10) | collective-permute-done | bytes 393248 | tf_op jit(solution)/shard_map/ppermute | solution.py:150
  120.4 6.9 %collective-permute-done.9 = bf16[2,128,768]{2,1,0:T(8,128)(2,1)S(1)} collective-permute-done((bf16[2,128,768]{2,1,0:T(8,128)(2,1)S(1)}, bf16[2,128,768]{2,1,0:T(8,128)(2,1)S(1)}, u32[]{:S(2)}, u32[]{:S(2)}) %collective-permute-start.9) | collective-permute-done | bytes 393248 | tf_op jit(solution)/shard_map/ppermute | solution.py:150
  127.3 0.1 maximum_bitcast_fusion.1
  127.3 2.9 %maximum_convert_fusion.col_ref = f32[4,4,128,768]{3,2,1,0:T(8,128)} fusion(bf16[1,4,128,768]{3,2,1,0:T(8,128)(2,1)S(1)} %maximum_bitcast_fusion.3, bf16[1,4,128,768]{3,2,1,0:T(8,128)(2,1)S(1)} %maximum_bitcast_fusion.2, bf16[1,4,128,768]{3,2,1,0:T(8,128)(2,1)S(1)} %maximum_bitcast_fusion.1, bf16[1,4,128,768]{3,2,1,0:T(8,128)(2,1)S(1)} %maximum_bitcast_fusion), kind=kLoop, calls=%fused_computation.13 | loop fusion | flops 6291456 | bytes 9437184 | tf_op jit(solution)/shard_map/convert_element_type | solution.py:222
  130.2 73.2 %shard_map.37 = bf16[4,64,128,256]{3,2,1,0:T(8,128)(2,1)} custom-call(s32[4,2]{1,0:T(4,128)S(1)} %pad_add_fusion.pairs_ref, f32[4,4,64,768]{3,2,1,0:T(8,128)S(1)} %maximum_convert_fusion.1.row_ref, f32[4,4,128,768]{3,2,1,0:T(8,128)} %maximum_convert_fusion.col_ref, bf16[768,256]{1,0:T(8,128)(2,1)S(1)} %pad_maximum_fusion.lags_ref), custom_call_target="tpu_custom_call" | custom-call | flops 13287555072 | bytes 26214400 | tf_op jit(solution)/shard_map/pallas_call | solution.py:125
  (22 shorter events, 0.3 us)
Async XLA Ops:
  1.3 33.2 %collective-permute-start = (bf16[128,4352]{1,0:T(8,128)(2,1)S(1)}, bf16[128,4352]{1,0:T(8,128)(2,1)S(1)}, u32[]{:S(2)}, u32[]{:S(2)}) collective-permute-start(bf16[128,4352]{1,0:T(8,128)(2,1)S(1)} %slice.17), channel_id=1, source_target_pairs={{16,0},{17,1},{18,2},{19,3},{20,4},{21,5},{22,6},{23,7},{24,8},{25... | collective-permute-start | bytes 3342344 | tf_op jit(solution)/shard_map/ppermute | solution.py:27
  24.8 9.5 %copy-start = (bf16[128,7680]{1,0:T(8,128)(2,1)S(1)}, bf16[128,7680]{1,0:T(8,128)(2,1)}, u32[]{:S(2)}) copy-start(bf16[128,7680]{1,0:T(8,128)(2,1)} %param.3) | copy-start | bytes 5898244
  43.0 7.8 %collective-permute-start.1 = (bf16[2,64,768]{2,1,0:T(8,128)(2,1)S(1)}, bf16[2,64,768]{2,1,0:T(8,128)(2,1)S(1)}, u32[]{:S(2)}, u32[]{:S(2)}) collective-permute-start(bf16[2,64,768]{2,1,0:T(8,128)(2,1)S(1)} %get-tuple-element.18), channel_id=1, source_target_pairs={{0,16},{1,17},{2,18},{3,19},{16,0},{17,1},{18,2},{19,3},{4,20},{5,... | collective-permute-start | bytes 589832 | tf_op jit(solution)/shard_map/ppermute | solution.py:150
  43.1 9.5 %collective-permute-start.7 = (bf16[2,64,768]{2,1,0:T(8,128)(2,1)S(1)}, bf16[2,64,768]{2,1,0:T(8,128)(2,1)S(1)}, u32[]{:S(2)}, u32[]{:S(2)}) collective-permute-start(bf16[2,64,768]{2,1,0:T(8,128)(2,1)S(1)} %get-tuple-element.18), channel_id=1, source_target_pairs={{0,17},{1,18},{2,19},{3,16},{16,1},{17,2},{18,3},{19,0},{4,21},{5,... | collective-permute-start | bytes 589832 | tf_op jit(solution)/shard_map/ppermute | solution.py:150
  44.0 11.2 %collective-permute-start.6 = (bf16[2,64,768]{2,1,0:T(8,128)(2,1)S(1)}, bf16[2,64,768]{2,1,0:T(8,128)(2,1)S(1)}, u32[]{:S(2)}, u32[]{:S(2)}) collective-permute-start(bf16[2,64,768]{2,1,0:T(8,128)(2,1)S(1)} %get-tuple-element.17), channel_id=1, source_target_pairs={{0,1},{1,2},{2,3},{3,0},{16,17},{17,18},{18,19},{19,16},{4,5},{5,6... | collective-permute-start | bytes 589832 | tf_op jit(solution)/shard_map/ppermute | solution.py:150
  45.3 13.9 %collective-permute-start.5 = (bf16[2,64,768]{2,1,0:T(8,128)(2,1)S(1)}, bf16[2,64,768]{2,1,0:T(8,128)(2,1)S(1)}, u32[]{:S(2)}, u32[]{:S(2)}) collective-permute-start(bf16[2,64,768]{2,1,0:T(8,128)(2,1)S(1)} %get-tuple-element.18), channel_id=1, source_target_pairs={{0,18},{1,19},{2,16},{3,17},{16,2},{17,3},{18,0},{19,1},{4,22},{5,... | collective-permute-start | bytes 589832 | tf_op jit(solution)/shard_map/ppermute | solution.py:150
  46.3 13.7 %collective-permute-start.4 = (bf16[2,64,768]{2,1,0:T(8,128)(2,1)S(1)}, bf16[2,64,768]{2,1,0:T(8,128)(2,1)S(1)}, u32[]{:S(2)}, u32[]{:S(2)}) collective-permute-start(bf16[2,64,768]{2,1,0:T(8,128)(2,1)S(1)} %get-tuple-element.17), channel_id=1, source_target_pairs={{0,2},{1,3},{2,0},{3,1},{16,18},{17,19},{18,16},{19,17},{4,6},{5,7... | collective-permute-start | bytes 589832 | tf_op jit(solution)/shard_map/ppermute | solution.py:150
  50.8 12.2 %collective-permute-start.3 = (bf16[2,64,768]{2,1,0:T(8,128)(2,1)S(1)}, bf16[2,64,768]{2,1,0:T(8,128)(2,1)S(1)}, u32[]{:S(2)}, u32[]{:S(2)}) collective-permute-start(bf16[2,64,768]{2,1,0:T(8,128)(2,1)S(1)} %get-tuple-element.18), channel_id=1, source_target_pairs={{0,19},{1,16},{2,17},{3,18},{16,3},{17,0},{18,1},{19,2},{4,23},{5,... | collective-permute-start | bytes 589832 | tf_op jit(solution)/shard_map/ppermute | solution.py:150
  52.5 11.8 %collective-permute-start.2 = (bf16[2,64,768]{2,1,0:T(8,128)(2,1)S(1)}, bf16[2,64,768]{2,1,0:T(8,128)(2,1)S(1)}, u32[]{:S(2)}, u32[]{:S(2)}) collective-permute-start(bf16[2,64,768]{2,1,0:T(8,128)(2,1)S(1)} %get-tuple-element.17), channel_id=1, source_target_pairs={{0,3},{1,0},{2,1},{3,2},{16,19},{17,16},{18,17},{19,18},{4,7},{5,4... | collective-permute-start | bytes 589832 | tf_op jit(solution)/shard_map/ppermute | solution.py:150
  55.2 10.7 %collective-permute-start.14 = (bf16[2,128,768]{2,1,0:T(8,128)(2,1)S(1)}, bf16[2,128,768]{2,1,0:T(8,128)(2,1)S(1)}, u32[]{:S(2)}, u32[]{:S(2)}) collective-permute-start(bf16[2,128,768]{2,1,0:T(8,128)(2,1)S(1)} %fusion.12), channel_id=1, source_target_pairs={{12,16},{28,0},{13,17},{29,1},{14,18},{30,2},{15,19},{31,3}} | collective-permute-start | bytes 1179656 | tf_op jit(solution)/shard_map/ppermute | solution.py:150
  59.2 22.4 %collective-permute-start.13 = (bf16[2,128,768]{2,1,0:T(8,128)(2,1)S(1)}, bf16[2,128,768]{2,1,0:T(8,128)(2,1)S(1)}, u32[]{:S(2)}, u32[]{:S(2)}) collective-permute-start(bf16[2,128,768]{2,1,0:T(8,128)(2,1)S(1)} %fusion.12), channel_id=1, source_target_pairs={{12,0},{28,16},{13,1},{29,17},{14,2},{30,18},{15,3},{31,19}} | collective-permute-start | bytes 1179656 | tf_op jit(solution)/shard_map/ppermute | solution.py:150
  59.9 13.6 %collective-permute-start.8 = (bf16[2,128,768]{2,1,0:T(8,128)(2,1)S(1)}, bf16[2,128,768]{2,1,0:T(8,128)(2,1)S(1)}, u32[]{:S(2)}, u32[]{:S(2)}) collective-permute-start(bf16[2,128,768]{2,1,0:T(8,128)(2,1)S(1)} %fusion.12), channel_id=1, source_target_pairs={{0,16},{4,20},{8,24},{12,28},{16,0},{20,4},{24,8},{28,12},{1,17},{... | collective-permute-start | bytes 1179656 | tf_op jit(solution)/shard_map/ppermute | solution.py:150
  63.0 23.6 %collective-permute-start.12 = (bf16[2,128,768]{2,1,0:T(8,128)(2,1)S(1)}, bf16[2,128,768]{2,1,0:T(8,128)(2,1)S(1)}, u32[]{:S(2)}, u32[]{:S(2)}) collective-permute-start(bf16[2,128,768]{2,1,0:T(8,128)(2,1)S(1)} %fusion.12), channel_id=1, source_target_pairs={{8,16},{12,20},{24,0},{28,4},{9,17},{13,21},{25,1},{29,5},{10,18},... | collective-permute-start | bytes 1179656 | tf_op jit(solution)/shard_map/ppermute | solution.py:150
  64.3 30.2 %collective-permute-start.11 = (bf16[2,128,768]{2,1,0:T(8,128)(2,1)S(1)}, bf16[2,128,768]{2,1,0:T(8,128)(2,1)S(1)}, u32[]{:S(2)}, u32[]{:S(2)}) collective-permute-start(bf16[2,128,768]{2,1,0:T(8,128)(2,1)S(1)} %fusion.12), channel_id=1, source_target_pairs={{8,0},{12,4},{24,16},{28,20},{9,1},{13,5},{25,17},{29,21},{10,2},{... | collective-permute-start | bytes 1179656 | tf_op jit(solution)/shard_map/ppermute | solution.py:150
  65.9 54.4 %collective-permute-start.10 = (bf16[2,128,768]{2,1,0:T(8,128)(2,1)S(1)}, bf16[2,128,768]{2,1,0:T(8,128)(2,1)S(1)}, u32[]{:S(2)}, u32[]{:S(2)}) collective-permute-start(bf16[2,128,768]{2,1,0:T(8,128)(2,1)S(1)} %fusion.12), channel_id=1, source_target_pairs={{4,16},{8,20},{12,24},{20,0},{24,4},{28,8},{5,17},{9,21},{13,25},{... | collective-permute-start | bytes 1179656 | tf_op jit(solution)/shard_map/ppermute | solution.py:150
  73.5 53.8 %collective-permute-start.9 = (bf16[2,128,768]{2,1,0:T(8,128)(2,1)S(1)}, bf16[2,128,768]{2,1,0:T(8,128)(2,1)S(1)}, u32[]{:S(2)}, u32[]{:S(2)}) collective-permute-start(bf16[2,128,768]{2,1,0:T(8,128)(2,1)S(1)} %fusion.12), channel_id=1, source_target_pairs={{4,0},{8,4},{12,8},{20,16},{24,20},{28,24},{5,1},{9,5},{13,9},{21,... | collective-permute-start | bytes 1179656 | tf_op jit(solution)/shard_map/ppermute | solution.py:150

commit v4 on v3

--- a/solution.py
+++ b/solution.py
@@ -41,13 +41,13 @@
     )
     high_cos, high_sin = high_cos[:, None, :], high_sin[:, None, :]
     low_cos, low_sin = low_cos[None], low_sin[None]
-    cos_full = (high_cos * low_cos - high_sin * low_sin).reshape(WIN, NF)
-    sin_full = (high_sin * low_cos + high_cos * low_sin).reshape(WIN, NF)
+    cos_full = high_cos * low_cos - high_sin * low_sin
+    sin_full = high_sin * low_cos + high_cos * low_sin
     sample_idx = jnp.arange(WIN, dtype=jnp.int32)
     taper_curve = 0.5 - 0.5 * jnp.cos(sample_idx.astype(jnp.float32) * (two_pi / WIN))
-    cosine = taper_curve[:, None] * cos_full
-    sine = -taper_curve[:, None] * sin_full
-    return jnp.concatenate([cosine, sine], axis=1).astype(jnp.bfloat16)
+    taper_curve = taper_curve.reshape(n_coarse, coarse, 1)
+    table = jnp.concatenate([taper_curve * cos_full, -taper_curve * sin_full], axis=2).astype(jnp.bfloat16)
+    return table.reshape(WIN, 2 * NF)
 
 
 def lag_table(count):
@@ -182,35 +182,26 @@
     whitened = whiten(spectra)
     half_rows = channels_here // n_tm
 
-    row_slots = []
-    for d in range(n_pcol):
-        per_tm = []
-        for e in range(n_tm):
-            half = (tm_index - e + n_tm) % n_tm
-            payload = lax.dynamic_slice_in_dim(whitened, half * half_rows, half_rows, 1)
-            if d == 0 and e == 0:
-                per_tm.append(payload)
-                continue
-            moved = exchange(
-                payload, ("tm", "pcol"), (n_tm, n_pcol),
-                lambda s, d=d, e=e: ((s[0] - e) % n_tm, (s[1] - d) % n_pcol),
-            )
-            per_tm.append(moved)
-        row_slots.append(jnp.concatenate(per_tm, axis=0))
+    row_windows = [lax.dynamic_slice_in_dim(whitened, tm_index * half_rows, half_rows, 1)]
+    for e in range(1, n_tm):
+        half = (tm_index - e + n_tm) % n_tm
+        payload = lax.dynamic_slice_in_dim(whitened, half * half_rows, half_rows, 1)
+        row_windows.append(exchange(payload, ("tm",), (n_tm,), lambda s, e=e: ((s[0] - e) % n_tm,)))
+    row_own = jnp.concatenate(row_windows, axis=0)
+    row_slots = [row_own]
+    for d in range(1, n_pcol):
+        row_slots.append(exchange(row_own, ("pcol",), (n_pcol,), lambda s, d=d: ((s[0] - d) % n_pcol,)))
     row_all = jnp.stack(row_slots, axis=0)
 
     col_slots = []
     for d in range(n_prow):
-        per_tm = []
-        for e in range(n_tm):
-            if d == 0 and e == 0:
-                per_tm.append(whitened)
-                continue
-            moved = exchange(
-                whitened, ("tm", "prow"), (n_tm, n_prow),
-                lambda s, d=d, e=e: ((s[0] - e) % n_tm, s[1] - d) if s[1] - d >= 0 else None,
-            )
-            per_tm.append(moved)
+        if d == 0:
+            near = whitened
+        else:
+            near = exchange(whitened, ("prow",), (n_prow,), lambda s, d=d: (s[0] - d,) if s[0] - d >= 0 else None)
+        per_tm = [near]
+        for e in range(1, n_tm):
+            per_tm.append(exchange(near, ("tm",), (n_tm,), lambda s, e=e: ((s[0] - e) % n_tm,)))
         col_slots.append(jnp.concatenate(per_tm, axis=0))
     col_all = jnp.stack(col_slots, axis=0)
 

time: 206 us -> 190 us (0.922)
  the two profiles are of different devices: /device:TPU:14 before, /device:TPU:0 now
where the time goes in v4:
time: 190 us
  Pallas kernels  73.2 us (39%)
  waiting for transfers between devices  54.1 us (28%)
  other arithmetic  33.7 us (18%)
  starting transfers between devices  13.5 us (7%)
  local copies, waits for them, and re-layouts  7.67 us (4%)
  matrix products  3.76 us (2%)
  between operations  3.62 us (2%)
    pallas_call x1, Pallas kernels, all_pairs(): pl.pallas_call(pair_kernel, grid_spec=grid_spec, out_shape=jax.ShapeDtype...  73.2 us
    ppermute x11, waiting for transfers between devices, exchange(): return lax.ppermute(value, axes, pairs)  54.1 us
    another operation x2, other arithmetic  16.2 us
    ppermute x11, starting transfers between devices, exchange(): return lax.ppermute(value, axes, pairs)  12.3 us
    sub x1, other arithmetic, forward_table(): cos_full = high_cos * low_cos - high_sin * low_sin  11.8 us
  transfers between devices with their start and end apart: 12, of which 5 were waited for; matrix products, arithmetic and copies ran while one was open for 17% of the time, Pallas kernels for 0%

profile of v4, /device:TPU:0, one launch (start us, length us, event | category | flops | bytes accessed | tf_op | source)
XLA Modules:
  0.0 189.5 jit_solution(8688863102293931529)
XLA Ops:
  0.0 2.3 %slice.17 = bf16[128,4352]{1,0:T(8,128)(2,1)} slice(bf16[128,7680]{1,0:T(8,128)(2,1)} %param.3), slice={[0:128], [0:4352]} | slice | bytes 2228224 | tf_op jit(solution)/shard_map/slice | solution.py:171
  2.3 1.3 collective-permute-start
  3.6 0.1 fusion.34
  3.8 0.1 subtract_bitcast_fusion
  3.9 0.8 fusion.22
  4.7 0.5 fusion.29
  5.2 11.8 %multiply_subtract_fusion = (f32[60,128,384]{2,1,0:T(8,128)}, f32[60,128,384]{2,1,0:T(8,128)}) fusion(f32[128,384]{1,0:T(8,128)S(1)} %get-tuple-element.12, f32[60,384]{1,0:T(8,128)S(1)} %get-tuple-element.11, f32[128,384]{1,0:T(8,128)S(1)} %get-tuple-element.10, f32[60,384]{1,0:T(8,128)S(1)} %get-tuple-element.9), kind=kLoop, calls=%fused_computation.9 | loop fusion | flops 17694720 | bytes 24170496 | tf_op jit(solution)/shard_map/sub | solution.py:44
  17.0 14.3 %fusion.3 = (bf16[7680,384]{1,0:T(8,128)(2,1)}, bf16[7680,384]{1,0:T(8,128)(2,1)}) fusion(f32[60,128,384]{2,1,0:T(8,128)} %get-tuple-element.16, f32[7680]{0:T(1024)S(1)} %fusion.34, f32[60,128,384]{2,1,0:T(8,128)} %get-tuple-element.15, f32[7680]{0:T(1024)S(1)} %subtract_bitcast_fusion), kind=kLoop, calls=%fused_computation.5 | loop fusion | flops 11796480 | bytes 35450880 | tf_op jit(solution)/shard_map/convert.3
  31.4 0.7 fusion.40
  34.7 0.1 copy.6
  34.8 0.1 copy.7
  35.6 0.1 constant_dynamic-update-slice_fusion.1
  35.8 0.1 constant_dynamic-update-slice_fusion
  35.9 1.6 constant_dynamic-slice_fusion.3
  37.5 0.3 pad_maximum_fusion
  37.7 0.2 slice-done.2
  37.9 1.3 slice-done
  39.2 0.5 slice-done.3
  39.7 0.7 slice-done.1
  40.4 3.2 %fusion = f32[2,128,768]{2,1,0:T(8,128)S(1)} fusion(bf16[2,128,7680]{2,1,0:T(8,128)(2,1)S(1)} %bitcast.42, bf16[7680,384]{1,0:T(8,128)(2,1)S(1)} %bitcast.39, bf16[7680,384]{1,0:T(8,128)(2,1)S(1)} %bitcast.41), kind=kOutput, calls=%fused_computation.1 | convolution fusion | flops 3043491840 | bytes 16515072 | tf_op jit(solution)/shard_map/dot_general | solution.py:180
  43.6 0.1 fusion.32
  43.7 0.6 fusion.7
  44.3 0.1 fusion.8
  44.4 3.1 %collective-permute-start.5 = (bf16[2,128,768]{2,1,0:T(8,128)(2,1)S(1)}, bf16[2,128,768]{2,1,0:T(8,128)(2,1)S(1)}, u32[]{:S(2)}, u32[]{:S(2)}) collective-permute-start(bf16[2,128,768]{2,1,0:T(8,128)(2,1)S(1)} %fusion.8), channel_id=1, source_target_pairs={{0,16},{16,0},{1,17},{17,1},{2,18},{18,2},{3,19},{19,3},{4,20},{20... | collective-permute-start | bytes 1179656 | tf_op jit(solution)/shard_map/ppermute | solution.py:150
  47.5 1.5 collective-permute-start.6
  49.0 0.1 collective-permute-start.1
  49.1 1.9 %multiply_convert_fusion.1 = (bf16[384,256]{1,0:T(8,128)(2,1)S(1)}, bf16[384,256]{1,0:T(8,128)(2,1)S(1)}) fusion(s32[256]{0:T(256)S(1)} %and_select_fusion, s32[384]{0:T(512)S(1)} %iota_add_fusion), kind=kLoop, calls=%fused_computation.34 | loop fusion | flops 1376256 | bytes 395776 | tf_op jit(solution)/shard_map/convert
  51.0 1.3 collective-permute-start.8
  52.3 1.3 collective-permute-start.10
  53.6 7.2 %collective-permute-done.1 = bf16[2,64,768]{2,1,0:T(8,128)(2,1)S(1)} collective-permute-done((bf16[2,64,768]{2,1,0:T(8,128)(2,1)S(1)}, bf16[2,64,768]{2,1,0:T(8,128)(2,1)S(1)}, u32[]{:S(2)}, u32[]{:S(2)}) %collective-permute-start.1) | collective-permute-done | bytes 196640 | tf_op jit(solution)/shard_map/ppermute | solution.py:150
  60.9 1.0 collective-permute-start.2
  61.9 1.5 collective-permute-start.3
  63.4 0.1 collective-permute-start.4
  63.6 23.5 %collective-permute-done.8 = bf16[2,128,768]{2,1,0:T(8,128)(2,1)S(1)} collective-permute-done((bf16[2,128,768]{2,1,0:T(8,128)(2,1)S(1)}, bf16[2,128,768]{2,1,0:T(8,128)(2,1)S(1)}, u32[]{:S(2)}, u32[]{:S(2)}) %collective-permute-start.8) | collective-permute-done | bytes 393248 | tf_op jit(solution)/shard_map/ppermute | solution.py:150
  87.1 0.3 collective-permute-start.7
  87.4 0.1 pad_add_fusion.pairs_ref
  87.5 1.7 collective-permute-start.9
  89.2 0.1 maximum_bitcast_fusion.2
  89.3 0.4 collective-permute-start.11
  89.7 0.3 maximum_convert_fusion.1.row_ref
  89.9 9.2 %collective-permute-done.7 = bf16[2,128,768]{2,1,0:T(8,128)(2,1)S(1)} collective-permute-done((bf16[2,128,768]{2,1,0:T(8,128)(2,1)S(1)}, bf16[2,128,768]{2,1,0:T(8,128)(2,1)S(1)}, u32[]{:S(2)}, u32[]{:S(2)}) %collective-permute-start.7) | collective-permute-done | bytes 393248 | tf_op jit(solution)/shard_map/ppermute | solution.py:150
  99.1 0.1 maximum_bitcast_fusion.3
  99.2 8.4 %collective-permute-done.9 = bf16[2,128,768]{2,1,0:T(8,128)(2,1)S(1)} collective-permute-done((bf16[2,128,768]{2,1,0:T(8,128)(2,1)S(1)}, bf16[2,128,768]{2,1,0:T(8,128)(2,1)S(1)}, u32[]{:S(2)}, u32[]{:S(2)}) %collective-permute-start.9) | collective-permute-done | bytes 393248 | tf_op jit(solution)/shard_map/ppermute | solution.py:150
  107.5 0.1 maximum_bitcast_fusion.4
  107.6 5.8 %collective-permute-done.11 = bf16[2,128,768]{2,1,0:T(8,128)(2,1)S(1)} collective-permute-done((bf16[2,128,768]{2,1,0:T(8,128)(2,1)S(1)}, bf16[2,128,768]{2,1,0:T(8,128)(2,1)S(1)}, u32[]{:S(2)}, u32[]{:S(2)}) %collective-permute-start.11) | collective-permute-done | bytes 393248 | tf_op jit(solution)/shard_map/ppermute | solution.py:150
  113.4 0.1 maximum_bitcast_fusion.5
  113.5 2.9 %maximum_convert_fusion.col_ref = f32[4,4,128,768]{3,2,1,0:T(8,128)} fusion(bf16[1,4,128,768]{3,2,1,0:T(8,128)(2,1)S(1)} %maximum_bitcast_fusion.5, bf16[1,4,128,768]{3,2,1,0:T(8,128)(2,1)S(1)} %maximum_bitcast_fusion.4, bf16[1,4,128,768]{3,2,1,0:T(8,128)(2,1)S(1)} %maximum_bitcast_fusion.3, bf16[1,4,128,768]{3,2,1,0:T(8,128)(2,1)S(1)} %maximum_bitcast_fusion.2), kind=kLoop, calls=%fused_computation.11 | loop fusion | flops 6291456 | bytes 9437184 | tf_op jit(solution)/shard_map/convert_element_type | solution.py:213
  116.3 73.2 %shard_map.37 = bf16[4,64,128,256]{3,2,1,0:T(8,128)(2,1)} custom-call(s32[4,2]{1,0:T(4,128)S(1)} %pad_add_fusion.pairs_ref, f32[4,4,64,768]{3,2,1,0:T(8,128)S(1)} %maximum_convert_fusion.1.row_ref, f32[4,4,128,768]{3,2,1,0:T(8,128)} %maximum_convert_fusion.col_ref, bf16[768,256]{1,0:T(8,128)(2,1)S(1)} %pad_maximum_fusion.2.lags_ref), custom_call_target="tpu_custom_call" | custom-call | flops 13287555072 | bytes 26214400 | tf_op jit(solution)/shard_map/pallas_call | solution.py:125
  (28 shorter events, 0.2 us)
Async XLA Ops:
  2.3 33.4 %collective-permute-start = (bf16[128,4352]{1,0:T(8,128)(2,1)}, bf16[128,4352]{1,0:T(8,128)(2,1)S(1)}, u32[]{:S(2)}, u32[]{:S(2)}) collective-permute-start(bf16[128,4352]{1,0:T(8,128)(2,1)} %slice.17), channel_id=1, source_target_pairs={{16,0},{17,1},{18,2},{19,3},{20,4},{21,5},{22,6},{23,7},{24,8},{25... | collective-permute-start | bytes 3342344 | tf_op jit(solution)/shard_map/ppermute | solution.py:27
  17.0 14.3 %copy-start.2 = (s32[1,1,4,2]{2,3,1,0:T(2,128)S(1)}, s32[1,1,4,2]{2,3,1,0:T(2,128)}, u32[]{:S(2)}) copy-start(s32[1,1,4,2]{2,3,1,0:T(2,128)} %param.5) | copy-start | bytes 100
  17.0 14.3 %copy-start.1 = (s32[4]{0:T(128)S(1)}, s32[4]{0:T(128)}, u32[]{:S(2)}) copy-start(s32[4]{0:T(128)} %param.4) | copy-start | bytes 52
  17.0 18.6 %copy-start = (bf16[128,7680]{1,0:T(8,128)(2,1)S(1)}, bf16[128,7680]{1,0:T(8,128)(2,1)}, u32[]{:S(2)}) copy-start(bf16[128,7680]{1,0:T(8,128)(2,1)} %param.3) | copy-start | bytes 5898244
  35.7 2.2 %slice-start.2 = ((s8[5898240]{0:T(1024)(128)(4,1)}), s8[4194304]{0:T(1024)(128)(4,1)S(1)}, s32[]{:S(2)}) async-start(s8[5898240]{0:T(1024)(128)(4,1)} %bitcast.40), calls=%async_computation.2 | async-start | bytes 8388608
  35.8 3.4 %slice-start = ((s8[5898240]{0:T(1024)(128)(4,1)}), s8[4194304]{0:T(1024)(128)(4,1)S(1)}, s32[]{:S(2)}) async-start(s8[5898240]{0:T(1024)(128)(4,1)} %bitcast.38), calls=%async_computation | async-start | bytes 8388608
  35.8 3.8 %slice-start.3 = ((s8[5898240]{0:T(1024)(128)(4,1)}), s8[1703936]{0:T(1024)(128)(4,1)S(1)}, s32[]{:S(2)}) async-start(s8[5898240]{0:T(1024)(128)(4,1)} %bitcast.40), calls=%async_computation.3 | async-start | bytes 3407872
  37.5 2.9 %slice-start.1 = ((s8[5898240]{0:T(1024)(128)(4,1)}), s8[1703936]{0:T(1024)(128)(4,1)S(1)}, s32[]{:S(2)}) async-start(s8[5898240]{0:T(1024)(128)(4,1)} %bitcast.38), calls=%async_computation.1 | async-start | bytes 3407872
  44.4 17.5 %collective-permute-start.5 = (bf16[2,128,768]{2,1,0:T(8,128)(2,1)S(1)}, bf16[2,128,768]{2,1,0:T(8,128)(2,1)S(1)}, u32[]{:S(2)}, u32[]{:S(2)}) collective-permute-start(bf16[2,128,768]{2,1,0:T(8,128)(2,1)S(1)} %fusion.8), channel_id=1, source_target_pairs={{0,16},{16,0},{1,17},{17,1},{2,18},{18,2},{3,19},{19,3},{4,20},{20... | collective-permute-start | bytes 1179656 | tf_op jit(solution)/shard_map/ppermute | solution.py:150
  47.5 15.9 %collective-permute-start.6 = (bf16[2,128,768]{2,1,0:T(8,128)(2,1)S(1)}, bf16[2,128,768]{2,1,0:T(8,128)(2,1)S(1)}, u32[]{:S(2)}, u32[]{:S(2)}) collective-permute-start(bf16[2,128,768]{2,1,0:T(8,128)(2,1)S(1)} %fusion.8), channel_id=1, source_target_pairs={{4,0},{8,4},{12,8},{5,1},{9,5},{13,9},{6,2},{10,6},{14,10},{7,3},{... | collective-permute-start | bytes 1179656 | tf_op jit(solution)/shard_map/ppermute | solution.py:150
  49.0 11.9 %collective-permute-start.1 = (bf16[2,64,768]{2,1,0:T(8,128)(2,1)S(1)}, bf16[2,64,768]{2,1,0:T(8,128)(2,1)S(1)}, u32[]{:S(2)}, u32[]{:S(2)}) collective-permute-start(bf16[2,64,768]{2,1,0:T(8,128)(2,1)S(1)} %get-tuple-element.20), channel_id=1, source_target_pairs={{0,16},{16,0},{1,17},{17,1},{2,18},{18,2},{3,19},{19,3},{4,20},{20... | collective-permute-start | bytes 589832 | tf_op jit(solution)/shard_map/ppermute | solution.py:150
  51.0 36.1 %collective-permute-start.8 = (bf16[2,128,768]{2,1,0:T(8,128)(2,1)S(1)}, bf16[2,128,768]{2,1,0:T(8,128)(2,1)S(1)}, u32[]{:S(2)}, u32[]{:S(2)}) collective-permute-start(bf16[2,128,768]{2,1,0:T(8,128)(2,1)S(1)} %fusion.8), channel_id=1, source_target_pairs={{8,0},{12,4},{9,1},{13,5},{10,2},{14,6},{11,3},{15,7},{24,16},{28,... | collective-permute-start | bytes 1179656 | tf_op jit(solution)/shard_map/ppermute | solution.py:150
  52.3 35.1 %collective-permute-start.10 = (bf16[2,128,768]{2,1,0:T(8,128)(2,1)S(1)}, bf16[2,128,768]{2,1,0:T(8,128)(2,1)S(1)}, u32[]{:S(2)}, u32[]{:S(2)}) collective-permute-start(bf16[2,128,768]{2,1,0:T(8,128)(2,1)S(1)} %fusion.8), channel_id=1, source_target_pairs={{12,0},{13,1},{14,2},{15,3},{28,16},{29,17},{30,18},{31,19}} | collective-permute-start | bytes 1179656 | tf_op jit(solution)/shard_map/ppermute | solution.py:150
  60.9 28.4 %collective-permute-start.2 = (bf16[4,64,768]{2,1,0:T(8,128)(2,1)S(1)}, bf16[4,64,768]{2,1,0:T(8,128)(2,1)S(1)}, u32[]{:S(2)}, u32[]{:S(2)}) collective-permute-start(bf16[4,64,768]{2,1,0:T(8,128)(2,1)S(1)} %get-tuple-element.18), channel_id=1, source_target_pairs={{0,3},{1,0},{2,1},{3,2},{4,7},{5,4},{6,5},{7,6},{8,11},{9,8},{10,9... | collective-permute-start | bytes 1179656 | tf_op jit(solution)/shard_map/ppermute | solution.py:150
  61.9 27.8 %collective-permute-start.3 = (bf16[4,64,768]{2,1,0:T(8,128)(2,1)S(1)}, bf16[4,64,768]{2,1,0:T(8,128)(2,1)S(1)}, u32[]{:S(2)}, u32[]{:S(2)}) collective-permute-start(bf16[4,64,768]{2,1,0:T(8,128)(2,1)S(1)} %get-tuple-element.18), channel_id=1, source_target_pairs={{0,2},{1,3},{2,0},{3,1},{4,6},{5,7},{6,4},{7,5},{8,10},{9,11},{10,... | collective-permute-start | bytes 1179656 | tf_op jit(solution)/shard_map/ppermute | solution.py:150
  63.4 26.3 %collective-permute-start.4 = (bf16[4,64,768]{2,1,0:T(8,128)(2,1)S(1)}, bf16[4,64,768]{2,1,0:T(8,128)(2,1)S(1)}, u32[]{:S(2)}, u32[]{:S(2)}) collective-permute-start(bf16[4,64,768]{2,1,0:T(8,128)(2,1)S(1)} %get-tuple-element.18), channel_id=1, source_target_pairs={{0,1},{1,2},{2,3},{3,0},{4,5},{5,6},{6,7},{7,4},{8,9},{9,10},{10,1... | collective-permute-start | bytes 1179656 | tf_op jit(solution)/shard_map/ppermute | solution.py:150
  87.1 12.0 %collective-permute-start.7 = (bf16[2,128,768]{2,1,0:T(8,128)(2,1)S(1)}, bf16[2,128,768]{2,1,0:T(8,128)(2,1)S(1)}, u32[]{:S(2)}, u32[]{:S(2)}) collective-permute-start(bf16[2,128,768]{2,1,0:T(8,128)(2,1)S(1)} %collective-permute-done.6), channel_id=1, source_target_pairs={{0,16},{16,0},{1,17},{17,1},{2,18},{18,2},{3,19},{19,3},{4,20},{20... | collective-permute-start | bytes 1179656 | tf_op jit(solution)/shard_map/ppermute | solution.py:150
  87.5 20.0 %collective-permute-start.9 = (bf16[2,128,768]{2,1,0:T(8,128)(2,1)S(1)}, bf16[2,128,768]{2,1,0:T(8,128)(2,1)S(1)}, u32[]{:S(2)}, u32[]{:S(2)}) collective-permute-start(bf16[2,128,768]{2,1,0:T(8,128)(2,1)S(1)} %collective-permute-done.8), channel_id=1, source_target_pairs={{0,16},{16,0},{1,17},{17,1},{2,18},{18,2},{3,19},{19,3},{4,20},{20... | collective-permute-start | bytes 1179656 | tf_op jit(solution)/shard_map/ppermute | solution.py:150
  89.3 24.1 %collective-permute-start.11 = (bf16[2,128,768]{2,1,0:T(8,128)(2,1)S(1)}, bf16[2,128,768]{2,1,0:T(8,128)(2,1)S(1)}, u32[]{:S(2)}, u32[]{:S(2)}) collective-permute-start(bf16[2,128,768]{2,1,0:T(8,128)(2,1)S(1)} %collective-permute-done.10), channel_id=1, source_target_pairs={{0,16},{16,0},{1,17},{17,1},{2,18},{18,2},{3,19},{19,3},{4,20},{20... | collective-permute-start | bytes 1179656 | tf_op jit(solution)/shard_map/ppermute | solution.py:150

commit v5 on v4

--- a/solution.py
+++ b/solution.py
@@ -25,6 +25,16 @@
     count = lax.axis_size(axis)
     initial, last = (max(0, -steps), min(count, count - steps))
     return lax.ppermute(value, axis, [(source, source + steps) for source in range(initial, last)])
+
+
+def table_kernel(high_cos_ref, high_sin_ref, low_cos_ref, low_sin_ref, taper_ref, out_ref):
+    hc = high_cos_ref[0]
+    hs = high_sin_ref[0]
+    lc = low_cos_ref[...]
+    ls = low_sin_ref[...]
+    taper = taper_ref[...]
+    out_ref[:, :NF] = (taper * (hc * lc - hs * ls)).astype(out_ref.dtype)
+    out_ref[:, NF:] = (-(taper * (hs * lc + hc * ls))).astype(out_ref.dtype)
 
 
 def forward_table():
@@ -36,18 +46,25 @@
     low_idx = jnp.arange(coarse, dtype=jnp.int32)[:, None] * freq_bins[None, :] % WIN
     high_angle = high_idx.astype(jnp.float32) * scale
     low_angle = low_idx.astype(jnp.float32) * scale
-    high_cos, high_sin, low_cos, low_sin = lax.optimization_barrier(
-        (jnp.cos(high_angle), jnp.sin(high_angle), jnp.cos(low_angle), jnp.sin(low_angle))
-    )
-    high_cos, high_sin = high_cos[:, None, :], high_sin[:, None, :]
-    low_cos, low_sin = low_cos[None], low_sin[None]
-    cos_full = high_cos * low_cos - high_sin * low_sin
-    sin_full = high_sin * low_cos + high_cos * low_sin
+    high_cos = jnp.cos(high_angle).reshape(n_coarse, 1, NF)
+    high_sin = jnp.sin(high_angle).reshape(n_coarse, 1, NF)
+    low_cos, low_sin = jnp.cos(low_angle), jnp.sin(low_angle)
     sample_idx = jnp.arange(WIN, dtype=jnp.int32)
     taper_curve = 0.5 - 0.5 * jnp.cos(sample_idx.astype(jnp.float32) * (two_pi / WIN))
-    taper_curve = taper_curve.reshape(n_coarse, coarse, 1)
-    table = jnp.concatenate([taper_curve * cos_full, -taper_curve * sin_full], axis=2).astype(jnp.bfloat16)
-    return table.reshape(WIN, 2 * NF)
+    taper_curve = taper_curve[:, None]
+    return pl.pallas_call(
+        table_kernel,
+        grid=(n_coarse,),
+        in_specs=[
+            pl.BlockSpec((1, 1, NF), lambda q: (q, 0, 0)),
+            pl.BlockSpec((1, 1, NF), lambda q: (q, 0, 0)),
+            pl.BlockSpec((coarse, NF), lambda q: (0, 0)),
+            pl.BlockSpec((coarse, NF), lambda q: (0, 0)),
+            pl.BlockSpec((coarse, 1), lambda q: (q, 0)),
+        ],
+        out_specs=pl.BlockSpec((coarse, 2 * NF), lambda q: (q, 0)),
+        out_shape=jax.ShapeDtypeStruct((WIN, 2 * NF), jnp.bfloat16),
+    )(high_cos, high_sin, low_cos, low_sin, taper_curve)
 
 
 def lag_table(count):

time: 190 us -> 216 us (1.14)
  the two profiles are of different devices: /device:TPU:0 before, /device:TPU:14 now
where the time goes in v5:
time: 216 us; the launch traced here: 213 us
  Pallas kernels  108 us (50%)
  waiting for transfers between devices  54.1 us (25%)
  other arithmetic  25.6 us (12%)
  starting transfers between devices  11.3 us (5%)
  local copies, waits for them, and re-layouts  7.51 us (3%)
  matrix products  3.76 us (2%)
  between operations  3.42 us (2%)
    pallas_call x1, Pallas kernels, all_pairs(): pl.pallas_call(pair_kernel, grid_spec=grid_spec, out_shape=jax.ShapeDtype...  73.5 us
    ppermute x11, waiting for transfers between devices, exchange(): return lax.ppermute(value, axes, pairs)  54.1 us
    pallas_call x1, Pallas kernels, forward_table(): pl.pallas_call(table_kernel, grid=(n_coarse,), in_specs=[pl.BlockSpec((1,...  34 us
    sub x1, other arithmetic, forward_table(): 0.5 - 0.5 * jnp.cos(sample_idx.astype(jnp.float32) * (two_pi / WIN))  13.9 us
    ppermute x11, starting transfers between devices, exchange(): return lax.ppermute(value, axes, pairs)  8.77 us
  transfers between devices with their start and end apart: 12, of which 7 were waited for; matrix products, arithmetic and copies ran while one was open for 11% of the time, Pallas kernels for 16%

profile of v5, /device:TPU:14, one launch (start us, length us, event | category | flops | bytes accessed | tf_op | source)
XLA Modules:
  0.0 213.1 jit_solution(5690055728345681260)
XLA Ops:
  0.0 2.3 %slice.17 = bf16[128,4352]{1,0:T(8,128)(2,1)} slice(bf16[128,7680]{1,0:T(8,128)(2,1)} %param.3), slice={[0:128], [0:4352]} | slice | bytes 2228224 | tf_op jit(solution)/shard_map/slice | solution.py:188
  2.3 2.5 %collective-permute-start = (bf16[128,4352]{1,0:T(8,128)(2,1)}, bf16[128,4352]{1,0:T(8,128)(2,1)S(1)}, u32[]{:S(2)}, u32[]{:S(2)}) collective-permute-start(bf16[128,4352]{1,0:T(8,128)(2,1)} %slice.17), channel_id=1, source_target_pairs={{16,0},{17,1},{18,2},{19,3},{20,4},{21,5},{22,6},{23,7},{24,8},{25... | collective-permute-start | bytes 3342344 | tf_op jit(solution)/shard_map/ppermute | solution.py:27
  4.9 13.9 %multiply_subtract_fusion.taper_ref = f32[7680,1]{1,0:T(8,128)} fusion(), kind=kLoop, calls=%fused_computation.4 | loop fusion | flops 30720 | bytes 30720 | tf_op jit(solution)/shard_map/sub | solution.py:53
  18.8 1.6 fusion.21
  20.4 4.2 %fusion.28 = (f32[60,1,384]{2,1,0:T(1,128)}, f32[60,1,384]{2,1,0:T(1,128)}) fusion(s32[384]{0:T(512)S(1)} %iota_add_fusion, s32[60]{0:T(128)S(1)} %iota_multiply_fusion), kind=kLoop, calls=%fused_computation.49 | loop fusion | flops 207360 | bytes 186096 | tf_op jit(solution)/shard_map/sin | solution.py:50
  24.6 0.6 fusion.35
  27.8 0.1 copy.10
  27.9 0.1 copy.11
  28.6 0.0 copy-start.1
  28.6 34.0 %shard_map.37 = bf16[7680,768]{1,0:T(8,128)(2,1)} custom-call(f32[60,1,384]{2,1,0:T(1,128)} %get-tuple-element.14.high_cos_ref, f32[60,1,384]{2,1,0:T(1,128)} %get-tuple-element.13.high_sin_ref, f32[128,384]{1,0:T(8,128)} %get-tuple-element.16.low_cos_ref, f32[128,384]{1,0:T(8,128)} %get-tuple-element.15.low_sin_ref, f32[7680,1]{1,0:T(8,128)} %multiply_subtract_fusion.taper_ref), custom_call_target="tpu_custom_call" | custom-call | tf_op jit(solution)/shard_map/pallas_call | solution.py:55
  62.7 0.0 copy-start
  62.7 0.1 constant_dynamic-update-slice_fusion.1
  62.9 0.1 constant_dynamic-update-slice_fusion
  62.9 1.6 constant_dynamic-slice_fusion.3
  64.5 2.5 %copy-done = bf16[7680,768]{1,0:T(8,128)(2,1)S(1)} copy-done((bf16[7680,768]{1,0:T(8,128)(2,1)S(1)}, bf16[7680,768]{1,0:T(8,128)(2,1)}, u32[]{:S(2)}) %copy-start) | copy-done | bytes 11796504
  67.1 3.2 %fusion = f32[256,768]{1,0:T(8,128)S(1)} fusion(bf16[7680,768]{1,0:T(8,128)(2,1)S(1)} %copy-done, bf16[128,7680]{1,0:T(8,128)(2,1)S(1)} %get-tuple-element.6, bf16[128,7680]{1,0:T(8,128)(2,1)S(1)} %get-tuple-element.5), kind=kOutput, calls=%fused_computation | convolution fusion | flops 3027763200 | bytes 16515072 | tf_op jit(solution)/shard_map/dot_general | solution.py:197
  70.3 0.1 fusion.26
  70.4 0.6 fusion.6
  71.0 0.1 fusion.7
  71.1 1.3 collective-permute-start.8
  72.4 2.4 %collective-permute-start.6 = (bf16[2,128,768]{2,1,0:T(8,128)(2,1)S(1)}, bf16[2,128,768]{2,1,0:T(8,128)(2,1)S(1)}, u32[]{:S(2)}, u32[]{:S(2)}) collective-permute-start(bf16[2,128,768]{2,1,0:T(8,128)(2,1)S(1)} %fusion.7), channel_id=1, source_target_pairs={{4,0},{8,4},{12,8},{5,1},{9,5},{13,9},{6,2},{10,6},{14,10},{7,3},{... | collective-permute-start | bytes 1179656 | tf_op jit(solution)/shard_map/ppermute | solution.py:167
  74.8 0.1 collective-permute-start.1
  74.8 2.0 multiply_convert_fusion.1
  76.8 2.1 collective-permute-start.5
  78.9 0.7 collective-permute-start.10
  79.5 3.1 %collective-permute-done.1 = bf16[2,64,768]{2,1,0:T(8,128)(2,1)S(1)} collective-permute-done((bf16[2,64,768]{2,1,0:T(8,128)(2,1)S(1)}, bf16[2,64,768]{2,1,0:T(8,128)(2,1)S(1)}, u32[]{:S(2)}, u32[]{:S(2)}) %collective-permute-start.1) | collective-permute-done | bytes 196640 | tf_op jit(solution)/shard_map/ppermute | solution.py:167
  82.6 0.1 fusion.33
  82.7 0.1 collective-permute-start.3
  82.8 3.0 %collective-permute-done.8 = bf16[2,128,768]{2,1,0:T(8,128)(2,1)S(1)} collective-permute-done((bf16[2,128,768]{2,1,0:T(8,128)(2,1)S(1)}, bf16[2,128,768]{2,1,0:T(8,128)(2,1)S(1)}, u32[]{:S(2)}, u32[]{:S(2)}) %collective-permute-start.8) | collective-permute-done | bytes 393248 | tf_op jit(solution)/shard_map/ppermute | solution.py:167
  85.8 0.0 collective-permute-start.2
  85.8 22.9 %collective-permute-done.6 = bf16[2,128,768]{2,1,0:T(8,128)(2,1)S(1)} collective-permute-done((bf16[2,128,768]{2,1,0:T(8,128)(2,1)S(1)}, bf16[2,128,768]{2,1,0:T(8,128)(2,1)S(1)}, u32[]{:S(2)}, u32[]{:S(2)}) %collective-permute-start.6) | collective-permute-done | bytes 393248 | tf_op jit(solution)/shard_map/ppermute | solution.py:167
  108.7 0.0 collective-permute-start.4
  108.8 0.1 collective-permute-start.9
  108.8 0.1 pad_add_fusion.pairs_ref
  108.9 0.0 collective-permute-done.10
  108.9 2.0 collective-permute-start.7
  110.9 0.1 maximum_bitcast_fusion
  111.0 0.1 collective-permute-start.11
  111.1 4.8 %collective-permute-done.4 = bf16[4,64,768]{2,1,0:T(8,128)(2,1)S(1)} collective-permute-done((bf16[4,64,768]{2,1,0:T(8,128)(2,1)S(1)}, bf16[4,64,768]{2,1,0:T(8,128)(2,1)S(1)}, u32[]{:S(2)}, u32[]{:S(2)}) %collective-permute-start.4) | collective-permute-done | bytes 393248 | tf_op jit(solution)/shard_map/ppermute | solution.py:167
  115.9 0.3 maximum_convert_fusion.1.row_ref
  116.2 4.6 %collective-permute-done.9 = bf16[2,128,768]{2,1,0:T(8,128)(2,1)S(1)} collective-permute-done((bf16[2,128,768]{2,1,0:T(8,128)(2,1)S(1)}, bf16[2,128,768]{2,1,0:T(8,128)(2,1)S(1)}, u32[]{:S(2)}, u32[]{:S(2)}) %collective-permute-start.9) | collective-permute-done | bytes 393248 | tf_op jit(solution)/shard_map/ppermute | solution.py:167
  120.8 0.1 maximum_bitcast_fusion.2
  120.9 8.4 %collective-permute-done.7 = bf16[2,128,768]{2,1,0:T(8,128)(2,1)S(1)} collective-permute-done((bf16[2,128,768]{2,1,0:T(8,128)(2,1)S(1)}, bf16[2,128,768]{2,1,0:T(8,128)(2,1)S(1)}, u32[]{:S(2)}, u32[]{:S(2)}) %collective-permute-start.7) | collective-permute-done | bytes 393248 | tf_op jit(solution)/shard_map/ppermute | solution.py:167
  129.2 0.1 maximum_bitcast_fusion.1
  129.3 7.3 %collective-permute-done.11 = bf16[2,128,768]{2,1,0:T(8,128)(2,1)S(1)} collective-permute-done((bf16[2,128,768]{2,1,0:T(8,128)(2,1)S(1)}, bf16[2,128,768]{2,1,0:T(8,128)(2,1)S(1)}, u32[]{:S(2)}, u32[]{:S(2)}) %collective-permute-start.11) | collective-permute-done | bytes 393248 | tf_op jit(solution)/shard_map/ppermute | solution.py:167
  136.6 0.1 maximum_bitcast_fusion.3
  136.7 2.9 %maximum_convert_fusion.col_ref = f32[4,4,128,768]{3,2,1,0:T(8,128)} fusion(bf16[1,4,128,768]{3,2,1,0:T(8,128)(2,1)S(1)} %maximum_bitcast_fusion.3, bf16[1,4,128,768]{3,2,1,0:T(8,128)(2,1)S(1)} %maximum_bitcast_fusion.2, bf16[1,4,128,768]{3,2,1,0:T(8,128)(2,1)S(1)} %maximum_bitcast_fusion.1, bf16[1,4,128,768]{3,2,1,0:T(8,128)(2,1)S(1)} %maximum_bitcast_fusion), kind=kLoop, calls=%fused_computation.5 | loop fusion | flops 6291456 | bytes 9437184 | tf_op jit(solution)/shard_map/convert_element_type | solution.py:230
  139.6 73.5 %shard_map.38 = bf16[4,64,128,256]{3,2,1,0:T(8,128)(2,1)} custom-call(s32[4,2]{1,0:T(4,128)S(1)} %pad_add_fusion.pairs_ref, f32[4,4,64,768]{3,2,1,0:T(8,128)S(1)} %maximum_convert_fusion.1.row_ref, f32[4,4,128,768]{3,2,1,0:T(8,128)} %maximum_convert_fusion.col_ref, bf16[768,256]{1,0:T(8,128)(2,1)S(1)} %pad_maximum_fusion.1.lags_ref), custom_call_target="tpu_custom_call" | custom-call | flops 13287555072 | bytes 26214400 | tf_op jit(solution)/shard_map/pallas_call | solution.py:142
  (17 shorter events, 0.1 us)
Async XLA Ops:
  0.0 24.6 %copy-start.3 = (s32[1,1,4,2]{2,3,1,0:T(2,128)S(1)}, s32[1,1,4,2]{2,3,1,0:T(2,128)}, u32[]{:S(2)}) copy-start(s32[1,1,4,2]{2,3,1,0:T(2,128)} %param.5) | copy-start | bytes 100
  0.0 24.6 %copy-start.2 = (s32[4]{0:T(128)S(1)}, s32[4]{0:T(128)}, u32[]{:S(2)}) copy-start(s32[4]{0:T(128)} %param.4) | copy-start | bytes 52
  2.3 60.5 %collective-permute-start = (bf16[128,4352]{1,0:T(8,128)(2,1)}, bf16[128,4352]{1,0:T(8,128)(2,1)S(1)}, u32[]{:S(2)}, u32[]{:S(2)}) collective-permute-start(bf16[128,4352]{1,0:T(8,128)(2,1)} %slice.17), channel_id=1, source_target_pairs={{16,0},{17,1},{18,2},{19,3},{20,4},{21,5},{22,6},{23,7},{24,8},{25... | collective-permute-start | bytes 3342344 | tf_op jit(solution)/shard_map/ppermute | solution.py:27
  28.6 34.1 %copy-start.1 = (bf16[128,7680]{1,0:T(8,128)(2,1)S(1)}, bf16[128,7680]{1,0:T(8,128)(2,1)}, u32[]{:S(2)}) copy-start(bf16[128,7680]{1,0:T(8,128)(2,1)} %param.3) | copy-start | bytes 5898244
  62.7 4.4 %copy-start = (bf16[7680,768]{1,0:T(8,128)(2,1)S(1)}, bf16[7680,768]{1,0:T(8,128)(2,1)}, u32[]{:S(2)}) copy-start(bf16[7680,768]{1,0:T(8,128)(2,1)} %shard_map.37) | copy-start | bytes 35389444
  71.1 14.8 %collective-permute-start.8 = (bf16[2,128,768]{2,1,0:T(8,128)(2,1)S(1)}, bf16[2,128,768]{2,1,0:T(8,128)(2,1)S(1)}, u32[]{:S(2)}, u32[]{:S(2)}) collective-permute-start(bf16[2,128,768]{2,1,0:T(8,128)(2,1)S(1)} %fusion.7), channel_id=1, source_target_pairs={{8,0},{12,4},{9,1},{13,5},{10,2},{14,6},{11,3},{15,7},{24,16},{28,... | collective-permute-start | bytes 1179656 | tf_op jit(solution)/shard_map/ppermute | solution.py:167
  72.4 36.3 %collective-permute-start.6 = (bf16[2,128,768]{2,1,0:T(8,128)(2,1)S(1)}, bf16[2,128,768]{2,1,0:T(8,128)(2,1)S(1)}, u32[]{:S(2)}, u32[]{:S(2)}) collective-permute-start(bf16[2,128,768]{2,1,0:T(8,128)(2,1)S(1)} %fusion.7), channel_id=1, source_target_pairs={{4,0},{8,4},{12,8},{5,1},{9,5},{13,9},{6,2},{10,6},{14,10},{7,3},{... | collective-permute-start | bytes 1179656 | tf_op jit(solution)/shard_map/ppermute | solution.py:167
  74.8 7.8 %collective-permute-start.1 = (bf16[2,64,768]{2,1,0:T(8,128)(2,1)S(1)}, bf16[2,64,768]{2,1,0:T(8,128)(2,1)S(1)}, u32[]{:S(2)}, u32[]{:S(2)}) collective-permute-start(bf16[2,64,768]{2,1,0:T(8,128)(2,1)S(1)} %get-tuple-element.10), channel_id=1, source_target_pairs={{0,16},{16,0},{1,17},{17,1},{2,18},{18,2},{3,19},{19,3},{4,20},{20... | collective-permute-start | bytes 589832 | tf_op jit(solution)/shard_map/ppermute | solution.py:167
  76.8 31.9 %collective-permute-start.5 = (bf16[2,128,768]{2,1,0:T(8,128)(2,1)S(1)}, bf16[2,128,768]{2,1,0:T(8,128)(2,1)S(1)}, u32[]{:S(2)}, u32[]{:S(2)}) collective-permute-start(bf16[2,128,768]{2,1,0:T(8,128)(2,1)S(1)} %fusion.7), channel_id=1, source_target_pairs={{0,16},{16,0},{1,17},{17,1},{2,18},{18,2},{3,19},{19,3},{4,20},{20... | collective-permute-start | bytes 1179656 | tf_op jit(solution)/shard_map/ppermute | solution.py:167
  78.9 30.1 %collective-permute-start.10 = (bf16[2,128,768]{2,1,0:T(8,128)(2,1)S(1)}, bf16[2,128,768]{2,1,0:T(8,128)(2,1)S(1)}, u32[]{:S(2)}, u32[]{:S(2)}) collective-permute-start(bf16[2,128,768]{2,1,0:T(8,128)(2,1)S(1)} %fusion.7), channel_id=1, source_target_pairs={{12,0},{13,1},{14,2},{15,3},{28,16},{29,17},{30,18},{31,19}} | collective-permute-start | bytes 1179656 | tf_op jit(solution)/shard_map/ppermute | solution.py:167
  82.7 28.3 %collective-permute-start.3 = (bf16[4,64,768]{2,1,0:T(8,128)(2,1)S(1)}, bf16[4,64,768]{2,1,0:T(8,128)(2,1)S(1)}, u32[]{:S(2)}, u32[]{:S(2)}) collective-permute-start(bf16[4,64,768]{2,1,0:T(8,128)(2,1)S(1)} %get-tuple-element.8), channel_id=1, source_target_pairs={{0,2},{1,3},{2,0},{3,1},{4,6},{5,7},{6,4},{7,5},{8,10},{9,11},{10,... | collective-permute-start | bytes 1179656 | tf_op jit(solution)/shard_map/ppermute | solution.py:167
  85.8 25.3 %collective-permute-start.2 = (bf16[4,64,768]{2,1,0:T(8,128)(2,1)S(1)}, bf16[4,64,768]{2,1,0:T(8,128)(2,1)S(1)}, u32[]{:S(2)}, u32[]{:S(2)}) collective-permute-start(bf16[4,64,768]{2,1,0:T(8,128)(2,1)S(1)} %get-tuple-element.8), channel_id=1, source_target_pairs={{0,3},{1,0},{2,1},{3,2},{4,7},{5,4},{6,5},{7,6},{8,11},{9,8},{10,9... | collective-permute-start | bytes 1179656 | tf_op jit(solution)/shard_map/ppermute | solution.py:167
  108.7 7.2 %collective-permute-start.4 = (bf16[4,64,768]{2,1,0:T(8,128)(2,1)S(1)}, bf16[4,64,768]{2,1,0:T(8,128)(2,1)S(1)}, u32[]{:S(2)}, u32[]{:S(2)}) collective-permute-start(bf16[4,64,768]{2,1,0:T(8,128)(2,1)S(1)} %get-tuple-element.8), channel_id=1, source_target_pairs={{0,1},{1,2},{2,3},{3,0},{4,5},{5,6},{6,7},{7,4},{8,9},{9,10},{10,1... | collective-permute-start | bytes 1179656 | tf_op jit(solution)/shard_map/ppermute | solution.py:167
  108.8 12.1 %collective-permute-start.9 = (bf16[2,128,768]{2,1,0:T(8,128)(2,1)S(1)}, bf16[2,128,768]{2,1,0:T(8,128)(2,1)S(1)}, u32[]{:S(2)}, u32[]{:S(2)}) collective-permute-start(bf16[2,128,768]{2,1,0:T(8,128)(2,1)S(1)} %collective-permute-done.8), channel_id=1, source_target_pairs={{0,16},{16,0},{1,17},{17,1},{2,18},{18,2},{3,19},{19,3},{4,20},{20... | collective-permute-start | bytes 1179656 | tf_op jit(solution)/shard_map/ppermute | solution.py:167
  108.9 20.3 %collective-permute-start.7 = (bf16[2,128,768]{2,1,0:T(8,128)(2,1)S(1)}, bf16[2,128,768]{2,1,0:T(8,128)(2,1)S(1)}, u32[]{:S(2)}, u32[]{:S(2)}) collective-permute-start(bf16[2,128,768]{2,1,0:T(8,128)(2,1)S(1)} %collective-permute-done.6), channel_id=1, source_target_pairs={{0,16},{16,0},{1,17},{17,1},{2,18},{18,2},{3,19},{19,3},{4,20},{20... | collective-permute-start | bytes 1179656 | tf_op jit(solution)/shard_map/ppermute | solution.py:167
  111.0 25.6 %collective-permute-start.11 = (bf16[2,128,768]{2,1,0:T(8,128)(2,1)S(1)}, bf16[2,128,768]{2,1,0:T(8,128)(2,1)S(1)}, u32[]{:S(2)}, u32[]{:S(2)}) collective-permute-start(bf16[2,128,768]{2,1,0:T(8,128)(2,1)S(1)} %collective-permute-done.10), channel_id=1, source_target_pairs={{0,16},{16,0},{1,17},{17,1},{2,18},{18,2},{3,19},{19,3},{4,20},{20... | collective-permute-start | bytes 1179656 | tf_op jit(solution)/shard_map/ppermute | solution.py:167

commit v6 on v5

--- a/solution.py
+++ b/solution.py
@@ -27,14 +27,22 @@
     return lax.ppermute(value, axis, [(source, source + steps) for source in range(initial, last)])
 
 
-def table_kernel(high_cos_ref, high_sin_ref, low_cos_ref, low_sin_ref, taper_ref, out_ref):
-    hc = high_cos_ref[0]
-    hs = high_sin_ref[0]
+TABLE_Q = 12
+
+
+def table_kernel(high_cos_ref, high_sin_ref, low_cos_ref, low_sin_ref, out_ref):
+    coarse = low_cos_ref.shape[0]
     lc = low_cos_ref[...]
     ls = low_sin_ref[...]
-    taper = taper_ref[...]
-    out_ref[:, :NF] = (taper * (hc * lc - hs * ls)).astype(out_ref.dtype)
-    out_ref[:, NF:] = (-(taper * (hs * lc + hc * ls))).astype(out_ref.dtype)
+    for qq in range(TABLE_Q):
+        hc = high_cos_ref[qq]
+        hs = high_sin_ref[qq]
+        first = (pl.program_id(0) * TABLE_Q + qq) * coarse
+        sample = (first + lax.broadcasted_iota(jnp.int32, (coarse, 1), 0)).astype(jnp.float32)
+        taper = 0.5 - 0.5 * jnp.cos(sample * (two_pi / WIN))
+        rows = pl.ds(qq * coarse, coarse)
+        out_ref[rows, :NF] = (taper * (hc * lc - hs * ls)).astype(out_ref.dtype)
+        out_ref[rows, NF:] = (-(taper * (hs * lc + hc * ls))).astype(out_ref.dtype)
 
 
 def forward_table():
@@ -49,22 +57,18 @@
     high_cos = jnp.cos(high_angle).reshape(n_coarse, 1, NF)
     high_sin = jnp.sin(high_angle).reshape(n_coarse, 1, NF)
     low_cos, low_sin = jnp.cos(low_angle), jnp.sin(low_angle)
-    sample_idx = jnp.arange(WIN, dtype=jnp.int32)
-    taper_curve = 0.5 - 0.5 * jnp.cos(sample_idx.astype(jnp.float32) * (two_pi / WIN))
-    taper_curve = taper_curve[:, None]
     return pl.pallas_call(
         table_kernel,
-        grid=(n_coarse,),
+        grid=(n_coarse // TABLE_Q,),
         in_specs=[
-            pl.BlockSpec((1, 1, NF), lambda q: (q, 0, 0)),
-            pl.BlockSpec((1, 1, NF), lambda q: (q, 0, 0)),
+            pl.BlockSpec((TABLE_Q, 1, NF), lambda q: (q, 0, 0)),
+            pl.BlockSpec((TABLE_Q, 1, NF), lambda q: (q, 0, 0)),
             pl.BlockSpec((coarse, NF), lambda q: (0, 0)),
             pl.BlockSpec((coarse, NF), lambda q: (0, 0)),
-            pl.BlockSpec((coarse, 1), lambda q: (q, 0)),
         ],
-        out_specs=pl.BlockSpec((coarse, 2 * NF), lambda q: (q, 0)),
+        out_specs=pl.BlockSpec((TABLE_Q * coarse, 2 * NF), lambda q: (q, 0)),
         out_shape=jax.ShapeDtypeStruct((WIN, 2 * NF), jnp.bfloat16),
-    )(high_cos, high_sin, low_cos, low_sin, taper_curve)
+    )(high_cos, high_sin, low_cos, low_sin)
 
 
 def lag_table(count):

time: 216 us -> 187 us (0.87); the launches traced: 213 us -> 186 us
  Pallas kernels: 108 us -> 93.4 us
  other arithmetic: 25.6 us -> 11.6 us
    pallas_call x1, Pallas kernels: 34 us -> 20 us  [forward_table(): pl.pallas_call(table_kernel, grid=(n_coarse // TABLE_Q,), in_specs=[pl.Bl...]
    sub x1 -> x0, other arithmetic: 13.9 us -> none  [forward_table(): 0.5 - 0.5 * jnp.cos(sample_idx.astype(jnp.float32) * (two_pi / WIN))]
  transfers between devices with their start and end apart: 12 -> 12, of which waited for: 7 -> 7; matrix products, arithmetic and copies ran while one was open for 11% -> 6% of each run, Pallas kernels for 16% -> 11%
where the time goes in v6:
time: 187 us; the launch traced here: 186 us
  Pallas kernels  93.4 us (50%)
  waiting for transfers between devices  54.1 us (29%)
  other arithmetic  11.6 us (6%)
  starting transfers between devices  11.3 us (6%)
  local copies, waits for them, and re-layouts  8.94 us (5%)
  matrix products  3.76 us (2%)
  between operations  3.26 us (2%)
    pallas_call x1, Pallas kernels, all_pairs(): pl.pallas_call(pair_kernel, grid_spec=grid_spec, out_shape=jax.ShapeDtype...  73.5 us
    ppermute x11, waiting for transfers between devices, exchange(): return lax.ppermute(value, axes, pairs)  54.1 us
    pallas_call x1, Pallas kernels, forward_table(): pl.pallas_call(table_kernel, grid=(n_coarse // TABLE_Q,), in_specs=[pl.Bl...  20 us
    ppermute x11, starting transfers between devices, exchange(): return lax.ppermute(value, axes, pairs)  8.76 us
    sin x1, other arithmetic, forward_table(): high_sin = jnp.sin(high_angle).reshape(n_coarse, 1, NF)  4.2 us
  transfers between devices with their start and end apart: 12, of which 7 were waited for; matrix products, arithmetic and copies ran while one was open for 6% of the time, Pallas kernels for 11%

profile of v6, /device:TPU:14, one launch (start us, length us, event | category | flops | bytes accessed | tf_op | source)
XLA Modules:
  0.0 186.3 jit_solution(9598804503943142860)
XLA Ops:
  0.0 2.3 %slice.17 = bf16[128,4352]{1,0:T(8,128)(2,1)} slice(bf16[128,7680]{1,0:T(8,128)(2,1)} %param.3), slice={[0:128], [0:4352]} | slice | bytes 2228224 | tf_op jit(solution)/shard_map/slice | solution.py:192
  2.3 2.5 %collective-permute-start = (bf16[128,4352]{1,0:T(8,128)(2,1)}, bf16[128,4352]{1,0:T(8,128)(2,1)S(1)}, u32[]{:S(2)}, u32[]{:S(2)}) collective-permute-start(bf16[128,4352]{1,0:T(8,128)(2,1)} %slice.17), channel_id=1, source_target_pairs={{16,0},{17,1},{18,2},{19,3},{20,4},{21,5},{22,6},{23,7},{24,8},{25... | collective-permute-start | bytes 3342344 | tf_op jit(solution)/shard_map/ppermute | solution.py:27
  4.9 1.6 fusion.21
  6.4 4.2 %fusion.28 = (f32[60,1,384]{2,1,0:T(1,128)}, f32[60,1,384]{2,1,0:T(1,128)}) fusion(s32[384]{0:T(512)S(1)} %iota_add_fusion, s32[60]{0:T(128)S(1)} %iota_multiply_fusion), kind=kLoop, calls=%fused_computation.48 | loop fusion | flops 207360 | bytes 186096 | tf_op jit(solution)/shard_map/sin | solution.py:58
  10.6 0.8 fusion.34
  11.4 1.3 fusion.35
  15.1 0.1 copy.6
  15.2 0.1 copy.7
  15.9 0.0 copy-start.1
  15.9 20.0 %shard_map.37 = bf16[7680,768]{1,0:T(8,128)(2,1)} custom-call(f32[60,1,384]{2,1,0:T(1,128)} %get-tuple-element.14.high_cos_ref, f32[60,1,384]{2,1,0:T(1,128)} %get-tuple-element.13.high_sin_ref, f32[128,384]{1,0:T(8,128)} %get-tuple-element.16.low_cos_ref, f32[128,384]{1,0:T(8,128)} %get-tuple-element.15.low_sin_ref), custom_call_target="tpu_custom_call" | custom-call | tf_op jit(solution)/shard_map/pallas_call | solution.py:60
  36.0 0.0 copy-start
  36.0 0.1 constant_dynamic-update-slice_fusion.1
  36.1 0.1 constant_dynamic-update-slice_fusion
  36.2 1.6 constant_dynamic-slice_fusion.3
  37.8 2.5 %copy-done = bf16[7680,768]{1,0:T(8,128)(2,1)S(1)} copy-done((bf16[7680,768]{1,0:T(8,128)(2,1)S(1)}, bf16[7680,768]{1,0:T(8,128)(2,1)}, u32[]{:S(2)}) %copy-start) | copy-done | bytes 11796504
  40.3 3.2 %fusion = f32[256,768]{1,0:T(8,128)S(1)} fusion(bf16[7680,768]{1,0:T(8,128)(2,1)S(1)} %copy-done, bf16[128,7680]{1,0:T(8,128)(2,1)S(1)} %get-tuple-element.6, bf16[128,7680]{1,0:T(8,128)(2,1)S(1)} %get-tuple-element.5), kind=kOutput, calls=%fused_computation | convolution fusion | flops 3027763200 | bytes 16515072 | tf_op jit(solution)/shard_map/dot_general | solution.py:201
  43.5 0.1 fusion.26
  43.7 0.6 fusion.6
  44.2 0.1 fusion.7
  44.3 1.3 collective-permute-start.8
  45.6 2.4 %collective-permute-start.6 = (bf16[2,128,768]{2,1,0:T(8,128)(2,1)S(1)}, bf16[2,128,768]{2,1,0:T(8,128)(2,1)S(1)}, u32[]{:S(2)}, u32[]{:S(2)}) collective-permute-start(bf16[2,128,768]{2,1,0:T(8,128)(2,1)S(1)} %fusion.7), channel_id=1, source_target_pairs={{4,0},{8,4},{12,8},{5,1},{9,5},{13,9},{6,2},{10,6},{14,10},{7,3},{... | collective-permute-start | bytes 1179656 | tf_op jit(solution)/shard_map/ppermute | solution.py:171
  48.0 0.1 collective-permute-start.1
  48.1 2.0 %multiply_convert_fusion.1 = (bf16[384,256]{1,0:T(8,128)(2,1)S(1)}, bf16[384,256]{1,0:T(8,128)(2,1)S(1)}) fusion(s32[256]{0:T(256)S(1)} %and_select_fusion.1, s32[384]{0:T(512)S(1)} %iota_add_fusion), kind=kLoop, calls=%fused_computation.27 | loop fusion | flops 1376256 | bytes 395776 | tf_op jit(solution)/shard_map/convert
  50.1 2.1 %collective-permute-start.5 = (bf16[2,128,768]{2,1,0:T(8,128)(2,1)S(1)}, bf16[2,128,768]{2,1,0:T(8,128)(2,1)S(1)}, u32[]{:S(2)}, u32[]{:S(2)}) collective-permute-start(bf16[2,128,768]{2,1,0:T(8,128)(2,1)S(1)} %fusion.7), channel_id=1, source_target_pairs={{0,16},{16,0},{1,17},{17,1},{2,18},{18,2},{3,19},{19,3},{4,20},{20... | collective-permute-start | bytes 1179656 | tf_op jit(solution)/shard_map/ppermute | solution.py:171
  52.1 0.7 collective-permute-start.10
  52.8 3.1 %collective-permute-done.1 = bf16[2,64,768]{2,1,0:T(8,128)(2,1)S(1)} collective-permute-done((bf16[2,64,768]{2,1,0:T(8,128)(2,1)S(1)}, bf16[2,64,768]{2,1,0:T(8,128)(2,1)S(1)}, u32[]{:S(2)}, u32[]{:S(2)}) %collective-permute-start.1) | collective-permute-done | bytes 196640 | tf_op jit(solution)/shard_map/ppermute | solution.py:171
  55.9 0.1 fusion.33
  55.9 0.1 collective-permute-start.3
  56.1 3.0 %collective-permute-done.8 = bf16[2,128,768]{2,1,0:T(8,128)(2,1)S(1)} collective-permute-done((bf16[2,128,768]{2,1,0:T(8,128)(2,1)S(1)}, bf16[2,128,768]{2,1,0:T(8,128)(2,1)S(1)}, u32[]{:S(2)}, u32[]{:S(2)}) %collective-permute-start.8) | collective-permute-done | bytes 393248 | tf_op jit(solution)/shard_map/ppermute | solution.py:171
  59.1 0.0 collective-permute-start.2
  59.1 22.9 %collective-permute-done.6 = bf16[2,128,768]{2,1,0:T(8,128)(2,1)S(1)} collective-permute-done((bf16[2,128,768]{2,1,0:T(8,128)(2,1)S(1)}, bf16[2,128,768]{2,1,0:T(8,128)(2,1)S(1)}, u32[]{:S(2)}, u32[]{:S(2)}) %collective-permute-start.6) | collective-permute-done | bytes 393248 | tf_op jit(solution)/shard_map/ppermute | solution.py:171
  82.0 0.0 collective-permute-start.4
  82.0 0.1 collective-permute-start.9
  82.1 0.1 pad_add_fusion.pairs_ref
  82.2 2.0 %collective-permute-start.7 = (bf16[2,128,768]{2,1,0:T(8,128)(2,1)S(1)}, bf16[2,128,768]{2,1,0:T(8,128)(2,1)S(1)}, u32[]{:S(2)}, u32[]{:S(2)}) collective-permute-start(bf16[2,128,768]{2,1,0:T(8,128)(2,1)S(1)} %collective-permute-done.6), channel_id=1, source_target_pairs={{0,16},{16,0},{1,17},{17,1},{2,18},{18,2},{3,19},{19,3},{4,20},{20... | collective-permute-start | bytes 1179656 | tf_op jit(solution)/shard_map/ppermute | solution.py:171
  84.2 0.1 maximum_bitcast_fusion
  84.3 0.1 collective-permute-start.11
  84.4 0.0 collective-permute-done.2
  84.4 4.8 %collective-permute-done.4 = bf16[4,64,768]{2,1,0:T(8,128)(2,1)S(1)} collective-permute-done((bf16[4,64,768]{2,1,0:T(8,128)(2,1)S(1)}, bf16[4,64,768]{2,1,0:T(8,128)(2,1)S(1)}, u32[]{:S(2)}, u32[]{:S(2)}) %collective-permute-start.4) | collective-permute-done | bytes 393248 | tf_op jit(solution)/shard_map/ppermute | solution.py:171
  89.2 0.3 maximum_convert_fusion.1.row_ref
  89.4 4.6 %collective-permute-done.9 = bf16[2,128,768]{2,1,0:T(8,128)(2,1)S(1)} collective-permute-done((bf16[2,128,768]{2,1,0:T(8,128)(2,1)S(1)}, bf16[2,128,768]{2,1,0:T(8,128)(2,1)S(1)}, u32[]{:S(2)}, u32[]{:S(2)}) %collective-permute-start.9) | collective-permute-done | bytes 393248 | tf_op jit(solution)/shard_map/ppermute | solution.py:171
  94.1 0.1 maximum_bitcast_fusion.2
  94.1 8.4 %collective-permute-done.7 = bf16[2,128,768]{2,1,0:T(8,128)(2,1)S(1)} collective-permute-done((bf16[2,128,768]{2,1,0:T(8,128)(2,1)S(1)}, bf16[2,128,768]{2,1,0:T(8,128)(2,1)S(1)}, u32[]{:S(2)}, u32[]{:S(2)}) %collective-permute-start.7) | collective-permute-done | bytes 393248 | tf_op jit(solution)/shard_map/ppermute | solution.py:171
  102.5 0.1 maximum_bitcast_fusion.1
  102.6 7.3 %collective-permute-done.11 = bf16[2,128,768]{2,1,0:T(8,128)(2,1)S(1)} collective-permute-done((bf16[2,128,768]{2,1,0:T(8,128)(2,1)S(1)}, bf16[2,128,768]{2,1,0:T(8,128)(2,1)S(1)}, u32[]{:S(2)}, u32[]{:S(2)}) %collective-permute-start.11) | collective-permute-done | bytes 393248 | tf_op jit(solution)/shard_map/ppermute | solution.py:171
  109.9 0.1 maximum_bitcast_fusion.3
  110.0 2.9 %maximum_convert_fusion.col_ref = f32[4,4,128,768]{3,2,1,0:T(8,128)} fusion(bf16[1,4,128,768]{3,2,1,0:T(8,128)(2,1)S(1)} %maximum_bitcast_fusion.3, bf16[1,4,128,768]{3,2,1,0:T(8,128)(2,1)S(1)} %maximum_bitcast_fusion.2, bf16[1,4,128,768]{3,2,1,0:T(8,128)(2,1)S(1)} %maximum_bitcast_fusion.1, bf16[1,4,128,768]{3,2,1,0:T(8,128)(2,1)S(1)} %maximum_bitcast_fusion), kind=kLoop, calls=%fused_computation.4 | loop fusion | flops 6291456 | bytes 9437184 | tf_op jit(solution)/shard_map/convert_element_type | solution.py:234
  112.9 73.5 %shard_map.38 = bf16[4,64,128,256]{3,2,1,0:T(8,128)(2,1)} custom-call(s32[4,2]{1,0:T(4,128)S(1)} %pad_add_fusion.pairs_ref, f32[4,4,64,768]{3,2,1,0:T(8,128)S(1)} %maximum_convert_fusion.1.row_ref, f32[4,4,128,768]{3,2,1,0:T(8,128)} %maximum_convert_fusion.col_ref, bf16[768,256]{1,0:T(8,128)(2,1)S(1)} %pad_maximum_fusion.1.lags_ref), custom_call_target="tpu_custom_call" | custom-call | flops 13287555072 | bytes 26214400 | tf_op jit(solution)/shard_map/pallas_call | solution.py:146
  (12 shorter events, 0.1 us)
Async XLA Ops:
  2.3 33.8 %collective-permute-start = (bf16[128,4352]{1,0:T(8,128)(2,1)}, bf16[128,4352]{1,0:T(8,128)(2,1)S(1)}, u32[]{:S(2)}, u32[]{:S(2)}) collective-permute-start(bf16[128,4352]{1,0:T(8,128)(2,1)} %slice.17), channel_id=1, source_target_pairs={{16,0},{17,1},{18,2},{19,3},{20,4},{21,5},{22,6},{23,7},{24,8},{25... | collective-permute-start | bytes 3342344 | tf_op jit(solution)/shard_map/ppermute | solution.py:27
  15.9 20.0 %copy-start.1 = (bf16[128,7680]{1,0:T(8,128)(2,1)S(1)}, bf16[128,7680]{1,0:T(8,128)(2,1)}, u32[]{:S(2)}) copy-start(bf16[128,7680]{1,0:T(8,128)(2,1)} %param.3) | copy-start | bytes 5898244
  36.0 4.4 %copy-start = (bf16[7680,768]{1,0:T(8,128)(2,1)S(1)}, bf16[7680,768]{1,0:T(8,128)(2,1)}, u32[]{:S(2)}) copy-start(bf16[7680,768]{1,0:T(8,128)(2,1)} %shard_map.37) | copy-start | bytes 35389444
  44.3 14.8 %collective-permute-start.8 = (bf16[2,128,768]{2,1,0:T(8,128)(2,1)S(1)}, bf16[2,128,768]{2,1,0:T(8,128)(2,1)S(1)}, u32[]{:S(2)}, u32[]{:S(2)}) collective-permute-start(bf16[2,128,768]{2,1,0:T(8,128)(2,1)S(1)} %fusion.7), channel_id=1, source_target_pairs={{8,0},{12,4},{9,1},{13,5},{10,2},{14,6},{11,3},{15,7},{24,16},{28,... | collective-permute-start | bytes 1179656 | tf_op jit(solution)/shard_map/ppermute | solution.py:171
  45.6 36.3 %collective-permute-start.6 = (bf16[2,128,768]{2,1,0:T(8,128)(2,1)S(1)}, bf16[2,128,768]{2,1,0:T(8,128)(2,1)S(1)}, u32[]{:S(2)}, u32[]{:S(2)}) collective-permute-start(bf16[2,128,768]{2,1,0:T(8,128)(2,1)S(1)} %fusion.7), channel_id=1, source_target_pairs={{4,0},{8,4},{12,8},{5,1},{9,5},{13,9},{6,2},{10,6},{14,10},{7,3},{... | collective-permute-start | bytes 1179656 | tf_op jit(solution)/shard_map/ppermute | solution.py:171
  48.0 7.8 %collective-permute-start.1 = (bf16[2,64,768]{2,1,0:T(8,128)(2,1)S(1)}, bf16[2,64,768]{2,1,0:T(8,128)(2,1)S(1)}, u32[]{:S(2)}, u32[]{:S(2)}) collective-permute-start(bf16[2,64,768]{2,1,0:T(8,128)(2,1)S(1)} %get-tuple-element.10), channel_id=1, source_target_pairs={{0,16},{16,0},{1,17},{17,1},{2,18},{18,2},{3,19},{19,3},{4,20},{20... | collective-permute-start | bytes 589832 | tf_op jit(solution)/shard_map/ppermute | solution.py:171
  50.1 31.9 %collective-permute-start.5 = (bf16[2,128,768]{2,1,0:T(8,128)(2,1)S(1)}, bf16[2,128,768]{2,1,0:T(8,128)(2,1)S(1)}, u32[]{:S(2)}, u32[]{:S(2)}) collective-permute-start(bf16[2,128,768]{2,1,0:T(8,128)(2,1)S(1)} %fusion.7), channel_id=1, source_target_pairs={{0,16},{16,0},{1,17},{17,1},{2,18},{18,2},{3,19},{19,3},{4,20},{20... | collective-permute-start | bytes 1179656 | tf_op jit(solution)/shard_map/ppermute | solution.py:171
  52.1 30.0 %collective-permute-start.10 = (bf16[2,128,768]{2,1,0:T(8,128)(2,1)S(1)}, bf16[2,128,768]{2,1,0:T(8,128)(2,1)S(1)}, u32[]{:S(2)}, u32[]{:S(2)}) collective-permute-start(bf16[2,128,768]{2,1,0:T(8,128)(2,1)S(1)} %fusion.7), channel_id=1, source_target_pairs={{12,0},{13,1},{14,2},{15,3},{28,16},{29,17},{30,18},{31,19}} | collective-permute-start | bytes 1179656 | tf_op jit(solution)/shard_map/ppermute | solution.py:171
  55.9 28.3 %collective-permute-start.3 = (bf16[4,64,768]{2,1,0:T(8,128)(2,1)S(1)}, bf16[4,64,768]{2,1,0:T(8,128)(2,1)S(1)}, u32[]{:S(2)}, u32[]{:S(2)}) collective-permute-start(bf16[4,64,768]{2,1,0:T(8,128)(2,1)S(1)} %get-tuple-element.8), channel_id=1, source_target_pairs={{0,2},{1,3},{2,0},{3,1},{4,6},{5,7},{6,4},{7,5},{8,10},{9,11},{10,... | collective-permute-start | bytes 1179656 | tf_op jit(solution)/shard_map/ppermute | solution.py:171
  59.1 25.3 %collective-permute-start.2 = (bf16[4,64,768]{2,1,0:T(8,128)(2,1)S(1)}, bf16[4,64,768]{2,1,0:T(8,128)(2,1)S(1)}, u32[]{:S(2)}, u32[]{:S(2)}) collective-permute-start(bf16[4,64,768]{2,1,0:T(8,128)(2,1)S(1)} %get-tuple-element.8), channel_id=1, source_target_pairs={{0,3},{1,0},{2,1},{3,2},{4,7},{5,4},{6,5},{7,6},{8,11},{9,8},{10,9... | collective-permute-start | bytes 1179656 | tf_op jit(solution)/shard_map/ppermute | solution.py:171
  82.0 7.2 %collective-permute-start.4 = (bf16[4,64,768]{2,1,0:T(8,128)(2,1)S(1)}, bf16[4,64,768]{2,1,0:T(8,128)(2,1)S(1)}, u32[]{:S(2)}, u32[]{:S(2)}) collective-permute-start(bf16[4,64,768]{2,1,0:T(8,128)(2,1)S(1)} %get-tuple-element.8), channel_id=1, source_target_pairs={{0,1},{1,2},{2,3},{3,0},{4,5},{5,6},{6,7},{7,4},{8,9},{9,10},{10,1... | collective-permute-start | bytes 1179656 | tf_op jit(solution)/shard_map/ppermute | solution.py:171
  82.0 12.1 %collective-permute-start.9 = (bf16[2,128,768]{2,1,0:T(8,128)(2,1)S(1)}, bf16[2,128,768]{2,1,0:T(8,128)(2,1)S(1)}, u32[]{:S(2)}, u32[]{:S(2)}) collective-permute-start(bf16[2,128,768]{2,1,0:T(8,128)(2,1)S(1)} %collective-permute-done.8), channel_id=1, source_target_pairs={{0,16},{16,0},{1,17},{17,1},{2,18},{18,2},{3,19},{19,3},{4,20},{20... | collective-permute-start | bytes 1179656 | tf_op jit(solution)/shard_map/ppermute | solution.py:171
  82.2 20.3 %collective-permute-start.7 = (bf16[2,128,768]{2,1,0:T(8,128)(2,1)S(1)}, bf16[2,128,768]{2,1,0:T(8,128)(2,1)S(1)}, u32[]{:S(2)}, u32[]{:S(2)}) collective-permute-start(bf16[2,128,768]{2,1,0:T(8,128)(2,1)S(1)} %collective-permute-done.6), channel_id=1, source_target_pairs={{0,16},{16,0},{1,17},{17,1},{2,18},{18,2},{3,19},{19,3},{4,20},{20... | collective-permute-start | bytes 1179656 | tf_op jit(solution)/shard_map/ppermute | solution.py:171
  84.3 25.6 %collective-permute-start.11 = (bf16[2,128,768]{2,1,0:T(8,128)(2,1)S(1)}, bf16[2,128,768]{2,1,0:T(8,128)(2,1)S(1)}, u32[]{:S(2)}, u32[]{:S(2)}) collective-permute-start(bf16[2,128,768]{2,1,0:T(8,128)(2,1)S(1)} %collective-permute-done.10), channel_id=1, source_target_pairs={{0,16},{16,0},{1,17},{17,1},{2,18},{18,2},{3,19},{19,3},{4,20},{20... | collective-permute-start | bytes 1179656 | tf_op jit(solution)/shard_map/ppermute | solution.py:171

commit v7 on v6

--- a/solution.py
+++ b/solution.py
@@ -101,10 +101,9 @@
 F_CHUNK = 128
 
 
-def pair_kernel(pairs_ref, row_ref, col_ref, lags_ref, out_ref, cross_ref):
+def cross_tile(row_ref, col_ref, cross_ref):
     windows = row_ref.shape[1]
     cols = col_ref.shape[2]
-
     for i in range(row_ref.shape[2]):
         for jc in range(cols // J_CHUNK):
             js = pl.ds(jc * J_CHUNK, J_CHUNK)
@@ -123,24 +122,58 @@
                 rows = pl.ds(i * cols + jc * J_CHUNK, J_CHUNK)
                 cross_ref[rows, fr] = acc_re.astype(jnp.bfloat16)
                 cross_ref[rows, fi] = acc_im.astype(jnp.bfloat16)
-    result = jnp.dot(cross_ref[...], lags_ref[...], preferred_element_type=jnp.float32)
-    out_ref[0] = result.reshape(out_ref.shape[1:]).astype(out_ref.dtype)
+
+
+def pair_kernel(pairs_ref, row_ref, col_ref, lags_ref, out_ref, cross_even, cross_odd):
+    step = pl.program_id(0)
+
+    def lag_matmul(cross_ref):
+        result = jnp.dot(cross_ref[...], lags_ref[...], preferred_element_type=jnp.float32)
+        out_ref[0] = result.reshape(out_ref.shape[1:]).astype(out_ref.dtype)
+
+    @pl.when(step % 2 == 0)
+    def _():
+        lag_matmul(cross_odd)
+        cross_tile(row_ref, col_ref, cross_even)
+
+    @pl.when(step % 2 == 1)
+    def _():
+        lag_matmul(cross_even)
+        cross_tile(row_ref, col_ref, cross_odd)
 
 
 def all_pairs(pairs, row_all, col_all, lags):
     n_pairs = pairs.shape[0]
     windows, rows, cols = row_all.shape[1], row_all.shape[2], col_all.shape[2]
     tiles = rows // ROW_TILE
+    last = n_pairs * tiles - 1
+
+    def compute_tile(s):
+        return jnp.minimum(s, last)
+
+    def written_tile(s):
+        return jnp.maximum(s - 1, 0)
+
     grid_spec = pltpu.PrefetchScalarGridSpec(
         num_scalar_prefetch=1,
-        grid=(n_pairs, tiles),
+        grid=(n_pairs * tiles + 1,),
         in_specs=[
-            pl.BlockSpec((1, windows, ROW_TILE, 2 * NF), lambda p, t, pr: (pr[p, 0], 0, t, 0)),
-            pl.BlockSpec((1, windows, cols, 2 * NF), lambda p, t, pr: (pr[p, 1], 0, 0, 0)),
-            pl.BlockSpec((2 * NF, LAGS), lambda p, t, pr: (0, 0)),
+            pl.BlockSpec(
+                (1, windows, ROW_TILE, 2 * NF),
+                lambda s, pr: (pr[compute_tile(s) // tiles, 0], 0, compute_tile(s) % tiles, 0),
+            ),
+            pl.BlockSpec(
+                (1, windows, cols, 2 * NF), lambda s, pr: (pr[compute_tile(s) // tiles, 1], 0, 0, 0)
+            ),
+            pl.BlockSpec((2 * NF, LAGS), lambda s, pr: (0, 0)),
         ],
-        out_specs=pl.BlockSpec((1, ROW_TILE, cols, LAGS), lambda p, t, pr: (p, t, 0, 0)),
-        scratch_shapes=[pltpu.VMEM((ROW_TILE * cols, 2 * NF), jnp.bfloat16)],
+        out_specs=pl.BlockSpec(
+            (1, ROW_TILE, cols, LAGS), lambda s, pr: (written_tile(s) // tiles, written_tile(s) % tiles, 0, 0)
+        ),
+        scratch_shapes=[
+            pltpu.VMEM((ROW_TILE * cols, 2 * NF), jnp.bfloat16),
+            pltpu.VMEM((ROW_TILE * cols, 2 * NF), jnp.bfloat16),
+        ],
     )
     flops = n_pairs * rows * cols * (2 * NF * windows * 4 + 2 * 2 * NF * LAGS)
     return pl.pallas_call(
@@ -148,7 +181,7 @@
         grid_spec=grid_spec,
         out_shape=jax.ShapeDtypeStruct((n_pairs, rows, cols, LAGS), jnp.bfloat16),
         compiler_params=pltpu.CompilerParams(
-            dimension_semantics=("arbitrary", "arbitrary"),
+            dimension_semantics=("arbitrary",),
             vmem_limit_bytes=48 * 1024 * 1024,
         ),
         cost_estimate=pl.CostEstimate(

time: 187 us -> 191 us (1.021)
  Pallas kernels: 93.4 us -> 97.7 us
    pallas_call x1, Pallas kernels: 73.5 us -> 77.7 us  [all_pairs(): pl.pallas_call(pair_kernel, grid_spec=grid_spec, out_shape=jax.ShapeDtype...]
  transfers between devices with their start and end apart: 12 -> 12, of which waited for: 7 -> 7; matrix products, arithmetic and copies ran while one was open for 6% -> 6% of each run, Pallas kernels for 11% -> 10%
where the time goes in v7:
time: 191 us
  Pallas kernels  97.7 us (51%)
  waiting for transfers between devices  54.1 us (28%)
  other arithmetic  11.6 us (6%)
  starting transfers between devices  11.3 us (6%)
  local copies, waits for them, and re-layouts  8.94 us (5%)
  matrix products  3.76 us (2%)
  between operations  3.26 us (2%)
    pallas_call x1, Pallas kernels, all_pairs(): pl.pallas_call(pair_kernel, grid_spec=grid_spec, out_shape=jax.ShapeDtype...  77.7 us
    ppermute x11, waiting for transfers between devices, exchange(): return lax.ppermute(value, axes, pairs)  54.1 us
    pallas_call x1, Pallas kernels, forward_table(): pl.pallas_call(table_kernel, grid=(n_coarse // TABLE_Q,), in_specs=[pl.Bl...  20 us
    ppermute x11, starting transfers between devices, exchange(): return lax.ppermute(value, axes, pairs)  8.76 us
    sin x1, other arithmetic, forward_table(): high_sin = jnp.sin(high_angle).reshape(n_coarse, 1, NF)  4.2 us
  transfers between devices with their start and end apart: 12, of which 7 were waited for; matrix products, arithmetic and copies ran while one was open for 6% of the time, Pallas kernels for 10%

profile of v7, /device:TPU:14, one launch (start us, length us, event | category | flops | bytes accessed | tf_op | source)
XLA Modules:
  0.0 190.6 jit_solution(2671956396538527251)
XLA Ops:
  0.0 2.3 %slice.17 = bf16[128,4352]{1,0:T(8,128)(2,1)} slice(bf16[128,7680]{1,0:T(8,128)(2,1)} %param.3), slice={[0:128], [0:4352]} | slice | bytes 2228224 | tf_op jit(solution)/shard_map/slice | solution.py:225
  2.3 2.5 %collective-permute-start = (bf16[128,4352]{1,0:T(8,128)(2,1)}, bf16[128,4352]{1,0:T(8,128)(2,1)S(1)}, u32[]{:S(2)}, u32[]{:S(2)}) collective-permute-start(bf16[128,4352]{1,0:T(8,128)(2,1)} %slice.17), channel_id=1, source_target_pairs={{16,0},{17,1},{18,2},{19,3},{20,4},{21,5},{22,6},{23,7},{24,8},{25... | collective-permute-start | bytes 3342344 | tf_op jit(solution)/shard_map/ppermute | solution.py:27
  4.9 1.6 fusion.21
  6.4 4.2 %fusion.28 = (f32[60,1,384]{2,1,0:T(1,128)}, f32[60,1,384]{2,1,0:T(1,128)}) fusion(s32[384]{0:T(512)S(1)} %iota_add_fusion, s32[60]{0:T(128)S(1)} %iota_multiply_fusion), kind=kLoop, calls=%fused_computation.48 | loop fusion | flops 207360 | bytes 186096 | tf_op jit(solution)/shard_map/sin | solution.py:58
  10.6 0.8 fusion.34
  11.4 1.3 fusion.35
  15.1 0.1 copy.6
  15.2 0.1 copy.7
  15.9 0.0 copy-start.1
  15.9 20.0 %shard_map.37 = bf16[7680,768]{1,0:T(8,128)(2,1)} custom-call(f32[60,1,384]{2,1,0:T(1,128)} %get-tuple-element.14.high_cos_ref, f32[60,1,384]{2,1,0:T(1,128)} %get-tuple-element.13.high_sin_ref, f32[128,384]{1,0:T(8,128)} %get-tuple-element.16.low_cos_ref, f32[128,384]{1,0:T(8,128)} %get-tuple-element.15.low_sin_ref), custom_call_target="tpu_custom_call" | custom-call | tf_op jit(solution)/shard_map/pallas_call | solution.py:60
  36.0 0.0 copy-start
  36.0 0.1 constant_dynamic-update-slice_fusion.1
  36.1 0.1 constant_dynamic-update-slice_fusion
  36.2 1.7 constant_dynamic-slice_fusion.3
  37.9 2.5 %copy-done = bf16[7680,768]{1,0:T(8,128)(2,1)S(1)} copy-done((bf16[7680,768]{1,0:T(8,128)(2,1)S(1)}, bf16[7680,768]{1,0:T(8,128)(2,1)}, u32[]{:S(2)}) %copy-start) | copy-done | bytes 11796504
  40.3 3.2 %fusion = f32[256,768]{1,0:T(8,128)S(1)} fusion(bf16[7680,768]{1,0:T(8,128)(2,1)S(1)} %copy-done, bf16[128,7680]{1,0:T(8,128)(2,1)S(1)} %get-tuple-element.6, bf16[128,7680]{1,0:T(8,128)(2,1)S(1)} %get-tuple-element.5), kind=kOutput, calls=%fused_computation | convolution fusion | flops 3027763200 | bytes 16515072 | tf_op jit(solution)/shard_map/dot_general | solution.py:234
  43.5 0.1 fusion.26
  43.7 0.6 fusion.6
  44.2 0.1 fusion.7
  44.3 1.3 collective-permute-start.8
  45.6 2.4 %collective-permute-start.6 = (bf16[2,128,768]{2,1,0:T(8,128)(2,1)S(1)}, bf16[2,128,768]{2,1,0:T(8,128)(2,1)S(1)}, u32[]{:S(2)}, u32[]{:S(2)}) collective-permute-start(bf16[2,128,768]{2,1,0:T(8,128)(2,1)S(1)} %fusion.7), channel_id=1, source_target_pairs={{4,0},{8,4},{12,8},{5,1},{9,5},{13,9},{6,2},{10,6},{14,10},{7,3},{... | collective-permute-start | bytes 1179656 | tf_op jit(solution)/shard_map/ppermute | solution.py:204
  48.0 0.1 collective-permute-start.1
  48.1 2.0 %multiply_convert_fusion.1 = (bf16[384,256]{1,0:T(8,128)(2,1)S(1)}, bf16[384,256]{1,0:T(8,128)(2,1)S(1)}) fusion(s32[256]{0:T(256)S(1)} %and_select_fusion.1, s32[384]{0:T(512)S(1)} %iota_add_fusion), kind=kLoop, calls=%fused_computation.27 | loop fusion | flops 1376256 | bytes 395776 | tf_op jit(solution)/shard_map/convert
  50.1 2.1 %collective-permute-start.5 = (bf16[2,128,768]{2,1,0:T(8,128)(2,1)S(1)}, bf16[2,128,768]{2,1,0:T(8,128)(2,1)S(1)}, u32[]{:S(2)}, u32[]{:S(2)}) collective-permute-start(bf16[2,128,768]{2,1,0:T(8,128)(2,1)S(1)} %fusion.7), channel_id=1, source_target_pairs={{0,16},{16,0},{1,17},{17,1},{2,18},{18,2},{3,19},{19,3},{4,20},{20... | collective-permute-start | bytes 1179656 | tf_op jit(solution)/shard_map/ppermute | solution.py:204
  52.1 0.7 collective-permute-start.10
  52.8 3.1 %collective-permute-done.1 = bf16[2,64,768]{2,1,0:T(8,128)(2,1)S(1)} collective-permute-done((bf16[2,64,768]{2,1,0:T(8,128)(2,1)S(1)}, bf16[2,64,768]{2,1,0:T(8,128)(2,1)S(1)}, u32[]{:S(2)}, u32[]{:S(2)}) %collective-permute-start.1) | collective-permute-done | bytes 196640 | tf_op jit(solution)/shard_map/ppermute | solution.py:204
  55.9 0.1 fusion.33
  55.9 0.1 collective-permute-start.3
  56.1 3.0 %collective-permute-done.8 = bf16[2,128,768]{2,1,0:T(8,128)(2,1)S(1)} collective-permute-done((bf16[2,128,768]{2,1,0:T(8,128)(2,1)S(1)}, bf16[2,128,768]{2,1,0:T(8,128)(2,1)S(1)}, u32[]{:S(2)}, u32[]{:S(2)}) %collective-permute-start.8) | collective-permute-done | bytes 393248 | tf_op jit(solution)/shard_map/ppermute | solution.py:204
  59.1 0.0 collective-permute-start.2
  59.1 22.9 %collective-permute-done.6 = bf16[2,128,768]{2,1,0:T(8,128)(2,1)S(1)} collective-permute-done((bf16[2,128,768]{2,1,0:T(8,128)(2,1)S(1)}, bf16[2,128,768]{2,1,0:T(8,128)(2,1)S(1)}, u32[]{:S(2)}, u32[]{:S(2)}) %collective-permute-start.6) | collective-permute-done | bytes 393248 | tf_op jit(solution)/shard_map/ppermute | solution.py:204
  82.0 0.0 collective-permute-start.4
  82.0 0.1 collective-permute-start.9
  82.1 0.1 pad_add_fusion.pairs_ref
  82.2 2.0 %collective-permute-start.7 = (bf16[2,128,768]{2,1,0:T(8,128)(2,1)S(1)}, bf16[2,128,768]{2,1,0:T(8,128)(2,1)S(1)}, u32[]{:S(2)}, u32[]{:S(2)}) collective-permute-start(bf16[2,128,768]{2,1,0:T(8,128)(2,1)S(1)} %collective-permute-done.6), channel_id=1, source_target_pairs={{0,16},{16,0},{1,17},{17,1},{2,18},{18,2},{3,19},{19,3},{4,20},{20... | collective-permute-start | bytes 1179656 | tf_op jit(solution)/shard_map/ppermute | solution.py:204
  84.2 0.1 maximum_bitcast_fusion
  84.3 0.1 collective-permute-start.11
  84.4 0.0 collective-permute-done.2
  84.4 4.8 %collective-permute-done.4 = bf16[4,64,768]{2,1,0:T(8,128)(2,1)S(1)} collective-permute-done((bf16[4,64,768]{2,1,0:T(8,128)(2,1)S(1)}, bf16[4,64,768]{2,1,0:T(8,128)(2,1)S(1)}, u32[]{:S(2)}, u32[]{:S(2)}) %collective-permute-start.4) | collective-permute-done | bytes 393248 | tf_op jit(solution)/shard_map/ppermute | solution.py:204
  89.2 0.3 maximum_convert_fusion.1.row_ref
  89.4 4.6 %collective-permute-done.9 = bf16[2,128,768]{2,1,0:T(8,128)(2,1)S(1)} collective-permute-done((bf16[2,128,768]{2,1,0:T(8,128)(2,1)S(1)}, bf16[2,128,768]{2,1,0:T(8,128)(2,1)S(1)}, u32[]{:S(2)}, u32[]{:S(2)}) %collective-permute-start.9) | collective-permute-done | bytes 393248 | tf_op jit(solution)/shard_map/ppermute | solution.py:204
  94.1 0.1 maximum_bitcast_fusion.2
  94.1 8.4 %collective-permute-done.7 = bf16[2,128,768]{2,1,0:T(8,128)(2,1)S(1)} collective-permute-done((bf16[2,128,768]{2,1,0:T(8,128)(2,1)S(1)}, bf16[2,128,768]{2,1,0:T(8,128)(2,1)S(1)}, u32[]{:S(2)}, u32[]{:S(2)}) %collective-permute-start.7) | collective-permute-done | bytes 393248 | tf_op jit(solution)/shard_map/ppermute | solution.py:204
  102.5 0.1 maximum_bitcast_fusion.1
  102.6 7.3 %collective-permute-done.11 = bf16[2,128,768]{2,1,0:T(8,128)(2,1)S(1)} collective-permute-done((bf16[2,128,768]{2,1,0:T(8,128)(2,1)S(1)}, bf16[2,128,768]{2,1,0:T(8,128)(2,1)S(1)}, u32[]{:S(2)}, u32[]{:S(2)}) %collective-permute-start.11) | collective-permute-done | bytes 393248 | tf_op jit(solution)/shard_map/ppermute | solution.py:204
  109.9 0.1 maximum_bitcast_fusion.3
  110.0 2.9 %maximum_convert_fusion.col_ref = f32[4,4,128,768]{3,2,1,0:T(8,128)} fusion(bf16[1,4,128,768]{3,2,1,0:T(8,128)(2,1)S(1)} %maximum_bitcast_fusion.3, bf16[1,4,128,768]{3,2,1,0:T(8,128)(2,1)S(1)} %maximum_bitcast_fusion.2, bf16[1,4,128,768]{3,2,1,0:T(8,128)(2,1)S(1)} %maximum_bitcast_fusion.1, bf16[1,4,128,768]{3,2,1,0:T(8,128)(2,1)S(1)} %maximum_bitcast_fusion), kind=kLoop, calls=%fused_computation.4 | loop fusion | flops 6291456 | bytes 9437184 | tf_op jit(solution)/shard_map/convert_element_type | solution.py:267
  112.9 77.7 %shard_map.38 = bf16[4,64,128,256]{3,2,1,0:T(8,128)(2,1)} custom-call(s32[4,2]{1,0:T(4,128)S(1)} %pad_add_fusion.pairs_ref, f32[4,4,64,768]{3,2,1,0:T(8,128)S(1)} %maximum_convert_fusion.1.row_ref, f32[4,4,128,768]{3,2,1,0:T(8,128)} %maximum_convert_fusion.col_ref, bf16[768,256]{1,0:T(8,128)(2,1)S(1)} %pad_maximum_fusion.1.lags_ref), custom_call_target="tpu_custom_call" | custom-call | flops 13287555072 | bytes 26214400 | tf_op jit(solution)/shard_map/pallas_call | solution.py:179
  (12 shorter events, 0.1 us)
Async XLA Ops:
  2.3 33.8 %collective-permute-start = (bf16[128,4352]{1,0:T(8,128)(2,1)}, bf16[128,4352]{1,0:T(8,128)(2,1)S(1)}, u32[]{:S(2)}, u32[]{:S(2)}) collective-permute-start(bf16[128,4352]{1,0:T(8,128)(2,1)} %slice.17), channel_id=1, source_target_pairs={{16,0},{17,1},{18,2},{19,3},{20,4},{21,5},{22,6},{23,7},{24,8},{25... | collective-permute-start | bytes 3342344 | tf_op jit(solution)/shard_map/ppermute | solution.py:27
  15.9 20.0 %copy-start.1 = (bf16[128,7680]{1,0:T(8,128)(2,1)S(1)}, bf16[128,7680]{1,0:T(8,128)(2,1)}, u32[]{:S(2)}) copy-start(bf16[128,7680]{1,0:T(8,128)(2,1)} %param.3) | copy-start | bytes 5898244
  36.0 4.4 %copy-start = (bf16[7680,768]{1,0:T(8,128)(2,1)S(1)}, bf16[7680,768]{1,0:T(8,128)(2,1)}, u32[]{:S(2)}) copy-start(bf16[7680,768]{1,0:T(8,128)(2,1)} %shard_map.37) | copy-start | bytes 35389444
  44.3 14.8 %collective-permute-start.8 = (bf16[2,128,768]{2,1,0:T(8,128)(2,1)S(1)}, bf16[2,128,768]{2,1,0:T(8,128)(2,1)S(1)}, u32[]{:S(2)}, u32[]{:S(2)}) collective-permute-start(bf16[2,128,768]{2,1,0:T(8,128)(2,1)S(1)} %fusion.7), channel_id=1, source_target_pairs={{8,0},{12,4},{9,1},{13,5},{10,2},{14,6},{11,3},{15,7},{24,16},{28,... | collective-permute-start | bytes 1179656 | tf_op jit(solution)/shard_map/ppermute | solution.py:204
  45.6 36.3 %collective-permute-start.6 = (bf16[2,128,768]{2,1,0:T(8,128)(2,1)S(1)}, bf16[2,128,768]{2,1,0:T(8,128)(2,1)S(1)}, u32[]{:S(2)}, u32[]{:S(2)}) collective-permute-start(bf16[2,128,768]{2,1,0:T(8,128)(2,1)S(1)} %fusion.7), channel_id=1, source_target_pairs={{4,0},{8,4},{12,8},{5,1},{9,5},{13,9},{6,2},{10,6},{14,10},{7,3},{... | collective-permute-start | bytes 1179656 | tf_op jit(solution)/shard_map/ppermute | solution.py:204
  48.0 7.8 %collective-permute-start.1 = (bf16[2,64,768]{2,1,0:T(8,128)(2,1)S(1)}, bf16[2,64,768]{2,1,0:T(8,128)(2,1)S(1)}, u32[]{:S(2)}, u32[]{:S(2)}) collective-permute-start(bf16[2,64,768]{2,1,0:T(8,128)(2,1)S(1)} %get-tuple-element.10), channel_id=1, source_target_pairs={{0,16},{16,0},{1,17},{17,1},{2,18},{18,2},{3,19},{19,3},{4,20},{20... | collective-permute-start | bytes 589832 | tf_op jit(solution)/shard_map/ppermute | solution.py:204
  50.1 31.9 %collective-permute-start.5 = (bf16[2,128,768]{2,1,0:T(8,128)(2,1)S(1)}, bf16[2,128,768]{2,1,0:T(8,128)(2,1)S(1)}, u32[]{:S(2)}, u32[]{:S(2)}) collective-permute-start(bf16[2,128,768]{2,1,0:T(8,128)(2,1)S(1)} %fusion.7), channel_id=1, source_target_pairs={{0,16},{16,0},{1,17},{17,1},{2,18},{18,2},{3,19},{19,3},{4,20},{20... | collective-permute-start | bytes 1179656 | tf_op jit(solution)/shard_map/ppermute | solution.py:204
  52.1 30.0 %collective-permute-start.10 = (bf16[2,128,768]{2,1,0:T(8,128)(2,1)S(1)}, bf16[2,128,768]{2,1,0:T(8,128)(2,1)S(1)}, u32[]{:S(2)}, u32[]{:S(2)}) collective-permute-start(bf16[2,128,768]{2,1,0:T(8,128)(2,1)S(1)} %fusion.7), channel_id=1, source_target_pairs={{12,0},{13,1},{14,2},{15,3},{28,16},{29,17},{30,18},{31,19}} | collective-permute-start | bytes 1179656 | tf_op jit(solution)/shard_map/ppermute | solution.py:204
  55.9 28.3 %collective-permute-start.3 = (bf16[4,64,768]{2,1,0:T(8,128)(2,1)S(1)}, bf16[4,64,768]{2,1,0:T(8,128)(2,1)S(1)}, u32[]{:S(2)}, u32[]{:S(2)}) collective-permute-start(bf16[4,64,768]{2,1,0:T(8,128)(2,1)S(1)} %get-tuple-element.8), channel_id=1, source_target_pairs={{0,2},{1,3},{2,0},{3,1},{4,6},{5,7},{6,4},{7,5},{8,10},{9,11},{10,... | collective-permute-start | bytes 1179656 | tf_op jit(solution)/shard_map/ppermute | solution.py:204
  59.1 25.3 %collective-permute-start.2 = (bf16[4,64,768]{2,1,0:T(8,128)(2,1)S(1)}, bf16[4,64,768]{2,1,0:T(8,128)(2,1)S(1)}, u32[]{:S(2)}, u32[]{:S(2)}) collective-permute-start(bf16[4,64,768]{2,1,0:T(8,128)(2,1)S(1)} %get-tuple-element.8), channel_id=1, source_target_pairs={{0,3},{1,0},{2,1},{3,2},{4,7},{5,4},{6,5},{7,6},{8,11},{9,8},{10,9... | collective-permute-start | bytes 1179656 | tf_op jit(solution)/shard_map/ppermute | solution.py:204
  82.0 7.2 %collective-permute-start.4 = (bf16[4,64,768]{2,1,0:T(8,128)(2,1)S(1)}, bf16[4,64,768]{2,1,0:T(8,128)(2,1)S(1)}, u32[]{:S(2)}, u32[]{:S(2)}) collective-permute-start(bf16[4,64,768]{2,1,0:T(8,128)(2,1)S(1)} %get-tuple-element.8), channel_id=1, source_target_pairs={{0,1},{1,2},{2,3},{3,0},{4,5},{5,6},{6,7},{7,4},{8,9},{9,10},{10,1... | collective-permute-start | bytes 1179656 | tf_op jit(solution)/shard_map/ppermute | solution.py:204
  82.0 12.1 %collective-permute-start.9 = (bf16[2,128,768]{2,1,0:T(8,128)(2,1)S(1)}, bf16[2,128,768]{2,1,0:T(8,128)(2,1)S(1)}, u32[]{:S(2)}, u32[]{:S(2)}) collective-permute-start(bf16[2,128,768]{2,1,0:T(8,128)(2,1)S(1)} %collective-permute-done.8), channel_id=1, source_target_pairs={{0,16},{16,0},{1,17},{17,1},{2,18},{18,2},{3,19},{19,3},{4,20},{20... | collective-permute-start | bytes 1179656 | tf_op jit(solution)/shard_map/ppermute | solution.py:204
  82.2 20.3 %collective-permute-start.7 = (bf16[2,128,768]{2,1,0:T(8,128)(2,1)S(1)}, bf16[2,128,768]{2,1,0:T(8,128)(2,1)S(1)}, u32[]{:S(2)}, u32[]{:S(2)}) collective-permute-start(bf16[2,128,768]{2,1,0:T(8,128)(2,1)S(1)} %collective-permute-done.6), channel_id=1, source_target_pairs={{0,16},{16,0},{1,17},{17,1},{2,18},{18,2},{3,19},{19,3},{4,20},{20... | collective-permute-start | bytes 1179656 | tf_op jit(solution)/shard_map/ppermute | solution.py:204
  84.3 25.6 %collective-permute-start.11 = (bf16[2,128,768]{2,1,0:T(8,128)(2,1)S(1)}, bf16[2,128,768]{2,1,0:T(8,128)(2,1)S(1)}, u32[]{:S(2)}, u32[]{:S(2)}) collective-permute-start(bf16[2,128,768]{2,1,0:T(8,128)(2,1)S(1)} %collective-permute-done.10), channel_id=1, source_target_pairs={{0,16},{16,0},{1,17},{17,1},{2,18},{18,2},{3,19},{19,3},{4,20},{20... | collective-permute-start | bytes 1179656 | tf_op jit(solution)/shard_map/ppermute | solution.py:204

commit v8 on v6

--- a/solution.py
+++ b/solution.py
@@ -104,27 +104,42 @@
 def pair_kernel(pairs_ref, row_ref, col_ref, lags_ref, out_ref, cross_ref):
     windows = row_ref.shape[1]
     cols = col_ref.shape[2]
-
     for i in range(row_ref.shape[2]):
         for jc in range(cols // J_CHUNK):
             js = pl.ds(jc * J_CHUNK, J_CHUNK)
             for fc in range(NF // F_CHUNK):
                 fr = pl.ds(fc * F_CHUNK, F_CHUNK)
                 fi = pl.ds(NF + fc * F_CHUNK, F_CHUNK)
+                fs = pl.ds(2 * NF + fc * F_CHUNK, F_CHUNK)
                 acc_re = jnp.zeros((J_CHUNK, F_CHUNK), jnp.float32)
                 acc_im = jnp.zeros((J_CHUNK, F_CHUNK), jnp.float32)
                 for w in range(windows):
                     xr = row_ref[0, w, i : i + 1, fr]
                     xi = row_ref[0, w, i : i + 1, fi]
+                    xs = row_ref[0, w, i : i + 1, fs]
                     yr = col_ref[0, w, js, fr]
-                    yi = col_ref[0, w, js, fi]
-                    acc_re = acc_re + xr * yr + xi * yi
-                    acc_im = acc_im + xi * yr - xr * yi
+                    yd = col_ref[0, w, js, fi]
+                    ys = col_ref[0, w, js, fs]
+                    both = yr * xs
+                    acc_re = acc_re + (both - xi * yd)
+                    acc_im = acc_im + (both - xr * ys)
                 rows = pl.ds(i * cols + jc * J_CHUNK, J_CHUNK)
                 cross_ref[rows, fr] = acc_re.astype(jnp.bfloat16)
                 cross_ref[rows, fi] = acc_im.astype(jnp.bfloat16)
     result = jnp.dot(cross_ref[...], lags_ref[...], preferred_element_type=jnp.float32)
     out_ref[0] = result.reshape(out_ref.shape[1:]).astype(out_ref.dtype)
+
+
+def with_sums(spectra):
+    real_part = spectra[..., :NF].astype(jnp.float32)
+    imag_part = spectra[..., NF:].astype(jnp.float32)
+    return jnp.concatenate([real_part, imag_part, real_part + imag_part], axis=-1)
+
+
+def with_differences(spectra):
+    real_part = spectra[..., :NF].astype(jnp.float32)
+    imag_part = spectra[..., NF:].astype(jnp.float32)
+    return jnp.concatenate([real_part, real_part - imag_part, real_part + imag_part], axis=-1)
 
 
 def all_pairs(pairs, row_all, col_all, lags):
@@ -135,8 +150,8 @@
         num_scalar_prefetch=1,
         grid=(n_pairs, tiles),
         in_specs=[
-            pl.BlockSpec((1, windows, ROW_TILE, 2 * NF), lambda p, t, pr: (pr[p, 0], 0, t, 0)),
-            pl.BlockSpec((1, windows, cols, 2 * NF), lambda p, t, pr: (pr[p, 1], 0, 0, 0)),
+            pl.BlockSpec((1, windows, ROW_TILE, 3 * NF), lambda p, t, pr: (pr[p, 0], 0, t, 0)),
+            pl.BlockSpec((1, windows, cols, 3 * NF), lambda p, t, pr: (pr[p, 1], 0, 0, 0)),
             pl.BlockSpec((2 * NF, LAGS), lambda p, t, pr: (0, 0)),
         ],
         out_specs=pl.BlockSpec((1, ROW_TILE, cols, LAGS), lambda p, t, pr: (p, t, 0, 0)),
@@ -231,7 +246,7 @@
     row_slot = (local_pairs[:, 0] - pcol_index + n_pcol) % n_pcol
     col_slot = jnp.clip(local_pairs[:, 1] - prow_index, 0, n_prow - 1)
     pairs = jnp.stack([row_slot, col_slot], axis=1).astype(jnp.int32)
-    result = all_pairs(pairs, row_all.astype(jnp.float32), col_all.astype(jnp.float32), lags)
+    result = all_pairs(pairs, with_sums(row_all), with_differences(col_all), lags)
     return result.reshape(1, 1, NP, half_rows, channels_here, LAGS)
 
 

time: 187 us -> 192 us (1.027)
  other arithmetic: 11.6 us -> 23.1 us
  waiting for transfers between devices: 54.1 us -> 49.2 us
  Pallas kernels: 93.4 us -> 88.7 us
  local copies, waits for them, and re-layouts: 8.94 us -> 11.3 us
    concatenate x0 -> x2, other arithmetic: none -> 9.89 us  [the longest x1 7.33 us: with_differences(): jnp.concatenate([real_part, real_part - imag_part, real_part + imag_part]...]
    ppermute x11, waiting for transfers between devices: 54.1 us -> 49.1 us  [exchange(): return lax.ppermute(value, axes, pairs)]
    pallas_call x1, Pallas kernels: 73.5 us -> 68.7 us  [all_pairs(): pl.pallas_call(pair_kernel, grid_spec=grid_spec, out_shape=jax.ShapeDtype...]
    sub x0 -> x1, other arithmetic: none -> 3.39 us  [with_differences(): real_part - imag_part]
    convert_element_type x2, other arithmetic: 3.17 us -> 0.66 us  [the longest x1 0.36 us: with_sums(): real_part = spectra[..., :NF].astype(jnp.float32)]
    unnamed x7 -> x9, local copies, waits for them, and re-layouts: 2.83 us -> 5.13 us
  transfers between devices with their start and end apart: 12 -> 12, of which waited for: 7 -> 5; matrix products, arithmetic and copies ran while one was open for 6% -> 7% of each run, Pallas kernels for 11% -> 10%
where the time goes in v8:
time: 192 us
  Pallas kernels  88.7 us (46%)
  waiting for transfers between devices  49.2 us (26%)
  other arithmetic  23.1 us (12%)
  starting transfers between devices  12.1 us (6%)
  local copies, waits for them, and re-layouts  11.3 us (6%)
  matrix products  3.76 us (2%)
  between operations  3.42 us (2%)
    pallas_call x1, Pallas kernels, all_pairs(): pl.pallas_call(pair_kernel, grid_spec=grid_spec, out_shape=jax.ShapeDtype...  68.7 us
    ppermute x11, waiting for transfers between devices, exchange(): return lax.ppermute(value, axes, pairs)  49.1 us
    pallas_call x1, Pallas kernels, forward_table(): pl.pallas_call(table_kernel, grid=(n_coarse // TABLE_Q,), in_specs=[pl.Bl...  20 us
    ppermute x11, starting transfers between devices, exchange(): return lax.ppermute(value, axes, pairs)  9.65 us
    concatenate x1, other arithmetic, with_differences(): jnp.concatenate([real_part, real_part - imag_part, real_part + imag_part]...  7.33 us
    unnamed x9, local copies, waits for them, and re-layouts  5.13 us
    sin x1, other arithmetic, forward_table(): high_sin = jnp.sin(high_angle).reshape(n_coarse, 1, NF)  4.17 us
  transfers between devices with their start and end apart: 12, of which 5 were waited for; matrix products, arithmetic and copies ran while one was open for 7% of the time, Pallas kernels for 10%

profile of v8, /device:TPU:14, one launch (start us, length us, event | category | flops | bytes accessed | tf_op | source)
XLA Modules:
  0.0 191.6 jit_solution(540205970656875350)
XLA Ops:
  0.0 2.3 %slice.29 = bf16[128,4352]{1,0:T(8,128)(2,1)} slice(bf16[128,7680]{1,0:T(8,128)(2,1)} %param.3), slice={[0:128], [0:4352]} | slice | bytes 2228224 | tf_op jit(solution)/shard_map/slice | solution.py:207
  2.4 2.5 %collective-permute-start = (bf16[128,4352]{1,0:T(8,128)(2,1)}, bf16[128,4352]{1,0:T(8,128)(2,1)S(1)}, u32[]{:S(2)}, u32[]{:S(2)}) collective-permute-start(bf16[128,4352]{1,0:T(8,128)(2,1)} %slice.29), channel_id=1, source_target_pairs={{16,0},{17,1},{18,2},{19,3},{20,4},{21,5},{22,6},{23,7},{24,8},{25... | collective-permute-start | bytes 3342344 | tf_op jit(solution)/shard_map/ppermute | solution.py:27
  4.9 1.6 fusion.22
  6.4 4.2 %fusion.29 = (f32[60,1,384]{2,1,0:T(1,128)}, f32[60,1,384]{2,1,0:T(1,128)}) fusion(s32[384]{0:T(512)S(1)} %iota_add_fusion, s32[60]{0:T(128)S(1)} %iota_multiply_fusion), kind=kLoop, calls=%fused_computation.56 | loop fusion | flops 207360 | bytes 186096 | tf_op jit(solution)/shard_map/sin | solution.py:58
  10.6 0.8 fusion.35
  11.4 1.3 fusion.36
  15.2 0.1 copy.6
  15.3 0.1 copy.7
  16.1 20.0 %shard_map.37 = bf16[7680,768]{1,0:T(8,128)(2,1)} custom-call(f32[60,1,384]{2,1,0:T(1,128)} %get-tuple-element.18.high_cos_ref, f32[60,1,384]{2,1,0:T(1,128)} %get-tuple-element.17.high_sin_ref, f32[128,384]{1,0:T(8,128)} %get-tuple-element.20.low_cos_ref, f32[128,384]{1,0:T(8,128)} %get-tuple-element.19.low_sin_ref), custom_call_target="tpu_custom_call" | custom-call | tf_op jit(solution)/shard_map/pallas_call | solution.py:60
  36.1 0.1 constant_dynamic-update-slice_fusion.1
  36.2 0.1 constant_dynamic-update-slice_fusion
  36.3 1.6 constant_dynamic-slice_fusion.3
  38.0 2.5 %copy-done.1 = bf16[7680,768]{1,0:T(8,128)(2,1)S(1)} copy-done((bf16[7680,768]{1,0:T(8,128)(2,1)S(1)}, bf16[7680,768]{1,0:T(8,128)(2,1)}, u32[]{:S(2)}) %copy-start.1) | copy-done | bytes 11796504
  40.4 3.2 %fusion = f32[256,768]{1,0:T(8,128)S(1)} fusion(bf16[7680,768]{1,0:T(8,128)(2,1)S(1)} %copy-done.1, bf16[128,7680]{1,0:T(8,128)(2,1)S(1)} %get-tuple-element.8, bf16[128,7680]{1,0:T(8,128)(2,1)S(1)} %get-tuple-element.7), kind=kOutput, calls=%fused_computation.2 | convolution fusion | flops 3027763200 | bytes 16515072 | tf_op jit(solution)/shard_map/dot_general | solution.py:216
  43.6 0.1 fusion.27
  43.8 0.6 fusion.6
  44.4 0.1 fusion.7
  44.5 1.3 collective-permute-start.8
  45.8 0.1 collective-permute-start.5
  45.9 2.1 %collective-permute-start.1 = (bf16[2,64,768]{2,1,0:T(8,128)(2,1)S(1)}, bf16[2,64,768]{2,1,0:T(8,128)(2,1)S(1)}, u32[]{:S(2)}, u32[]{:S(2)}) collective-permute-start(bf16[2,64,768]{2,1,0:T(8,128)(2,1)S(1)} %get-tuple-element.14), channel_id=1, source_target_pairs={{0,16},{16,0},{1,17},{17,1},{2,18},{18,2},{3,19},{19,3},{4,20},{20... | collective-permute-start | bytes 589832 | tf_op jit(solution)/shard_map/ppermute | solution.py:186
  48.0 1.9 %multiply_convert_fusion.1 = (bf16[384,256]{1,0:T(8,128)(2,1)S(1)}, bf16[384,256]{1,0:T(8,128)(2,1)S(1)}) fusion(s32[256]{0:T(256)S(1)} %and_select_fusion.1, s32[384]{0:T(512)S(1)} %iota_add_fusion), kind=kLoop, calls=%fused_computation.34 | loop fusion | flops 1376256 | bytes 395776 | tf_op jit(solution)/shard_map/convert
  49.9 2.4 %collective-permute-start.6 = (bf16[2,128,768]{2,1,0:T(8,128)(2,1)S(1)}, bf16[2,128,768]{2,1,0:T(8,128)(2,1)S(1)}, u32[]{:S(2)}, u32[]{:S(2)}) collective-permute-start(bf16[2,128,768]{2,1,0:T(8,128)(2,1)S(1)} %fusion.7), channel_id=1, source_target_pairs={{4,0},{8,4},{12,8},{5,1},{9,5},{13,9},{6,2},{10,6},{14,10},{7,3},{... | collective-permute-start | bytes 1179656 | tf_op jit(solution)/shard_map/ppermute | solution.py:186
  52.3 0.7 collective-permute-start.10
  52.9 7.7 %collective-permute-done.1 = bf16[2,64,768]{2,1,0:T(8,128)(2,1)S(1)} collective-permute-done((bf16[2,64,768]{2,1,0:T(8,128)(2,1)S(1)}, bf16[2,64,768]{2,1,0:T(8,128)(2,1)S(1)}, u32[]{:S(2)}, u32[]{:S(2)}) %collective-permute-start.1) | collective-permute-done | bytes 196640 | tf_op jit(solution)/shard_map/ppermute | solution.py:186
  60.6 0.1 fusion.34
  60.7 0.6 collective-permute-start.3
  61.3 0.5 collective-permute-start.4
  61.8 0.1 pad_add_fusion.pairs_ref
  61.9 0.1 maximum_bitcast_fusion
  62.0 20.2 %collective-permute-done.6 = bf16[2,128,768]{2,1,0:T(8,128)(2,1)S(1)} collective-permute-done((bf16[2,128,768]{2,1,0:T(8,128)(2,1)S(1)}, bf16[2,128,768]{2,1,0:T(8,128)(2,1)S(1)}, u32[]{:S(2)}, u32[]{:S(2)}) %collective-permute-start.6) | collective-permute-done | bytes 393248 | tf_op jit(solution)/shard_map/ppermute | solution.py:186
  82.2 2.0 %collective-permute-start.7 = (bf16[2,128,768]{2,1,0:T(8,128)(2,1)S(1)}, bf16[2,128,768]{2,1,0:T(8,128)(2,1)S(1)}, u32[]{:S(2)}, u32[]{:S(2)}) collective-permute-start(bf16[2,128,768]{2,1,0:T(8,128)(2,1)S(1)} %collective-permute-done.6), channel_id=1, source_target_pairs={{0,16},{16,0},{1,17},{17,1},{2,18},{18,2},{3,19},{19,3},{4,20},{20... | collective-permute-start | bytes 1179656 | tf_op jit(solution)/shard_map/ppermute | solution.py:186
  84.2 0.1 collective-permute-start.11
  84.3 0.2 pad_maximum_fusion.3
  84.5 0.2 fusion.16
  84.7 0.4 slice_convert_fusion.2
  85.0 2.6 %pad_maximum_fusion.1.row_ref = f32[4,4,64,1152]{3,2,1,0:T(8,128)} fusion(f32[4,4,64,384]{3,2,1,0:T(8,128)S(1)} %fusion.16, f32[4,4,64,384]{3,2,1,0:T(8,128)S(1)} %get-tuple-element.10, f32[4,4,64,384]{3,2,1,0:T(8,128)S(1)} %get-tuple-element.9), kind=kLoop, calls=%fused_computation.1 | loop fusion | flops 2359296 | bytes 9437184 | tf_op jit(solution)/shard_map/concatenate | solution.py:136
  87.6 6.5 %collective-permute-done.9 = bf16[2,128,768]{2,1,0:T(8,128)(2,1)S(1)} collective-permute-done((bf16[2,128,768]{2,1,0:T(8,128)(2,1)S(1)}, bf16[2,128,768]{2,1,0:T(8,128)(2,1)S(1)}, u32[]{:S(2)}, u32[]{:S(2)}) %collective-permute-start.9) | collective-permute-done | bytes 393248 | tf_op jit(solution)/shard_map/ppermute | solution.py:186
  94.1 0.1 maximum_bitcast_fusion.2
  94.2 8.4 %collective-permute-done.7 = bf16[2,128,768]{2,1,0:T(8,128)(2,1)S(1)} collective-permute-done((bf16[2,128,768]{2,1,0:T(8,128)(2,1)S(1)}, bf16[2,128,768]{2,1,0:T(8,128)(2,1)S(1)}, u32[]{:S(2)}, u32[]{:S(2)}) %collective-permute-start.7) | collective-permute-done | bytes 393248 | tf_op jit(solution)/shard_map/ppermute | solution.py:186
  102.6 0.1 maximum_bitcast_fusion.1
  102.6 6.4 %collective-permute-done.11 = bf16[2,128,768]{2,1,0:T(8,128)(2,1)S(1)} collective-permute-done((bf16[2,128,768]{2,1,0:T(8,128)(2,1)S(1)}, bf16[2,128,768]{2,1,0:T(8,128)(2,1)S(1)}, u32[]{:S(2)}, u32[]{:S(2)}) %collective-permute-start.11) | collective-permute-done | bytes 393248 | tf_op jit(solution)/shard_map/ppermute | solution.py:186
  109.0 0.1 maximum_bitcast_fusion.3
  109.1 0.4 pad_maximum_fusion.2
  109.5 0.3 slice_convert_fusion
  109.9 3.4 %convert_subtract_fusion = (f32[4,4,128,384]{3,2,1,0:T(8,128)}, f32[4,4,128,384]{3,2,1,0:T(8,128)}) fusion(bf16[4,4,128,768]{3,2,1,0:T(8,128)(2,1)S(1)} %pad_maximum_fusion.2), kind=kLoop, calls=%fused_computation.7 | loop fusion | flops 3145728 | bytes 9437184 | tf_op jit(solution)/shard_map/sub | solution.py:142
  113.2 7.3 %pad_maximum_fusion.col_ref = f32[4,4,128,1152]{3,2,1,0:T(8,128)} fusion(f32[4,4,128,384]{3,2,1,0:T(8,128)} %get-tuple-element.6, f32[4,4,128,384]{3,2,1,0:T(8,128)} %get-tuple-element.5, f32[4,4,128,384]{3,2,1,0:T(8,128)S(1)} %slice_convert_fusion), kind=kLoop, calls=%fused_computation | loop fusion | flops 4718592 | bytes 18874368 | tf_op jit(solution)/shard_map/concatenate | solution.py:142
  120.6 2.3 %copy-done = f32[4,4,64,1152]{3,2,1,0:T(8,128)S(1)} copy-done((f32[4,4,64,1152]{3,2,1,0:T(8,128)S(1)}, f32[4,4,64,1152]{3,2,1,0:T(8,128)}, u32[]{:S(2)}) %copy-start) | copy-done | bytes 4718616
  122.9 68.7 %shard_map.38 = bf16[4,64,128,256]{3,2,1,0:T(8,128)(2,1)} custom-call(s32[4,2]{1,0:T(4,128)S(1)} %pad_add_fusion.pairs_ref, f32[4,4,64,1152]{3,2,1,0:T(8,128)S(1)} %copy-done, f32[4,4,128,1152]{3,2,1,0:T(8,128)} %pad_maximum_fusion.col_ref, bf16[768,256]{1,0:T(8,128)(2,1)S(1)} %pad_maximum_fusion.5.lags_ref), custom_call_target="tpu_custom_call" | custom-call | flops 13287555072 | bytes 26214400 | tf_op jit(solution)/shard_map/pallas_call | solution.py:161
  (20 shorter events, 0.1 us)
Async XLA Ops:
  2.4 33.9 %collective-permute-start = (bf16[128,4352]{1,0:T(8,128)(2,1)}, bf16[128,4352]{1,0:T(8,128)(2,1)S(1)}, u32[]{:S(2)}, u32[]{:S(2)}) collective-permute-start(bf16[128,4352]{1,0:T(8,128)(2,1)} %slice.29), channel_id=1, source_target_pairs={{16,0},{17,1},{18,2},{19,3},{20,4},{21,5},{22,6},{23,7},{24,8},{25... | collective-permute-start | bytes 3342344 | tf_op jit(solution)/shard_map/ppermute | solution.py:27
  16.1 20.0 %copy-start.2 = (bf16[128,7680]{1,0:T(8,128)(2,1)S(1)}, bf16[128,7680]{1,0:T(8,128)(2,1)}, u32[]{:S(2)}) copy-start(bf16[128,7680]{1,0:T(8,128)(2,1)} %param.3) | copy-start | bytes 5898244
  36.1 4.4 %copy-start.1 = (bf16[7680,768]{1,0:T(8,128)(2,1)S(1)}, bf16[7680,768]{1,0:T(8,128)(2,1)}, u32[]{:S(2)}) copy-start(bf16[7680,768]{1,0:T(8,128)(2,1)} %shard_map.37) | copy-start | bytes 35389444
  44.5 16.8 %collective-permute-start.8 = (bf16[2,128,768]{2,1,0:T(8,128)(2,1)S(1)}, bf16[2,128,768]{2,1,0:T(8,128)(2,1)S(1)}, u32[]{:S(2)}, u32[]{:S(2)}) collective-permute-start(bf16[2,128,768]{2,1,0:T(8,128)(2,1)S(1)} %fusion.7), channel_id=1, source_target_pairs={{8,0},{12,4},{9,1},{13,5},{10,2},{14,6},{11,3},{15,7},{24,16},{28,... | collective-permute-start | bytes 1179656 | tf_op jit(solution)/shard_map/ppermute | solution.py:186
  45.8 15.5 %collective-permute-start.5 = (bf16[2,128,768]{2,1,0:T(8,128)(2,1)S(1)}, bf16[2,128,768]{2,1,0:T(8,128)(2,1)S(1)}, u32[]{:S(2)}, u32[]{:S(2)}) collective-permute-start(bf16[2,128,768]{2,1,0:T(8,128)(2,1)S(1)} %fusion.7), channel_id=1, source_target_pairs={{0,16},{16,0},{1,17},{17,1},{2,18},{18,2},{3,19},{19,3},{4,20},{20... | collective-permute-start | bytes 1179656 | tf_op jit(solution)/shard_map/ppermute | solution.py:186
  45.9 14.7 %collective-permute-start.1 = (bf16[2,64,768]{2,1,0:T(8,128)(2,1)S(1)}, bf16[2,64,768]{2,1,0:T(8,128)(2,1)S(1)}, u32[]{:S(2)}, u32[]{:S(2)}) collective-permute-start(bf16[2,64,768]{2,1,0:T(8,128)(2,1)S(1)} %get-tuple-element.14), channel_id=1, source_target_pairs={{0,16},{16,0},{1,17},{17,1},{2,18},{18,2},{3,19},{19,3},{4,20},{20... | collective-permute-start | bytes 589832 | tf_op jit(solution)/shard_map/ppermute | solution.py:186
  49.9 32.3 %collective-permute-start.6 = (bf16[2,128,768]{2,1,0:T(8,128)(2,1)S(1)}, bf16[2,128,768]{2,1,0:T(8,128)(2,1)S(1)}, u32[]{:S(2)}, u32[]{:S(2)}) collective-permute-start(bf16[2,128,768]{2,1,0:T(8,128)(2,1)S(1)} %fusion.7), channel_id=1, source_target_pairs={{4,0},{8,4},{12,8},{5,1},{9,5},{13,9},{6,2},{10,6},{14,10},{7,3},{... | collective-permute-start | bytes 1179656 | tf_op jit(solution)/shard_map/ppermute | solution.py:186
  52.3 29.9 %collective-permute-start.10 = (bf16[2,128,768]{2,1,0:T(8,128)(2,1)S(1)}, bf16[2,128,768]{2,1,0:T(8,128)(2,1)S(1)}, u32[]{:S(2)}, u32[]{:S(2)}) collective-permute-start(bf16[2,128,768]{2,1,0:T(8,128)(2,1)S(1)} %fusion.7), channel_id=1, source_target_pairs={{12,0},{13,1},{14,2},{15,3},{28,16},{29,17},{30,18},{31,19}} | collective-permute-start | bytes 1179656 | tf_op jit(solution)/shard_map/ppermute | solution.py:186
  60.7 23.5 %collective-permute-start.3 = (bf16[4,64,768]{2,1,0:T(8,128)(2,1)S(1)}, bf16[4,64,768]{2,1,0:T(8,128)(2,1)S(1)}, u32[]{:S(2)}, u32[]{:S(2)}) collective-permute-start(bf16[4,64,768]{2,1,0:T(8,128)(2,1)S(1)} %get-tuple-element.12), channel_id=1, source_target_pairs={{0,2},{1,3},{2,0},{3,1},{4,6},{5,7},{6,4},{7,5},{8,10},{9,11},{10,... | collective-permute-start | bytes 1179656 | tf_op jit(solution)/shard_map/ppermute | solution.py:186
  61.2 23.0 %collective-permute-start.2 = (bf16[4,64,768]{2,1,0:T(8,128)(2,1)S(1)}, bf16[4,64,768]{2,1,0:T(8,128)(2,1)S(1)}, u32[]{:S(2)}, u32[]{:S(2)}) collective-permute-start(bf16[4,64,768]{2,1,0:T(8,128)(2,1)S(1)} %get-tuple-element.12), channel_id=1, source_target_pairs={{0,3},{1,0},{2,1},{3,2},{4,7},{5,4},{6,5},{7,6},{8,11},{9,8},{10,9... | collective-permute-start | bytes 1179656 | tf_op jit(solution)/shard_map/ppermute | solution.py:186
  61.3 23.0 %collective-permute-start.4 = (bf16[4,64,768]{2,1,0:T(8,128)(2,1)S(1)}, bf16[4,64,768]{2,1,0:T(8,128)(2,1)S(1)}, u32[]{:S(2)}, u32[]{:S(2)}) collective-permute-start(bf16[4,64,768]{2,1,0:T(8,128)(2,1)S(1)} %get-tuple-element.12), channel_id=1, source_target_pairs={{0,1},{1,2},{2,3},{3,0},{4,5},{5,6},{6,7},{7,4},{8,9},{9,10},{10,1... | collective-permute-start | bytes 1179656 | tf_op jit(solution)/shard_map/ppermute | solution.py:186
  82.1 12.0 %collective-permute-start.9 = (bf16[2,128,768]{2,1,0:T(8,128)(2,1)S(1)}, bf16[2,128,768]{2,1,0:T(8,128)(2,1)S(1)}, u32[]{:S(2)}, u32[]{:S(2)}) collective-permute-start(bf16[2,128,768]{2,1,0:T(8,128)(2,1)S(1)} %collective-permute-done.8), channel_id=1, source_target_pairs={{0,16},{16,0},{1,17},{17,1},{2,18},{18,2},{3,19},{19,3},{4,20},{20... | collective-permute-start | bytes 1179656 | tf_op jit(solution)/shard_map/ppermute | solution.py:186
  82.2 20.4 %collective-permute-start.7 = (bf16[2,128,768]{2,1,0:T(8,128)(2,1)S(1)}, bf16[2,128,768]{2,1,0:T(8,128)(2,1)S(1)}, u32[]{:S(2)}, u32[]{:S(2)}) collective-permute-start(bf16[2,128,768]{2,1,0:T(8,128)(2,1)S(1)} %collective-permute-done.6), channel_id=1, source_target_pairs={{0,16},{16,0},{1,17},{17,1},{2,18},{18,2},{3,19},{19,3},{4,20},{20... | collective-permute-start | bytes 1179656 | tf_op jit(solution)/shard_map/ppermute | solution.py:186
  84.2 24.8 %collective-permute-start.11 = (bf16[2,128,768]{2,1,0:T(8,128)(2,1)S(1)}, bf16[2,128,768]{2,1,0:T(8,128)(2,1)S(1)}, u32[]{:S(2)}, u32[]{:S(2)}) collective-permute-start(bf16[2,128,768]{2,1,0:T(8,128)(2,1)S(1)} %collective-permute-done.10), channel_id=1, source_target_pairs={{0,16},{16,0},{1,17},{17,1},{2,18},{18,2},{3,19},{19,3},{4,20},{20... | collective-permute-start | bytes 1179656 | tf_op jit(solution)/shard_map/ppermute | solution.py:186
  120.6 2.3 %copy-start = (f32[4,4,64,1152]{3,2,1,0:T(8,128)S(1)}, f32[4,4,64,1152]{3,2,1,0:T(8,128)}, u32[]{:S(2)}) copy-start(f32[4,4,64,1152]{3,2,1,0:T(8,128)} %pad_maximum_fusion.1.row_ref) | copy-start | bytes 14155780

commit v9 on v6

--- a/solution.py
+++ b/solution.py
@@ -101,9 +101,25 @@
 F_CHUNK = 128
 
 
-def pair_kernel(pairs_ref, row_ref, col_ref, lags_ref, out_ref, cross_ref):
+def pair_kernel(pairs_ref, row_ref, col_ref, lags_ref, out_ref, cross_ref, row32_ref, col32_ref):
     windows = row_ref.shape[1]
     cols = col_ref.shape[2]
+
+    @pl.when(pl.program_id(1) == 0)
+    def _():
+        for w in range(windows):
+            col_real = col_ref[0, w, :, :NF].astype(jnp.float32)
+            col_imag = col_ref[0, w, :, NF:].astype(jnp.float32)
+            col32_ref[w, :, :NF] = col_real
+            col32_ref[w, :, NF : 2 * NF] = col_real - col_imag
+            col32_ref[w, :, 2 * NF :] = col_real + col_imag
+
+    for w in range(windows):
+        row_real = row_ref[0, w, :, :NF].astype(jnp.float32)
+        row_imag = row_ref[0, w, :, NF:].astype(jnp.float32)
+        row32_ref[w, :, :NF] = row_real
+        row32_ref[w, :, NF : 2 * NF] = row_imag
+        row32_ref[w, :, 2 * NF :] = row_real + row_imag
 
     for i in range(row_ref.shape[2]):
         for jc in range(cols // J_CHUNK):
@@ -111,15 +127,19 @@
             for fc in range(NF // F_CHUNK):
                 fr = pl.ds(fc * F_CHUNK, F_CHUNK)
                 fi = pl.ds(NF + fc * F_CHUNK, F_CHUNK)
+                fs = pl.ds(2 * NF + fc * F_CHUNK, F_CHUNK)
                 acc_re = jnp.zeros((J_CHUNK, F_CHUNK), jnp.float32)
                 acc_im = jnp.zeros((J_CHUNK, F_CHUNK), jnp.float32)
                 for w in range(windows):
-                    xr = row_ref[0, w, i : i + 1, fr]
-                    xi = row_ref[0, w, i : i + 1, fi]
-                    yr = col_ref[0, w, js, fr]
-                    yi = col_ref[0, w, js, fi]
-                    acc_re = acc_re + xr * yr + xi * yi
-                    acc_im = acc_im + xi * yr - xr * yi
+                    xr = row32_ref[w, i : i + 1, fr]
+                    xi = row32_ref[w, i : i + 1, fi]
+                    xs = row32_ref[w, i : i + 1, fs]
+                    yr = col32_ref[w, js, fr]
+                    yd = col32_ref[w, js, fi]
+                    ys = col32_ref[w, js, fs]
+                    both = yr * xs
+                    acc_re = acc_re + (both - xi * yd)
+                    acc_im = acc_im + (both - xr * ys)
                 rows = pl.ds(i * cols + jc * J_CHUNK, J_CHUNK)
                 cross_ref[rows, fr] = acc_re.astype(jnp.bfloat16)
                 cross_ref[rows, fi] = acc_im.astype(jnp.bfloat16)
@@ -140,7 +160,11 @@
             pl.BlockSpec((2 * NF, LAGS), lambda p, t, pr: (0, 0)),
         ],
         out_specs=pl.BlockSpec((1, ROW_TILE, cols, LAGS), lambda p, t, pr: (p, t, 0, 0)),
-        scratch_shapes=[pltpu.VMEM((ROW_TILE * cols, 2 * NF), jnp.bfloat16)],
+        scratch_shapes=[
+            pltpu.VMEM((ROW_TILE * cols, 2 * NF), jnp.bfloat16),
+            pltpu.VMEM((windows, ROW_TILE, 3 * NF), jnp.float32),
+            pltpu.VMEM((windows, cols, 3 * NF), jnp.float32),
+        ],
     )
     flops = n_pairs * rows * cols * (2 * NF * windows * 4 + 2 * 2 * NF * LAGS)
     return pl.pallas_call(
@@ -154,7 +178,7 @@
         cost_estimate=pl.CostEstimate(
             flops=flops,
             transcendentals=0,
-            bytes_accessed=n_pairs * (rows + cols) * windows * 2 * NF * 4 + n_pairs * rows * cols * LAGS * 2,
+            bytes_accessed=n_pairs * (rows + cols) * windows * 2 * NF * 2 + n_pairs * rows * cols * LAGS * 2,
         ),
     )(pairs, row_all, col_all, lags)
 
@@ -231,7 +255,7 @@
     row_slot = (local_pairs[:, 0] - pcol_index + n_pcol) % n_pcol
     col_slot = jnp.clip(local_pairs[:, 1] - prow_index, 0, n_prow - 1)
     pairs = jnp.stack([row_slot, col_slot], axis=1).astype(jnp.int32)
-    result = all_pairs(pairs, row_all.astype(jnp.float32), col_all.astype(jnp.float32), lags)
+    result = all_pairs(pairs, row_all, col_all, lags)
     return result.reshape(1, 1, NP, half_rows, channels_here, LAGS)
 
 

time: 187 us -> 183 us (0.979)
  other arithmetic: 11.6 us -> 9.06 us
  Pallas kernels: 93.4 us -> 91.5 us
    convert_element_type x2 -> x0, other arithmetic: 3.17 us -> none  [the longest x1 2.9 us: on_device(): col_all.astype(jnp.float32)]
    pallas_call x1, Pallas kernels: 73.5 us -> 71.5 us  [all_pairs(): pl.pallas_call(pair_kernel, grid_spec=grid_spec, out_shape=jax.ShapeDtype...]
where the time goes in v9:
time: 183 us; the launch traced here: 182 us
  Pallas kernels  91.5 us (50%)
  waiting for transfers between devices  54.2 us (30%)
  starting transfers between devices  11.3 us (6%)
  other arithmetic  9.06 us (5%)
  local copies, waits for them, and re-layouts  8.94 us (5%)
  matrix products  3.76 us (2%)
  between operations  3.27 us (2%)
    pallas_call x1, Pallas kernels, all_pairs(): pl.pallas_call(pair_kernel, grid_spec=grid_spec, out_shape=jax.ShapeDtype...  71.5 us
    ppermute x11, waiting for transfers between devices, exchange(): return lax.ppermute(value, axes, pairs)  54.2 us
    pallas_call x1, Pallas kernels, forward_table(): pl.pallas_call(table_kernel, grid=(n_coarse // TABLE_Q,), in_specs=[pl.Bl...  20 us
    ppermute x11, starting transfers between devices, exchange(): return lax.ppermute(value, axes, pairs)  8.76 us
    sin x1, other arithmetic, forward_table(): high_sin = jnp.sin(high_angle).reshape(n_coarse, 1, NF)  4.2 us
  transfers between devices with their start and end apart: 12, of which 7 were waited for; matrix products, arithmetic and copies ran while one was open for 6% of the time, Pallas kernels for 11%

profile of v9, /device:TPU:14, one launch (start us, length us, event | category | flops | bytes accessed | tf_op | source)
XLA Modules:
  0.0 181.9 jit_solution(16610142941770528567)
XLA Ops:
  0.0 2.3 %slice.17 = bf16[128,4352]{1,0:T(8,128)(2,1)} slice(bf16[128,7680]{1,0:T(8,128)(2,1)} %param.3), slice={[0:128], [0:4352]} | slice | bytes 2228224 | tf_op jit(solution)/shard_map/slice | solution.py:216
  2.3 2.5 %collective-permute-start = (bf16[128,4352]{1,0:T(8,128)(2,1)}, bf16[128,4352]{1,0:T(8,128)(2,1)S(1)}, u32[]{:S(2)}, u32[]{:S(2)}) collective-permute-start(bf16[128,4352]{1,0:T(8,128)(2,1)} %slice.17), channel_id=1, source_target_pairs={{16,0},{17,1},{18,2},{19,3},{20,4},{21,5},{22,6},{23,7},{24,8},{25... | collective-permute-start | bytes 3342344 | tf_op jit(solution)/shard_map/ppermute | solution.py:27
  4.9 1.6 fusion.21
  6.4 4.2 %fusion.28 = (f32[60,1,384]{2,1,0:T(1,128)}, f32[60,1,384]{2,1,0:T(1,128)}) fusion(s32[384]{0:T(512)S(1)} %iota_add_fusion, s32[60]{0:T(128)S(1)} %iota_multiply_fusion), kind=kLoop, calls=%fused_computation.48 | loop fusion | flops 207360 | bytes 186096 | tf_op jit(solution)/shard_map/sin | solution.py:58
  10.6 0.8 fusion.34
  11.4 1.3 fusion.35
  15.1 0.1 copy.6
  15.2 0.1 copy.7
  15.9 0.0 copy-start.1
  15.9 20.0 %shard_map.37 = bf16[7680,768]{1,0:T(8,128)(2,1)} custom-call(f32[60,1,384]{2,1,0:T(1,128)} %get-tuple-element.14.high_cos_ref, f32[60,1,384]{2,1,0:T(1,128)} %get-tuple-element.13.high_sin_ref, f32[128,384]{1,0:T(8,128)} %get-tuple-element.16.low_cos_ref, f32[128,384]{1,0:T(8,128)} %get-tuple-element.15.low_sin_ref), custom_call_target="tpu_custom_call" | custom-call | tf_op jit(solution)/shard_map/pallas_call | solution.py:60
  36.0 0.0 copy-start
  36.0 0.1 constant_dynamic-update-slice_fusion.1
  36.1 0.1 constant_dynamic-update-slice_fusion
  36.2 1.6 constant_dynamic-slice_fusion.3
  37.8 2.5 %copy-done = bf16[7680,768]{1,0:T(8,128)(2,1)S(1)} copy-done((bf16[7680,768]{1,0:T(8,128)(2,1)S(1)}, bf16[7680,768]{1,0:T(8,128)(2,1)}, u32[]{:S(2)}) %copy-start) | copy-done | bytes 11796504
  40.3 3.2 %fusion = f32[256,768]{1,0:T(8,128)S(1)} fusion(bf16[7680,768]{1,0:T(8,128)(2,1)S(1)} %copy-done, bf16[128,7680]{1,0:T(8,128)(2,1)S(1)} %get-tuple-element.6, bf16[128,7680]{1,0:T(8,128)(2,1)S(1)} %get-tuple-element.5), kind=kOutput, calls=%fused_computation | convolution fusion | flops 3027763200 | bytes 16515072 | tf_op jit(solution)/shard_map/dot_general | solution.py:225
  43.5 0.1 fusion.26
  43.7 0.6 fusion.6
  44.2 0.1 fusion.7
  44.3 1.3 collective-permute-start.8
  45.6 2.4 %collective-permute-start.6 = (bf16[2,128,768]{2,1,0:T(8,128)(2,1)S(1)}, bf16[2,128,768]{2,1,0:T(8,128)(2,1)S(1)}, u32[]{:S(2)}, u32[]{:S(2)}) collective-permute-start(bf16[2,128,768]{2,1,0:T(8,128)(2,1)S(1)} %fusion.7), channel_id=1, source_target_pairs={{4,0},{8,4},{12,8},{5,1},{9,5},{13,9},{6,2},{10,6},{14,10},{7,3},{... | collective-permute-start | bytes 1179656 | tf_op jit(solution)/shard_map/ppermute | solution.py:195
  48.0 0.1 collective-permute-start.1
  48.1 2.0 %multiply_convert_fusion.1 = (bf16[384,256]{1,0:T(8,128)(2,1)S(1)}, bf16[384,256]{1,0:T(8,128)(2,1)S(1)}) fusion(s32[256]{0:T(256)S(1)} %and_select_fusion.1, s32[384]{0:T(512)S(1)} %iota_add_fusion), kind=kLoop, calls=%fused_computation.27 | loop fusion | flops 1376256 | bytes 395776 | tf_op jit(solution)/shard_map/convert
  50.1 2.1 %collective-permute-start.5 = (bf16[2,128,768]{2,1,0:T(8,128)(2,1)S(1)}, bf16[2,128,768]{2,1,0:T(8,128)(2,1)S(1)}, u32[]{:S(2)}, u32[]{:S(2)}) collective-permute-start(bf16[2,128,768]{2,1,0:T(8,128)(2,1)S(1)} %fusion.7), channel_id=1, source_target_pairs={{0,16},{16,0},{1,17},{17,1},{2,18},{18,2},{3,19},{19,3},{4,20},{20... | collective-permute-start | bytes 1179656 | tf_op jit(solution)/shard_map/ppermute | solution.py:195
  52.1 0.7 collective-permute-start.10
  52.8 3.1 %collective-permute-done.1 = bf16[2,64,768]{2,1,0:T(8,128)(2,1)S(1)} collective-permute-done((bf16[2,64,768]{2,1,0:T(8,128)(2,1)S(1)}, bf16[2,64,768]{2,1,0:T(8,128)(2,1)S(1)}, u32[]{:S(2)}, u32[]{:S(2)}) %collective-permute-start.1) | collective-permute-done | bytes 196640 | tf_op jit(solution)/shard_map/ppermute | solution.py:195
  55.9 0.1 fusion.33
  55.9 0.1 collective-permute-start.3
  56.1 3.0 %collective-permute-done.8 = bf16[2,128,768]{2,1,0:T(8,128)(2,1)S(1)} collective-permute-done((bf16[2,128,768]{2,1,0:T(8,128)(2,1)S(1)}, bf16[2,128,768]{2,1,0:T(8,128)(2,1)S(1)}, u32[]{:S(2)}, u32[]{:S(2)}) %collective-permute-start.8) | collective-permute-done | bytes 393248 | tf_op jit(solution)/shard_map/ppermute | solution.py:195
  59.1 0.0 collective-permute-start.2
  59.1 22.9 %collective-permute-done.6 = bf16[2,128,768]{2,1,0:T(8,128)(2,1)S(1)} collective-permute-done((bf16[2,128,768]{2,1,0:T(8,128)(2,1)S(1)}, bf16[2,128,768]{2,1,0:T(8,128)(2,1)S(1)}, u32[]{:S(2)}, u32[]{:S(2)}) %collective-permute-start.6) | collective-permute-done | bytes 393248 | tf_op jit(solution)/shard_map/ppermute | solution.py:195
  82.0 0.0 collective-permute-start.4
  82.0 0.1 collective-permute-start.9
  82.1 0.1 pad_add_fusion.pairs_ref
  82.2 2.0 %collective-permute-start.7 = (bf16[2,128,768]{2,1,0:T(8,128)(2,1)S(1)}, bf16[2,128,768]{2,1,0:T(8,128)(2,1)S(1)}, u32[]{:S(2)}, u32[]{:S(2)}) collective-permute-start(bf16[2,128,768]{2,1,0:T(8,128)(2,1)S(1)} %collective-permute-done.6), channel_id=1, source_target_pairs={{0,16},{16,0},{1,17},{17,1},{2,18},{18,2},{3,19},{19,3},{4,20},{20... | collective-permute-start | bytes 1179656 | tf_op jit(solution)/shard_map/ppermute | solution.py:195
  84.2 0.1 maximum_bitcast_fusion
  84.3 0.1 collective-permute-start.11
  84.4 0.0 collective-permute-done.2
  84.4 4.8 %collective-permute-done.4 = bf16[4,64,768]{2,1,0:T(8,128)(2,1)S(1)} collective-permute-done((bf16[4,64,768]{2,1,0:T(8,128)(2,1)S(1)}, bf16[4,64,768]{2,1,0:T(8,128)(2,1)S(1)}, u32[]{:S(2)}, u32[]{:S(2)}) %collective-permute-start.4) | collective-permute-done | bytes 393248 | tf_op jit(solution)/shard_map/ppermute | solution.py:195
  89.2 0.2 pad_maximum_fusion.1.row_ref
  89.4 4.7 %collective-permute-done.9 = bf16[2,128,768]{2,1,0:T(8,128)(2,1)S(1)} collective-permute-done((bf16[2,128,768]{2,1,0:T(8,128)(2,1)S(1)}, bf16[2,128,768]{2,1,0:T(8,128)(2,1)S(1)}, u32[]{:S(2)}, u32[]{:S(2)}) %collective-permute-start.9) | collective-permute-done | bytes 393248 | tf_op jit(solution)/shard_map/ppermute | solution.py:195
  94.1 0.1 maximum_bitcast_fusion.2
  94.1 8.4 %collective-permute-done.7 = bf16[2,128,768]{2,1,0:T(8,128)(2,1)S(1)} collective-permute-done((bf16[2,128,768]{2,1,0:T(8,128)(2,1)S(1)}, bf16[2,128,768]{2,1,0:T(8,128)(2,1)S(1)}, u32[]{:S(2)}, u32[]{:S(2)}) %collective-permute-start.7) | collective-permute-done | bytes 393248 | tf_op jit(solution)/shard_map/ppermute | solution.py:195
  102.5 0.1 maximum_bitcast_fusion.1
  102.6 7.3 %collective-permute-done.11 = bf16[2,128,768]{2,1,0:T(8,128)(2,1)S(1)} collective-permute-done((bf16[2,128,768]{2,1,0:T(8,128)(2,1)S(1)}, bf16[2,128,768]{2,1,0:T(8,128)(2,1)S(1)}, u32[]{:S(2)}, u32[]{:S(2)}) %collective-permute-start.11) | collective-permute-done | bytes 393248 | tf_op jit(solution)/shard_map/ppermute | solution.py:195
  109.9 0.1 maximum_bitcast_fusion.3
  110.0 0.4 pad_maximum_fusion.col_ref
  110.4 71.5 %shard_map.38 = bf16[4,64,128,256]{3,2,1,0:T(8,128)(2,1)} custom-call(s32[4,2]{1,0:T(4,128)S(1)} %pad_add_fusion.pairs_ref, bf16[4,4,64,768]{3,2,1,0:T(8,128)(2,1)S(1)} %pad_maximum_fusion.1.row_ref, bf16[4,4,128,768]{3,2,1,0:T(8,128)(2,1)S(1)} %pad_maximum_fusion.col_ref, bf16[768,256]{1,0:T(8,128)(2,1)S(1)} %pad_maximum_fusion.3.lags_ref), custom_call_target="tpu_custom_call" | custom-call | flops 13287555072 | bytes 21495808 | tf_op jit(solution)/shard_map/pallas_call | solution.py:170
  (12 shorter events, 0.1 us)
Async XLA Ops:
  2.3 33.8 %collective-permute-start = (bf16[128,4352]{1,0:T(8,128)(2,1)}, bf16[128,4352]{1,0:T(8,128)(2,1)S(1)}, u32[]{:S(2)}, u32[]{:S(2)}) collective-permute-start(bf16[128,4352]{1,0:T(8,128)(2,1)} %slice.17), channel_id=1, source_target_pairs={{16,0},{17,1},{18,2},{19,3},{20,4},{21,5},{22,6},{23,7},{24,8},{25... | collective-permute-start | bytes 3342344 | tf_op jit(solution)/shard_map/ppermute | solution.py:27
  15.9 20.0 %copy-start.1 = (bf16[128,7680]{1,0:T(8,128)(2,1)S(1)}, bf16[128,7680]{1,0:T(8,128)(2,1)}, u32[]{:S(2)}) copy-start(bf16[128,7680]{1,0:T(8,128)(2,1)} %param.3) | copy-start | bytes 5898244
  36.0 4.4 %copy-start = (bf16[7680,768]{1,0:T(8,128)(2,1)S(1)}, bf16[7680,768]{1,0:T(8,128)(2,1)}, u32[]{:S(2)}) copy-start(bf16[7680,768]{1,0:T(8,128)(2,1)} %shard_map.37) | copy-start | bytes 35389444
  44.3 14.8 %collective-permute-start.8 = (bf16[2,128,768]{2,1,0:T(8,128)(2,1)S(1)}, bf16[2,128,768]{2,1,0:T(8,128)(2,1)S(1)}, u32[]{:S(2)}, u32[]{:S(2)}) collective-permute-start(bf16[2,128,768]{2,1,0:T(8,128)(2,1)S(1)} %fusion.7), channel_id=1, source_target_pairs={{8,0},{12,4},{9,1},{13,5},{10,2},{14,6},{11,3},{15,7},{24,16},{28,... | collective-permute-start | bytes 1179656 | tf_op jit(solution)/shard_map/ppermute | solution.py:195
  45.6 36.3 %collective-permute-start.6 = (bf16[2,128,768]{2,1,0:T(8,128)(2,1)S(1)}, bf16[2,128,768]{2,1,0:T(8,128)(2,1)S(1)}, u32[]{:S(2)}, u32[]{:S(2)}) collective-permute-start(bf16[2,128,768]{2,1,0:T(8,128)(2,1)S(1)} %fusion.7), channel_id=1, source_target_pairs={{4,0},{8,4},{12,8},{5,1},{9,5},{13,9},{6,2},{10,6},{14,10},{7,3},{... | collective-permute-start | bytes 1179656 | tf_op jit(solution)/shard_map/ppermute | solution.py:195
  48.0 7.8 %collective-permute-start.1 = (bf16[2,64,768]{2,1,0:T(8,128)(2,1)S(1)}, bf16[2,64,768]{2,1,0:T(8,128)(2,1)S(1)}, u32[]{:S(2)}, u32[]{:S(2)}) collective-permute-start(bf16[2,64,768]{2,1,0:T(8,128)(2,1)S(1)} %get-tuple-element.10), channel_id=1, source_target_pairs={{0,16},{16,0},{1,17},{17,1},{2,18},{18,2},{3,19},{19,3},{4,20},{20... | collective-permute-start | bytes 589832 | tf_op jit(solution)/shard_map/ppermute | solution.py:195
  50.1 31.9 %collective-permute-start.5 = (bf16[2,128,768]{2,1,0:T(8,128)(2,1)S(1)}, bf16[2,128,768]{2,1,0:T(8,128)(2,1)S(1)}, u32[]{:S(2)}, u32[]{:S(2)}) collective-permute-start(bf16[2,128,768]{2,1,0:T(8,128)(2,1)S(1)} %fusion.7), channel_id=1, source_target_pairs={{0,16},{16,0},{1,17},{17,1},{2,18},{18,2},{3,19},{19,3},{4,20},{20... | collective-permute-start | bytes 1179656 | tf_op jit(solution)/shard_map/ppermute | solution.py:195
  52.1 30.0 %collective-permute-start.10 = (bf16[2,128,768]{2,1,0:T(8,128)(2,1)S(1)}, bf16[2,128,768]{2,1,0:T(8,128)(2,1)S(1)}, u32[]{:S(2)}, u32[]{:S(2)}) collective-permute-start(bf16[2,128,768]{2,1,0:T(8,128)(2,1)S(1)} %fusion.7), channel_id=1, source_target_pairs={{12,0},{13,1},{14,2},{15,3},{28,16},{29,17},{30,18},{31,19}} | collective-permute-start | bytes 1179656 | tf_op jit(solution)/shard_map/ppermute | solution.py:195
  55.9 28.3 %collective-permute-start.3 = (bf16[4,64,768]{2,1,0:T(8,128)(2,1)S(1)}, bf16[4,64,768]{2,1,0:T(8,128)(2,1)S(1)}, u32[]{:S(2)}, u32[]{:S(2)}) collective-permute-start(bf16[4,64,768]{2,1,0:T(8,128)(2,1)S(1)} %get-tuple-element.8), channel_id=1, source_target_pairs={{0,2},{1,3},{2,0},{3,1},{4,6},{5,7},{6,4},{7,5},{8,10},{9,11},{10,... | collective-permute-start | bytes 1179656 | tf_op jit(solution)/shard_map/ppermute | solution.py:195
  59.1 25.3 %collective-permute-start.2 = (bf16[4,64,768]{2,1,0:T(8,128)(2,1)S(1)}, bf16[4,64,768]{2,1,0:T(8,128)(2,1)S(1)}, u32[]{:S(2)}, u32[]{:S(2)}) collective-permute-start(bf16[4,64,768]{2,1,0:T(8,128)(2,1)S(1)} %get-tuple-element.8), channel_id=1, source_target_pairs={{0,3},{1,0},{2,1},{3,2},{4,7},{5,4},{6,5},{7,6},{8,11},{9,8},{10,9... | collective-permute-start | bytes 1179656 | tf_op jit(solution)/shard_map/ppermute | solution.py:195
  82.0 7.2 %collective-permute-start.4 = (bf16[4,64,768]{2,1,0:T(8,128)(2,1)S(1)}, bf16[4,64,768]{2,1,0:T(8,128)(2,1)S(1)}, u32[]{:S(2)}, u32[]{:S(2)}) collective-permute-start(bf16[4,64,768]{2,1,0:T(8,128)(2,1)S(1)} %get-tuple-element.8), channel_id=1, source_target_pairs={{0,1},{1,2},{2,3},{3,0},{4,5},{5,6},{6,7},{7,4},{8,9},{9,10},{10,1... | collective-permute-start | bytes 1179656 | tf_op jit(solution)/shard_map/ppermute | solution.py:195
  82.0 12.1 %collective-permute-start.9 = (bf16[2,128,768]{2,1,0:T(8,128)(2,1)S(1)}, bf16[2,128,768]{2,1,0:T(8,128)(2,1)S(1)}, u32[]{:S(2)}, u32[]{:S(2)}) collective-permute-start(bf16[2,128,768]{2,1,0:T(8,128)(2,1)S(1)} %collective-permute-done.8), channel_id=1, source_target_pairs={{0,16},{16,0},{1,17},{17,1},{2,18},{18,2},{3,19},{19,3},{4,20},{20... | collective-permute-start | bytes 1179656 | tf_op jit(solution)/shard_map/ppermute | solution.py:195
  82.2 20.3 %collective-permute-start.7 = (bf16[2,128,768]{2,1,0:T(8,128)(2,1)S(1)}, bf16[2,128,768]{2,1,0:T(8,128)(2,1)S(1)}, u32[]{:S(2)}, u32[]{:S(2)}) collective-permute-start(bf16[2,128,768]{2,1,0:T(8,128)(2,1)S(1)} %collective-permute-done.6), channel_id=1, source_target_pairs={{0,16},{16,0},{1,17},{17,1},{2,18},{18,2},{3,19},{19,3},{4,20},{20... | collective-permute-start | bytes 1179656 | tf_op jit(solution)/shard_map/ppermute | solution.py:195
  84.3 25.6 %collective-permute-start.11 = (bf16[2,128,768]{2,1,0:T(8,128)(2,1)S(1)}, bf16[2,128,768]{2,1,0:T(8,128)(2,1)S(1)}, u32[]{:S(2)}, u32[]{:S(2)}) collective-permute-start(bf16[2,128,768]{2,1,0:T(8,128)(2,1)S(1)} %collective-permute-done.10), channel_id=1, source_target_pairs={{0,16},{16,0},{1,17},{17,1},{2,18},{18,2},{3,19},{19,3},{4,20},{20... | collective-permute-start | bytes 1179656 | tf_op jit(solution)/shard_map/ppermute | solution.py:195

commit v10 on v9

--- a/solution.py
+++ b/solution.py
@@ -243,7 +243,9 @@
         if d == 0:
             near = whitened
         else:
-            near = exchange(whitened, ("prow",), (n_prow,), lambda s, d=d: (s[0] - d,) if s[0] - d >= 0 else None)
+            near = exchange(
+                near, ("prow",), (n_prow,), lambda s, d=d: (s[0] - 1,) if 1 <= s[0] <= n_prow - d else None
+            )
         per_tm = [near]
         for e in range(1, n_tm):
             per_tm.append(exchange(near, ("tm",), (n_tm,), lambda s, e=e: ((s[0] - e) % n_tm,)))

time: 183 us -> 172 us (0.940)
  waiting for transfers between devices: 54.2 us -> 39.1 us
  starting transfers between devices: 11.3 us -> 14.8 us
    ppermute x11, waiting for transfers between devices: 54.2 us -> 39.1 us  [exchange(): return lax.ppermute(value, axes, pairs)]
    ppermute x11, starting transfers between devices: 8.76 us -> 12.3 us  [exchange(): return lax.ppermute(value, axes, pairs)]
  transfers between devices with their start and end apart: 12 -> 12, of which waited for: 7 -> 10; matrix products, arithmetic and copies ran while one was open for 6% -> 6% of each run, Pallas kernels for 11% -> 12%
where the time goes in v10:
time: 172 us; the launch traced here: 170 us
  Pallas kernels  91.5 us (53%)
  waiting for transfers between devices  39.1 us (23%)
  starting transfers between devices  14.8 us (9%)
  other arithmetic  9.06 us (5%)
  local copies, waits for them, and re-layouts  8.23 us (5%)
  matrix products  3.76 us (2%)
  between operations  3.43 us (2%)
    pallas_call x1, Pallas kernels, all_pairs(): pl.pallas_call(pair_kernel, grid_spec=grid_spec, out_shape=jax.ShapeDtype...  71.5 us
    ppermute x11, waiting for transfers between devices, exchange(): return lax.ppermute(value, axes, pairs)  39.1 us
    pallas_call x1, Pallas kernels, forward_table(): pl.pallas_call(table_kernel, grid=(n_coarse // TABLE_Q,), in_specs=[pl.Bl...  20 us
    ppermute x11, starting transfers between devices, exchange(): return lax.ppermute(value, axes, pairs)  12.3 us
    sin x1, other arithmetic, forward_table(): high_sin = jnp.sin(high_angle).reshape(n_coarse, 1, NF)  4.21 us
  transfers between devices with their start and end apart: 12, of which 10 were waited for; matrix products, arithmetic and copies ran while one was open for 6% of the time, Pallas kernels for 12%

profile of v10, /device:TPU:14, one launch (start us, length us, event | category | flops | bytes accessed | tf_op | source)
XLA Modules:
  0.0 169.9 jit_solution(8101508639951722230)
XLA Ops:
  0.0 2.3 %slice.17 = bf16[128,4352]{1,0:T(8,128)(2,1)} slice(bf16[128,7680]{1,0:T(8,128)(2,1)} %param.3), slice={[0:128], [0:4352]} | slice | bytes 2228224 | tf_op jit(solution)/shard_map/slice | solution.py:216
  2.3 2.5 %collective-permute-start = (bf16[128,4352]{1,0:T(8,128)(2,1)}, bf16[128,4352]{1,0:T(8,128)(2,1)S(1)}, u32[]{:S(2)}, u32[]{:S(2)}) collective-permute-start(bf16[128,4352]{1,0:T(8,128)(2,1)} %slice.17), channel_id=1, source_target_pairs={{16,0},{17,1},{18,2},{19,3},{20,4},{21,5},{22,6},{23,7},{24,8},{25... | collective-permute-start | bytes 3342344 | tf_op jit(solution)/shard_map/ppermute | solution.py:27
  4.9 1.3 fusion.35
  8.8 1.6 fusion.21
  11.0 4.2 %fusion.28 = (f32[60,1,384]{2,1,0:T(1,128)}, f32[60,1,384]{2,1,0:T(1,128)}) fusion(s32[384]{0:T(512)S(1)} %iota_add_fusion, s32[60]{0:T(128)S(1)} %iota_multiply_fusion), kind=kLoop, calls=%fused_computation.48 | loop fusion | flops 207360 | bytes 186096 | tf_op jit(solution)/shard_map/sin | solution.py:58
  15.2 20.0 %shard_map.37 = bf16[7680,768]{1,0:T(8,128)(2,1)} custom-call(f32[60,1,384]{2,1,0:T(1,128)} %get-tuple-element.14.high_cos_ref, f32[60,1,384]{2,1,0:T(1,128)} %get-tuple-element.13.high_sin_ref, f32[128,384]{1,0:T(8,128)} %get-tuple-element.16.low_cos_ref, f32[128,384]{1,0:T(8,128)} %get-tuple-element.15.low_sin_ref), custom_call_target="tpu_custom_call" | custom-call | tf_op jit(solution)/shard_map/pallas_call | solution.py:60
  35.2 0.1 constant_dynamic-update-slice_fusion.1
  35.3 0.0 collective-permute-done
  35.3 0.1 constant_dynamic-update-slice_fusion
  35.4 1.6 constant_dynamic-slice_fusion.3
  37.0 2.5 %copy-done = bf16[7680,768]{1,0:T(8,128)(2,1)S(1)} copy-done((bf16[7680,768]{1,0:T(8,128)(2,1)S(1)}, bf16[7680,768]{1,0:T(8,128)(2,1)}, u32[]{:S(2)}) %copy-start) | copy-done | bytes 11796504
  39.5 3.2 %fusion = f32[256,768]{1,0:T(8,128)S(1)} fusion(bf16[7680,768]{1,0:T(8,128)(2,1)S(1)} %copy-done, bf16[128,7680]{1,0:T(8,128)(2,1)S(1)} %get-tuple-element.6, bf16[128,7680]{1,0:T(8,128)(2,1)S(1)} %get-tuple-element.5), kind=kOutput, calls=%fused_computation | convolution fusion | flops 3027763200 | bytes 16515072 | tf_op jit(solution)/shard_map/dot_general | solution.py:225
  42.7 0.0 copy-start.2
  42.7 0.1 fusion.26
  42.9 0.6 fusion.6
  43.5 0.1 fusion.7
  43.5 2.4 %collective-permute-start.6 = (bf16[2,128,768]{2,1,0:T(8,128)(2,1)S(1)}, bf16[2,128,768]{2,1,0:T(8,128)(2,1)S(1)}, u32[]{:S(2)}, u32[]{:S(2)}) collective-permute-start(bf16[2,128,768]{2,1,0:T(8,128)(2,1)S(1)} %fusion.7), channel_id=1, source_target_pairs={{4,0},{8,4},{12,8},{5,1},{9,5},{13,9},{6,2},{10,6},{14,10},{7,3},{... | collective-permute-start | bytes 1179656 | tf_op jit(solution)/shard_map/ppermute | solution.py:195
  46.0 0.1 copy.6
  46.0 0.1 copy.7
  46.2 9.9 %collective-permute-done.6 = bf16[2,128,768]{2,1,0:T(8,128)(2,1)S(1)} collective-permute-done((bf16[2,128,768]{2,1,0:T(8,128)(2,1)S(1)}, bf16[2,128,768]{2,1,0:T(8,128)(2,1)S(1)}, u32[]{:S(2)}, u32[]{:S(2)}) %collective-permute-start.6) | collective-permute-done | bytes 393248 | tf_op jit(solution)/shard_map/ppermute | solution.py:195
  56.0 2.3 %collective-permute-start.8 = (bf16[2,128,768]{2,1,0:T(8,128)(2,1)S(1)}, bf16[2,128,768]{2,1,0:T(8,128)(2,1)S(1)}, u32[]{:S(2)}, u32[]{:S(2)}) collective-permute-start(bf16[2,128,768]{2,1,0:T(8,128)(2,1)S(1)} %collective-permute-done.6), channel_id=1, source_target_pairs={{4,0},{8,4},{5,1},{9,5},{6,2},{10,6},{7,3},{11,7},{20,16},{24,20},... | collective-permute-start | bytes 1179656 | tf_op jit(solution)/shard_map/ppermute | solution.py:195
  58.4 0.1 collective-permute-start.1
  58.5 2.0 %multiply_convert_fusion.1 = (bf16[384,256]{1,0:T(8,128)(2,1)S(1)}, bf16[384,256]{1,0:T(8,128)(2,1)S(1)}) fusion(s32[256]{0:T(256)S(1)} %and_select_fusion.1, s32[384]{0:T(512)S(1)} %iota_add_fusion), kind=kLoop, calls=%fused_computation.27 | loop fusion | flops 1376256 | bytes 395776 | tf_op jit(solution)/shard_map/convert
  60.5 2.1 %collective-permute-start.5 = (bf16[2,128,768]{2,1,0:T(8,128)(2,1)S(1)}, bf16[2,128,768]{2,1,0:T(8,128)(2,1)S(1)}, u32[]{:S(2)}, u32[]{:S(2)}) collective-permute-start(bf16[2,128,768]{2,1,0:T(8,128)(2,1)S(1)} %fusion.7), channel_id=1, source_target_pairs={{0,16},{16,0},{1,17},{17,1},{2,18},{18,2},{3,19},{19,3},{4,20},{20... | collective-permute-start | bytes 1179656 | tf_op jit(solution)/shard_map/ppermute | solution.py:195
  62.5 3.7 %collective-permute-done.1 = bf16[2,64,768]{2,1,0:T(8,128)(2,1)S(1)} collective-permute-done((bf16[2,64,768]{2,1,0:T(8,128)(2,1)S(1)}, bf16[2,64,768]{2,1,0:T(8,128)(2,1)S(1)}, u32[]{:S(2)}, u32[]{:S(2)}) %collective-permute-start.1) | collective-permute-done | bytes 196640 | tf_op jit(solution)/shard_map/ppermute | solution.py:195
  66.3 0.1 fusion.33
  66.3 0.4 collective-permute-start.3
  66.7 0.0 collective-permute-start.2
  66.7 0.5 collective-permute-start.4
  67.2 0.4 collective-permute-done.8
  67.6 2.4 %collective-permute-start.10 = (bf16[2,128,768]{2,1,0:T(8,128)(2,1)S(1)}, bf16[2,128,768]{2,1,0:T(8,128)(2,1)S(1)}, u32[]{:S(2)}, u32[]{:S(2)}) collective-permute-start(bf16[2,128,768]{2,1,0:T(8,128)(2,1)S(1)} %collective-permute-done.8), channel_id=1, source_target_pairs={{4,0},{5,1},{6,2},{7,3},{20,16},{21,17},{22,18},{23,19}} | collective-permute-start | bytes 1179656 | tf_op jit(solution)/shard_map/ppermute | solution.py:195
  70.0 2.1 %collective-permute-done.5 = bf16[2,128,768]{2,1,0:T(8,128)(2,1)S(1)} collective-permute-done((bf16[2,128,768]{2,1,0:T(8,128)(2,1)S(1)}, bf16[2,128,768]{2,1,0:T(8,128)(2,1)S(1)}, u32[]{:S(2)}, u32[]{:S(2)}) %collective-permute-start.5) | collective-permute-done | bytes 393248 | tf_op jit(solution)/shard_map/ppermute | solution.py:195
  72.1 0.4 collective-permute-start.7
  72.6 0.1 pad_add_fusion.pairs_ref
  72.7 5.5 %collective-permute-done.3 = bf16[4,64,768]{2,1,0:T(8,128)(2,1)S(1)} collective-permute-done((bf16[4,64,768]{2,1,0:T(8,128)(2,1)S(1)}, bf16[4,64,768]{2,1,0:T(8,128)(2,1)S(1)}, u32[]{:S(2)}, u32[]{:S(2)}) %collective-permute-start.3) | collective-permute-done | bytes 393248 | tf_op jit(solution)/shard_map/ppermute | solution.py:195
  78.2 0.1 maximum_bitcast_fusion
  78.3 0.3 collective-permute-done.10
  78.6 1.8 %collective-permute-start.11 = (bf16[2,128,768]{2,1,0:T(8,128)(2,1)S(1)}, bf16[2,128,768]{2,1,0:T(8,128)(2,1)S(1)}, u32[]{:S(2)}, u32[]{:S(2)}) collective-permute-start(bf16[2,128,768]{2,1,0:T(8,128)(2,1)S(1)} %collective-permute-done.10), channel_id=1, source_target_pairs={{0,16},{16,0},{1,17},{17,1},{2,18},{18,2},{3,19},{19,3},{4,20},{20... | collective-permute-start | bytes 1179656 | tf_op jit(solution)/shard_map/ppermute | solution.py:195
  80.4 0.1 collective-permute-done.2
  80.4 0.2 pad_maximum_fusion.1.row_ref
  80.6 3.5 %collective-permute-done.7 = bf16[2,128,768]{2,1,0:T(8,128)(2,1)S(1)} collective-permute-done((bf16[2,128,768]{2,1,0:T(8,128)(2,1)S(1)}, bf16[2,128,768]{2,1,0:T(8,128)(2,1)S(1)}, u32[]{:S(2)}, u32[]{:S(2)}) %collective-permute-start.7) | collective-permute-done | bytes 393248 | tf_op jit(solution)/shard_map/ppermute | solution.py:195
  84.1 0.1 maximum_bitcast_fusion.1
  84.2 8.4 %collective-permute-done.9 = bf16[2,128,768]{2,1,0:T(8,128)(2,1)S(1)} collective-permute-done((bf16[2,128,768]{2,1,0:T(8,128)(2,1)S(1)}, bf16[2,128,768]{2,1,0:T(8,128)(2,1)S(1)}, u32[]{:S(2)}, u32[]{:S(2)}) %collective-permute-start.9) | collective-permute-done | bytes 393248 | tf_op jit(solution)/shard_map/ppermute | solution.py:195
  92.5 0.1 maximum_bitcast_fusion.2
  92.6 5.2 %collective-permute-done.11 = bf16[2,128,768]{2,1,0:T(8,128)(2,1)S(1)} collective-permute-done((bf16[2,128,768]{2,1,0:T(8,128)(2,1)S(1)}, bf16[2,128,768]{2,1,0:T(8,128)(2,1)S(1)}, u32[]{:S(2)}, u32[]{:S(2)}) %collective-permute-start.11) | collective-permute-done | bytes 393248 | tf_op jit(solution)/shard_map/ppermute | solution.py:195
  97.8 0.1 maximum_bitcast_fusion.3
  97.9 0.4 pad_maximum_fusion.col_ref
  98.4 71.5 %shard_map.38 = bf16[4,64,128,256]{3,2,1,0:T(8,128)(2,1)} custom-call(s32[4,2]{1,0:T(4,128)S(1)} %pad_add_fusion.pairs_ref, bf16[4,4,64,768]{3,2,1,0:T(8,128)(2,1)S(1)} %pad_maximum_fusion.1.row_ref, bf16[4,4,128,768]{3,2,1,0:T(8,128)(2,1)S(1)} %pad_maximum_fusion.col_ref, bf16[768,256]{1,0:T(8,128)(2,1)S(1)} %pad_maximum_fusion.3.lags_ref), custom_call_target="tpu_custom_call" | custom-call | flops 13287555072 | bytes 21495808 | tf_op jit(solution)/shard_map/pallas_call | solution.py:170
  (14 shorter events, 0.1 us)
Async XLA Ops:
  2.3 33.0 %collective-permute-start = (bf16[128,4352]{1,0:T(8,128)(2,1)}, bf16[128,4352]{1,0:T(8,128)(2,1)S(1)}, u32[]{:S(2)}, u32[]{:S(2)}) collective-permute-start(bf16[128,4352]{1,0:T(8,128)(2,1)} %slice.17), channel_id=1, source_target_pairs={{16,0},{17,1},{18,2},{19,3},{20,4},{21,5},{22,6},{23,7},{24,8},{25... | collective-permute-start | bytes 3342344 | tf_op jit(solution)/shard_map/ppermute | solution.py:27
  15.2 20.0 %copy-start.1 = (bf16[128,7680]{1,0:T(8,128)(2,1)S(1)}, bf16[128,7680]{1,0:T(8,128)(2,1)}, u32[]{:S(2)}) copy-start(bf16[128,7680]{1,0:T(8,128)(2,1)} %param.3) | copy-start | bytes 5898244
  35.2 4.4 %copy-start = (bf16[7680,768]{1,0:T(8,128)(2,1)S(1)}, bf16[7680,768]{1,0:T(8,128)(2,1)}, u32[]{:S(2)}) copy-start(bf16[7680,768]{1,0:T(8,128)(2,1)} %shard_map.37) | copy-start | bytes 35389444
  42.7 3.2 %copy-start.2 = (s32[1,1,4,2]{2,3,1,0:T(2,128)S(1)}, s32[1,1,4,2]{2,3,1,0:T(2,128)}, u32[]{:S(2)}) copy-start(s32[1,1,4,2]{2,3,1,0:T(2,128)} %param.5) | copy-start | bytes 100
  43.5 12.5 %collective-permute-start.6 = (bf16[2,128,768]{2,1,0:T(8,128)(2,1)S(1)}, bf16[2,128,768]{2,1,0:T(8,128)(2,1)S(1)}, u32[]{:S(2)}, u32[]{:S(2)}) collective-permute-start(bf16[2,128,768]{2,1,0:T(8,128)(2,1)S(1)} %fusion.7), channel_id=1, source_target_pairs={{4,0},{8,4},{12,8},{5,1},{9,5},{13,9},{6,2},{10,6},{14,10},{7,3},{... | collective-permute-start | bytes 1179656 | tf_op jit(solution)/shard_map/ppermute | solution.py:195
  56.0 11.6 %collective-permute-start.8 = (bf16[2,128,768]{2,1,0:T(8,128)(2,1)S(1)}, bf16[2,128,768]{2,1,0:T(8,128)(2,1)S(1)}, u32[]{:S(2)}, u32[]{:S(2)}) collective-permute-start(bf16[2,128,768]{2,1,0:T(8,128)(2,1)S(1)} %collective-permute-done.6), channel_id=1, source_target_pairs={{4,0},{8,4},{5,1},{9,5},{6,2},{10,6},{7,3},{11,7},{20,16},{24,20},... | collective-permute-start | bytes 1179656 | tf_op jit(solution)/shard_map/ppermute | solution.py:195
  58.4 7.8 %collective-permute-start.1 = (bf16[2,64,768]{2,1,0:T(8,128)(2,1)S(1)}, bf16[2,64,768]{2,1,0:T(8,128)(2,1)S(1)}, u32[]{:S(2)}, u32[]{:S(2)}) collective-permute-start(bf16[2,64,768]{2,1,0:T(8,128)(2,1)S(1)} %get-tuple-element.10), channel_id=1, source_target_pairs={{0,16},{16,0},{1,17},{17,1},{2,18},{18,2},{3,19},{19,3},{4,20},{20... | collective-permute-start | bytes 589832 | tf_op jit(solution)/shard_map/ppermute | solution.py:195
  60.5 11.7 %collective-permute-start.5 = (bf16[2,128,768]{2,1,0:T(8,128)(2,1)S(1)}, bf16[2,128,768]{2,1,0:T(8,128)(2,1)S(1)}, u32[]{:S(2)}, u32[]{:S(2)}) collective-permute-start(bf16[2,128,768]{2,1,0:T(8,128)(2,1)S(1)} %fusion.7), channel_id=1, source_target_pairs={{0,16},{16,0},{1,17},{17,1},{2,18},{18,2},{3,19},{19,3},{4,20},{20... | collective-permute-start | bytes 1179656 | tf_op jit(solution)/shard_map/ppermute | solution.py:195
  66.3 11.9 %collective-permute-start.3 = (bf16[4,64,768]{2,1,0:T(8,128)(2,1)S(1)}, bf16[4,64,768]{2,1,0:T(8,128)(2,1)S(1)}, u32[]{:S(2)}, u32[]{:S(2)}) collective-permute-start(bf16[4,64,768]{2,1,0:T(8,128)(2,1)S(1)} %get-tuple-element.8), channel_id=1, source_target_pairs={{0,2},{1,3},{2,0},{3,1},{4,6},{5,7},{6,4},{7,5},{8,10},{9,11},{10,... | collective-permute-start | bytes 1179656 | tf_op jit(solution)/shard_map/ppermute | solution.py:195
  66.7 13.7 %collective-permute-start.2 = (bf16[4,64,768]{2,1,0:T(8,128)(2,1)S(1)}, bf16[4,64,768]{2,1,0:T(8,128)(2,1)S(1)}, u32[]{:S(2)}, u32[]{:S(2)}) collective-permute-start(bf16[4,64,768]{2,1,0:T(8,128)(2,1)S(1)} %get-tuple-element.8), channel_id=1, source_target_pairs={{0,3},{1,0},{2,1},{3,2},{4,7},{5,4},{6,5},{7,6},{8,11},{9,8},{10,9... | collective-permute-start | bytes 1179656 | tf_op jit(solution)/shard_map/ppermute | solution.py:195
  66.7 13.7 %collective-permute-start.4 = (bf16[4,64,768]{2,1,0:T(8,128)(2,1)S(1)}, bf16[4,64,768]{2,1,0:T(8,128)(2,1)S(1)}, u32[]{:S(2)}, u32[]{:S(2)}) collective-permute-start(bf16[4,64,768]{2,1,0:T(8,128)(2,1)S(1)} %get-tuple-element.8), channel_id=1, source_target_pairs={{0,1},{1,2},{2,3},{3,0},{4,5},{5,6},{6,7},{7,4},{8,9},{9,10},{10,1... | collective-permute-start | bytes 1179656 | tf_op jit(solution)/shard_map/ppermute | solution.py:195
  67.6 11.0 %collective-permute-start.10 = (bf16[2,128,768]{2,1,0:T(8,128)(2,1)S(1)}, bf16[2,128,768]{2,1,0:T(8,128)(2,1)S(1)}, u32[]{:S(2)}, u32[]{:S(2)}) collective-permute-start(bf16[2,128,768]{2,1,0:T(8,128)(2,1)S(1)} %collective-permute-done.8), channel_id=1, source_target_pairs={{4,0},{5,1},{6,2},{7,3},{20,16},{21,17},{22,18},{23,19}} | collective-permute-start | bytes 1179656 | tf_op jit(solution)/shard_map/ppermute | solution.py:195
  72.1 12.0 %collective-permute-start.7 = (bf16[2,128,768]{2,1,0:T(8,128)(2,1)S(1)}, bf16[2,128,768]{2,1,0:T(8,128)(2,1)S(1)}, u32[]{:S(2)}, u32[]{:S(2)}) collective-permute-start(bf16[2,128,768]{2,1,0:T(8,128)(2,1)S(1)} %collective-permute-done.6), channel_id=1, source_target_pairs={{0,16},{16,0},{1,17},{17,1},{2,18},{18,2},{3,19},{19,3},{4,20},{20... | collective-permute-start | bytes 1179656 | tf_op jit(solution)/shard_map/ppermute | solution.py:195
  78.2 14.4 %collective-permute-start.9 = (bf16[2,128,768]{2,1,0:T(8,128)(2,1)S(1)}, bf16[2,128,768]{2,1,0:T(8,128)(2,1)S(1)}, u32[]{:S(2)}, u32[]{:S(2)}) collective-permute-start(bf16[2,128,768]{2,1,0:T(8,128)(2,1)S(1)} %collective-permute-done.8), channel_id=1, source_target_pairs={{0,16},{16,0},{1,17},{17,1},{2,18},{18,2},{3,19},{19,3},{4,20},{20... | collective-permute-start | bytes 1179656 | tf_op jit(solution)/shard_map/ppermute | solution.py:195
  78.6 19.2 %collective-permute-start.11 = (bf16[2,128,768]{2,1,0:T(8,128)(2,1)S(1)}, bf16[2,128,768]{2,1,0:T(8,128)(2,1)S(1)}, u32[]{:S(2)}, u32[]{:S(2)}) collective-permute-start(bf16[2,128,768]{2,1,0:T(8,128)(2,1)S(1)} %collective-permute-done.10), channel_id=1, source_target_pairs={{0,16},{16,0},{1,17},{17,1},{2,18},{18,2},{3,19},{19,3},{4,20},{20... | collective-permute-start | bytes 1179656 | tf_op jit(solution)/shard_map/ppermute | solution.py:195

commit v11 on v10

--- a/solution.py
+++ b/solution.py
@@ -30,19 +30,19 @@
 TABLE_Q = 12
 
 
-def table_kernel(high_cos_ref, high_sin_ref, low_cos_ref, low_sin_ref, out_ref):
+def table_kernel(high_cos_ref, high_sin_ref, low_cos_ref, low_sin_ref, taper_ref, out_ref):
     coarse = low_cos_ref.shape[0]
-    lc = low_cos_ref[...]
-    ls = low_sin_ref[...]
     for qq in range(TABLE_Q):
-        hc = high_cos_ref[qq]
-        hs = high_sin_ref[qq]
-        first = (pl.program_id(0) * TABLE_Q + qq) * coarse
-        sample = (first + lax.broadcasted_iota(jnp.int32, (coarse, 1), 0)).astype(jnp.float32)
-        taper = 0.5 - 0.5 * jnp.cos(sample * (two_pi / WIN))
         rows = pl.ds(qq * coarse, coarse)
-        out_ref[rows, :NF] = (taper * (hc * lc - hs * ls)).astype(out_ref.dtype)
-        out_ref[rows, NF:] = (-(taper * (hs * lc + hc * ls))).astype(out_ref.dtype)
+        taper = taper_ref[rows, :]
+        for fc in range(NF // F_CHUNK):
+            lanes = pl.ds(fc * F_CHUNK, F_CHUNK)
+            hc = high_cos_ref[qq, :, lanes]
+            hs = high_sin_ref[qq, :, lanes]
+            lc = low_cos_ref[:, lanes]
+            ls = low_sin_ref[:, lanes]
+            out_ref[rows, lanes] = (taper * (hc * lc - hs * ls)).astype(out_ref.dtype)
+            out_ref[rows, pl.ds(NF + fc * F_CHUNK, F_CHUNK)] = (-(taper * (hs * lc + hc * ls))).astype(out_ref.dtype)
 
 
 def forward_table():
@@ -57,6 +57,9 @@
     high_cos = jnp.cos(high_angle).reshape(n_coarse, 1, NF)
     high_sin = jnp.sin(high_angle).reshape(n_coarse, 1, NF)
     low_cos, low_sin = jnp.cos(low_angle), jnp.sin(low_angle)
+    sample_idx = jnp.arange(WIN, dtype=jnp.int32)
+    taper_curve = 0.5 - 0.5 * jnp.cos(sample_idx.astype(jnp.float32) * (two_pi / WIN))
+    taper_lanes = jnp.broadcast_to(taper_curve[:, None], (WIN, F_CHUNK))
     return pl.pallas_call(
         table_kernel,
         grid=(n_coarse // TABLE_Q,),
@@ -65,10 +68,11 @@
             pl.BlockSpec((TABLE_Q, 1, NF), lambda q: (q, 0, 0)),
             pl.BlockSpec((coarse, NF), lambda q: (0, 0)),
             pl.BlockSpec((coarse, NF), lambda q: (0, 0)),
+            pl.BlockSpec((TABLE_Q * coarse, F_CHUNK), lambda q: (q, 0)),
         ],
         out_specs=pl.BlockSpec((TABLE_Q * coarse, 2 * NF), lambda q: (q, 0)),
         out_shape=jax.ShapeDtypeStruct((WIN, 2 * NF), jnp.bfloat16),
-    )(high_cos, high_sin, low_cos, low_sin)
+    )(high_cos, high_sin, low_cos, low_sin, taper_lanes)
 
 
 def lag_table(count):

time: 172 us -> 165 us (0.959)
  Pallas kernels: 91.5 us -> 80.6 us
  local copies, waits for them, and re-layouts: 8.23 us -> 12.6 us
    pallas_call x1, Pallas kernels: 20 us -> 9.11 us  [forward_table(): pl.pallas_call(table_kernel, grid=(n_coarse // TABLE_Q,), in_specs=[pl.Bl...]
    broadcast_in_dim x0 -> x1, local copies, waits for them, and re-layouts: none -> 4.43 us  [forward_table(): taper_lanes = jnp.broadcast_to(taper_curve[:, None], (WIN, F_CHUNK))]
  transfers between devices with their start and end apart: 12 -> 12, of which waited for: 10 -> 10; matrix products, arithmetic and copies ran while one was open for 6% -> 9% of each run, Pallas kernels for 12% -> 6%
where the time goes in v11:
time: 165 us; the launch traced here: 164 us
  Pallas kernels  80.6 us (49%)
  waiting for transfers between devices  39.1 us (24%)
  starting transfers between devices  15 us (9%)
  local copies, waits for them, and re-layouts  12.6 us (8%)
  other arithmetic  9.15 us (6%)
  matrix products  3.76 us (2%)
  between operations  3.43 us (2%)
    pallas_call x1, Pallas kernels, all_pairs(): pl.pallas_call(pair_kernel, grid_spec=grid_spec, out_shape=jax.ShapeDtype...  71.5 us
    ppermute x11, waiting for transfers between devices, exchange(): return lax.ppermute(value, axes, pairs)  39.1 us
    ppermute x11, starting transfers between devices, exchange(): return lax.ppermute(value, axes, pairs)  12.5 us
    pallas_call x1, Pallas kernels, forward_table(): pl.pallas_call(table_kernel, grid=(n_coarse // TABLE_Q,), in_specs=[pl.Bl...  9.11 us
    broadcast_in_dim x1, local copies, waits for them, and re-layouts, forward_table(): taper_lanes = jnp.broadcast_to(taper_curve[:, None], (WIN, F_CHUNK))  4.43 us
    sin x1, other arithmetic, forward_table(): high_sin = jnp.sin(high_angle).reshape(n_coarse, 1, NF)  4.15 us
  transfers between devices with their start and end apart: 12, of which 10 were waited for; matrix products, arithmetic and copies ran while one was open for 9% of the time, Pallas kernels for 6%

profile of v11, /device:TPU:14, one launch (start us, length us, event | category | flops | bytes accessed | tf_op | source)
XLA Modules:
  0.0 163.7 jit_solution(17703777793585458913)
XLA Ops:
  0.0 2.3 %slice.17 = bf16[128,4352]{1,0:T(8,128)(2,1)} slice(bf16[128,7680]{1,0:T(8,128)(2,1)} %param.3), slice={[0:128], [0:4352]} | slice | bytes 2228224 | tf_op jit(solution)/shard_map/slice | solution.py:220
  2.3 2.5 %collective-permute-start = (bf16[128,4352]{1,0:T(8,128)(2,1)}, bf16[128,4352]{1,0:T(8,128)(2,1)S(1)}, u32[]{:S(2)}, u32[]{:S(2)}) collective-permute-start(bf16[128,4352]{1,0:T(8,128)(2,1)} %slice.17), channel_id=1, source_target_pairs={{16,0},{17,1},{18,2},{19,3},{20,4},{21,5},{22,6},{23,7},{24,8},{25... | collective-permute-start | bytes 3342344 | tf_op jit(solution)/shard_map/ppermute | solution.py:27
  4.8 1.6 fusion.21
  6.4 4.2 %fusion.28 = (f32[60,1,384]{2,1,0:T(1,128)}, f32[60,1,384]{2,1,0:T(1,128)}) fusion(s32[384]{0:T(512)S(1)} %iota_add_fusion, s32[60]{0:T(128)S(1)} %iota_multiply_fusion), kind=kLoop, calls=%fused_computation.49 | loop fusion | flops 207360 | bytes 186096 | tf_op jit(solution)/shard_map/sin | solution.py:58
  10.6 1.3 fusion.35
  15.1 0.1 multiply_subtract_fusion
  15.2 4.4 %broadcast_in_dim.2.taper_ref = f32[7680,128]{1,0:T(8,128)} broadcast(f32[7680]{0:T(1024)S(1)} %multiply_subtract_fusion), dimensions={0} | broadcast | bytes 3962880 | tf_op jit(solution)/shard_map/broadcast_in_dim | solution.py:62
  19.7 9.1 %shard_map.37 = bf16[7680,768]{1,0:T(8,128)(2,1)} custom-call(f32[60,1,384]{2,1,0:T(1,128)} %get-tuple-element.14.high_cos_ref, f32[60,1,384]{2,1,0:T(1,128)} %get-tuple-element.13.high_sin_ref, f32[128,384]{1,0:T(8,128)} %get-tuple-element.16.low_cos_ref, f32[128,384]{1,0:T(8,128)} %get-tuple-element.15.low_sin_ref, f32[7680,128]{1,0:T(8,128)} %broadcast_in_dim.2.taper_ref), custom_call_target="tpu_custom_call" | custom-call | tf_op jit(solution)/shard_map/pallas_call | solution.py:63
  28.8 0.1 constant_dynamic-update-slice_fusion.1
  28.9 0.1 constant_dynamic-update-slice_fusion
  29.0 1.6 constant_dynamic-slice_fusion.3
  30.7 2.5 %copy-done = bf16[7680,768]{1,0:T(8,128)(2,1)S(1)} copy-done((bf16[7680,768]{1,0:T(8,128)(2,1)S(1)}, bf16[7680,768]{1,0:T(8,128)(2,1)}, u32[]{:S(2)}) %copy-start) | copy-done | bytes 11796504
  33.1 3.2 %fusion = f32[256,768]{1,0:T(8,128)S(1)} fusion(bf16[7680,768]{1,0:T(8,128)(2,1)S(1)} %copy-done, bf16[128,7680]{1,0:T(8,128)(2,1)S(1)} %get-tuple-element.6, bf16[128,7680]{1,0:T(8,128)(2,1)S(1)} %get-tuple-element.5), kind=kOutput, calls=%fused_computation | convolution fusion | flops 3027763200 | bytes 16515072 | tf_op jit(solution)/shard_map/dot_general | solution.py:229
  36.3 0.0 copy-start.2
  36.3 0.1 fusion.26
  36.5 0.6 fusion.6
  37.1 0.1 fusion.7
  37.2 2.4 %collective-permute-start.6 = (bf16[2,128,768]{2,1,0:T(8,128)(2,1)S(1)}, bf16[2,128,768]{2,1,0:T(8,128)(2,1)S(1)}, u32[]{:S(2)}, u32[]{:S(2)}) collective-permute-start(bf16[2,128,768]{2,1,0:T(8,128)(2,1)S(1)} %fusion.7), channel_id=1, source_target_pairs={{4,0},{8,4},{12,8},{5,1},{9,5},{13,9},{6,2},{10,6},{14,10},{7,3},{... | collective-permute-start | bytes 1179656 | tf_op jit(solution)/shard_map/ppermute | solution.py:199
  39.6 0.1 copy.6
  39.7 0.1 copy.7
  39.8 9.9 %collective-permute-done.6 = bf16[2,128,768]{2,1,0:T(8,128)(2,1)S(1)} collective-permute-done((bf16[2,128,768]{2,1,0:T(8,128)(2,1)S(1)}, bf16[2,128,768]{2,1,0:T(8,128)(2,1)S(1)}, u32[]{:S(2)}, u32[]{:S(2)}) %collective-permute-start.6) | collective-permute-done | bytes 393248 | tf_op jit(solution)/shard_map/ppermute | solution.py:199
  49.6 2.3 %collective-permute-start.8 = (bf16[2,128,768]{2,1,0:T(8,128)(2,1)S(1)}, bf16[2,128,768]{2,1,0:T(8,128)(2,1)S(1)}, u32[]{:S(2)}, u32[]{:S(2)}) collective-permute-start(bf16[2,128,768]{2,1,0:T(8,128)(2,1)S(1)} %collective-permute-done.6), channel_id=1, source_target_pairs={{4,0},{8,4},{5,1},{9,5},{6,2},{10,6},{7,3},{11,7},{20,16},{24,20},... | collective-permute-start | bytes 1179656 | tf_op jit(solution)/shard_map/ppermute | solution.py:199
  52.0 0.1 collective-permute-start.1
  52.1 2.0 %multiply_convert_fusion.1 = (bf16[384,256]{1,0:T(8,128)(2,1)S(1)}, bf16[384,256]{1,0:T(8,128)(2,1)S(1)}) fusion(s32[256]{0:T(256)S(1)} %and_select_fusion.1, s32[384]{0:T(512)S(1)} %iota_add_fusion), kind=kLoop, calls=%fused_computation.27 | loop fusion | flops 1376256 | bytes 395776 | tf_op jit(solution)/shard_map/convert
  54.1 2.1 %collective-permute-start.5 = (bf16[2,128,768]{2,1,0:T(8,128)(2,1)S(1)}, bf16[2,128,768]{2,1,0:T(8,128)(2,1)S(1)}, u32[]{:S(2)}, u32[]{:S(2)}) collective-permute-start(bf16[2,128,768]{2,1,0:T(8,128)(2,1)S(1)} %fusion.7), channel_id=1, source_target_pairs={{0,16},{16,0},{1,17},{17,1},{2,18},{18,2},{3,19},{19,3},{4,20},{20... | collective-permute-start | bytes 1179656 | tf_op jit(solution)/shard_map/ppermute | solution.py:199
  56.1 3.7 %collective-permute-done.1 = bf16[2,64,768]{2,1,0:T(8,128)(2,1)S(1)} collective-permute-done((bf16[2,64,768]{2,1,0:T(8,128)(2,1)S(1)}, bf16[2,64,768]{2,1,0:T(8,128)(2,1)S(1)}, u32[]{:S(2)}, u32[]{:S(2)}) %collective-permute-start.1) | collective-permute-done | bytes 196640 | tf_op jit(solution)/shard_map/ppermute | solution.py:199
  59.9 0.1 fusion.33
  59.9 0.4 collective-permute-start.3
  60.3 0.5 collective-permute-start.4
  60.8 0.4 collective-permute-done.8
  61.2 2.5 %collective-permute-start.10 = (bf16[2,128,768]{2,1,0:T(8,128)(2,1)S(1)}, bf16[2,128,768]{2,1,0:T(8,128)(2,1)S(1)}, u32[]{:S(2)}, u32[]{:S(2)}) collective-permute-start(bf16[2,128,768]{2,1,0:T(8,128)(2,1)S(1)} %collective-permute-done.8), channel_id=1, source_target_pairs={{4,0},{5,1},{6,2},{7,3},{20,16},{21,17},{22,18},{23,19}} | collective-permute-start | bytes 1179656 | tf_op jit(solution)/shard_map/ppermute | solution.py:199
  63.8 1.9 %collective-permute-done.5 = bf16[2,128,768]{2,1,0:T(8,128)(2,1)S(1)} collective-permute-done((bf16[2,128,768]{2,1,0:T(8,128)(2,1)S(1)}, bf16[2,128,768]{2,1,0:T(8,128)(2,1)S(1)}, u32[]{:S(2)}, u32[]{:S(2)}) %collective-permute-start.5) | collective-permute-done | bytes 393248 | tf_op jit(solution)/shard_map/ppermute | solution.py:199
  65.7 0.5 collective-permute-start.7
  66.2 0.1 pad_add_fusion.pairs_ref
  66.3 5.5 %collective-permute-done.3 = bf16[4,64,768]{2,1,0:T(8,128)(2,1)S(1)} collective-permute-done((bf16[4,64,768]{2,1,0:T(8,128)(2,1)S(1)}, bf16[4,64,768]{2,1,0:T(8,128)(2,1)S(1)}, u32[]{:S(2)}, u32[]{:S(2)}) %collective-permute-start.3) | collective-permute-done | bytes 393248 | tf_op jit(solution)/shard_map/ppermute | solution.py:199
  71.8 0.1 maximum_bitcast_fusion
  71.9 0.3 collective-permute-done.10
  72.2 1.8 %collective-permute-start.11 = (bf16[2,128,768]{2,1,0:T(8,128)(2,1)S(1)}, bf16[2,128,768]{2,1,0:T(8,128)(2,1)S(1)}, u32[]{:S(2)}, u32[]{:S(2)}) collective-permute-start(bf16[2,128,768]{2,1,0:T(8,128)(2,1)S(1)} %collective-permute-done.10), channel_id=1, source_target_pairs={{0,16},{16,0},{1,17},{17,1},{2,18},{18,2},{3,19},{19,3},{4,20},{20... | collective-permute-start | bytes 1179656 | tf_op jit(solution)/shard_map/ppermute | solution.py:199
  74.0 0.1 collective-permute-done.2
  74.1 0.2 pad_maximum_fusion.1.row_ref
  74.3 3.5 %collective-permute-done.7 = bf16[2,128,768]{2,1,0:T(8,128)(2,1)S(1)} collective-permute-done((bf16[2,128,768]{2,1,0:T(8,128)(2,1)S(1)}, bf16[2,128,768]{2,1,0:T(8,128)(2,1)S(1)}, u32[]{:S(2)}, u32[]{:S(2)}) %collective-permute-start.7) | collective-permute-done | bytes 393248 | tf_op jit(solution)/shard_map/ppermute | solution.py:199
  77.7 0.1 maximum_bitcast_fusion.1
  77.8 8.4 %collective-permute-done.9 = bf16[2,128,768]{2,1,0:T(8,128)(2,1)S(1)} collective-permute-done((bf16[2,128,768]{2,1,0:T(8,128)(2,1)S(1)}, bf16[2,128,768]{2,1,0:T(8,128)(2,1)S(1)}, u32[]{:S(2)}, u32[]{:S(2)}) %collective-permute-start.9) | collective-permute-done | bytes 393248 | tf_op jit(solution)/shard_map/ppermute | solution.py:199
  86.2 0.1 maximum_bitcast_fusion.2
  86.2 5.4 %collective-permute-done.11 = bf16[2,128,768]{2,1,0:T(8,128)(2,1)S(1)} collective-permute-done((bf16[2,128,768]{2,1,0:T(8,128)(2,1)S(1)}, bf16[2,128,768]{2,1,0:T(8,128)(2,1)S(1)}, u32[]{:S(2)}, u32[]{:S(2)}) %collective-permute-start.11) | collective-permute-done | bytes 393248 | tf_op jit(solution)/shard_map/ppermute | solution.py:199
  91.6 0.1 maximum_bitcast_fusion.3
  91.7 0.4 pad_maximum_fusion.col_ref
  92.2 71.5 %shard_map.38 = bf16[4,64,128,256]{3,2,1,0:T(8,128)(2,1)} custom-call(s32[4,2]{1,0:T(4,128)S(1)} %pad_add_fusion.pairs_ref, bf16[4,4,64,768]{3,2,1,0:T(8,128)(2,1)S(1)} %pad_maximum_fusion.1.row_ref, bf16[4,4,128,768]{3,2,1,0:T(8,128)(2,1)S(1)} %pad_maximum_fusion.col_ref, bf16[768,256]{1,0:T(8,128)(2,1)S(1)} %pad_maximum_fusion.3.lags_ref), custom_call_target="tpu_custom_call" | custom-call | flops 13287555072 | bytes 21495808 | tf_op jit(solution)/shard_map/pallas_call | solution.py:174
  (16 shorter events, 0.1 us)
Async XLA Ops:
  2.3 26.6 %collective-permute-start = (bf16[128,4352]{1,0:T(8,128)(2,1)}, bf16[128,4352]{1,0:T(8,128)(2,1)S(1)}, u32[]{:S(2)}, u32[]{:S(2)}) collective-permute-start(bf16[128,4352]{1,0:T(8,128)(2,1)} %slice.17), channel_id=1, source_target_pairs={{16,0},{17,1},{18,2},{19,3},{20,4},{21,5},{22,6},{23,7},{24,8},{25... | collective-permute-start | bytes 3342344 | tf_op jit(solution)/shard_map/ppermute | solution.py:27
  19.7 9.1 %copy-start.1 = (bf16[128,7680]{1,0:T(8,128)(2,1)S(1)}, bf16[128,7680]{1,0:T(8,128)(2,1)}, u32[]{:S(2)}) copy-start(bf16[128,7680]{1,0:T(8,128)(2,1)} %param.3) | copy-start | bytes 5898244
  28.8 4.4 %copy-start = (bf16[7680,768]{1,0:T(8,128)(2,1)S(1)}, bf16[7680,768]{1,0:T(8,128)(2,1)}, u32[]{:S(2)}) copy-start(bf16[7680,768]{1,0:T(8,128)(2,1)} %shard_map.37) | copy-start | bytes 35389444
  36.3 3.2 %copy-start.2 = (s32[1,1,4,2]{2,3,1,0:T(2,128)S(1)}, s32[1,1,4,2]{2,3,1,0:T(2,128)}, u32[]{:S(2)}) copy-start(s32[1,1,4,2]{2,3,1,0:T(2,128)} %param.5) | copy-start | bytes 100
  37.2 12.5 %collective-permute-start.6 = (bf16[2,128,768]{2,1,0:T(8,128)(2,1)S(1)}, bf16[2,128,768]{2,1,0:T(8,128)(2,1)S(1)}, u32[]{:S(2)}, u32[]{:S(2)}) collective-permute-start(bf16[2,128,768]{2,1,0:T(8,128)(2,1)S(1)} %fusion.7), channel_id=1, source_target_pairs={{4,0},{8,4},{12,8},{5,1},{9,5},{13,9},{6,2},{10,6},{14,10},{7,3},{... | collective-permute-start | bytes 1179656 | tf_op jit(solution)/shard_map/ppermute | solution.py:199
  49.6 11.6 %collective-permute-start.8 = (bf16[2,128,768]{2,1,0:T(8,128)(2,1)S(1)}, bf16[2,128,768]{2,1,0:T(8,128)(2,1)S(1)}, u32[]{:S(2)}, u32[]{:S(2)}) collective-permute-start(bf16[2,128,768]{2,1,0:T(8,128)(2,1)S(1)} %collective-permute-done.6), channel_id=1, source_target_pairs={{4,0},{8,4},{5,1},{9,5},{6,2},{10,6},{7,3},{11,7},{20,16},{24,20},... | collective-permute-start | bytes 1179656 | tf_op jit(solution)/shard_map/ppermute | solution.py:199
  52.0 7.8 %collective-permute-start.1 = (bf16[2,64,768]{2,1,0:T(8,128)(2,1)S(1)}, bf16[2,64,768]{2,1,0:T(8,128)(2,1)S(1)}, u32[]{:S(2)}, u32[]{:S(2)}) collective-permute-start(bf16[2,64,768]{2,1,0:T(8,128)(2,1)S(1)} %get-tuple-element.10), channel_id=1, source_target_pairs={{0,16},{16,0},{1,17},{17,1},{2,18},{18,2},{3,19},{19,3},{4,20},{20... | collective-permute-start | bytes 589832 | tf_op jit(solution)/shard_map/ppermute | solution.py:199
  54.1 11.7 %collective-permute-start.5 = (bf16[2,128,768]{2,1,0:T(8,128)(2,1)S(1)}, bf16[2,128,768]{2,1,0:T(8,128)(2,1)S(1)}, u32[]{:S(2)}, u32[]{:S(2)}) collective-permute-start(bf16[2,128,768]{2,1,0:T(8,128)(2,1)S(1)} %fusion.7), channel_id=1, source_target_pairs={{0,16},{16,0},{1,17},{17,1},{2,18},{18,2},{3,19},{19,3},{4,20},{20... | collective-permute-start | bytes 1179656 | tf_op jit(solution)/shard_map/ppermute | solution.py:199
  59.9 11.9 %collective-permute-start.3 = (bf16[4,64,768]{2,1,0:T(8,128)(2,1)S(1)}, bf16[4,64,768]{2,1,0:T(8,128)(2,1)S(1)}, u32[]{:S(2)}, u32[]{:S(2)}) collective-permute-start(bf16[4,64,768]{2,1,0:T(8,128)(2,1)S(1)} %get-tuple-element.8), channel_id=1, source_target_pairs={{0,2},{1,3},{2,0},{3,1},{4,6},{5,7},{6,4},{7,5},{8,10},{9,11},{10,... | collective-permute-start | bytes 1179656 | tf_op jit(solution)/shard_map/ppermute | solution.py:199
  60.3 13.7 %collective-permute-start.2 = (bf16[4,64,768]{2,1,0:T(8,128)(2,1)S(1)}, bf16[4,64,768]{2,1,0:T(8,128)(2,1)S(1)}, u32[]{:S(2)}, u32[]{:S(2)}) collective-permute-start(bf16[4,64,768]{2,1,0:T(8,128)(2,1)S(1)} %get-tuple-element.8), channel_id=1, source_target_pairs={{0,3},{1,0},{2,1},{3,2},{4,7},{5,4},{6,5},{7,6},{8,11},{9,8},{10,9... | collective-permute-start | bytes 1179656 | tf_op jit(solution)/shard_map/ppermute | solution.py:199
  60.3 13.7 %collective-permute-start.4 = (bf16[4,64,768]{2,1,0:T(8,128)(2,1)S(1)}, bf16[4,64,768]{2,1,0:T(8,128)(2,1)S(1)}, u32[]{:S(2)}, u32[]{:S(2)}) collective-permute-start(bf16[4,64,768]{2,1,0:T(8,128)(2,1)S(1)} %get-tuple-element.8), channel_id=1, source_target_pairs={{0,1},{1,2},{2,3},{3,0},{4,5},{5,6},{6,7},{7,4},{8,9},{9,10},{10,1... | collective-permute-start | bytes 1179656 | tf_op jit(solution)/shard_map/ppermute | solution.py:199
  61.2 11.0 %collective-permute-start.10 = (bf16[2,128,768]{2,1,0:T(8,128)(2,1)S(1)}, bf16[2,128,768]{2,1,0:T(8,128)(2,1)S(1)}, u32[]{:S(2)}, u32[]{:S(2)}) collective-permute-start(bf16[2,128,768]{2,1,0:T(8,128)(2,1)S(1)} %collective-permute-done.8), channel_id=1, source_target_pairs={{4,0},{5,1},{6,2},{7,3},{20,16},{21,17},{22,18},{23,19}} | collective-permute-start | bytes 1179656 | tf_op jit(solution)/shard_map/ppermute | solution.py:199
  65.7 12.0 %collective-permute-start.7 = (bf16[2,128,768]{2,1,0:T(8,128)(2,1)S(1)}, bf16[2,128,768]{2,1,0:T(8,128)(2,1)S(1)}, u32[]{:S(2)}, u32[]{:S(2)}) collective-permute-start(bf16[2,128,768]{2,1,0:T(8,128)(2,1)S(1)} %collective-permute-done.6), channel_id=1, source_target_pairs={{0,16},{16,0},{1,17},{17,1},{2,18},{18,2},{3,19},{19,3},{4,20},{20... | collective-permute-start | bytes 1179656 | tf_op jit(solution)/shard_map/ppermute | solution.py:199
  71.8 14.4 %collective-permute-start.9 = (bf16[2,128,768]{2,1,0:T(8,128)(2,1)S(1)}, bf16[2,128,768]{2,1,0:T(8,128)(2,1)S(1)}, u32[]{:S(2)}, u32[]{:S(2)}) collective-permute-start(bf16[2,128,768]{2,1,0:T(8,128)(2,1)S(1)} %collective-permute-done.8), channel_id=1, source_target_pairs={{0,16},{16,0},{1,17},{17,1},{2,18},{18,2},{3,19},{19,3},{4,20},{20... | collective-permute-start | bytes 1179656 | tf_op jit(solution)/shard_map/ppermute | solution.py:199
  72.2 19.4 %collective-permute-start.11 = (bf16[2,128,768]{2,1,0:T(8,128)(2,1)S(1)}, bf16[2,128,768]{2,1,0:T(8,128)(2,1)S(1)}, u32[]{:S(2)}, u32[]{:S(2)}) collective-permute-start(bf16[2,128,768]{2,1,0:T(8,128)(2,1)S(1)} %collective-permute-done.10), channel_id=1, source_target_pairs={{0,16},{16,0},{1,17},{17,1},{2,18},{18,2},{3,19},{19,3},{4,20},{20... | collective-permute-start | bytes 1179656 | tf_op jit(solution)/shard_map/ppermute | solution.py:199

commit v12 on v11

--- a/solution.py
+++ b/solution.py
@@ -100,7 +100,7 @@
     return (spectra * jnp.concatenate([weight, weight], axis=-1)).astype(jnp.bfloat16)
 
 
-ROW_TILE = 8
+ROW_TILE = 16
 J_CHUNK = 64
 F_CHUNK = 128
 

time: 165 us -> 163 us (0.988)
  Pallas kernels: 80.6 us -> 77.9 us
    pallas_call x1, Pallas kernels: 71.5 us -> 68.8 us  [all_pairs(): pl.pallas_call(pair_kernel, grid_spec=grid_spec, out_shape=jax.ShapeDtype...]
where the time goes in v12:
time: 163 us; the launch traced here: 161 us
  Pallas kernels  77.9 us (48%)
  waiting for transfers between devices  39.1 us (24%)
  starting transfers between devices  15 us (9%)
  local copies, waits for them, and re-layouts  12.6 us (8%)
  other arithmetic  9.15 us (6%)
  matrix products  3.76 us (2%)
  between operations  3.43 us (2%)
    pallas_call x1, Pallas kernels, all_pairs(): pl.pallas_call(pair_kernel, grid_spec=grid_spec, out_shape=jax.ShapeDtype...  68.8 us
    ppermute x11, waiting for transfers between devices, exchange(): return lax.ppermute(value, axes, pairs)  39.1 us
    ppermute x11, starting transfers between devices, exchange(): return lax.ppermute(value, axes, pairs)  12.5 us
    pallas_call x1, Pallas kernels, forward_table(): pl.pallas_call(table_kernel, grid=(n_coarse // TABLE_Q,), in_specs=[pl.Bl...  9.11 us
    broadcast_in_dim x1, local copies, waits for them, and re-layouts, forward_table(): taper_lanes = jnp.broadcast_to(taper_curve[:, None], (WIN, F_CHUNK))  4.43 us
    sin x1, other arithmetic, forward_table(): high_sin = jnp.sin(high_angle).reshape(n_coarse, 1, NF)  4.15 us
  transfers between devices with their start and end apart: 12, of which 10 were waited for; matrix products, arithmetic and copies ran while one was open for 9% of the time, Pallas kernels for 6%

profile of v12, /device:TPU:14, one launch (start us, length us, event | category | flops | bytes accessed | tf_op | source)
XLA Modules:
  0.0 161.0 jit_solution(17645986315789769601)
XLA Ops:
  0.0 2.3 %slice.17 = bf16[128,4352]{1,0:T(8,128)(2,1)} slice(bf16[128,7680]{1,0:T(8,128)(2,1)} %param.3), slice={[0:128], [0:4352]} | slice | bytes 2228224 | tf_op jit(solution)/shard_map/slice | solution.py:220
  2.3 2.5 %collective-permute-start = (bf16[128,4352]{1,0:T(8,128)(2,1)}, bf16[128,4352]{1,0:T(8,128)(2,1)S(1)}, u32[]{:S(2)}, u32[]{:S(2)}) collective-permute-start(bf16[128,4352]{1,0:T(8,128)(2,1)} %slice.17), channel_id=1, source_target_pairs={{16,0},{17,1},{18,2},{19,3},{20,4},{21,5},{22,6},{23,7},{24,8},{25... | collective-permute-start | bytes 3342344 | tf_op jit(solution)/shard_map/ppermute | solution.py:27
  4.8 1.6 fusion.21
  6.4 4.2 %fusion.28 = (f32[60,1,384]{2,1,0:T(1,128)}, f32[60,1,384]{2,1,0:T(1,128)}) fusion(s32[384]{0:T(512)S(1)} %iota_add_fusion, s32[60]{0:T(128)S(1)} %iota_multiply_fusion), kind=kLoop, calls=%fused_computation.49 | loop fusion | flops 207360 | bytes 186096 | tf_op jit(solution)/shard_map/sin | solution.py:58
  10.6 1.3 fusion.35
  15.1 0.1 multiply_subtract_fusion
  15.2 4.4 %broadcast_in_dim.2.taper_ref = f32[7680,128]{1,0:T(8,128)} broadcast(f32[7680]{0:T(1024)S(1)} %multiply_subtract_fusion), dimensions={0} | broadcast | bytes 3962880 | tf_op jit(solution)/shard_map/broadcast_in_dim | solution.py:62
  19.7 9.1 %shard_map.37 = bf16[7680,768]{1,0:T(8,128)(2,1)} custom-call(f32[60,1,384]{2,1,0:T(1,128)} %get-tuple-element.14.high_cos_ref, f32[60,1,384]{2,1,0:T(1,128)} %get-tuple-element.13.high_sin_ref, f32[128,384]{1,0:T(8,128)} %get-tuple-element.16.low_cos_ref, f32[128,384]{1,0:T(8,128)} %get-tuple-element.15.low_sin_ref, f32[7680,128]{1,0:T(8,128)} %broadcast_in_dim.2.taper_ref), custom_call_target="tpu_custom_call" | custom-call | tf_op jit(solution)/shard_map/pallas_call | solution.py:63
  28.8 0.1 constant_dynamic-update-slice_fusion.1
  28.9 0.1 constant_dynamic-update-slice_fusion
  29.0 1.6 constant_dynamic-slice_fusion.3
  30.6 2.5 %copy-done = bf16[7680,768]{1,0:T(8,128)(2,1)S(1)} copy-done((bf16[7680,768]{1,0:T(8,128)(2,1)S(1)}, bf16[7680,768]{1,0:T(8,128)(2,1)}, u32[]{:S(2)}) %copy-start) | copy-done | bytes 11796504
  33.1 3.2 %fusion = f32[256,768]{1,0:T(8,128)S(1)} fusion(bf16[7680,768]{1,0:T(8,128)(2,1)S(1)} %copy-done, bf16[128,7680]{1,0:T(8,128)(2,1)S(1)} %get-tuple-element.6, bf16[128,7680]{1,0:T(8,128)(2,1)S(1)} %get-tuple-element.5), kind=kOutput, calls=%fused_computation | convolution fusion | flops 3027763200 | bytes 16515072 | tf_op jit(solution)/shard_map/dot_general | solution.py:229
  36.3 0.0 copy-start.2
  36.3 0.1 fusion.26
  36.5 0.6 fusion.6
  37.1 0.1 fusion.7
  37.2 2.4 %collective-permute-start.6 = (bf16[2,128,768]{2,1,0:T(8,128)(2,1)S(1)}, bf16[2,128,768]{2,1,0:T(8,128)(2,1)S(1)}, u32[]{:S(2)}, u32[]{:S(2)}) collective-permute-start(bf16[2,128,768]{2,1,0:T(8,128)(2,1)S(1)} %fusion.7), channel_id=1, source_target_pairs={{4,0},{8,4},{12,8},{5,1},{9,5},{13,9},{6,2},{10,6},{14,10},{7,3},{... | collective-permute-start | bytes 1179656 | tf_op jit(solution)/shard_map/ppermute | solution.py:199
  39.6 0.1 copy.6
  39.7 0.1 copy.7
  39.8 9.9 %collective-permute-done.6 = bf16[2,128,768]{2,1,0:T(8,128)(2,1)S(1)} collective-permute-done((bf16[2,128,768]{2,1,0:T(8,128)(2,1)S(1)}, bf16[2,128,768]{2,1,0:T(8,128)(2,1)S(1)}, u32[]{:S(2)}, u32[]{:S(2)}) %collective-permute-start.6) | collective-permute-done | bytes 393248 | tf_op jit(solution)/shard_map/ppermute | solution.py:199
  49.6 2.3 %collective-permute-start.8 = (bf16[2,128,768]{2,1,0:T(8,128)(2,1)S(1)}, bf16[2,128,768]{2,1,0:T(8,128)(2,1)S(1)}, u32[]{:S(2)}, u32[]{:S(2)}) collective-permute-start(bf16[2,128,768]{2,1,0:T(8,128)(2,1)S(1)} %collective-permute-done.6), channel_id=1, source_target_pairs={{4,0},{8,4},{5,1},{9,5},{6,2},{10,6},{7,3},{11,7},{20,16},{24,20},... | collective-permute-start | bytes 1179656 | tf_op jit(solution)/shard_map/ppermute | solution.py:199
  52.0 0.1 collective-permute-start.1
  52.1 2.0 %multiply_convert_fusion.1 = (bf16[384,256]{1,0:T(8,128)(2,1)S(1)}, bf16[384,256]{1,0:T(8,128)(2,1)S(1)}) fusion(s32[256]{0:T(256)S(1)} %and_select_fusion.1, s32[384]{0:T(512)S(1)} %iota_add_fusion), kind=kLoop, calls=%fused_computation.27 | loop fusion | flops 1376256 | bytes 395776 | tf_op jit(solution)/shard_map/convert
  54.1 2.1 %collective-permute-start.5 = (bf16[2,128,768]{2,1,0:T(8,128)(2,1)S(1)}, bf16[2,128,768]{2,1,0:T(8,128)(2,1)S(1)}, u32[]{:S(2)}, u32[]{:S(2)}) collective-permute-start(bf16[2,128,768]{2,1,0:T(8,128)(2,1)S(1)} %fusion.7), channel_id=1, source_target_pairs={{0,16},{16,0},{1,17},{17,1},{2,18},{18,2},{3,19},{19,3},{4,20},{20... | collective-permute-start | bytes 1179656 | tf_op jit(solution)/shard_map/ppermute | solution.py:199
  56.1 3.7 %collective-permute-done.1 = bf16[2,64,768]{2,1,0:T(8,128)(2,1)S(1)} collective-permute-done((bf16[2,64,768]{2,1,0:T(8,128)(2,1)S(1)}, bf16[2,64,768]{2,1,0:T(8,128)(2,1)S(1)}, u32[]{:S(2)}, u32[]{:S(2)}) %collective-permute-start.1) | collective-permute-done | bytes 196640 | tf_op jit(solution)/shard_map/ppermute | solution.py:199
  59.9 0.1 fusion.33
  59.9 0.4 collective-permute-start.3
  60.3 0.5 collective-permute-start.4
  60.8 0.4 collective-permute-done.8
  61.2 2.5 %collective-permute-start.10 = (bf16[2,128,768]{2,1,0:T(8,128)(2,1)S(1)}, bf16[2,128,768]{2,1,0:T(8,128)(2,1)S(1)}, u32[]{:S(2)}, u32[]{:S(2)}) collective-permute-start(bf16[2,128,768]{2,1,0:T(8,128)(2,1)S(1)} %collective-permute-done.8), channel_id=1, source_target_pairs={{4,0},{5,1},{6,2},{7,3},{20,16},{21,17},{22,18},{23,19}} | collective-permute-start | bytes 1179656 | tf_op jit(solution)/shard_map/ppermute | solution.py:199
  63.8 1.9 %collective-permute-done.5 = bf16[2,128,768]{2,1,0:T(8,128)(2,1)S(1)} collective-permute-done((bf16[2,128,768]{2,1,0:T(8,128)(2,1)S(1)}, bf16[2,128,768]{2,1,0:T(8,128)(2,1)S(1)}, u32[]{:S(2)}, u32[]{:S(2)}) %collective-permute-start.5) | collective-permute-done | bytes 393248 | tf_op jit(solution)/shard_map/ppermute | solution.py:199
  65.7 0.5 collective-permute-start.7
  66.2 0.1 pad_add_fusion.pairs_ref
  66.3 5.5 %collective-permute-done.3 = bf16[4,64,768]{2,1,0:T(8,128)(2,1)S(1)} collective-permute-done((bf16[4,64,768]{2,1,0:T(8,128)(2,1)S(1)}, bf16[4,64,768]{2,1,0:T(8,128)(2,1)S(1)}, u32[]{:S(2)}, u32[]{:S(2)}) %collective-permute-start.3) | collective-permute-done | bytes 393248 | tf_op jit(solution)/shard_map/ppermute | solution.py:199
  71.8 0.1 maximum_bitcast_fusion
  71.9 0.3 collective-permute-done.10
  72.2 1.8 %collective-permute-start.11 = (bf16[2,128,768]{2,1,0:T(8,128)(2,1)S(1)}, bf16[2,128,768]{2,1,0:T(8,128)(2,1)S(1)}, u32[]{:S(2)}, u32[]{:S(2)}) collective-permute-start(bf16[2,128,768]{2,1,0:T(8,128)(2,1)S(1)} %collective-permute-done.10), channel_id=1, source_target_pairs={{0,16},{16,0},{1,17},{17,1},{2,18},{18,2},{3,19},{19,3},{4,20},{20... | collective-permute-start | bytes 1179656 | tf_op jit(solution)/shard_map/ppermute | solution.py:199
  74.0 0.1 collective-permute-done.2
  74.1 0.2 pad_maximum_fusion.1.row_ref
  74.3 3.5 %collective-permute-done.7 = bf16[2,128,768]{2,1,0:T(8,128)(2,1)S(1)} collective-permute-done((bf16[2,128,768]{2,1,0:T(8,128)(2,1)S(1)}, bf16[2,128,768]{2,1,0:T(8,128)(2,1)S(1)}, u32[]{:S(2)}, u32[]{:S(2)}) %collective-permute-start.7) | collective-permute-done | bytes 393248 | tf_op jit(solution)/shard_map/ppermute | solution.py:199
  77.7 0.1 maximum_bitcast_fusion.1
  77.8 8.4 %collective-permute-done.9 = bf16[2,128,768]{2,1,0:T(8,128)(2,1)S(1)} collective-permute-done((bf16[2,128,768]{2,1,0:T(8,128)(2,1)S(1)}, bf16[2,128,768]{2,1,0:T(8,128)(2,1)S(1)}, u32[]{:S(2)}, u32[]{:S(2)}) %collective-permute-start.9) | collective-permute-done | bytes 393248 | tf_op jit(solution)/shard_map/ppermute | solution.py:199
  86.2 0.1 maximum_bitcast_fusion.2
  86.2 5.4 %collective-permute-done.11 = bf16[2,128,768]{2,1,0:T(8,128)(2,1)S(1)} collective-permute-done((bf16[2,128,768]{2,1,0:T(8,128)(2,1)S(1)}, bf16[2,128,768]{2,1,0:T(8,128)(2,1)S(1)}, u32[]{:S(2)}, u32[]{:S(2)}) %collective-permute-start.11) | collective-permute-done | bytes 393248 | tf_op jit(solution)/shard_map/ppermute | solution.py:199
  91.6 0.1 maximum_bitcast_fusion.3
  91.7 0.4 pad_maximum_fusion.col_ref
  92.2 68.8 %shard_map.38 = bf16[4,64,128,256]{3,2,1,0:T(8,128)(2,1)} custom-call(s32[4,2]{1,0:T(4,128)S(1)} %pad_add_fusion.pairs_ref, bf16[4,4,64,768]{3,2,1,0:T(8,128)(2,1)S(1)} %pad_maximum_fusion.1.row_ref, bf16[4,4,128,768]{3,2,1,0:T(8,128)(2,1)S(1)} %pad_maximum_fusion.col_ref, bf16[768,256]{1,0:T(8,128)(2,1)S(1)} %pad_maximum_fusion.3.lags_ref), custom_call_target="tpu_custom_call" | custom-call | flops 13287555072 | bytes 21495808 | tf_op jit(solution)/shard_map/pallas_call | solution.py:174
  (16 shorter events, 0.1 us)
Async XLA Ops:
  2.3 26.6 %collective-permute-start = (bf16[128,4352]{1,0:T(8,128)(2,1)}, bf16[128,4352]{1,0:T(8,128)(2,1)S(1)}, u32[]{:S(2)}, u32[]{:S(2)}) collective-permute-start(bf16[128,4352]{1,0:T(8,128)(2,1)} %slice.17), channel_id=1, source_target_pairs={{16,0},{17,1},{18,2},{19,3},{20,4},{21,5},{22,6},{23,7},{24,8},{25... | collective-permute-start | bytes 3342344 | tf_op jit(solution)/shard_map/ppermute | solution.py:27
  19.7 9.1 %copy-start.1 = (bf16[128,7680]{1,0:T(8,128)(2,1)S(1)}, bf16[128,7680]{1,0:T(8,128)(2,1)}, u32[]{:S(2)}) copy-start(bf16[128,7680]{1,0:T(8,128)(2,1)} %param.3) | copy-start | bytes 5898244
  28.8 4.4 %copy-start = (bf16[7680,768]{1,0:T(8,128)(2,1)S(1)}, bf16[7680,768]{1,0:T(8,128)(2,1)}, u32[]{:S(2)}) copy-start(bf16[7680,768]{1,0:T(8,128)(2,1)} %shard_map.37) | copy-start | bytes 35389444
  36.3 3.2 %copy-start.2 = (s32[1,1,4,2]{2,3,1,0:T(2,128)S(1)}, s32[1,1,4,2]{2,3,1,0:T(2,128)}, u32[]{:S(2)}) copy-start(s32[1,1,4,2]{2,3,1,0:T(2,128)} %param.5) | copy-start | bytes 100
  37.2 12.5 %collective-permute-start.6 = (bf16[2,128,768]{2,1,0:T(8,128)(2,1)S(1)}, bf16[2,128,768]{2,1,0:T(8,128)(2,1)S(1)}, u32[]{:S(2)}, u32[]{:S(2)}) collective-permute-start(bf16[2,128,768]{2,1,0:T(8,128)(2,1)S(1)} %fusion.7), channel_id=1, source_target_pairs={{4,0},{8,4},{12,8},{5,1},{9,5},{13,9},{6,2},{10,6},{14,10},{7,3},{... | collective-permute-start | bytes 1179656 | tf_op jit(solution)/shard_map/ppermute | solution.py:199
  49.6 11.6 %collective-permute-start.8 = (bf16[2,128,768]{2,1,0:T(8,128)(2,1)S(1)}, bf16[2,128,768]{2,1,0:T(8,128)(2,1)S(1)}, u32[]{:S(2)}, u32[]{:S(2)}) collective-permute-start(bf16[2,128,768]{2,1,0:T(8,128)(2,1)S(1)} %collective-permute-done.6), channel_id=1, source_target_pairs={{4,0},{8,4},{5,1},{9,5},{6,2},{10,6},{7,3},{11,7},{20,16},{24,20},... | collective-permute-start | bytes 1179656 | tf_op jit(solution)/shard_map/ppermute | solution.py:199
  52.0 7.8 %collective-permute-start.1 = (bf16[2,64,768]{2,1,0:T(8,128)(2,1)S(1)}, bf16[2,64,768]{2,1,0:T(8,128)(2,1)S(1)}, u32[]{:S(2)}, u32[]{:S(2)}) collective-permute-start(bf16[2,64,768]{2,1,0:T(8,128)(2,1)S(1)} %get-tuple-element.10), channel_id=1, source_target_pairs={{0,16},{16,0},{1,17},{17,1},{2,18},{18,2},{3,19},{19,3},{4,20},{20... | collective-permute-start | bytes 589832 | tf_op jit(solution)/shard_map/ppermute | solution.py:199
  54.1 11.7 %collective-permute-start.5 = (bf16[2,128,768]{2,1,0:T(8,128)(2,1)S(1)}, bf16[2,128,768]{2,1,0:T(8,128)(2,1)S(1)}, u32[]{:S(2)}, u32[]{:S(2)}) collective-permute-start(bf16[2,128,768]{2,1,0:T(8,128)(2,1)S(1)} %fusion.7), channel_id=1, source_target_pairs={{0,16},{16,0},{1,17},{17,1},{2,18},{18,2},{3,19},{19,3},{4,20},{20... | collective-permute-start | bytes 1179656 | tf_op jit(solution)/shard_map/ppermute | solution.py:199
  59.9 11.9 %collective-permute-start.3 = (bf16[4,64,768]{2,1,0:T(8,128)(2,1)S(1)}, bf16[4,64,768]{2,1,0:T(8,128)(2,1)S(1)}, u32[]{:S(2)}, u32[]{:S(2)}) collective-permute-start(bf16[4,64,768]{2,1,0:T(8,128)(2,1)S(1)} %get-tuple-element.8), channel_id=1, source_target_pairs={{0,2},{1,3},{2,0},{3,1},{4,6},{5,7},{6,4},{7,5},{8,10},{9,11},{10,... | collective-permute-start | bytes 1179656 | tf_op jit(solution)/shard_map/ppermute | solution.py:199
  60.3 13.7 %collective-permute-start.2 = (bf16[4,64,768]{2,1,0:T(8,128)(2,1)S(1)}, bf16[4,64,768]{2,1,0:T(8,128)(2,1)S(1)}, u32[]{:S(2)}, u32[]{:S(2)}) collective-permute-start(bf16[4,64,768]{2,1,0:T(8,128)(2,1)S(1)} %get-tuple-element.8), channel_id=1, source_target_pairs={{0,3},{1,0},{2,1},{3,2},{4,7},{5,4},{6,5},{7,6},{8,11},{9,8},{10,9... | collective-permute-start | bytes 1179656 | tf_op jit(solution)/shard_map/ppermute | solution.py:199
  60.3 13.7 %collective-permute-start.4 = (bf16[4,64,768]{2,1,0:T(8,128)(2,1)S(1)}, bf16[4,64,768]{2,1,0:T(8,128)(2,1)S(1)}, u32[]{:S(2)}, u32[]{:S(2)}) collective-permute-start(bf16[4,64,768]{2,1,0:T(8,128)(2,1)S(1)} %get-tuple-element.8), channel_id=1, source_target_pairs={{0,1},{1,2},{2,3},{3,0},{4,5},{5,6},{6,7},{7,4},{8,9},{9,10},{10,1... | collective-permute-start | bytes 1179656 | tf_op jit(solution)/shard_map/ppermute | solution.py:199
  61.2 11.0 %collective-permute-start.10 = (bf16[2,128,768]{2,1,0:T(8,128)(2,1)S(1)}, bf16[2,128,768]{2,1,0:T(8,128)(2,1)S(1)}, u32[]{:S(2)}, u32[]{:S(2)}) collective-permute-start(bf16[2,128,768]{2,1,0:T(8,128)(2,1)S(1)} %collective-permute-done.8), channel_id=1, source_target_pairs={{4,0},{5,1},{6,2},{7,3},{20,16},{21,17},{22,18},{23,19}} | collective-permute-start | bytes 1179656 | tf_op jit(solution)/shard_map/ppermute | solution.py:199
  65.7 12.0 %collective-permute-start.7 = (bf16[2,128,768]{2,1,0:T(8,128)(2,1)S(1)}, bf16[2,128,768]{2,1,0:T(8,128)(2,1)S(1)}, u32[]{:S(2)}, u32[]{:S(2)}) collective-permute-start(bf16[2,128,768]{2,1,0:T(8,128)(2,1)S(1)} %collective-permute-done.6), channel_id=1, source_target_pairs={{0,16},{16,0},{1,17},{17,1},{2,18},{18,2},{3,19},{19,3},{4,20},{20... | collective-permute-start | bytes 1179656 | tf_op jit(solution)/shard_map/ppermute | solution.py:199
  71.8 14.4 %collective-permute-start.9 = (bf16[2,128,768]{2,1,0:T(8,128)(2,1)S(1)}, bf16[2,128,768]{2,1,0:T(8,128)(2,1)S(1)}, u32[]{:S(2)}, u32[]{:S(2)}) collective-permute-start(bf16[2,128,768]{2,1,0:T(8,128)(2,1)S(1)} %collective-permute-done.8), channel_id=1, source_target_pairs={{0,16},{16,0},{1,17},{17,1},{2,18},{18,2},{3,19},{19,3},{4,20},{20... | collective-permute-start | bytes 1179656 | tf_op jit(solution)/shard_map/ppermute | solution.py:199
  72.2 19.4 %collective-permute-start.11 = (bf16[2,128,768]{2,1,0:T(8,128)(2,1)S(1)}, bf16[2,128,768]{2,1,0:T(8,128)(2,1)S(1)}, u32[]{:S(2)}, u32[]{:S(2)}) collective-permute-start(bf16[2,128,768]{2,1,0:T(8,128)(2,1)S(1)} %collective-permute-done.10), channel_id=1, source_target_pairs={{0,16},{16,0},{1,17},{17,1},{2,18},{18,2},{3,19},{19,3},{4,20},{20... | collective-permute-start | bytes 1179656 | tf_op jit(solution)/shard_map/ppermute | solution.py:199

commit v13 on v12

--- a/solution.py
+++ b/solution.py
@@ -30,11 +30,14 @@
 TABLE_Q = 12
 
 
-def table_kernel(high_cos_ref, high_sin_ref, low_cos_ref, low_sin_ref, taper_ref, out_ref):
+def table_kernel(high_cos_ref, high_sin_ref, low_cos_ref, low_sin_ref, start_cos_ref, start_sin_ref,
+                 step_cos_ref, step_sin_ref, out_ref):
     coarse = low_cos_ref.shape[0]
+    step_cos = step_cos_ref[...]
+    step_sin = step_sin_ref[...]
     for qq in range(TABLE_Q):
         rows = pl.ds(qq * coarse, coarse)
-        taper = taper_ref[rows, :]
+        taper = 0.5 - 0.5 * (start_cos_ref[qq] * step_cos - start_sin_ref[qq] * step_sin)
         for fc in range(NF // F_CHUNK):
             lanes = pl.ds(fc * F_CHUNK, F_CHUNK)
             hc = high_cos_ref[qq, :, lanes]
@@ -57,9 +60,12 @@
     high_cos = jnp.cos(high_angle).reshape(n_coarse, 1, NF)
     high_sin = jnp.sin(high_angle).reshape(n_coarse, 1, NF)
     low_cos, low_sin = jnp.cos(low_angle), jnp.sin(low_angle)
-    sample_idx = jnp.arange(WIN, dtype=jnp.int32)
-    taper_curve = 0.5 - 0.5 * jnp.cos(sample_idx.astype(jnp.float32) * (two_pi / WIN))
-    taper_lanes = jnp.broadcast_to(taper_curve[:, None], (WIN, F_CHUNK))
+    start_angle = (jnp.arange(n_coarse, dtype=jnp.int32) * coarse).astype(jnp.float32) * scale
+    step_angle = jnp.arange(coarse, dtype=jnp.int32).astype(jnp.float32) * scale
+    start_cos = jnp.broadcast_to(jnp.cos(start_angle)[:, None, None], (n_coarse, 1, F_CHUNK))
+    start_sin = jnp.broadcast_to(jnp.sin(start_angle)[:, None, None], (n_coarse, 1, F_CHUNK))
+    step_cos = jnp.broadcast_to(jnp.cos(step_angle)[:, None], (coarse, F_CHUNK))
+    step_sin = jnp.broadcast_to(jnp.sin(step_angle)[:, None], (coarse, F_CHUNK))
     return pl.pallas_call(
         table_kernel,
         grid=(n_coarse // TABLE_Q,),
@@ -68,11 +74,14 @@
             pl.BlockSpec((TABLE_Q, 1, NF), lambda q: (q, 0, 0)),
             pl.BlockSpec((coarse, NF), lambda q: (0, 0)),
             pl.BlockSpec((coarse, NF), lambda q: (0, 0)),
-            pl.BlockSpec((TABLE_Q * coarse, F_CHUNK), lambda q: (q, 0)),
+            pl.BlockSpec((TABLE_Q, 1, F_CHUNK), lambda q: (q, 0, 0)),
+            pl.BlockSpec((TABLE_Q, 1, F_CHUNK), lambda q: (q, 0, 0)),
+            pl.BlockSpec((coarse, F_CHUNK), lambda q: (0, 0)),
+            pl.BlockSpec((coarse, F_CHUNK), lambda q: (0, 0)),
         ],
         out_specs=pl.BlockSpec((TABLE_Q * coarse, 2 * NF), lambda q: (q, 0)),
         out_shape=jax.ShapeDtypeStruct((WIN, 2 * NF), jnp.bfloat16),
-    )(high_cos, high_sin, low_cos, low_sin, taper_lanes)
+    )(high_cos, high_sin, low_cos, low_sin, start_cos, start_sin, step_cos, step_sin)
 
 
 def lag_table(count):

time: 163 us -> 161 us (0.988)
  local copies, waits for them, and re-layouts: 12.6 us -> 9.31 us
    unnamed x9, local copies, waits for them, and re-layouts: 2.84 us -> 0.96 us
    ppermute x1, waiting for transfers between devices: 0.01 us -> 1.87 us  [from_behind(): lax.ppermute(value, axis, [(source, source + steps) for source in range(i...]
    broadcast_in_dim x1 -> x4, local copies, waits for them, and re-layouts: 4.43 us -> 2.86 us  [the longest x1 0.73 us: forward_table(): jnp.broadcast_to(jnp.sin(start_angle)[:, None, None], (n_coarse, 1, F_CHU...]
  transfers between devices with their start and end apart: 12 -> 12, of which waited for: 10 -> 9; matrix products, arithmetic and copies ran while one was open for 9% -> 8% of each run, Pallas kernels for 6% -> 5%
where the time goes in v13:
time: 161 us; the launch traced here: 159 us
  Pallas kernels  77.3 us (48%)
  waiting for transfers between devices  39.7 us (25%)
  starting transfers between devices  16.3 us (10%)
  local copies, waits for them, and re-layouts  9.31 us (6%)
  other arithmetic  9.19 us (6%)
  matrix products  3.76 us (2%)
  between operations  3.56 us (2%)
    pallas_call x1, Pallas kernels, all_pairs(): pl.pallas_call(pair_kernel, grid_spec=grid_spec, out_shape=jax.ShapeDtype...  68.8 us
    ppermute x11, waiting for transfers between devices, exchange(): return lax.ppermute(value, axes, pairs)  37.8 us
    ppermute x11, starting transfers between devices, exchange(): return lax.ppermute(value, axes, pairs)  13.8 us
    pallas_call x1, Pallas kernels, forward_table(): pl.pallas_call(table_kernel, grid=(n_coarse // TABLE_Q,), in_specs=[pl.Bl...  8.49 us
    sin x1, other arithmetic, forward_table(): high_sin = jnp.sin(high_angle).reshape(n_coarse, 1, NF)  4.19 us
  transfers between devices with their start and end apart: 12, of which 9 were waited for; matrix products, arithmetic and copies ran while one was open for 8% of the time, Pallas kernels for 5%

profile of v13, /device:TPU:14, one launch (start us, length us, event | category | flops | bytes accessed | tf_op | source)
XLA Modules:
  0.0 159.1 jit_solution(14193142080962991295)
XLA Ops:
  0.0 2.3 %slice.17 = bf16[128,4352]{1,0:T(8,128)(2,1)} slice(bf16[128,7680]{1,0:T(8,128)(2,1)} %param.3), slice={[0:128], [0:4352]} | slice | bytes 2228224 | tf_op jit(solution)/shard_map/slice | solution.py:229
  2.3 2.5 %collective-permute-start = (bf16[128,4352]{1,0:T(8,128)(2,1)}, bf16[128,4352]{1,0:T(8,128)(2,1)S(1)}, u32[]{:S(2)}, u32[]{:S(2)}) collective-permute-start(bf16[128,4352]{1,0:T(8,128)(2,1)} %slice.17), channel_id=1, source_target_pairs={{16,0},{17,1},{18,2},{19,3},{20,4},{21,5},{22,6},{23,7},{24,8},{25... | collective-permute-start | bytes 3342344 | tf_op jit(solution)/shard_map/ppermute | solution.py:27
  5.0 1.6 fusion.21
  6.5 4.2 %fusion.28 = (f32[60,1,384]{2,1,0:T(1,128)}, f32[60,1,384]{2,1,0:T(1,128)}) fusion(s32[384]{0:T(512)S(1)} %iota_add_fusion, s32[60]{0:T(128)S(1)} %iota_multiply_fusion), kind=kLoop, calls=%fused_computation.48 | loop fusion | flops 207360 | bytes 186096 | tf_op jit(solution)/shard_map/sin | solution.py:61
  10.8 1.4 fusion.39
  15.5 0.7 broadcast_in_dim.9.start_sin_ref
  16.3 0.7 broadcast_in_dim.8.start_cos_ref
  17.0 0.7 broadcast_in_dim.11.step_sin_ref
  17.7 0.7 broadcast_in_dim.10.step_cos_ref
  18.4 8.5 %shard_map.37 = bf16[7680,768]{1,0:T(8,128)(2,1)} custom-call(f32[60,1,384]{2,1,0:T(1,128)} %get-tuple-element.14.high_cos_ref, f32[60,1,384]{2,1,0:T(1,128)} %get-tuple-element.13.high_sin_ref, f32[128,384]{1,0:T(8,128)} %get-tuple-element.16.low_cos_ref, f32[128,384]{1,0:T(8,128)} %get-tuple-element.15.low_sin_ref, ...), custom_call_target="tpu_custom_call" | custom-call | tf_op jit(solution)/shard_map/pallas_call | solution.py:69
  26.9 0.1 constant_dynamic-update-slice_fusion.1
  27.0 1.9 %collective-permute-done = bf16[128,4352]{1,0:T(8,128)(2,1)S(1)} collective-permute-done((bf16[128,4352]{1,0:T(8,128)(2,1)}, bf16[128,4352]{1,0:T(8,128)(2,1)S(1)}, u32[]{:S(2)}, u32[]{:S(2)}) %collective-permute-start) | collective-permute-done | bytes 1114144 | tf_op jit(solution)/shard_map/ppermute | solution.py:27
  28.9 0.1 constant_dynamic-update-slice_fusion
  29.0 1.6 %constant_dynamic-slice_fusion.3 = (bf16[128,7680]{1,0:T(8,128)(2,1)S(1)}, bf16[128,7680]{1,0:T(8,128)(2,1)S(1)}) fusion(bf16[128,12032]{1,0:T(8,128)(2,1)S(1)} %constant_dynamic-update-slice_fusion, s32[]{:T(128)S(6)} %select_n.81, s32[]{:T(128)S(6)} %select_n.83), kind=kLoop, calls=%fused_computation.61 | loop fusion | bytes 7864328 | tf_op jit(solution)/shard_map/dynamic_slice | solution.py:234
  30.6 0.6 copy-done
  31.2 3.2 %fusion = f32[256,768]{1,0:T(8,128)S(1)} fusion(bf16[7680,768]{1,0:T(8,128)(2,1)S(1)} %copy-done, bf16[128,7680]{1,0:T(8,128)(2,1)S(1)} %get-tuple-element.6, bf16[128,7680]{1,0:T(8,128)(2,1)S(1)} %get-tuple-element.5), kind=kOutput, calls=%fused_computation | convolution fusion | flops 3027763200 | bytes 16515072 | tf_op jit(solution)/shard_map/dot_general | solution.py:238
  34.5 0.1 fusion.26
  34.6 0.6 fusion.6
  35.2 0.1 fusion.7
  35.3 2.4 %collective-permute-start.6 = (bf16[2,128,768]{2,1,0:T(8,128)(2,1)S(1)}, bf16[2,128,768]{2,1,0:T(8,128)(2,1)S(1)}, u32[]{:S(2)}, u32[]{:S(2)}) collective-permute-start(bf16[2,128,768]{2,1,0:T(8,128)(2,1)S(1)} %fusion.7), channel_id=1, source_target_pairs={{4,0},{8,4},{12,8},{5,1},{9,5},{13,9},{6,2},{10,6},{14,10},{7,3},{... | collective-permute-start | bytes 1179656 | tf_op jit(solution)/shard_map/ppermute | solution.py:208
  37.7 0.1 copy.6
  37.8 0.1 copy.7
  37.9 9.9 %collective-permute-done.6 = bf16[2,128,768]{2,1,0:T(8,128)(2,1)S(1)} collective-permute-done((bf16[2,128,768]{2,1,0:T(8,128)(2,1)S(1)}, bf16[2,128,768]{2,1,0:T(8,128)(2,1)S(1)}, u32[]{:S(2)}, u32[]{:S(2)}) %collective-permute-start.6) | collective-permute-done | bytes 393248 | tf_op jit(solution)/shard_map/ppermute | solution.py:208
  47.7 2.3 %collective-permute-start.8 = (bf16[2,128,768]{2,1,0:T(8,128)(2,1)S(1)}, bf16[2,128,768]{2,1,0:T(8,128)(2,1)S(1)}, u32[]{:S(2)}, u32[]{:S(2)}) collective-permute-start(bf16[2,128,768]{2,1,0:T(8,128)(2,1)S(1)} %collective-permute-done.6), channel_id=1, source_target_pairs={{4,0},{8,4},{5,1},{9,5},{6,2},{10,6},{7,3},{11,7},{20,16},{24,20},... | collective-permute-start | bytes 1179656 | tf_op jit(solution)/shard_map/ppermute | solution.py:208
  50.1 1.2 collective-permute-start.1
  51.4 1.9 %multiply_convert_fusion.1 = (bf16[384,256]{1,0:T(8,128)(2,1)S(1)}, bf16[384,256]{1,0:T(8,128)(2,1)S(1)}) fusion(s32[256]{0:T(256)S(1)} %and_select_fusion.1, s32[384]{0:T(512)S(1)} %iota_add_fusion), kind=kLoop, calls=%fused_computation.27 | loop fusion | flops 1376256 | bytes 395776 | tf_op jit(solution)/shard_map/convert
  53.3 0.9 collective-permute-start.5
  54.2 3.7 %collective-permute-done.1 = bf16[2,64,768]{2,1,0:T(8,128)(2,1)S(1)} collective-permute-done((bf16[2,64,768]{2,1,0:T(8,128)(2,1)S(1)}, bf16[2,64,768]{2,1,0:T(8,128)(2,1)S(1)}, u32[]{:S(2)}, u32[]{:S(2)}) %collective-permute-start.1) | collective-permute-done | bytes 196640 | tf_op jit(solution)/shard_map/ppermute | solution.py:208
  58.0 0.4 collective-permute-start.3
  58.4 0.5 collective-permute-start.4
  58.9 0.4 collective-permute-done.8
  59.3 2.5 %collective-permute-start.10 = (bf16[2,128,768]{2,1,0:T(8,128)(2,1)S(1)}, bf16[2,128,768]{2,1,0:T(8,128)(2,1)S(1)}, u32[]{:S(2)}, u32[]{:S(2)}) collective-permute-start(bf16[2,128,768]{2,1,0:T(8,128)(2,1)S(1)} %collective-permute-done.8), channel_id=1, source_target_pairs={{4,0},{5,1},{6,2},{7,3},{20,16},{21,17},{22,18},{23,19}} | collective-permute-start | bytes 1179656 | tf_op jit(solution)/shard_map/ppermute | solution.py:208
  61.9 2.1 %collective-permute-done.5 = bf16[2,128,768]{2,1,0:T(8,128)(2,1)S(1)} collective-permute-done((bf16[2,128,768]{2,1,0:T(8,128)(2,1)S(1)}, bf16[2,128,768]{2,1,0:T(8,128)(2,1)S(1)}, u32[]{:S(2)}, u32[]{:S(2)}) %collective-permute-start.5) | collective-permute-done | bytes 393248 | tf_op jit(solution)/shard_map/ppermute | solution.py:208
  64.1 1.4 collective-permute-start.7
  65.5 0.1 pad_add_fusion.pairs_ref
  65.5 4.4 %collective-permute-done.3 = bf16[4,64,768]{2,1,0:T(8,128)(2,1)S(1)} collective-permute-done((bf16[4,64,768]{2,1,0:T(8,128)(2,1)S(1)}, bf16[4,64,768]{2,1,0:T(8,128)(2,1)S(1)}, u32[]{:S(2)}, u32[]{:S(2)}) %collective-permute-start.3) | collective-permute-done | bytes 393248 | tf_op jit(solution)/shard_map/ppermute | solution.py:208
  69.9 1.2 collective-permute-start.9
  71.1 0.1 maximum_bitcast_fusion
  71.2 0.9 collective-permute-start.11
  72.1 0.2 pad_maximum_fusion.1.row_ref
  72.3 3.7 %collective-permute-done.7 = bf16[2,128,768]{2,1,0:T(8,128)(2,1)S(1)} collective-permute-done((bf16[2,128,768]{2,1,0:T(8,128)(2,1)S(1)}, bf16[2,128,768]{2,1,0:T(8,128)(2,1)S(1)}, u32[]{:S(2)}, u32[]{:S(2)}) %collective-permute-start.7) | collective-permute-done | bytes 393248 | tf_op jit(solution)/shard_map/ppermute | solution.py:208
  76.1 0.1 maximum_bitcast_fusion.1
  76.1 8.4 %collective-permute-done.9 = bf16[2,128,768]{2,1,0:T(8,128)(2,1)S(1)} collective-permute-done((bf16[2,128,768]{2,1,0:T(8,128)(2,1)S(1)}, bf16[2,128,768]{2,1,0:T(8,128)(2,1)S(1)}, u32[]{:S(2)}, u32[]{:S(2)}) %collective-permute-start.9) | collective-permute-done | bytes 393248 | tf_op jit(solution)/shard_map/ppermute | solution.py:208
  84.5 0.1 maximum_bitcast_fusion.2
  84.6 5.2 %collective-permute-done.11 = bf16[2,128,768]{2,1,0:T(8,128)(2,1)S(1)} collective-permute-done((bf16[2,128,768]{2,1,0:T(8,128)(2,1)S(1)}, bf16[2,128,768]{2,1,0:T(8,128)(2,1)S(1)}, u32[]{:S(2)}, u32[]{:S(2)}) %collective-permute-start.11) | collective-permute-done | bytes 393248 | tf_op jit(solution)/shard_map/ppermute | solution.py:208
  89.7 0.1 maximum_bitcast_fusion.3
  89.8 0.4 pad_maximum_fusion.col_ref
  90.3 68.8 %shard_map.38 = bf16[4,64,128,256]{3,2,1,0:T(8,128)(2,1)} custom-call(s32[4,2]{1,0:T(4,128)S(1)} %pad_add_fusion.pairs_ref, bf16[4,4,64,768]{3,2,1,0:T(8,128)(2,1)S(1)} %pad_maximum_fusion.1.row_ref, bf16[4,4,128,768]{3,2,1,0:T(8,128)(2,1)S(1)} %pad_maximum_fusion.col_ref, bf16[768,256]{1,0:T(8,128)(2,1)S(1)} %pad_maximum_fusion.3.lags_ref), custom_call_target="tpu_custom_call" | custom-call | flops 13287555072 | bytes 21495808 | tf_op jit(solution)/shard_map/pallas_call | solution.py:183
  (22 shorter events, 0.4 us)
Async XLA Ops:
  2.3 26.6 %collective-permute-start = (bf16[128,4352]{1,0:T(8,128)(2,1)}, bf16[128,4352]{1,0:T(8,128)(2,1)S(1)}, u32[]{:S(2)}, u32[]{:S(2)}) collective-permute-start(bf16[128,4352]{1,0:T(8,128)(2,1)} %slice.17), channel_id=1, source_target_pairs={{16,0},{17,1},{18,2},{19,3},{20,4},{21,5},{22,6},{23,7},{24,8},{25... | collective-permute-start | bytes 3342344 | tf_op jit(solution)/shard_map/ppermute | solution.py:27
  18.4 8.5 %copy-start.1 = (bf16[128,7680]{1,0:T(8,128)(2,1)S(1)}, bf16[128,7680]{1,0:T(8,128)(2,1)}, u32[]{:S(2)}) copy-start(bf16[128,7680]{1,0:T(8,128)(2,1)} %param.3) | copy-start | bytes 5898244
  26.9 4.4 %copy-start = (bf16[7680,768]{1,0:T(8,128)(2,1)S(1)}, bf16[7680,768]{1,0:T(8,128)(2,1)}, u32[]{:S(2)}) copy-start(bf16[7680,768]{1,0:T(8,128)(2,1)} %shard_map.37) | copy-start | bytes 35389444
  34.4 3.2 %copy-start.2 = (s32[1,1,4,2]{2,3,1,0:T(2,128)S(1)}, s32[1,1,4,2]{2,3,1,0:T(2,128)}, u32[]{:S(2)}) copy-start(s32[1,1,4,2]{2,3,1,0:T(2,128)} %param.5) | copy-start | bytes 100
  35.3 12.5 %collective-permute-start.6 = (bf16[2,128,768]{2,1,0:T(8,128)(2,1)S(1)}, bf16[2,128,768]{2,1,0:T(8,128)(2,1)S(1)}, u32[]{:S(2)}, u32[]{:S(2)}) collective-permute-start(bf16[2,128,768]{2,1,0:T(8,128)(2,1)S(1)} %fusion.7), channel_id=1, source_target_pairs={{4,0},{8,4},{12,8},{5,1},{9,5},{13,9},{6,2},{10,6},{14,10},{7,3},{... | collective-permute-start | bytes 1179656 | tf_op jit(solution)/shard_map/ppermute | solution.py:208
  47.7 11.6 %collective-permute-start.8 = (bf16[2,128,768]{2,1,0:T(8,128)(2,1)S(1)}, bf16[2,128,768]{2,1,0:T(8,128)(2,1)S(1)}, u32[]{:S(2)}, u32[]{:S(2)}) collective-permute-start(bf16[2,128,768]{2,1,0:T(8,128)(2,1)S(1)} %collective-permute-done.6), channel_id=1, source_target_pairs={{4,0},{8,4},{5,1},{9,5},{6,2},{10,6},{7,3},{11,7},{20,16},{24,20},... | collective-permute-start | bytes 1179656 | tf_op jit(solution)/shard_map/ppermute | solution.py:208
  50.1 7.8 %collective-permute-start.1 = (bf16[2,64,768]{2,1,0:T(8,128)(2,1)S(1)}, bf16[2,64,768]{2,1,0:T(8,128)(2,1)S(1)}, u32[]{:S(2)}, u32[]{:S(2)}) collective-permute-start(bf16[2,64,768]{2,1,0:T(8,128)(2,1)S(1)} %get-tuple-element.10), channel_id=1, source_target_pairs={{0,16},{16,0},{1,17},{17,1},{2,18},{18,2},{3,19},{19,3},{4,20},{20... | collective-permute-start | bytes 589832 | tf_op jit(solution)/shard_map/ppermute | solution.py:208
  53.3 10.8 %collective-permute-start.5 = (bf16[2,128,768]{2,1,0:T(8,128)(2,1)S(1)}, bf16[2,128,768]{2,1,0:T(8,128)(2,1)S(1)}, u32[]{:S(2)}, u32[]{:S(2)}) collective-permute-start(bf16[2,128,768]{2,1,0:T(8,128)(2,1)S(1)} %fusion.7), channel_id=1, source_target_pairs={{0,16},{16,0},{1,17},{17,1},{2,18},{18,2},{3,19},{19,3},{4,20},{20... | collective-permute-start | bytes 1179656 | tf_op jit(solution)/shard_map/ppermute | solution.py:208
  58.0 11.9 %collective-permute-start.3 = (bf16[4,64,768]{2,1,0:T(8,128)(2,1)S(1)}, bf16[4,64,768]{2,1,0:T(8,128)(2,1)S(1)}, u32[]{:S(2)}, u32[]{:S(2)}) collective-permute-start(bf16[4,64,768]{2,1,0:T(8,128)(2,1)S(1)} %get-tuple-element.8), channel_id=1, source_target_pairs={{0,2},{1,3},{2,0},{3,1},{4,6},{5,7},{6,4},{7,5},{8,10},{9,11},{10,... | collective-permute-start | bytes 1179656 | tf_op jit(solution)/shard_map/ppermute | solution.py:208
  58.4 13.7 %collective-permute-start.2 = (bf16[4,64,768]{2,1,0:T(8,128)(2,1)S(1)}, bf16[4,64,768]{2,1,0:T(8,128)(2,1)S(1)}, u32[]{:S(2)}, u32[]{:S(2)}) collective-permute-start(bf16[4,64,768]{2,1,0:T(8,128)(2,1)S(1)} %get-tuple-element.8), channel_id=1, source_target_pairs={{0,3},{1,0},{2,1},{3,2},{4,7},{5,4},{6,5},{7,6},{8,11},{9,8},{10,9... | collective-permute-start | bytes 1179656 | tf_op jit(solution)/shard_map/ppermute | solution.py:208
  58.4 13.7 %collective-permute-start.4 = (bf16[4,64,768]{2,1,0:T(8,128)(2,1)S(1)}, bf16[4,64,768]{2,1,0:T(8,128)(2,1)S(1)}, u32[]{:S(2)}, u32[]{:S(2)}) collective-permute-start(bf16[4,64,768]{2,1,0:T(8,128)(2,1)S(1)} %get-tuple-element.8), channel_id=1, source_target_pairs={{0,1},{1,2},{2,3},{3,0},{4,5},{5,6},{6,7},{7,4},{8,9},{9,10},{10,1... | collective-permute-start | bytes 1179656 | tf_op jit(solution)/shard_map/ppermute | solution.py:208
  59.3 11.8 %collective-permute-start.10 = (bf16[2,128,768]{2,1,0:T(8,128)(2,1)S(1)}, bf16[2,128,768]{2,1,0:T(8,128)(2,1)S(1)}, u32[]{:S(2)}, u32[]{:S(2)}) collective-permute-start(bf16[2,128,768]{2,1,0:T(8,128)(2,1)S(1)} %collective-permute-done.8), channel_id=1, source_target_pairs={{4,0},{5,1},{6,2},{7,3},{20,16},{21,17},{22,18},{23,19}} | collective-permute-start | bytes 1179656 | tf_op jit(solution)/shard_map/ppermute | solution.py:208
  64.1 12.0 %collective-permute-start.7 = (bf16[2,128,768]{2,1,0:T(8,128)(2,1)S(1)}, bf16[2,128,768]{2,1,0:T(8,128)(2,1)S(1)}, u32[]{:S(2)}, u32[]{:S(2)}) collective-permute-start(bf16[2,128,768]{2,1,0:T(8,128)(2,1)S(1)} %collective-permute-done.6), channel_id=1, source_target_pairs={{0,16},{16,0},{1,17},{17,1},{2,18},{18,2},{3,19},{19,3},{4,20},{20... | collective-permute-start | bytes 1179656 | tf_op jit(solution)/shard_map/ppermute | solution.py:208
  69.9 14.6 %collective-permute-start.9 = (bf16[2,128,768]{2,1,0:T(8,128)(2,1)S(1)}, bf16[2,128,768]{2,1,0:T(8,128)(2,1)S(1)}, u32[]{:S(2)}, u32[]{:S(2)}) collective-permute-start(bf16[2,128,768]{2,1,0:T(8,128)(2,1)S(1)} %collective-permute-done.8), channel_id=1, source_target_pairs={{0,16},{16,0},{1,17},{17,1},{2,18},{18,2},{3,19},{19,3},{4,20},{20... | collective-permute-start | bytes 1179656 | tf_op jit(solution)/shard_map/ppermute | solution.py:208
  71.2 18.6 %collective-permute-start.11 = (bf16[2,128,768]{2,1,0:T(8,128)(2,1)S(1)}, bf16[2,128,768]{2,1,0:T(8,128)(2,1)S(1)}, u32[]{:S(2)}, u32[]{:S(2)}) collective-permute-start(bf16[2,128,768]{2,1,0:T(8,128)(2,1)S(1)} %collective-permute-done.10), channel_id=1, source_target_pairs={{0,16},{16,0},{1,17},{17,1},{2,18},{18,2},{3,19},{19,3},{4,20},{20... | collective-permute-start | bytes 1179656 | tf_op jit(solution)/shard_map/ppermute | solution.py:208

commit v14 on v13

--- a/solution.py
+++ b/solution.py
@@ -109,7 +109,7 @@
     return (spectra * jnp.concatenate([weight, weight], axis=-1)).astype(jnp.bfloat16)
 
 
-ROW_TILE = 16
+ROW_TILE = 32
 J_CHUNK = 64
 F_CHUNK = 128
 

time: 161 us -> 161 us (level)
  transfers between devices with their start and end apart: 12 -> 12, of which waited for: 9 -> 10; matrix products, arithmetic and copies ran while one was open for 8% -> 8% of each run, Pallas kernels for 5% -> 5%
where the time goes in v14:
time: 161 us; the launch traced here: 159 us
  Pallas kernels  77.4 us (48%)
  waiting for transfers between devices  39.7 us (25%)
  starting transfers between devices  16.3 us (10%)
  local copies, waits for them, and re-layouts  9.31 us (6%)
  other arithmetic  9.19 us (6%)
  matrix products  3.76 us (2%)
  between operations  3.56 us (2%)
    pallas_call x1, Pallas kernels, all_pairs(): pl.pallas_call(pair_kernel, grid_spec=grid_spec, out_shape=jax.ShapeDtype...  68.9 us
    ppermute x11, waiting for transfers between devices, exchange(): return lax.ppermute(value, axes, pairs)  37.8 us
    ppermute x11, starting transfers between devices, exchange(): return lax.ppermute(value, axes, pairs)  13.8 us
    pallas_call x1, Pallas kernels, forward_table(): pl.pallas_call(table_kernel, grid=(n_coarse // TABLE_Q,), in_specs=[pl.Bl...  8.49 us
    sin x1, other arithmetic, forward_table(): high_sin = jnp.sin(high_angle).reshape(n_coarse, 1, NF)  4.19 us
  transfers between devices with their start and end apart: 12, of which 10 were waited for; matrix products, arithmetic and copies ran while one was open for 8% of the time, Pallas kernels for 5%

profile of v14, /device:TPU:14, one launch (start us, length us, event | category | flops | bytes accessed | tf_op | source)
XLA Modules:
  0.0 159.1 jit_solution(6361458970328598752)
XLA Ops:
  0.0 2.3 %slice.17 = bf16[128,4352]{1,0:T(8,128)(2,1)} slice(bf16[128,7680]{1,0:T(8,128)(2,1)} %param.3), slice={[0:128], [0:4352]} | slice | bytes 2228224 | tf_op jit(solution)/shard_map/slice | solution.py:229
  2.3 2.5 %collective-permute-start = (bf16[128,4352]{1,0:T(8,128)(2,1)}, bf16[128,4352]{1,0:T(8,128)(2,1)S(1)}, u32[]{:S(2)}, u32[]{:S(2)}) collective-permute-start(bf16[128,4352]{1,0:T(8,128)(2,1)} %slice.17), channel_id=1, source_target_pairs={{16,0},{17,1},{18,2},{19,3},{20,4},{21,5},{22,6},{23,7},{24,8},{25... | collective-permute-start | bytes 3342344 | tf_op jit(solution)/shard_map/ppermute | solution.py:27
  5.0 1.6 fusion.21
  6.5 4.2 %fusion.28 = (f32[60,1,384]{2,1,0:T(1,128)}, f32[60,1,384]{2,1,0:T(1,128)}) fusion(s32[384]{0:T(512)S(1)} %iota_add_fusion, s32[60]{0:T(128)S(1)} %iota_multiply_fusion), kind=kLoop, calls=%fused_computation.48 | loop fusion | flops 207360 | bytes 186096 | tf_op jit(solution)/shard_map/sin | solution.py:61
  10.8 1.4 fusion.39
  15.5 0.7 broadcast_in_dim.9.start_sin_ref
  16.3 0.7 broadcast_in_dim.8.start_cos_ref
  17.0 0.7 broadcast_in_dim.11.step_sin_ref
  17.7 0.7 broadcast_in_dim.10.step_cos_ref
  18.4 8.5 %shard_map.37 = bf16[7680,768]{1,0:T(8,128)(2,1)} custom-call(f32[60,1,384]{2,1,0:T(1,128)} %get-tuple-element.14.high_cos_ref, f32[60,1,384]{2,1,0:T(1,128)} %get-tuple-element.13.high_sin_ref, f32[128,384]{1,0:T(8,128)} %get-tuple-element.16.low_cos_ref, f32[128,384]{1,0:T(8,128)} %get-tuple-element.15.low_sin_ref, ...), custom_call_target="tpu_custom_call" | custom-call | tf_op jit(solution)/shard_map/pallas_call | solution.py:69
  26.9 0.1 constant_dynamic-update-slice_fusion.1
  27.0 1.9 %collective-permute-done = bf16[128,4352]{1,0:T(8,128)(2,1)S(1)} collective-permute-done((bf16[128,4352]{1,0:T(8,128)(2,1)}, bf16[128,4352]{1,0:T(8,128)(2,1)S(1)}, u32[]{:S(2)}, u32[]{:S(2)}) %collective-permute-start) | collective-permute-done | bytes 1114144 | tf_op jit(solution)/shard_map/ppermute | solution.py:27
  28.9 0.1 constant_dynamic-update-slice_fusion
  29.0 1.6 %constant_dynamic-slice_fusion.3 = (bf16[128,7680]{1,0:T(8,128)(2,1)S(1)}, bf16[128,7680]{1,0:T(8,128)(2,1)S(1)}) fusion(bf16[128,12032]{1,0:T(8,128)(2,1)S(1)} %constant_dynamic-update-slice_fusion, s32[]{:T(128)S(6)} %select_n.81, s32[]{:T(128)S(6)} %select_n.83), kind=kLoop, calls=%fused_computation.61 | loop fusion | bytes 7864328 | tf_op jit(solution)/shard_map/dynamic_slice | solution.py:234
  30.6 0.7 copy-done
  31.2 3.2 %fusion = f32[256,768]{1,0:T(8,128)S(1)} fusion(bf16[7680,768]{1,0:T(8,128)(2,1)S(1)} %copy-done, bf16[128,7680]{1,0:T(8,128)(2,1)S(1)} %get-tuple-element.6, bf16[128,7680]{1,0:T(8,128)(2,1)S(1)} %get-tuple-element.5), kind=kOutput, calls=%fused_computation | convolution fusion | flops 3027763200 | bytes 16515072 | tf_op jit(solution)/shard_map/dot_general | solution.py:238
  34.5 0.1 fusion.26
  34.6 0.6 fusion.6
  35.2 0.1 fusion.7
  35.3 2.4 %collective-permute-start.6 = (bf16[2,128,768]{2,1,0:T(8,128)(2,1)S(1)}, bf16[2,128,768]{2,1,0:T(8,128)(2,1)S(1)}, u32[]{:S(2)}, u32[]{:S(2)}) collective-permute-start(bf16[2,128,768]{2,1,0:T(8,128)(2,1)S(1)} %fusion.7), channel_id=1, source_target_pairs={{4,0},{8,4},{12,8},{5,1},{9,5},{13,9},{6,2},{10,6},{14,10},{7,3},{... | collective-permute-start | bytes 1179656 | tf_op jit(solution)/shard_map/ppermute | solution.py:208
  37.7 0.1 copy.6
  37.8 0.1 copy.7
  37.9 9.9 %collective-permute-done.6 = bf16[2,128,768]{2,1,0:T(8,128)(2,1)S(1)} collective-permute-done((bf16[2,128,768]{2,1,0:T(8,128)(2,1)S(1)}, bf16[2,128,768]{2,1,0:T(8,128)(2,1)S(1)}, u32[]{:S(2)}, u32[]{:S(2)}) %collective-permute-start.6) | collective-permute-done | bytes 393248 | tf_op jit(solution)/shard_map/ppermute | solution.py:208
  47.7 2.3 %collective-permute-start.8 = (bf16[2,128,768]{2,1,0:T(8,128)(2,1)S(1)}, bf16[2,128,768]{2,1,0:T(8,128)(2,1)S(1)}, u32[]{:S(2)}, u32[]{:S(2)}) collective-permute-start(bf16[2,128,768]{2,1,0:T(8,128)(2,1)S(1)} %collective-permute-done.6), channel_id=1, source_target_pairs={{4,0},{8,4},{5,1},{9,5},{6,2},{10,6},{7,3},{11,7},{20,16},{24,20},... | collective-permute-start | bytes 1179656 | tf_op jit(solution)/shard_map/ppermute | solution.py:208
  50.1 1.2 collective-permute-start.1
  51.3 1.9 %multiply_convert_fusion.1 = (bf16[384,256]{1,0:T(8,128)(2,1)S(1)}, bf16[384,256]{1,0:T(8,128)(2,1)S(1)}) fusion(s32[256]{0:T(256)S(1)} %and_select_fusion.1, s32[384]{0:T(512)S(1)} %iota_add_fusion), kind=kLoop, calls=%fused_computation.27 | loop fusion | flops 1376256 | bytes 395776 | tf_op jit(solution)/shard_map/convert
  53.3 0.9 collective-permute-start.5
  54.2 3.7 %collective-permute-done.1 = bf16[2,64,768]{2,1,0:T(8,128)(2,1)S(1)} collective-permute-done((bf16[2,64,768]{2,1,0:T(8,128)(2,1)S(1)}, bf16[2,64,768]{2,1,0:T(8,128)(2,1)S(1)}, u32[]{:S(2)}, u32[]{:S(2)}) %collective-permute-start.1) | collective-permute-done | bytes 196640 | tf_op jit(solution)/shard_map/ppermute | solution.py:208
  58.0 0.4 collective-permute-start.3
  58.4 0.5 collective-permute-start.4
  58.9 0.4 collective-permute-done.8
  59.3 2.5 %collective-permute-start.10 = (bf16[2,128,768]{2,1,0:T(8,128)(2,1)S(1)}, bf16[2,128,768]{2,1,0:T(8,128)(2,1)S(1)}, u32[]{:S(2)}, u32[]{:S(2)}) collective-permute-start(bf16[2,128,768]{2,1,0:T(8,128)(2,1)S(1)} %collective-permute-done.8), channel_id=1, source_target_pairs={{4,0},{5,1},{6,2},{7,3},{20,16},{21,17},{22,18},{23,19}} | collective-permute-start | bytes 1179656 | tf_op jit(solution)/shard_map/ppermute | solution.py:208
  61.9 2.1 %collective-permute-done.5 = bf16[2,128,768]{2,1,0:T(8,128)(2,1)S(1)} collective-permute-done((bf16[2,128,768]{2,1,0:T(8,128)(2,1)S(1)}, bf16[2,128,768]{2,1,0:T(8,128)(2,1)S(1)}, u32[]{:S(2)}, u32[]{:S(2)}) %collective-permute-start.5) | collective-permute-done | bytes 393248 | tf_op jit(solution)/shard_map/ppermute | solution.py:208
  64.0 1.4 collective-permute-start.7
  65.4 0.1 pad_add_fusion.pairs_ref
  65.5 4.4 %collective-permute-done.3 = bf16[4,64,768]{2,1,0:T(8,128)(2,1)S(1)} collective-permute-done((bf16[4,64,768]{2,1,0:T(8,128)(2,1)S(1)}, bf16[4,64,768]{2,1,0:T(8,128)(2,1)S(1)}, u32[]{:S(2)}, u32[]{:S(2)}) %collective-permute-start.3) | collective-permute-done | bytes 393248 | tf_op jit(solution)/shard_map/ppermute | solution.py:208
  69.9 1.1 collective-permute-start.9
  71.0 0.1 maximum_bitcast_fusion
  71.1 1.0 collective-permute-start.11
  72.1 0.2 pad_maximum_fusion.1.row_ref
  72.3 3.7 %collective-permute-done.7 = bf16[2,128,768]{2,1,0:T(8,128)(2,1)S(1)} collective-permute-done((bf16[2,128,768]{2,1,0:T(8,128)(2,1)S(1)}, bf16[2,128,768]{2,1,0:T(8,128)(2,1)S(1)}, u32[]{:S(2)}, u32[]{:S(2)}) %collective-permute-start.7) | collective-permute-done | bytes 393248 | tf_op jit(solution)/shard_map/ppermute | solution.py:208
  76.0 0.1 maximum_bitcast_fusion.1
  76.1 8.4 %collective-permute-done.9 = bf16[2,128,768]{2,1,0:T(8,128)(2,1)S(1)} collective-permute-done((bf16[2,128,768]{2,1,0:T(8,128)(2,1)S(1)}, bf16[2,128,768]{2,1,0:T(8,128)(2,1)S(1)}, u32[]{:S(2)}, u32[]{:S(2)}) %collective-permute-start.9) | collective-permute-done | bytes 393248 | tf_op jit(solution)/shard_map/ppermute | solution.py:208
  84.4 0.1 maximum_bitcast_fusion.2
  84.5 5.2 %collective-permute-done.11 = bf16[2,128,768]{2,1,0:T(8,128)(2,1)S(1)} collective-permute-done((bf16[2,128,768]{2,1,0:T(8,128)(2,1)S(1)}, bf16[2,128,768]{2,1,0:T(8,128)(2,1)S(1)}, u32[]{:S(2)}, u32[]{:S(2)}) %collective-permute-start.11) | collective-permute-done | bytes 393248 | tf_op jit(solution)/shard_map/ppermute | solution.py:208
  89.7 0.1 maximum_bitcast_fusion.3
  89.8 0.4 pad_maximum_fusion.col_ref
  90.3 68.9 %shard_map.38 = bf16[4,64,128,256]{3,2,1,0:T(8,128)(2,1)} custom-call(s32[4,2]{1,0:T(4,128)S(1)} %pad_add_fusion.pairs_ref, bf16[4,4,64,768]{3,2,1,0:T(8,128)(2,1)S(1)} %pad_maximum_fusion.1.row_ref, bf16[4,4,128,768]{3,2,1,0:T(8,128)(2,1)S(1)} %pad_maximum_fusion.col_ref, bf16[768,256]{1,0:T(8,128)(2,1)S(1)} %pad_maximum_fusion.3.lags_ref), custom_call_target="tpu_custom_call" | custom-call | flops 13287555072 | bytes 21495808 | tf_op jit(solution)/shard_map/pallas_call | solution.py:183
  (22 shorter events, 0.4 us)
Async XLA Ops:
  2.3 26.6 %collective-permute-start = (bf16[128,4352]{1,0:T(8,128)(2,1)}, bf16[128,4352]{1,0:T(8,128)(2,1)S(1)}, u32[]{:S(2)}, u32[]{:S(2)}) collective-permute-start(bf16[128,4352]{1,0:T(8,128)(2,1)} %slice.17), channel_id=1, source_target_pairs={{16,0},{17,1},{18,2},{19,3},{20,4},{21,5},{22,6},{23,7},{24,8},{25... | collective-permute-start | bytes 3342344 | tf_op jit(solution)/shard_map/ppermute | solution.py:27
  18.4 8.5 %copy-start.1 = (bf16[128,7680]{1,0:T(8,128)(2,1)S(1)}, bf16[128,7680]{1,0:T(8,128)(2,1)}, u32[]{:S(2)}) copy-start(bf16[128,7680]{1,0:T(8,128)(2,1)} %param.3) | copy-start | bytes 5898244
  26.9 4.4 %copy-start = (bf16[7680,768]{1,0:T(8,128)(2,1)S(1)}, bf16[7680,768]{1,0:T(8,128)(2,1)}, u32[]{:S(2)}) copy-start(bf16[7680,768]{1,0:T(8,128)(2,1)} %shard_map.37) | copy-start | bytes 35389444
  34.4 3.2 %copy-start.2 = (s32[1,1,4,2]{2,3,1,0:T(2,128)S(1)}, s32[1,1,4,2]{2,3,1,0:T(2,128)}, u32[]{:S(2)}) copy-start(s32[1,1,4,2]{2,3,1,0:T(2,128)} %param.5) | copy-start | bytes 100
  35.3 12.5 %collective-permute-start.6 = (bf16[2,128,768]{2,1,0:T(8,128)(2,1)S(1)}, bf16[2,128,768]{2,1,0:T(8,128)(2,1)S(1)}, u32[]{:S(2)}, u32[]{:S(2)}) collective-permute-start(bf16[2,128,768]{2,1,0:T(8,128)(2,1)S(1)} %fusion.7), channel_id=1, source_target_pairs={{4,0},{8,4},{12,8},{5,1},{9,5},{13,9},{6,2},{10,6},{14,10},{7,3},{... | collective-permute-start | bytes 1179656 | tf_op jit(solution)/shard_map/ppermute | solution.py:208
  47.7 11.6 %collective-permute-start.8 = (bf16[2,128,768]{2,1,0:T(8,128)(2,1)S(1)}, bf16[2,128,768]{2,1,0:T(8,128)(2,1)S(1)}, u32[]{:S(2)}, u32[]{:S(2)}) collective-permute-start(bf16[2,128,768]{2,1,0:T(8,128)(2,1)S(1)} %collective-permute-done.6), channel_id=1, source_target_pairs={{4,0},{8,4},{5,1},{9,5},{6,2},{10,6},{7,3},{11,7},{20,16},{24,20},... | collective-permute-start | bytes 1179656 | tf_op jit(solution)/shard_map/ppermute | solution.py:208
  50.1 7.8 %collective-permute-start.1 = (bf16[2,64,768]{2,1,0:T(8,128)(2,1)S(1)}, bf16[2,64,768]{2,1,0:T(8,128)(2,1)S(1)}, u32[]{:S(2)}, u32[]{:S(2)}) collective-permute-start(bf16[2,64,768]{2,1,0:T(8,128)(2,1)S(1)} %get-tuple-element.10), channel_id=1, source_target_pairs={{0,16},{16,0},{1,17},{17,1},{2,18},{18,2},{3,19},{19,3},{4,20},{20... | collective-permute-start | bytes 589832 | tf_op jit(solution)/shard_map/ppermute | solution.py:208
  53.3 10.8 %collective-permute-start.5 = (bf16[2,128,768]{2,1,0:T(8,128)(2,1)S(1)}, bf16[2,128,768]{2,1,0:T(8,128)(2,1)S(1)}, u32[]{:S(2)}, u32[]{:S(2)}) collective-permute-start(bf16[2,128,768]{2,1,0:T(8,128)(2,1)S(1)} %fusion.7), channel_id=1, source_target_pairs={{0,16},{16,0},{1,17},{17,1},{2,18},{18,2},{3,19},{19,3},{4,20},{20... | collective-permute-start | bytes 1179656 | tf_op jit(solution)/shard_map/ppermute | solution.py:208
  58.0 11.9 %collective-permute-start.3 = (bf16[4,64,768]{2,1,0:T(8,128)(2,1)S(1)}, bf16[4,64,768]{2,1,0:T(8,128)(2,1)S(1)}, u32[]{:S(2)}, u32[]{:S(2)}) collective-permute-start(bf16[4,64,768]{2,1,0:T(8,128)(2,1)S(1)} %get-tuple-element.8), channel_id=1, source_target_pairs={{0,2},{1,3},{2,0},{3,1},{4,6},{5,7},{6,4},{7,5},{8,10},{9,11},{10,... | collective-permute-start | bytes 1179656 | tf_op jit(solution)/shard_map/ppermute | solution.py:208
  58.4 13.7 %collective-permute-start.2 = (bf16[4,64,768]{2,1,0:T(8,128)(2,1)S(1)}, bf16[4,64,768]{2,1,0:T(8,128)(2,1)S(1)}, u32[]{:S(2)}, u32[]{:S(2)}) collective-permute-start(bf16[4,64,768]{2,1,0:T(8,128)(2,1)S(1)} %get-tuple-element.8), channel_id=1, source_target_pairs={{0,3},{1,0},{2,1},{3,2},{4,7},{5,4},{6,5},{7,6},{8,11},{9,8},{10,9... | collective-permute-start | bytes 1179656 | tf_op jit(solution)/shard_map/ppermute | solution.py:208
  58.4 13.7 %collective-permute-start.4 = (bf16[4,64,768]{2,1,0:T(8,128)(2,1)S(1)}, bf16[4,64,768]{2,1,0:T(8,128)(2,1)S(1)}, u32[]{:S(2)}, u32[]{:S(2)}) collective-permute-start(bf16[4,64,768]{2,1,0:T(8,128)(2,1)S(1)} %get-tuple-element.8), channel_id=1, source_target_pairs={{0,1},{1,2},{2,3},{3,0},{4,5},{5,6},{6,7},{7,4},{8,9},{9,10},{10,1... | collective-permute-start | bytes 1179656 | tf_op jit(solution)/shard_map/ppermute | solution.py:208
  59.3 11.7 %collective-permute-start.10 = (bf16[2,128,768]{2,1,0:T(8,128)(2,1)S(1)}, bf16[2,128,768]{2,1,0:T(8,128)(2,1)S(1)}, u32[]{:S(2)}, u32[]{:S(2)}) collective-permute-start(bf16[2,128,768]{2,1,0:T(8,128)(2,1)S(1)} %collective-permute-done.8), channel_id=1, source_target_pairs={{4,0},{5,1},{6,2},{7,3},{20,16},{21,17},{22,18},{23,19}} | collective-permute-start | bytes 1179656 | tf_op jit(solution)/shard_map/ppermute | solution.py:208
  64.0 12.0 %collective-permute-start.7 = (bf16[2,128,768]{2,1,0:T(8,128)(2,1)S(1)}, bf16[2,128,768]{2,1,0:T(8,128)(2,1)S(1)}, u32[]{:S(2)}, u32[]{:S(2)}) collective-permute-start(bf16[2,128,768]{2,1,0:T(8,128)(2,1)S(1)} %collective-permute-done.6), channel_id=1, source_target_pairs={{0,16},{16,0},{1,17},{17,1},{2,18},{18,2},{3,19},{19,3},{4,20},{20... | collective-permute-start | bytes 1179656 | tf_op jit(solution)/shard_map/ppermute | solution.py:208
  69.9 14.5 %collective-permute-start.9 = (bf16[2,128,768]{2,1,0:T(8,128)(2,1)S(1)}, bf16[2,128,768]{2,1,0:T(8,128)(2,1)S(1)}, u32[]{:S(2)}, u32[]{:S(2)}) collective-permute-start(bf16[2,128,768]{2,1,0:T(8,128)(2,1)S(1)} %collective-permute-done.8), channel_id=1, source_target_pairs={{0,16},{16,0},{1,17},{17,1},{2,18},{18,2},{3,19},{19,3},{4,20},{20... | collective-permute-start | bytes 1179656 | tf_op jit(solution)/shard_map/ppermute | solution.py:208
  71.1 18.6 %collective-permute-start.11 = (bf16[2,128,768]{2,1,0:T(8,128)(2,1)S(1)}, bf16[2,128,768]{2,1,0:T(8,128)(2,1)S(1)}, u32[]{:S(2)}, u32[]{:S(2)}) collective-permute-start(bf16[2,128,768]{2,1,0:T(8,128)(2,1)S(1)} %collective-permute-done.10), channel_id=1, source_target_pairs={{0,16},{16,0},{1,17},{17,1},{2,18},{18,2},{3,19},{19,3},{4,20},{20... | collective-permute-start | bytes 1179656 | tf_op jit(solution)/shard_map/ppermute | solution.py:208

commit v15 on v13

--- a/solution.py
+++ b/solution.py
@@ -141,6 +141,7 @@
                 fr = pl.ds(fc * F_CHUNK, F_CHUNK)
                 fi = pl.ds(NF + fc * F_CHUNK, F_CHUNK)
                 fs = pl.ds(2 * NF + fc * F_CHUNK, F_CHUNK)
+                acc_both = jnp.zeros((J_CHUNK, F_CHUNK), jnp.float32)
                 acc_re = jnp.zeros((J_CHUNK, F_CHUNK), jnp.float32)
                 acc_im = jnp.zeros((J_CHUNK, F_CHUNK), jnp.float32)
                 for w in range(windows):
@@ -150,9 +151,11 @@
                     yr = col32_ref[w, js, fr]
                     yd = col32_ref[w, js, fi]
                     ys = col32_ref[w, js, fs]
-                    both = yr * xs
-                    acc_re = acc_re + (both - xi * yd)
-                    acc_im = acc_im + (both - xr * ys)
+                    acc_both = acc_both + yr * xs
+                    acc_re = acc_re + xi * yd
+                    acc_im = acc_im + xr * ys
+                acc_re = acc_both - acc_re
+                acc_im = acc_both - acc_im
                 rows = pl.ds(i * cols + jc * J_CHUNK, J_CHUNK)
                 cross_ref[rows, fr] = acc_re.astype(jnp.bfloat16)
                 cross_ref[rows, fi] = acc_im.astype(jnp.bfloat16)

time: 161 us -> 156 us (0.969)
  Pallas kernels: 77.3 us -> 71.6 us
    pallas_call x1, Pallas kernels: 68.8 us -> 63.1 us  [all_pairs(): pl.pallas_call(pair_kernel, grid_spec=grid_spec, out_shape=jax.ShapeDtype...]
  transfers between devices with their start and end apart: 12 -> 12, of which waited for: 9 -> 9; matrix products, arithmetic and copies ran while one was open for 8% -> 9% of each run, Pallas kernels for 5% -> 6%
where the time goes in v15:
time: 156 us; the launch traced here: 153 us
  Pallas kernels  71.6 us (46%)
  waiting for transfers between devices  39.7 us (25%)
  starting transfers between devices  16.3 us (10%)
  local copies, waits for them, and re-layouts  9.31 us (6%)
  other arithmetic  9.19 us (6%)
  matrix products  3.76 us (2%)
  between operations  3.56 us (2%)
    pallas_call x1, Pallas kernels, all_pairs(): pl.pallas_call(pair_kernel, grid_spec=grid_spec, out_shape=jax.ShapeDtype...  63.1 us
    ppermute x11, waiting for transfers between devices, exchange(): return lax.ppermute(value, axes, pairs)  37.8 us
    ppermute x11, starting transfers between devices, exchange(): return lax.ppermute(value, axes, pairs)  13.8 us
    pallas_call x1, Pallas kernels, forward_table(): pl.pallas_call(table_kernel, grid=(n_coarse // TABLE_Q,), in_specs=[pl.Bl...  8.49 us
    sin x1, other arithmetic, forward_table(): high_sin = jnp.sin(high_angle).reshape(n_coarse, 1, NF)  4.19 us
    dot_general x1, matrix products, on_device(): spectra = jnp.dot(stacked, dft_table, preferred_element_type=jnp.float32)  3.2 us
  transfers between devices with their start and end apart: 12, of which 9 were waited for; matrix products, arithmetic and copies ran while one was open for 9% of the time, Pallas kernels for 6%

profile of v15, /device:TPU:14, one launch (start us, length us, event | category | flops | bytes accessed | tf_op | source)
XLA Modules:
  0.0 153.4 jit_solution(7923706434242825555)
XLA Ops:
  0.0 2.3 %slice.17 = bf16[128,4352]{1,0:T(8,128)(2,1)} slice(bf16[128,7680]{1,0:T(8,128)(2,1)} %param.3), slice={[0:128], [0:4352]} | slice | bytes 2228224 | tf_op jit(solution)/shard_map/slice | solution.py:232
  2.3 2.5 %collective-permute-start = (bf16[128,4352]{1,0:T(8,128)(2,1)}, bf16[128,4352]{1,0:T(8,128)(2,1)S(1)}, u32[]{:S(2)}, u32[]{:S(2)}) collective-permute-start(bf16[128,4352]{1,0:T(8,128)(2,1)} %slice.17), channel_id=1, source_target_pairs={{16,0},{17,1},{18,2},{19,3},{20,4},{21,5},{22,6},{23,7},{24,8},{25... | collective-permute-start | bytes 3342344 | tf_op jit(solution)/shard_map/ppermute | solution.py:27
  5.0 1.6 %fusion.21 = (f32[128,384]{1,0:T(8,128)}, f32[128,384]{1,0:T(8,128)}) fusion(s32[384]{0:T(512)S(1)} %iota_add_fusion), kind=kLoop, calls=%fused_computation.40 | loop fusion | flops 442368 | bytes 394752 | tf_op jit(solution)/shard_map/sin | solution.py:62
  6.5 4.2 %fusion.28 = (f32[60,1,384]{2,1,0:T(1,128)}, f32[60,1,384]{2,1,0:T(1,128)}) fusion(s32[384]{0:T(512)S(1)} %iota_add_fusion, s32[60]{0:T(128)S(1)} %iota_multiply_fusion), kind=kLoop, calls=%fused_computation.48 | loop fusion | flops 207360 | bytes 186096 | tf_op jit(solution)/shard_map/sin | solution.py:61
  10.8 1.4 fusion.39
  15.5 0.7 broadcast_in_dim.9.start_sin_ref
  16.3 0.7 broadcast_in_dim.8.start_cos_ref
  17.0 0.7 broadcast_in_dim.11.step_sin_ref
  17.7 0.7 broadcast_in_dim.10.step_cos_ref
  18.4 8.5 %shard_map.37 = bf16[7680,768]{1,0:T(8,128)(2,1)} custom-call(f32[60,1,384]{2,1,0:T(1,128)} %get-tuple-element.14.high_cos_ref, f32[60,1,384]{2,1,0:T(1,128)} %get-tuple-element.13.high_sin_ref, f32[128,384]{1,0:T(8,128)} %get-tuple-element.16.low_cos_ref, f32[128,384]{1,0:T(8,128)} %get-tuple-element.15.low_sin_ref, ...), custom_call_target="tpu_custom_call" | custom-call | tf_op jit(solution)/shard_map/pallas_call | solution.py:69
  26.9 0.1 constant_dynamic-update-slice_fusion.1
  27.0 1.9 %collective-permute-done = bf16[128,4352]{1,0:T(8,128)(2,1)S(1)} collective-permute-done((bf16[128,4352]{1,0:T(8,128)(2,1)}, bf16[128,4352]{1,0:T(8,128)(2,1)S(1)}, u32[]{:S(2)}, u32[]{:S(2)}) %collective-permute-start) | collective-permute-done | bytes 1114144 | tf_op jit(solution)/shard_map/ppermute | solution.py:27
  28.9 0.1 constant_dynamic-update-slice_fusion
  29.0 1.6 %constant_dynamic-slice_fusion.3 = (bf16[128,7680]{1,0:T(8,128)(2,1)S(1)}, bf16[128,7680]{1,0:T(8,128)(2,1)S(1)}) fusion(bf16[128,12032]{1,0:T(8,128)(2,1)S(1)} %constant_dynamic-update-slice_fusion, s32[]{:T(128)S(6)} %select_n.81, s32[]{:T(128)S(6)} %select_n.83), kind=kLoop, calls=%fused_computation.61 | loop fusion | bytes 7864328 | tf_op jit(solution)/shard_map/dynamic_slice | solution.py:237
  30.6 0.6 copy-done
  31.2 3.2 %fusion = f32[256,768]{1,0:T(8,128)S(1)} fusion(bf16[7680,768]{1,0:T(8,128)(2,1)S(1)} %copy-done, bf16[128,7680]{1,0:T(8,128)(2,1)S(1)} %get-tuple-element.6, bf16[128,7680]{1,0:T(8,128)(2,1)S(1)} %get-tuple-element.5), kind=kOutput, calls=%fused_computation | convolution fusion | flops 3027763200 | bytes 16515072 | tf_op jit(solution)/shard_map/dot_general | solution.py:241
  34.5 0.1 fusion.26
  34.6 0.6 fusion.6
  35.2 0.1 fusion.7
  35.3 2.4 %collective-permute-start.6 = (bf16[2,128,768]{2,1,0:T(8,128)(2,1)S(1)}, bf16[2,128,768]{2,1,0:T(8,128)(2,1)S(1)}, u32[]{:S(2)}, u32[]{:S(2)}) collective-permute-start(bf16[2,128,768]{2,1,0:T(8,128)(2,1)S(1)} %fusion.7), channel_id=1, source_target_pairs={{4,0},{8,4},{12,8},{5,1},{9,5},{13,9},{6,2},{10,6},{14,10},{7,3},{... | collective-permute-start | bytes 1179656 | tf_op jit(solution)/shard_map/ppermute | solution.py:211
  37.7 0.1 copy.6
  37.8 0.1 copy.7
  37.9 9.9 %collective-permute-done.6 = bf16[2,128,768]{2,1,0:T(8,128)(2,1)S(1)} collective-permute-done((bf16[2,128,768]{2,1,0:T(8,128)(2,1)S(1)}, bf16[2,128,768]{2,1,0:T(8,128)(2,1)S(1)}, u32[]{:S(2)}, u32[]{:S(2)}) %collective-permute-start.6) | collective-permute-done | bytes 393248 | tf_op jit(solution)/shard_map/ppermute | solution.py:211
  47.7 2.3 %collective-permute-start.8 = (bf16[2,128,768]{2,1,0:T(8,128)(2,1)S(1)}, bf16[2,128,768]{2,1,0:T(8,128)(2,1)S(1)}, u32[]{:S(2)}, u32[]{:S(2)}) collective-permute-start(bf16[2,128,768]{2,1,0:T(8,128)(2,1)S(1)} %collective-permute-done.6), channel_id=1, source_target_pairs={{4,0},{8,4},{5,1},{9,5},{6,2},{10,6},{7,3},{11,7},{20,16},{24,20},... | collective-permute-start | bytes 1179656 | tf_op jit(solution)/shard_map/ppermute | solution.py:211
  50.1 1.2 collective-permute-start.1
  51.4 1.9 %multiply_convert_fusion.1 = (bf16[384,256]{1,0:T(8,128)(2,1)S(1)}, bf16[384,256]{1,0:T(8,128)(2,1)S(1)}) fusion(s32[256]{0:T(256)S(1)} %and_select_fusion.1, s32[384]{0:T(512)S(1)} %iota_add_fusion), kind=kLoop, calls=%fused_computation.27 | loop fusion | flops 1376256 | bytes 395776 | tf_op jit(solution)/shard_map/convert
  53.3 0.9 collective-permute-start.5
  54.2 3.7 %collective-permute-done.1 = bf16[2,64,768]{2,1,0:T(8,128)(2,1)S(1)} collective-permute-done((bf16[2,64,768]{2,1,0:T(8,128)(2,1)S(1)}, bf16[2,64,768]{2,1,0:T(8,128)(2,1)S(1)}, u32[]{:S(2)}, u32[]{:S(2)}) %collective-permute-start.1) | collective-permute-done | bytes 196640 | tf_op jit(solution)/shard_map/ppermute | solution.py:211
  58.0 0.4 collective-permute-start.3
  58.4 0.5 collective-permute-start.4
  58.9 0.4 collective-permute-done.8
  59.3 2.5 %collective-permute-start.10 = (bf16[2,128,768]{2,1,0:T(8,128)(2,1)S(1)}, bf16[2,128,768]{2,1,0:T(8,128)(2,1)S(1)}, u32[]{:S(2)}, u32[]{:S(2)}) collective-permute-start(bf16[2,128,768]{2,1,0:T(8,128)(2,1)S(1)} %collective-permute-done.8), channel_id=1, source_target_pairs={{4,0},{5,1},{6,2},{7,3},{20,16},{21,17},{22,18},{23,19}} | collective-permute-start | bytes 1179656 | tf_op jit(solution)/shard_map/ppermute | solution.py:211
  61.9 2.1 %collective-permute-done.5 = bf16[2,128,768]{2,1,0:T(8,128)(2,1)S(1)} collective-permute-done((bf16[2,128,768]{2,1,0:T(8,128)(2,1)S(1)}, bf16[2,128,768]{2,1,0:T(8,128)(2,1)S(1)}, u32[]{:S(2)}, u32[]{:S(2)}) %collective-permute-start.5) | collective-permute-done | bytes 393248 | tf_op jit(solution)/shard_map/ppermute | solution.py:211
  64.1 1.4 collective-permute-start.7
  65.5 0.1 pad_add_fusion.pairs_ref
  65.5 4.4 %collective-permute-done.3 = bf16[4,64,768]{2,1,0:T(8,128)(2,1)S(1)} collective-permute-done((bf16[4,64,768]{2,1,0:T(8,128)(2,1)S(1)}, bf16[4,64,768]{2,1,0:T(8,128)(2,1)S(1)}, u32[]{:S(2)}, u32[]{:S(2)}) %collective-permute-start.3) | collective-permute-done | bytes 393248 | tf_op jit(solution)/shard_map/ppermute | solution.py:211
  69.9 1.2 collective-permute-start.9
  71.1 0.1 maximum_bitcast_fusion
  71.2 0.9 collective-permute-start.11
  72.1 0.2 pad_maximum_fusion.1.row_ref
  72.3 3.7 %collective-permute-done.7 = bf16[2,128,768]{2,1,0:T(8,128)(2,1)S(1)} collective-permute-done((bf16[2,128,768]{2,1,0:T(8,128)(2,1)S(1)}, bf16[2,128,768]{2,1,0:T(8,128)(2,1)S(1)}, u32[]{:S(2)}, u32[]{:S(2)}) %collective-permute-start.7) | collective-permute-done | bytes 393248 | tf_op jit(solution)/shard_map/ppermute | solution.py:211
  76.1 0.1 maximum_bitcast_fusion.1
  76.1 8.4 %collective-permute-done.9 = bf16[2,128,768]{2,1,0:T(8,128)(2,1)S(1)} collective-permute-done((bf16[2,128,768]{2,1,0:T(8,128)(2,1)S(1)}, bf16[2,128,768]{2,1,0:T(8,128)(2,1)S(1)}, u32[]{:S(2)}, u32[]{:S(2)}) %collective-permute-start.9) | collective-permute-done | bytes 393248 | tf_op jit(solution)/shard_map/ppermute | solution.py:211
  84.5 0.1 maximum_bitcast_fusion.2
  84.6 5.2 %collective-permute-done.11 = bf16[2,128,768]{2,1,0:T(8,128)(2,1)S(1)} collective-permute-done((bf16[2,128,768]{2,1,0:T(8,128)(2,1)S(1)}, bf16[2,128,768]{2,1,0:T(8,128)(2,1)S(1)}, u32[]{:S(2)}, u32[]{:S(2)}) %collective-permute-start.11) | collective-permute-done | bytes 393248 | tf_op jit(solution)/shard_map/ppermute | solution.py:211
  89.7 0.1 maximum_bitcast_fusion.3
  89.8 0.4 pad_maximum_fusion.col_ref
  90.3 63.1 %shard_map.38 = bf16[4,64,128,256]{3,2,1,0:T(8,128)(2,1)} custom-call(s32[4,2]{1,0:T(4,128)S(1)} %pad_add_fusion.pairs_ref, bf16[4,4,64,768]{3,2,1,0:T(8,128)(2,1)S(1)} %pad_maximum_fusion.1.row_ref, bf16[4,4,128,768]{3,2,1,0:T(8,128)(2,1)S(1)} %pad_maximum_fusion.col_ref, bf16[768,256]{1,0:T(8,128)(2,1)S(1)} %pad_maximum_fusion.3.lags_ref), custom_call_target="tpu_custom_call" | custom-call | flops 13287555072 | bytes 21495808 | tf_op jit(solution)/shard_map/pallas_call | solution.py:186
  (22 shorter events, 0.4 us)
Async XLA Ops:
  2.3 26.6 %collective-permute-start = (bf16[128,4352]{1,0:T(8,128)(2,1)}, bf16[128,4352]{1,0:T(8,128)(2,1)S(1)}, u32[]{:S(2)}, u32[]{:S(2)}) collective-permute-start(bf16[128,4352]{1,0:T(8,128)(2,1)} %slice.17), channel_id=1, source_target_pairs={{16,0},{17,1},{18,2},{19,3},{20,4},{21,5},{22,6},{23,7},{24,8},{25... | collective-permute-start | bytes 3342344 | tf_op jit(solution)/shard_map/ppermute | solution.py:27
  18.4 8.5 %copy-start.1 = (bf16[128,7680]{1,0:T(8,128)(2,1)S(1)}, bf16[128,7680]{1,0:T(8,128)(2,1)}, u32[]{:S(2)}) copy-start(bf16[128,7680]{1,0:T(8,128)(2,1)} %param.3) | copy-start | bytes 5898244
  26.9 4.4 %copy-start = (bf16[7680,768]{1,0:T(8,128)(2,1)S(1)}, bf16[7680,768]{1,0:T(8,128)(2,1)}, u32[]{:S(2)}) copy-start(bf16[7680,768]{1,0:T(8,128)(2,1)} %shard_map.37) | copy-start | bytes 35389444
  34.4 3.2 %copy-start.2 = (s32[1,1,4,2]{2,3,1,0:T(2,128)S(1)}, s32[1,1,4,2]{2,3,1,0:T(2,128)}, u32[]{:S(2)}) copy-start(s32[1,1,4,2]{2,3,1,0:T(2,128)} %param.5) | copy-start | bytes 100
  35.3 12.5 %collective-permute-start.6 = (bf16[2,128,768]{2,1,0:T(8,128)(2,1)S(1)}, bf16[2,128,768]{2,1,0:T(8,128)(2,1)S(1)}, u32[]{:S(2)}, u32[]{:S(2)}) collective-permute-start(bf16[2,128,768]{2,1,0:T(8,128)(2,1)S(1)} %fusion.7), channel_id=1, source_target_pairs={{4,0},{8,4},{12,8},{5,1},{9,5},{13,9},{6,2},{10,6},{14,10},{7,3},{... | collective-permute-start | bytes 1179656 | tf_op jit(solution)/shard_map/ppermute | solution.py:211
  47.7 11.6 %collective-permute-start.8 = (bf16[2,128,768]{2,1,0:T(8,128)(2,1)S(1)}, bf16[2,128,768]{2,1,0:T(8,128)(2,1)S(1)}, u32[]{:S(2)}, u32[]{:S(2)}) collective-permute-start(bf16[2,128,768]{2,1,0:T(8,128)(2,1)S(1)} %collective-permute-done.6), channel_id=1, source_target_pairs={{4,0},{8,4},{5,1},{9,5},{6,2},{10,6},{7,3},{11,7},{20,16},{24,20},... | collective-permute-start | bytes 1179656 | tf_op jit(solution)/shard_map/ppermute | solution.py:211
  50.1 7.8 %collective-permute-start.1 = (bf16[2,64,768]{2,1,0:T(8,128)(2,1)S(1)}, bf16[2,64,768]{2,1,0:T(8,128)(2,1)S(1)}, u32[]{:S(2)}, u32[]{:S(2)}) collective-permute-start(bf16[2,64,768]{2,1,0:T(8,128)(2,1)S(1)} %get-tuple-element.10), channel_id=1, source_target_pairs={{0,16},{16,0},{1,17},{17,1},{2,18},{18,2},{3,19},{19,3},{4,20},{20... | collective-permute-start | bytes 589832 | tf_op jit(solution)/shard_map/ppermute | solution.py:211
  53.3 10.8 %collective-permute-start.5 = (bf16[2,128,768]{2,1,0:T(8,128)(2,1)S(1)}, bf16[2,128,768]{2,1,0:T(8,128)(2,1)S(1)}, u32[]{:S(2)}, u32[]{:S(2)}) collective-permute-start(bf16[2,128,768]{2,1,0:T(8,128)(2,1)S(1)} %fusion.7), channel_id=1, source_target_pairs={{0,16},{16,0},{1,17},{17,1},{2,18},{18,2},{3,19},{19,3},{4,20},{20... | collective-permute-start | bytes 1179656 | tf_op jit(solution)/shard_map/ppermute | solution.py:211
  58.0 11.9 %collective-permute-start.3 = (bf16[4,64,768]{2,1,0:T(8,128)(2,1)S(1)}, bf16[4,64,768]{2,1,0:T(8,128)(2,1)S(1)}, u32[]{:S(2)}, u32[]{:S(2)}) collective-permute-start(bf16[4,64,768]{2,1,0:T(8,128)(2,1)S(1)} %get-tuple-element.8), channel_id=1, source_target_pairs={{0,2},{1,3},{2,0},{3,1},{4,6},{5,7},{6,4},{7,5},{8,10},{9,11},{10,... | collective-permute-start | bytes 1179656 | tf_op jit(solution)/shard_map/ppermute | solution.py:211
  58.4 13.7 %collective-permute-start.2 = (bf16[4,64,768]{2,1,0:T(8,128)(2,1)S(1)}, bf16[4,64,768]{2,1,0:T(8,128)(2,1)S(1)}, u32[]{:S(2)}, u32[]{:S(2)}) collective-permute-start(bf16[4,64,768]{2,1,0:T(8,128)(2,1)S(1)} %get-tuple-element.8), channel_id=1, source_target_pairs={{0,3},{1,0},{2,1},{3,2},{4,7},{5,4},{6,5},{7,6},{8,11},{9,8},{10,9... | collective-permute-start | bytes 1179656 | tf_op jit(solution)/shard_map/ppermute | solution.py:211
  58.4 13.7 %collective-permute-start.4 = (bf16[4,64,768]{2,1,0:T(8,128)(2,1)S(1)}, bf16[4,64,768]{2,1,0:T(8,128)(2,1)S(1)}, u32[]{:S(2)}, u32[]{:S(2)}) collective-permute-start(bf16[4,64,768]{2,1,0:T(8,128)(2,1)S(1)} %get-tuple-element.8), channel_id=1, source_target_pairs={{0,1},{1,2},{2,3},{3,0},{4,5},{5,6},{6,7},{7,4},{8,9},{9,10},{10,1... | collective-permute-start | bytes 1179656 | tf_op jit(solution)/shard_map/ppermute | solution.py:211
  59.3 11.8 %collective-permute-start.10 = (bf16[2,128,768]{2,1,0:T(8,128)(2,1)S(1)}, bf16[2,128,768]{2,1,0:T(8,128)(2,1)S(1)}, u32[]{:S(2)}, u32[]{:S(2)}) collective-permute-start(bf16[2,128,768]{2,1,0:T(8,128)(2,1)S(1)} %collective-permute-done.8), channel_id=1, source_target_pairs={{4,0},{5,1},{6,2},{7,3},{20,16},{21,17},{22,18},{23,19}} | collective-permute-start | bytes 1179656 | tf_op jit(solution)/shard_map/ppermute | solution.py:211
  64.1 12.0 %collective-permute-start.7 = (bf16[2,128,768]{2,1,0:T(8,128)(2,1)S(1)}, bf16[2,128,768]{2,1,0:T(8,128)(2,1)S(1)}, u32[]{:S(2)}, u32[]{:S(2)}) collective-permute-start(bf16[2,128,768]{2,1,0:T(8,128)(2,1)S(1)} %collective-permute-done.6), channel_id=1, source_target_pairs={{0,16},{16,0},{1,17},{17,1},{2,18},{18,2},{3,19},{19,3},{4,20},{20... | collective-permute-start | bytes 1179656 | tf_op jit(solution)/shard_map/ppermute | solution.py:211
  69.9 14.6 %collective-permute-start.9 = (bf16[2,128,768]{2,1,0:T(8,128)(2,1)S(1)}, bf16[2,128,768]{2,1,0:T(8,128)(2,1)S(1)}, u32[]{:S(2)}, u32[]{:S(2)}) collective-permute-start(bf16[2,128,768]{2,1,0:T(8,128)(2,1)S(1)} %collective-permute-done.8), channel_id=1, source_target_pairs={{0,16},{16,0},{1,17},{17,1},{2,18},{18,2},{3,19},{19,3},{4,20},{20... | collective-permute-start | bytes 1179656 | tf_op jit(solution)/shard_map/ppermute | solution.py:211
  71.2 18.6 %collective-permute-start.11 = (bf16[2,128,768]{2,1,0:T(8,128)(2,1)S(1)}, bf16[2,128,768]{2,1,0:T(8,128)(2,1)S(1)}, u32[]{:S(2)}, u32[]{:S(2)}) collective-permute-start(bf16[2,128,768]{2,1,0:T(8,128)(2,1)S(1)} %collective-permute-done.10), channel_id=1, source_target_pairs={{0,16},{16,0},{1,17},{17,1},{2,18},{18,2},{3,19},{19,3},{4,20},{20... | collective-permute-start | bytes 1179656 | tf_op jit(solution)/shard_map/ppermute | solution.py:211

commit v16 on v15

--- a/solution.py
+++ b/solution.py
@@ -110,7 +110,7 @@
 
 
 ROW_TILE = 16
-J_CHUNK = 64
+J_CHUNK = 32
 F_CHUNK = 128
 
 

time: 156 us -> 156 us (level)
  no operation moved by 1% of the time
where the time goes in v16:
time: 156 us; the launch traced here: 153 us
  Pallas kernels  71.6 us (46%)
  waiting for transfers between devices  39.7 us (25%)
  starting transfers between devices  16.3 us (10%)
  local copies, waits for them, and re-layouts  9.31 us (6%)
  other arithmetic  9.19 us (6%)
  matrix products  3.76 us (2%)
  between operations  3.56 us (2%)
    pallas_call x1, Pallas kernels, all_pairs(): pl.pallas_call(pair_kernel, grid_spec=grid_spec, out_shape=jax.ShapeDtype...  63.1 us
    ppermute x11, waiting for transfers between devices, exchange(): return lax.ppermute(value, axes, pairs)  37.8 us
    ppermute x11, starting transfers between devices, exchange(): return lax.ppermute(value, axes, pairs)  13.8 us
    pallas_call x1, Pallas kernels, forward_table(): pl.pallas_call(table_kernel, grid=(n_coarse // TABLE_Q,), in_specs=[pl.Bl...  8.49 us
    sin x1, other arithmetic, forward_table(): high_sin = jnp.sin(high_angle).reshape(n_coarse, 1, NF)  4.19 us
    dot_general x1, matrix products, on_device(): spectra = jnp.dot(stacked, dft_table, preferred_element_type=jnp.float32)  3.2 us
  transfers between devices with their start and end apart: 12, of which 9 were waited for; matrix products, arithmetic and copies ran while one was open for 9% of the time, Pallas kernels for 6%

profile of v16, /device:TPU:14, one launch (start us, length us, event | category | flops | bytes accessed | tf_op | source)
XLA Modules:
  0.0 153.4 jit_solution(7923706434242825555)
XLA Ops:
  0.0 2.3 %slice.17 = bf16[128,4352]{1,0:T(8,128)(2,1)} slice(bf16[128,7680]{1,0:T(8,128)(2,1)} %param.3), slice={[0:128], [0:4352]} | slice | bytes 2228224 | tf_op jit(solution)/shard_map/slice | solution.py:232
  2.3 2.5 %collective-permute-start = (bf16[128,4352]{1,0:T(8,128)(2,1)}, bf16[128,4352]{1,0:T(8,128)(2,1)S(1)}, u32[]{:S(2)}, u32[]{:S(2)}) collective-permute-start(bf16[128,4352]{1,0:T(8,128)(2,1)} %slice.17), channel_id=1, source_target_pairs={{16,0},{17,1},{18,2},{19,3},{20,4},{21,5},{22,6},{23,7},{24,8},{25... | collective-permute-start | bytes 3342344 | tf_op jit(solution)/shard_map/ppermute | solution.py:27
  5.0 1.6 %fusion.21 = (f32[128,384]{1,0:T(8,128)}, f32[128,384]{1,0:T(8,128)}) fusion(s32[384]{0:T(512)S(1)} %iota_add_fusion), kind=kLoop, calls=%fused_computation.40 | loop fusion | flops 442368 | bytes 394752 | tf_op jit(solution)/shard_map/sin | solution.py:62
  6.5 4.2 %fusion.28 = (f32[60,1,384]{2,1,0:T(1,128)}, f32[60,1,384]{2,1,0:T(1,128)}) fusion(s32[384]{0:T(512)S(1)} %iota_add_fusion, s32[60]{0:T(128)S(1)} %iota_multiply_fusion), kind=kLoop, calls=%fused_computation.48 | loop fusion | flops 207360 | bytes 186096 | tf_op jit(solution)/shard_map/sin | solution.py:61
  10.8 1.4 fusion.39
  15.5 0.7 broadcast_in_dim.9.start_sin_ref
  16.3 0.7 broadcast_in_dim.8.start_cos_ref
  17.0 0.7 broadcast_in_dim.11.step_sin_ref
  17.7 0.7 broadcast_in_dim.10.step_cos_ref
  18.4 8.5 %shard_map.37 = bf16[7680,768]{1,0:T(8,128)(2,1)} custom-call(f32[60,1,384]{2,1,0:T(1,128)} %get-tuple-element.14.high_cos_ref, f32[60,1,384]{2,1,0:T(1,128)} %get-tuple-element.13.high_sin_ref, f32[128,384]{1,0:T(8,128)} %get-tuple-element.16.low_cos_ref, f32[128,384]{1,0:T(8,128)} %get-tuple-element.15.low_sin_ref, ...), custom_call_target="tpu_custom_call" | custom-call | tf_op jit(solution)/shard_map/pallas_call | solution.py:69
  26.9 0.1 constant_dynamic-update-slice_fusion.1
  27.0 1.9 %collective-permute-done = bf16[128,4352]{1,0:T(8,128)(2,1)S(1)} collective-permute-done((bf16[128,4352]{1,0:T(8,128)(2,1)}, bf16[128,4352]{1,0:T(8,128)(2,1)S(1)}, u32[]{:S(2)}, u32[]{:S(2)}) %collective-permute-start) | collective-permute-done | bytes 1114144 | tf_op jit(solution)/shard_map/ppermute | solution.py:27
  28.9 0.1 constant_dynamic-update-slice_fusion
  29.0 1.6 %constant_dynamic-slice_fusion.3 = (bf16[128,7680]{1,0:T(8,128)(2,1)S(1)}, bf16[128,7680]{1,0:T(8,128)(2,1)S(1)}) fusion(bf16[128,12032]{1,0:T(8,128)(2,1)S(1)} %constant_dynamic-update-slice_fusion, s32[]{:T(128)S(6)} %select_n.81, s32[]{:T(128)S(6)} %select_n.83), kind=kLoop, calls=%fused_computation.61 | loop fusion | bytes 7864328 | tf_op jit(solution)/shard_map/dynamic_slice | solution.py:237
  30.6 0.6 copy-done
  31.2 3.2 %fusion = f32[256,768]{1,0:T(8,128)S(1)} fusion(bf16[7680,768]{1,0:T(8,128)(2,1)S(1)} %copy-done, bf16[128,7680]{1,0:T(8,128)(2,1)S(1)} %get-tuple-element.6, bf16[128,7680]{1,0:T(8,128)(2,1)S(1)} %get-tuple-element.5), kind=kOutput, calls=%fused_computation | convolution fusion | flops 3027763200 | bytes 16515072 | tf_op jit(solution)/shard_map/dot_general | solution.py:241
  34.5 0.1 fusion.26
  34.6 0.6 fusion.6
  35.2 0.1 fusion.7
  35.3 2.4 %collective-permute-start.6 = (bf16[2,128,768]{2,1,0:T(8,128)(2,1)S(1)}, bf16[2,128,768]{2,1,0:T(8,128)(2,1)S(1)}, u32[]{:S(2)}, u32[]{:S(2)}) collective-permute-start(bf16[2,128,768]{2,1,0:T(8,128)(2,1)S(1)} %fusion.7), channel_id=1, source_target_pairs={{4,0},{8,4},{12,8},{5,1},{9,5},{13,9},{6,2},{10,6},{14,10},{7,3},{... | collective-permute-start | bytes 1179656 | tf_op jit(solution)/shard_map/ppermute | solution.py:211
  37.7 0.1 copy.6
  37.8 0.1 copy.7
  37.9 9.9 %collective-permute-done.6 = bf16[2,128,768]{2,1,0:T(8,128)(2,1)S(1)} collective-permute-done((bf16[2,128,768]{2,1,0:T(8,128)(2,1)S(1)}, bf16[2,128,768]{2,1,0:T(8,128)(2,1)S(1)}, u32[]{:S(2)}, u32[]{:S(2)}) %collective-permute-start.6) | collective-permute-done | bytes 393248 | tf_op jit(solution)/shard_map/ppermute | solution.py:211
  47.7 2.3 %collective-permute-start.8 = (bf16[2,128,768]{2,1,0:T(8,128)(2,1)S(1)}, bf16[2,128,768]{2,1,0:T(8,128)(2,1)S(1)}, u32[]{:S(2)}, u32[]{:S(2)}) collective-permute-start(bf16[2,128,768]{2,1,0:T(8,128)(2,1)S(1)} %collective-permute-done.6), channel_id=1, source_target_pairs={{4,0},{8,4},{5,1},{9,5},{6,2},{10,6},{7,3},{11,7},{20,16},{24,20},... | collective-permute-start | bytes 1179656 | tf_op jit(solution)/shard_map/ppermute | solution.py:211
  50.1 1.3 collective-permute-start.1
  51.4 1.9 %multiply_convert_fusion.1 = (bf16[384,256]{1,0:T(8,128)(2,1)S(1)}, bf16[384,256]{1,0:T(8,128)(2,1)S(1)}) fusion(s32[256]{0:T(256)S(1)} %and_select_fusion.1, s32[384]{0:T(512)S(1)} %iota_add_fusion), kind=kLoop, calls=%fused_computation.27 | loop fusion | flops 1376256 | bytes 395776 | tf_op jit(solution)/shard_map/convert
  53.3 0.9 collective-permute-start.5
  54.2 3.7 %collective-permute-done.1 = bf16[2,64,768]{2,1,0:T(8,128)(2,1)S(1)} collective-permute-done((bf16[2,64,768]{2,1,0:T(8,128)(2,1)S(1)}, bf16[2,64,768]{2,1,0:T(8,128)(2,1)S(1)}, u32[]{:S(2)}, u32[]{:S(2)}) %collective-permute-start.1) | collective-permute-done | bytes 196640 | tf_op jit(solution)/shard_map/ppermute | solution.py:211
  58.0 0.3 collective-permute-start.3
  58.4 0.5 collective-permute-start.4
  58.9 0.4 collective-permute-done.8
  59.3 2.5 %collective-permute-start.10 = (bf16[2,128,768]{2,1,0:T(8,128)(2,1)S(1)}, bf16[2,128,768]{2,1,0:T(8,128)(2,1)S(1)}, u32[]{:S(2)}, u32[]{:S(2)}) collective-permute-start(bf16[2,128,768]{2,1,0:T(8,128)(2,1)S(1)} %collective-permute-done.8), channel_id=1, source_target_pairs={{4,0},{5,1},{6,2},{7,3},{20,16},{21,17},{22,18},{23,19}} | collective-permute-start | bytes 1179656 | tf_op jit(solution)/shard_map/ppermute | solution.py:211
  61.9 2.1 %collective-permute-done.5 = bf16[2,128,768]{2,1,0:T(8,128)(2,1)S(1)} collective-permute-done((bf16[2,128,768]{2,1,0:T(8,128)(2,1)S(1)}, bf16[2,128,768]{2,1,0:T(8,128)(2,1)S(1)}, u32[]{:S(2)}, u32[]{:S(2)}) %collective-permute-start.5) | collective-permute-done | bytes 393248 | tf_op jit(solution)/shard_map/ppermute | solution.py:211
  64.1 1.4 collective-permute-start.7
  65.5 0.1 pad_add_fusion.pairs_ref
  65.6 4.4 %collective-permute-done.3 = bf16[4,64,768]{2,1,0:T(8,128)(2,1)S(1)} collective-permute-done((bf16[4,64,768]{2,1,0:T(8,128)(2,1)S(1)}, bf16[4,64,768]{2,1,0:T(8,128)(2,1)S(1)}, u32[]{:S(2)}, u32[]{:S(2)}) %collective-permute-start.3) | collective-permute-done | bytes 393248 | tf_op jit(solution)/shard_map/ppermute | solution.py:211
  69.9 1.2 collective-permute-start.9
  71.1 0.1 maximum_bitcast_fusion
  71.2 0.9 collective-permute-start.11
  72.1 0.2 pad_maximum_fusion.1.row_ref
  72.3 3.8 %collective-permute-done.7 = bf16[2,128,768]{2,1,0:T(8,128)(2,1)S(1)} collective-permute-done((bf16[2,128,768]{2,1,0:T(8,128)(2,1)S(1)}, bf16[2,128,768]{2,1,0:T(8,128)(2,1)S(1)}, u32[]{:S(2)}, u32[]{:S(2)}) %collective-permute-start.7) | collective-permute-done | bytes 393248 | tf_op jit(solution)/shard_map/ppermute | solution.py:211
  76.1 0.1 maximum_bitcast_fusion.1
  76.1 8.4 %collective-permute-done.9 = bf16[2,128,768]{2,1,0:T(8,128)(2,1)S(1)} collective-permute-done((bf16[2,128,768]{2,1,0:T(8,128)(2,1)S(1)}, bf16[2,128,768]{2,1,0:T(8,128)(2,1)S(1)}, u32[]{:S(2)}, u32[]{:S(2)}) %collective-permute-start.9) | collective-permute-done | bytes 393248 | tf_op jit(solution)/shard_map/ppermute | solution.py:211
  84.5 0.1 maximum_bitcast_fusion.2
  84.6 5.2 %collective-permute-done.11 = bf16[2,128,768]{2,1,0:T(8,128)(2,1)S(1)} collective-permute-done((bf16[2,128,768]{2,1,0:T(8,128)(2,1)S(1)}, bf16[2,128,768]{2,1,0:T(8,128)(2,1)S(1)}, u32[]{:S(2)}, u32[]{:S(2)}) %collective-permute-start.11) | collective-permute-done | bytes 393248 | tf_op jit(solution)/shard_map/ppermute | solution.py:211
  89.7 0.1 maximum_bitcast_fusion.3
  89.8 0.4 pad_maximum_fusion.col_ref
  90.3 63.1 %shard_map.38 = bf16[4,64,128,256]{3,2,1,0:T(8,128)(2,1)} custom-call(s32[4,2]{1,0:T(4,128)S(1)} %pad_add_fusion.pairs_ref, bf16[4,4,64,768]{3,2,1,0:T(8,128)(2,1)S(1)} %pad_maximum_fusion.1.row_ref, bf16[4,4,128,768]{3,2,1,0:T(8,128)(2,1)S(1)} %pad_maximum_fusion.col_ref, bf16[768,256]{1,0:T(8,128)(2,1)S(1)} %pad_maximum_fusion.3.lags_ref), custom_call_target="tpu_custom_call" | custom-call | flops 13287555072 | bytes 21495808 | tf_op jit(solution)/shard_map/pallas_call | solution.py:186
  (22 shorter events, 0.4 us)
Async XLA Ops:
  2.3 26.6 %collective-permute-start = (bf16[128,4352]{1,0:T(8,128)(2,1)}, bf16[128,4352]{1,0:T(8,128)(2,1)S(1)}, u32[]{:S(2)}, u32[]{:S(2)}) collective-permute-start(bf16[128,4352]{1,0:T(8,128)(2,1)} %slice.17), channel_id=1, source_target_pairs={{16,0},{17,1},{18,2},{19,3},{20,4},{21,5},{22,6},{23,7},{24,8},{25... | collective-permute-start | bytes 3342344 | tf_op jit(solution)/shard_map/ppermute | solution.py:27
  18.4 8.5 %copy-start.1 = (bf16[128,7680]{1,0:T(8,128)(2,1)S(1)}, bf16[128,7680]{1,0:T(8,128)(2,1)}, u32[]{:S(2)}) copy-start(bf16[128,7680]{1,0:T(8,128)(2,1)} %param.3) | copy-start | bytes 5898244
  26.9 4.4 %copy-start = (bf16[7680,768]{1,0:T(8,128)(2,1)S(1)}, bf16[7680,768]{1,0:T(8,128)(2,1)}, u32[]{:S(2)}) copy-start(bf16[7680,768]{1,0:T(8,128)(2,1)} %shard_map.37) | copy-start | bytes 35389444
  34.4 3.2 %copy-start.2 = (s32[1,1,4,2]{2,3,1,0:T(2,128)S(1)}, s32[1,1,4,2]{2,3,1,0:T(2,128)}, u32[]{:S(2)}) copy-start(s32[1,1,4,2]{2,3,1,0:T(2,128)} %param.5) | copy-start | bytes 100
  35.3 12.5 %collective-permute-start.6 = (bf16[2,128,768]{2,1,0:T(8,128)(2,1)S(1)}, bf16[2,128,768]{2,1,0:T(8,128)(2,1)S(1)}, u32[]{:S(2)}, u32[]{:S(2)}) collective-permute-start(bf16[2,128,768]{2,1,0:T(8,128)(2,1)S(1)} %fusion.7), channel_id=1, source_target_pairs={{4,0},{8,4},{12,8},{5,1},{9,5},{13,9},{6,2},{10,6},{14,10},{7,3},{... | collective-permute-start | bytes 1179656 | tf_op jit(solution)/shard_map/ppermute | solution.py:211
  47.7 11.6 %collective-permute-start.8 = (bf16[2,128,768]{2,1,0:T(8,128)(2,1)S(1)}, bf16[2,128,768]{2,1,0:T(8,128)(2,1)S(1)}, u32[]{:S(2)}, u32[]{:S(2)}) collective-permute-start(bf16[2,128,768]{2,1,0:T(8,128)(2,1)S(1)} %collective-permute-done.6), channel_id=1, source_target_pairs={{4,0},{8,4},{5,1},{9,5},{6,2},{10,6},{7,3},{11,7},{20,16},{24,20},... | collective-permute-start | bytes 1179656 | tf_op jit(solution)/shard_map/ppermute | solution.py:211
  50.1 7.8 %collective-permute-start.1 = (bf16[2,64,768]{2,1,0:T(8,128)(2,1)S(1)}, bf16[2,64,768]{2,1,0:T(8,128)(2,1)S(1)}, u32[]{:S(2)}, u32[]{:S(2)}) collective-permute-start(bf16[2,64,768]{2,1,0:T(8,128)(2,1)S(1)} %get-tuple-element.10), channel_id=1, source_target_pairs={{0,16},{16,0},{1,17},{17,1},{2,18},{18,2},{3,19},{19,3},{4,20},{20... | collective-permute-start | bytes 589832 | tf_op jit(solution)/shard_map/ppermute | solution.py:211
  53.3 10.8 %collective-permute-start.5 = (bf16[2,128,768]{2,1,0:T(8,128)(2,1)S(1)}, bf16[2,128,768]{2,1,0:T(8,128)(2,1)S(1)}, u32[]{:S(2)}, u32[]{:S(2)}) collective-permute-start(bf16[2,128,768]{2,1,0:T(8,128)(2,1)S(1)} %fusion.7), channel_id=1, source_target_pairs={{0,16},{16,0},{1,17},{17,1},{2,18},{18,2},{3,19},{19,3},{4,20},{20... | collective-permute-start | bytes 1179656 | tf_op jit(solution)/shard_map/ppermute | solution.py:211
  58.0 11.9 %collective-permute-start.3 = (bf16[4,64,768]{2,1,0:T(8,128)(2,1)S(1)}, bf16[4,64,768]{2,1,0:T(8,128)(2,1)S(1)}, u32[]{:S(2)}, u32[]{:S(2)}) collective-permute-start(bf16[4,64,768]{2,1,0:T(8,128)(2,1)S(1)} %get-tuple-element.8), channel_id=1, source_target_pairs={{0,2},{1,3},{2,0},{3,1},{4,6},{5,7},{6,4},{7,5},{8,10},{9,11},{10,... | collective-permute-start | bytes 1179656 | tf_op jit(solution)/shard_map/ppermute | solution.py:211
  58.4 13.7 %collective-permute-start.2 = (bf16[4,64,768]{2,1,0:T(8,128)(2,1)S(1)}, bf16[4,64,768]{2,1,0:T(8,128)(2,1)S(1)}, u32[]{:S(2)}, u32[]{:S(2)}) collective-permute-start(bf16[4,64,768]{2,1,0:T(8,128)(2,1)S(1)} %get-tuple-element.8), channel_id=1, source_target_pairs={{0,3},{1,0},{2,1},{3,2},{4,7},{5,4},{6,5},{7,6},{8,11},{9,8},{10,9... | collective-permute-start | bytes 1179656 | tf_op jit(solution)/shard_map/ppermute | solution.py:211
  58.4 13.7 %collective-permute-start.4 = (bf16[4,64,768]{2,1,0:T(8,128)(2,1)S(1)}, bf16[4,64,768]{2,1,0:T(8,128)(2,1)S(1)}, u32[]{:S(2)}, u32[]{:S(2)}) collective-permute-start(bf16[4,64,768]{2,1,0:T(8,128)(2,1)S(1)} %get-tuple-element.8), channel_id=1, source_target_pairs={{0,1},{1,2},{2,3},{3,0},{4,5},{5,6},{6,7},{7,4},{8,9},{9,10},{10,1... | collective-permute-start | bytes 1179656 | tf_op jit(solution)/shard_map/ppermute | solution.py:211
  59.3 11.8 %collective-permute-start.10 = (bf16[2,128,768]{2,1,0:T(8,128)(2,1)S(1)}, bf16[2,128,768]{2,1,0:T(8,128)(2,1)S(1)}, u32[]{:S(2)}, u32[]{:S(2)}) collective-permute-start(bf16[2,128,768]{2,1,0:T(8,128)(2,1)S(1)} %collective-permute-done.8), channel_id=1, source_target_pairs={{4,0},{5,1},{6,2},{7,3},{20,16},{21,17},{22,18},{23,19}} | collective-permute-start | bytes 1179656 | tf_op jit(solution)/shard_map/ppermute | solution.py:211
  64.1 12.0 %collective-permute-start.7 = (bf16[2,128,768]{2,1,0:T(8,128)(2,1)S(1)}, bf16[2,128,768]{2,1,0:T(8,128)(2,1)S(1)}, u32[]{:S(2)}, u32[]{:S(2)}) collective-permute-start(bf16[2,128,768]{2,1,0:T(8,128)(2,1)S(1)} %collective-permute-done.6), channel_id=1, source_target_pairs={{0,16},{16,0},{1,17},{17,1},{2,18},{18,2},{3,19},{19,3},{4,20},{20... | collective-permute-start | bytes 1179656 | tf_op jit(solution)/shard_map/ppermute | solution.py:211
  69.9 14.6 %collective-permute-start.9 = (bf16[2,128,768]{2,1,0:T(8,128)(2,1)S(1)}, bf16[2,128,768]{2,1,0:T(8,128)(2,1)S(1)}, u32[]{:S(2)}, u32[]{:S(2)}) collective-permute-start(bf16[2,128,768]{2,1,0:T(8,128)(2,1)S(1)} %collective-permute-done.8), channel_id=1, source_target_pairs={{0,16},{16,0},{1,17},{17,1},{2,18},{18,2},{3,19},{19,3},{4,20},{20... | collective-permute-start | bytes 1179656 | tf_op jit(solution)/shard_map/ppermute | solution.py:211
  71.2 18.6 %collective-permute-start.11 = (bf16[2,128,768]{2,1,0:T(8,128)(2,1)S(1)}, bf16[2,128,768]{2,1,0:T(8,128)(2,1)S(1)}, u32[]{:S(2)}, u32[]{:S(2)}) collective-permute-start(bf16[2,128,768]{2,1,0:T(8,128)(2,1)S(1)} %collective-permute-done.10), channel_id=1, source_target_pairs={{0,16},{16,0},{1,17},{17,1},{2,18},{18,2},{3,19},{19,3},{4,20},{20... | collective-permute-start | bytes 1179656 | tf_op jit(solution)/shard_map/ppermute | solution.py:211

commit v17 on v16

--- a/solution.py
+++ b/solution.py
@@ -110,8 +110,8 @@
 
 
 ROW_TILE = 16
-J_CHUNK = 32
-F_CHUNK = 128
+J_CHUNK = 16
+F_CHUNK = 384
 
 
 def pair_kernel(pairs_ref, row_ref, col_ref, lags_ref, out_ref, cross_ref, row32_ref, col32_ref):

time: 156 us -> 151 us (0.968)
  Pallas kernels: 71.6 us -> 67.6 us
    pallas_call x1, Pallas kernels: 63.1 us -> 58.2 us  [all_pairs(): pl.pallas_call(pair_kernel, grid_spec=grid_spec, out_shape=jax.ShapeDtype...]
  transfers between devices with their start and end apart: 12 -> 12, of which waited for: 9 -> 11; matrix products, arithmetic and copies ran while one was open for 9% -> 9% of each run, Pallas kernels for 6% -> 6%
where the time goes in v17:
time: 151 us; the launch traced here: 150 us
  Pallas kernels  67.6 us (45%)
  waiting for transfers between devices  39.8 us (26%)
  starting transfers between devices  15 us (10%)
  local copies, waits for them, and re-layouts  10.7 us (7%)
  other arithmetic  9.21 us (6%)
  matrix products  3.76 us (2%)
  between operations  3.55 us (2%)
    pallas_call x1, Pallas kernels, all_pairs(): pl.pallas_call(pair_kernel, grid_spec=grid_spec, out_shape=jax.ShapeDtype...  58.2 us
    ppermute x11, waiting for transfers between devices, exchange(): return lax.ppermute(value, axes, pairs)  39.1 us
    ppermute x11, starting transfers between devices, exchange(): return lax.ppermute(value, axes, pairs)  12.5 us
    pallas_call x1, Pallas kernels, forward_table(): pl.pallas_call(table_kernel, grid=(n_coarse // TABLE_Q,), in_specs=[pl.Bl...  9.44 us
    sin x1, other arithmetic, forward_table(): high_sin = jnp.sin(high_angle).reshape(n_coarse, 1, NF)  4.19 us
    dot_general x1, matrix products, on_device(): spectra = jnp.dot(stacked, dft_table, preferred_element_type=jnp.float32)  3.2 us
  transfers between devices with their start and end apart: 12, of which 11 were waited for; matrix products, arithmetic and copies ran while one was open for 9% of the time, Pallas kernels for 6%

profile of v17, /device:TPU:14, one launch (start us, length us, event | category | flops | bytes accessed | tf_op | source)
XLA Modules:
  0.0 149.6 jit_solution(13162319296669865297)
XLA Ops:
  0.0 2.3 %slice.17 = bf16[128,4352]{1,0:T(8,128)(2,1)} slice(bf16[128,7680]{1,0:T(8,128)(2,1)} %param.3), slice={[0:128], [0:4352]} | slice | bytes 2228224 | tf_op jit(solution)/shard_map/slice | solution.py:232
  2.3 2.5 %collective-permute-start = (bf16[128,4352]{1,0:T(8,128)(2,1)}, bf16[128,4352]{1,0:T(8,128)(2,1)S(1)}, u32[]{:S(2)}, u32[]{:S(2)}) collective-permute-start(bf16[128,4352]{1,0:T(8,128)(2,1)} %slice.17), channel_id=1, source_target_pairs={{16,0},{17,1},{18,2},{19,3},{20,4},{21,5},{22,6},{23,7},{24,8},{25... | collective-permute-start | bytes 3342344 | tf_op jit(solution)/shard_map/ppermute | solution.py:27
  5.0 1.6 %fusion.21 = (f32[128,384]{1,0:T(8,128)}, f32[128,384]{1,0:T(8,128)}) fusion(s32[384]{0:T(512)S(1)} %iota_add_fusion), kind=kLoop, calls=%fused_computation.40 | loop fusion | flops 442368 | bytes 394752 | tf_op jit(solution)/shard_map/sin | solution.py:62
  6.5 4.2 %fusion.28 = (f32[60,1,384]{2,1,0:T(1,128)}, f32[60,1,384]{2,1,0:T(1,128)}) fusion(s32[384]{0:T(512)S(1)} %iota_add_fusion, s32[60]{0:T(128)S(1)} %iota_multiply_fusion), kind=kLoop, calls=%fused_computation.48 | loop fusion | flops 207360 | bytes 186096 | tf_op jit(solution)/shard_map/sin | solution.py:61
  10.8 1.4 fusion.39
  15.5 0.8 broadcast_in_dim.9.start_sin_ref
  16.3 0.8 broadcast_in_dim.8.start_cos_ref
  17.1 0.8 broadcast_in_dim.11.step_sin_ref
  17.8 0.8 broadcast_in_dim.10.step_cos_ref
  18.6 9.4 %shard_map.37 = bf16[7680,768]{1,0:T(8,128)(2,1)} custom-call(f32[60,1,384]{2,1,0:T(1,128)} %get-tuple-element.14.high_cos_ref, f32[60,1,384]{2,1,0:T(1,128)} %get-tuple-element.13.high_sin_ref, f32[128,384]{1,0:T(8,128)} %get-tuple-element.16.low_cos_ref, f32[128,384]{1,0:T(8,128)} %get-tuple-element.15.low_sin_ref, ...), custom_call_target="tpu_custom_call" | custom-call | tf_op jit(solution)/shard_map/pallas_call | solution.py:69
  28.0 0.1 constant_dynamic-update-slice_fusion.1
  28.2 0.7 collective-permute-done
  28.9 0.1 constant_dynamic-update-slice_fusion
  29.0 1.6 %constant_dynamic-slice_fusion.3 = (bf16[128,7680]{1,0:T(8,128)(2,1)S(1)}, bf16[128,7680]{1,0:T(8,128)(2,1)S(1)}) fusion(bf16[128,12032]{1,0:T(8,128)(2,1)S(1)} %constant_dynamic-update-slice_fusion, s32[]{:T(128)S(6)} %select_n.81, s32[]{:T(128)S(6)} %select_n.83), kind=kLoop, calls=%fused_computation.61 | loop fusion | bytes 7864328 | tf_op jit(solution)/shard_map/dynamic_slice | solution.py:237
  30.6 1.8 %copy-done = bf16[7680,768]{1,0:T(8,128)(2,1)S(1)} copy-done((bf16[7680,768]{1,0:T(8,128)(2,1)S(1)}, bf16[7680,768]{1,0:T(8,128)(2,1)}, u32[]{:S(2)}) %copy-start) | copy-done | bytes 11796504
  32.4 3.2 %fusion = f32[256,768]{1,0:T(8,128)S(1)} fusion(bf16[7680,768]{1,0:T(8,128)(2,1)S(1)} %copy-done, bf16[128,7680]{1,0:T(8,128)(2,1)S(1)} %get-tuple-element.6, bf16[128,7680]{1,0:T(8,128)(2,1)S(1)} %get-tuple-element.5), kind=kOutput, calls=%fused_computation | convolution fusion | flops 3027763200 | bytes 16515072 | tf_op jit(solution)/shard_map/dot_general | solution.py:241
  35.6 0.1 fusion.26
  35.7 0.6 fusion.6
  36.3 0.1 fusion.7
  36.4 2.4 %collective-permute-start.6 = (bf16[2,128,768]{2,1,0:T(8,128)(2,1)S(1)}, bf16[2,128,768]{2,1,0:T(8,128)(2,1)S(1)}, u32[]{:S(2)}, u32[]{:S(2)}) collective-permute-start(bf16[2,128,768]{2,1,0:T(8,128)(2,1)S(1)} %fusion.7), channel_id=1, source_target_pairs={{4,0},{8,4},{12,8},{5,1},{9,5},{13,9},{6,2},{10,6},{14,10},{7,3},{... | collective-permute-start | bytes 1179656 | tf_op jit(solution)/shard_map/ppermute | solution.py:211
  38.8 0.1 copy.6
  38.9 0.1 copy.7
  39.0 9.9 %collective-permute-done.6 = bf16[2,128,768]{2,1,0:T(8,128)(2,1)S(1)} collective-permute-done((bf16[2,128,768]{2,1,0:T(8,128)(2,1)S(1)}, bf16[2,128,768]{2,1,0:T(8,128)(2,1)S(1)}, u32[]{:S(2)}, u32[]{:S(2)}) %collective-permute-start.6) | collective-permute-done | bytes 393248 | tf_op jit(solution)/shard_map/ppermute | solution.py:211
  48.9 2.3 %collective-permute-start.8 = (bf16[2,128,768]{2,1,0:T(8,128)(2,1)S(1)}, bf16[2,128,768]{2,1,0:T(8,128)(2,1)S(1)}, u32[]{:S(2)}, u32[]{:S(2)}) collective-permute-start(bf16[2,128,768]{2,1,0:T(8,128)(2,1)S(1)} %collective-permute-done.6), channel_id=1, source_target_pairs={{4,0},{8,4},{5,1},{9,5},{6,2},{10,6},{7,3},{11,7},{20,16},{24,20},... | collective-permute-start | bytes 1179656 | tf_op jit(solution)/shard_map/ppermute | solution.py:211
  51.3 0.1 collective-permute-start.1
  51.4 2.0 %multiply_convert_fusion.1 = (bf16[384,256]{1,0:T(8,128)(2,1)S(1)}, bf16[384,256]{1,0:T(8,128)(2,1)S(1)}) fusion(s32[256]{0:T(256)S(1)} %and_select_fusion.1, s32[384]{0:T(512)S(1)} %iota_add_fusion), kind=kLoop, calls=%fused_computation.27 | loop fusion | flops 1376256 | bytes 395776 | tf_op jit(solution)/shard_map/convert
  53.3 2.1 %collective-permute-start.5 = (bf16[2,128,768]{2,1,0:T(8,128)(2,1)S(1)}, bf16[2,128,768]{2,1,0:T(8,128)(2,1)S(1)}, u32[]{:S(2)}, u32[]{:S(2)}) collective-permute-start(bf16[2,128,768]{2,1,0:T(8,128)(2,1)S(1)} %fusion.7), channel_id=1, source_target_pairs={{0,16},{16,0},{1,17},{17,1},{2,18},{18,2},{3,19},{19,3},{4,20},{20... | collective-permute-start | bytes 1179656 | tf_op jit(solution)/shard_map/ppermute | solution.py:211
  55.4 3.7 %collective-permute-done.1 = bf16[2,64,768]{2,1,0:T(8,128)(2,1)S(1)} collective-permute-done((bf16[2,64,768]{2,1,0:T(8,128)(2,1)S(1)}, bf16[2,64,768]{2,1,0:T(8,128)(2,1)S(1)}, u32[]{:S(2)}, u32[]{:S(2)}) %collective-permute-start.1) | collective-permute-done | bytes 196640 | tf_op jit(solution)/shard_map/ppermute | solution.py:211
  59.2 0.4 collective-permute-start.3
  59.6 0.5 collective-permute-start.4
  60.1 0.4 collective-permute-done.8
  60.5 2.6 %collective-permute-start.10 = (bf16[2,128,768]{2,1,0:T(8,128)(2,1)S(1)}, bf16[2,128,768]{2,1,0:T(8,128)(2,1)S(1)}, u32[]{:S(2)}, u32[]{:S(2)}) collective-permute-start(bf16[2,128,768]{2,1,0:T(8,128)(2,1)S(1)} %collective-permute-done.8), channel_id=1, source_target_pairs={{4,0},{5,1},{6,2},{7,3},{20,16},{21,17},{22,18},{23,19}} | collective-permute-start | bytes 1179656 | tf_op jit(solution)/shard_map/ppermute | solution.py:211
  63.1 1.9 %collective-permute-done.5 = bf16[2,128,768]{2,1,0:T(8,128)(2,1)S(1)} collective-permute-done((bf16[2,128,768]{2,1,0:T(8,128)(2,1)S(1)}, bf16[2,128,768]{2,1,0:T(8,128)(2,1)S(1)}, u32[]{:S(2)}, u32[]{:S(2)}) %collective-permute-start.5) | collective-permute-done | bytes 393248 | tf_op jit(solution)/shard_map/ppermute | solution.py:211
  65.0 0.5 collective-permute-start.7
  65.5 0.1 pad_add_fusion.pairs_ref
  65.5 5.5 %collective-permute-done.3 = bf16[4,64,768]{2,1,0:T(8,128)(2,1)S(1)} collective-permute-done((bf16[4,64,768]{2,1,0:T(8,128)(2,1)S(1)}, bf16[4,64,768]{2,1,0:T(8,128)(2,1)S(1)}, u32[]{:S(2)}, u32[]{:S(2)}) %collective-permute-start.3) | collective-permute-done | bytes 393248 | tf_op jit(solution)/shard_map/ppermute | solution.py:211
  71.1 0.1 maximum_bitcast_fusion
  71.1 0.3 collective-permute-done.10
  71.5 1.8 %collective-permute-start.11 = (bf16[2,128,768]{2,1,0:T(8,128)(2,1)S(1)}, bf16[2,128,768]{2,1,0:T(8,128)(2,1)S(1)}, u32[]{:S(2)}, u32[]{:S(2)}) collective-permute-start(bf16[2,128,768]{2,1,0:T(8,128)(2,1)S(1)} %collective-permute-done.10), channel_id=1, source_target_pairs={{0,16},{16,0},{1,17},{17,1},{2,18},{18,2},{3,19},{19,3},{4,20},{20... | collective-permute-start | bytes 1179656 | tf_op jit(solution)/shard_map/ppermute | solution.py:211
  73.2 0.1 collective-permute-done.2
  73.3 0.2 pad_maximum_fusion.1.row_ref
  73.5 3.5 %collective-permute-done.7 = bf16[2,128,768]{2,1,0:T(8,128)(2,1)S(1)} collective-permute-done((bf16[2,128,768]{2,1,0:T(8,128)(2,1)S(1)}, bf16[2,128,768]{2,1,0:T(8,128)(2,1)S(1)}, u32[]{:S(2)}, u32[]{:S(2)}) %collective-permute-start.7) | collective-permute-done | bytes 393248 | tf_op jit(solution)/shard_map/ppermute | solution.py:211
  77.0 0.1 maximum_bitcast_fusion.1
  77.1 8.4 %collective-permute-done.9 = bf16[2,128,768]{2,1,0:T(8,128)(2,1)S(1)} collective-permute-done((bf16[2,128,768]{2,1,0:T(8,128)(2,1)S(1)}, bf16[2,128,768]{2,1,0:T(8,128)(2,1)S(1)}, u32[]{:S(2)}, u32[]{:S(2)}) %collective-permute-start.9) | collective-permute-done | bytes 393248 | tf_op jit(solution)/shard_map/ppermute | solution.py:211
  85.4 0.1 maximum_bitcast_fusion.2
  85.5 5.4 %collective-permute-done.11 = bf16[2,128,768]{2,1,0:T(8,128)(2,1)S(1)} collective-permute-done((bf16[2,128,768]{2,1,0:T(8,128)(2,1)S(1)}, bf16[2,128,768]{2,1,0:T(8,128)(2,1)S(1)}, u32[]{:S(2)}, u32[]{:S(2)}) %collective-permute-start.11) | collective-permute-done | bytes 393248 | tf_op jit(solution)/shard_map/ppermute | solution.py:211
  91.0 0.4 pad_maximum_fusion.col_ref
  91.4 58.2 %shard_map.38 = bf16[4,64,128,256]{3,2,1,0:T(8,128)(2,1)} custom-call(s32[4,2]{1,0:T(4,128)S(1)} %pad_add_fusion.pairs_ref, bf16[4,4,64,768]{3,2,1,0:T(8,128)(2,1)S(1)} %pad_maximum_fusion.1.row_ref, bf16[4,4,128,768]{3,2,1,0:T(8,128)(2,1)S(1)} %pad_maximum_fusion.col_ref, bf16[768,256]{1,0:T(8,128)(2,1)S(1)} %pad_maximum_fusion.3.lags_ref), custom_call_target="tpu_custom_call" | custom-call | flops 13287555072 | bytes 21495808 | tf_op jit(solution)/shard_map/pallas_call | solution.py:186
  (22 shorter events, 0.4 us)
Async XLA Ops:
  2.3 26.6 %collective-permute-start = (bf16[128,4352]{1,0:T(8,128)(2,1)}, bf16[128,4352]{1,0:T(8,128)(2,1)S(1)}, u32[]{:S(2)}, u32[]{:S(2)}) collective-permute-start(bf16[128,4352]{1,0:T(8,128)(2,1)} %slice.17), channel_id=1, source_target_pairs={{16,0},{17,1},{18,2},{19,3},{20,4},{21,5},{22,6},{23,7},{24,8},{25... | collective-permute-start | bytes 3342344 | tf_op jit(solution)/shard_map/ppermute | solution.py:27
  18.6 9.4 %copy-start.1 = (bf16[128,7680]{1,0:T(8,128)(2,1)S(1)}, bf16[128,7680]{1,0:T(8,128)(2,1)}, u32[]{:S(2)}) copy-start(bf16[128,7680]{1,0:T(8,128)(2,1)} %param.3) | copy-start | bytes 5898244
  28.0 4.4 %copy-start = (bf16[7680,768]{1,0:T(8,128)(2,1)S(1)}, bf16[7680,768]{1,0:T(8,128)(2,1)}, u32[]{:S(2)}) copy-start(bf16[7680,768]{1,0:T(8,128)(2,1)} %shard_map.37) | copy-start | bytes 35389444
  35.6 3.2 %copy-start.2 = (s32[1,1,4,2]{2,3,1,0:T(2,128)S(1)}, s32[1,1,4,2]{2,3,1,0:T(2,128)}, u32[]{:S(2)}) copy-start(s32[1,1,4,2]{2,3,1,0:T(2,128)} %param.5) | copy-start | bytes 100
  36.4 12.5 %collective-permute-start.6 = (bf16[2,128,768]{2,1,0:T(8,128)(2,1)S(1)}, bf16[2,128,768]{2,1,0:T(8,128)(2,1)S(1)}, u32[]{:S(2)}, u32[]{:S(2)}) collective-permute-start(bf16[2,128,768]{2,1,0:T(8,128)(2,1)S(1)} %fusion.7), channel_id=1, source_target_pairs={{4,0},{8,4},{12,8},{5,1},{9,5},{13,9},{6,2},{10,6},{14,10},{7,3},{... | collective-permute-start | bytes 1179656 | tf_op jit(solution)/shard_map/ppermute | solution.py:211
  48.9 11.6 %collective-permute-start.8 = (bf16[2,128,768]{2,1,0:T(8,128)(2,1)S(1)}, bf16[2,128,768]{2,1,0:T(8,128)(2,1)S(1)}, u32[]{:S(2)}, u32[]{:S(2)}) collective-permute-start(bf16[2,128,768]{2,1,0:T(8,128)(2,1)S(1)} %collective-permute-done.6), channel_id=1, source_target_pairs={{4,0},{8,4},{5,1},{9,5},{6,2},{10,6},{7,3},{11,7},{20,16},{24,20},... | collective-permute-start | bytes 1179656 | tf_op jit(solution)/shard_map/ppermute | solution.py:211
  51.3 7.8 %collective-permute-start.1 = (bf16[2,64,768]{2,1,0:T(8,128)(2,1)S(1)}, bf16[2,64,768]{2,1,0:T(8,128)(2,1)S(1)}, u32[]{:S(2)}, u32[]{:S(2)}) collective-permute-start(bf16[2,64,768]{2,1,0:T(8,128)(2,1)S(1)} %get-tuple-element.10), channel_id=1, source_target_pairs={{0,16},{16,0},{1,17},{17,1},{2,18},{18,2},{3,19},{19,3},{4,20},{20... | collective-permute-start | bytes 589832 | tf_op jit(solution)/shard_map/ppermute | solution.py:211
  53.3 11.7 %collective-permute-start.5 = (bf16[2,128,768]{2,1,0:T(8,128)(2,1)S(1)}, bf16[2,128,768]{2,1,0:T(8,128)(2,1)S(1)}, u32[]{:S(2)}, u32[]{:S(2)}) collective-permute-start(bf16[2,128,768]{2,1,0:T(8,128)(2,1)S(1)} %fusion.7), channel_id=1, source_target_pairs={{0,16},{16,0},{1,17},{17,1},{2,18},{18,2},{3,19},{19,3},{4,20},{20... | collective-permute-start | bytes 1179656 | tf_op jit(solution)/shard_map/ppermute | solution.py:211
  59.2 11.9 %collective-permute-start.3 = (bf16[4,64,768]{2,1,0:T(8,128)(2,1)S(1)}, bf16[4,64,768]{2,1,0:T(8,128)(2,1)S(1)}, u32[]{:S(2)}, u32[]{:S(2)}) collective-permute-start(bf16[4,64,768]{2,1,0:T(8,128)(2,1)S(1)} %get-tuple-element.8), channel_id=1, source_target_pairs={{0,2},{1,3},{2,0},{3,1},{4,6},{5,7},{6,4},{7,5},{8,10},{9,11},{10,... | collective-permute-start | bytes 1179656 | tf_op jit(solution)/shard_map/ppermute | solution.py:211
  59.6 13.7 %collective-permute-start.2 = (bf16[4,64,768]{2,1,0:T(8,128)(2,1)S(1)}, bf16[4,64,768]{2,1,0:T(8,128)(2,1)S(1)}, u32[]{:S(2)}, u32[]{:S(2)}) collective-permute-start(bf16[4,64,768]{2,1,0:T(8,128)(2,1)S(1)} %get-tuple-element.8), channel_id=1, source_target_pairs={{0,3},{1,0},{2,1},{3,2},{4,7},{5,4},{6,5},{7,6},{8,11},{9,8},{10,9... | collective-permute-start | bytes 1179656 | tf_op jit(solution)/shard_map/ppermute | solution.py:211
  59.6 13.7 %collective-permute-start.4 = (bf16[4,64,768]{2,1,0:T(8,128)(2,1)S(1)}, bf16[4,64,768]{2,1,0:T(8,128)(2,1)S(1)}, u32[]{:S(2)}, u32[]{:S(2)}) collective-permute-start(bf16[4,64,768]{2,1,0:T(8,128)(2,1)S(1)} %get-tuple-element.8), channel_id=1, source_target_pairs={{0,1},{1,2},{2,3},{3,0},{4,5},{5,6},{6,7},{7,4},{8,9},{9,10},{10,1... | collective-permute-start | bytes 1179656 | tf_op jit(solution)/shard_map/ppermute | solution.py:211
  60.5 11.0 %collective-permute-start.10 = (bf16[2,128,768]{2,1,0:T(8,128)(2,1)S(1)}, bf16[2,128,768]{2,1,0:T(8,128)(2,1)S(1)}, u32[]{:S(2)}, u32[]{:S(2)}) collective-permute-start(bf16[2,128,768]{2,1,0:T(8,128)(2,1)S(1)} %collective-permute-done.8), channel_id=1, source_target_pairs={{4,0},{5,1},{6,2},{7,3},{20,16},{21,17},{22,18},{23,19}} | collective-permute-start | bytes 1179656 | tf_op jit(solution)/shard_map/ppermute | solution.py:211
  65.0 12.0 %collective-permute-start.7 = (bf16[2,128,768]{2,1,0:T(8,128)(2,1)S(1)}, bf16[2,128,768]{2,1,0:T(8,128)(2,1)S(1)}, u32[]{:S(2)}, u32[]{:S(2)}) collective-permute-start(bf16[2,128,768]{2,1,0:T(8,128)(2,1)S(1)} %collective-permute-done.6), channel_id=1, source_target_pairs={{0,16},{16,0},{1,17},{17,1},{2,18},{18,2},{3,19},{19,3},{4,20},{20... | collective-permute-start | bytes 1179656 | tf_op jit(solution)/shard_map/ppermute | solution.py:211
  71.1 14.4 %collective-permute-start.9 = (bf16[2,128,768]{2,1,0:T(8,128)(2,1)S(1)}, bf16[2,128,768]{2,1,0:T(8,128)(2,1)S(1)}, u32[]{:S(2)}, u32[]{:S(2)}) collective-permute-start(bf16[2,128,768]{2,1,0:T(8,128)(2,1)S(1)} %collective-permute-done.8), channel_id=1, source_target_pairs={{0,16},{16,0},{1,17},{17,1},{2,18},{18,2},{3,19},{19,3},{4,20},{20... | collective-permute-start | bytes 1179656 | tf_op jit(solution)/shard_map/ppermute | solution.py:211
  71.5 19.4 %collective-permute-start.11 = (bf16[2,128,768]{2,1,0:T(8,128)(2,1)S(1)}, bf16[2,128,768]{2,1,0:T(8,128)(2,1)S(1)}, u32[]{:S(2)}, u32[]{:S(2)}) collective-permute-start(bf16[2,128,768]{2,1,0:T(8,128)(2,1)S(1)} %collective-permute-done.10), channel_id=1, source_target_pairs={{0,16},{16,0},{1,17},{17,1},{2,18},{18,2},{3,19},{19,3},{4,20},{20... | collective-permute-start | bytes 1179656 | tf_op jit(solution)/shard_map/ppermute | solution.py:211
